TPU v7x, 32 devices: a whole 2x2x4 slice. The times are simulated.
32 devices in a mesh: groups: 2 (over y), seq: 4 (over z), head: 4 (over x, core).
Axes of the slice: x: 2, y: 2, z: 4, core: 2. Of those that a mesh axis runs over, the one named last changes fastest.
Arguments:
- inner_acts: bfloat16 [4096, 2560], P(('groups', 'seq'), 'head'), parts along dimension 0, may hold values from -64 to 64
- gate_acts: bfloat16 [4096, 2560], P(('groups', 'seq'), 'head'), parts along dimension 0, may hold values from -6 to 6
- write_map: bfloat16 [2, 4096, 128], P(None, ('groups', 'seq')), parts along dimension 1, may hold values from -6 to 6
- read_map: bfloat16 [2, 4096, 128], P(None, ('groups', 'seq')), parts along dimension 1, may hold values from -0.5 to 0.5
- step_raw: float32 [2, 4096, 40], P(None, ('groups', 'seq'), 'head'), parts along dimension 1, may hold values from -3 to 90.50967
- step_bias: float32 [40], P('head'), may hold values from -7 to -1
- decay_log: float32 [40], P('head'), may hold values from -9 to -1
- skip_gain: float32 [40], P('head'), may hold values from 0.5 to 2
- norm_gain: float32 [2560], P('head'), may hold values from 0.5 to 1.5
- out_weight: bfloat16 [2560, 2560], P('head'), may hold values from -0.125 to 0.125
- residual: bfloat16 [4096, 2560], P(('groups', 'seq'), 'head'), parts along dimension 0, may hold values from -58 to 58
- final_gain: float32 [2560], replicated, may hold values from 0.5 to 1.5
- key_weight: bfloat16 [2560, 2048], P(None, 'head'), may hold values from -0.125 to 0.125
- value_weight: bfloat16 [2560, 2048], P(None, 'head'), may hold values from -0.125 to 0.125
Outputs:
- cross_keys: bfloat16 [4096, 2048], P(('groups', 'seq'), 'head'), parts along dimension 0
- cross_values: bfloat16 [4096, 2048], P(('groups', 'seq'), 'head'), parts along dimension 0
There are 2 independent parts, one for each index of `groups`. A program takes and returns all parts, laid end to end along the dimension named above; an argument that names none is the same for every part. Nothing has to cross between parts.
All inputs are finite; a program needn't handle non-finite values.
Results may differ from a plain program's by a relative error of at most 0.0054.
Values may be sent and summed in bfloat16 or wider, within the bound.
No kernel may reach another device: no remote copies, remote signals or barrier semaphores. Data moves between devices by JAX's collectives and lax.ppermute only.
A program may use at most 128 MiB of HBM per device.

v0:
```python
import jax
import jax.numpy as jnp
from jax import lax
from jax.sharding import PartitionSpec as P

STRETCH = 256
NORM_GROUPS = 4


epsilon = 1e-05
highest = lax.Precision.HIGHEST


def passed_along(value, axis, steps):
    count = lax.axis_size(axis)
    first, last = (max(0, -steps), min(count, count - steps))
    return lax.ppermute(value, axis, [(source, source + steps) for source in range(first, last)])


def block_step(state, acts, writes, reads, steps, rates):
    cum_rate = jnp.cumsum(rates, axis=0)
    along = jnp.transpose(cum_rate)
    permutation_index = jnp.arange(acts.shape[0])
    lower = permutation_index[:, None] >= permutation_index[None, :]
    spans = along[:, :, None] - along[:, None, :]
    decays = jnp.exp(jnp.where(lower[None], spans, -1e30))
    intersection = jnp.dot(reads, jnp.transpose(writes), preferred_element_type=jnp.float32)
    weights = (intersection[None] * decays * jnp.transpose(steps)[:, None, :]).astype(jnp.bfloat16)
    within = jnp.einsum("hts,shp->thp", weights, acts, preferred_element_type=jnp.float32)
    carried = jnp.einsum("tn,hpn->thp", reads.astype(jnp.float32), state, precision=highest)
    outputs = within + jnp.exp(cum_rate)[:, :, None] * carried
    tail = jnp.exp(cum_rate[-1][None, :] - cum_rate) * steps
    weighted = acts.astype(jnp.float32) * tail[:, :, None]
    new_state = jnp.exp(cum_rate[-1])[:, None, None] * state + jnp.einsum(
        "thp,tn->hpn", weighted, writes.astype(jnp.float32), precision=highest
    )
    return (outputs, new_state, cum_rate)


def local_blocks(acts, writes, reads, steps, rates):
    tokens = acts.shape[0]
    count = tokens // STRETCH
    heads = acts.shape[1]
    width = acts.shape[2]
    inputs = (
        acts.reshape(count, STRETCH, heads, width),
        writes.reshape(count, STRETCH, -1),
        reads.reshape(count, STRETCH, -1),
        steps.reshape(count, STRETCH, heads),
        rates.reshape(count, STRETCH, heads),
    )
    initial = (
        jnp.zeros((heads, width, writes.shape[1]), jnp.float32),
        jnp.zeros((heads,), jnp.float32),
    )

    def advance(carried, block):
        state, offset = carried
        outputs, new_state, cum_rate = block_step(state, *block)
        return ((new_state, offset + cum_rate[-1]), (outputs, offset[None, :] + cum_rate))

    (ending, total_rate), (results, cumulated) = lax.scan(advance, initial, inputs)
    return (
        results.reshape(tokens, heads, width),
        ending,
        cumulated.reshape(tokens, heads),
        total_rate,
    )


def per_device(
    inner_acts,
    gate_acts,
    write_map,
    read_map,
    step_raw,
    step_bias,
    decay_log,
    skip_gain,
    norm_gain,
    out_weight,
    residual,
    final_gain,
    key_weight,
    value_weight,
):
    tokens = inner_acts.shape[0]
    heads = step_bias.shape[0]
    width = inner_acts.shape[1] // heads
    acts = inner_acts.reshape(tokens, heads, width)
    decay_rate = -jnp.exp(decay_log)
    steps_fwd = jax.nn.softplus(step_raw[0] + step_bias[None, :])
    steps_bwd = jax.nn.softplus(step_raw[1] + step_bias[None, :])
    reads_bwd = read_map[1][::-1]
    fwd_out, fwd_state, fwd_cum, fwd_total = local_blocks(
        acts, write_map[0], read_map[0], steps_fwd, steps_fwd * decay_rate[None, :]
    )
    bwd_out, bwd_state, bwd_cum, bwd_total = local_blocks(
        acts[::-1],
        write_map[1][::-1],
        reads_bwd,
        steps_bwd[::-1],
        (steps_bwd * decay_rate[None, :])[::-1],
    )

    def relay_turn(turn_index, states):
        fwd_enter, bwd_enter = states
        fwd_leave = jnp.exp(fwd_total)[:, None, None] * fwd_enter + fwd_state
        bwd_leave = jnp.exp(bwd_total)[:, None, None] * bwd_enter + bwd_state
        return (passed_along(fwd_leave, "seq", 1), passed_along(bwd_leave, "seq", -1))

    fwd_in, bwd_in = lax.fori_loop(
        0,
        lax.axis_size("seq") - 1,
        relay_turn,
        (jnp.zeros_like(fwd_state), jnp.zeros_like(bwd_state)),
    )
    fwd_all = fwd_out + jnp.exp(fwd_cum)[:, :, None] * jnp.einsum(
        "tn,hpn->thp", read_map[0].astype(jnp.float32), fwd_in, precision=highest
    )
    bwd_all = bwd_out + jnp.exp(bwd_cum)[:, :, None] * jnp.einsum(
        "tn,hpn->thp", reads_bwd.astype(jnp.float32), bwd_in, precision=highest
    )
    summed = fwd_all + bwd_all[::-1] + skip_gain[None, :, None] * acts.astype(jnp.float32)
    gated = summed.reshape(tokens, heads * width) * jax.nn.silu(gate_acts.astype(jnp.float32))
    grouped = gated.reshape(tokens, NORM_GROUPS // lax.axis_size("head"), -1)
    scaled = grouped * lax.rsqrt(jnp.mean(grouped * grouped, axis=2, keepdims=True) + epsilon)
    mixed = (scaled.reshape(tokens, -1) * norm_gain[None, :]).astype(jnp.bfloat16)
    own_width = residual.shape[1]
    offset = lax.axis_index("head") * own_width
    partial_value = jnp.dot(mixed, out_weight, preferred_element_type=jnp.float32)
    own_cols = lax.dynamic_slice_in_dim(partial_value, offset, own_width, 1) + residual.astype(
        jnp.float32
    )
    partial_value = lax.dynamic_update_slice_in_dim(partial_value, own_cols, offset, 1)
    encoded = lax.psum(partial_value, "head")
    normed = (
        encoded
        * lax.rsqrt(jnp.mean(encoded * encoded, axis=1, keepdims=True) + epsilon)
        * final_gain[None, :]
    ).astype(jnp.bfloat16)
    key_sum = jnp.dot(normed, key_weight, preferred_element_type=jnp.float32)
    value_sum = jnp.dot(normed, value_weight, preferred_element_type=jnp.float32)
    return (key_sum.astype(jnp.bfloat16), value_sum.astype(jnp.bfloat16))


def solution(mesh):
    placed = (
        P(("groups", "seq"), "head"),
        P(("groups", "seq"), "head"),
        P(None, ("groups", "seq"), None),
        P(None, ("groups", "seq"), None),
        P(None, ("groups", "seq"), "head"),
        P("head"),
        P("head"),
        P("head"),
        P("head"),
        P("head", None),
        P(("groups", "seq"), "head"),
        P(),
        P(None, "head"),
        P(None, "head"),
    )
    return jax.shard_map(
        per_device,
        mesh=mesh,
        in_specs=placed,
        out_specs=(P(("groups", "seq"), "head"), P(("groups", "seq"), "head")),
        check_vma=False,
    )
```

profile of v0, /device:TPU:0, one launch (start us, length us, event | category | flops | bytes accessed | tf_op | source)
XLA Modules:
  0.0 365.4 jit_solution(5269894913678206467)
XLA Ops:
  23.0 3.4 rev.19
  31.6 60.0 %while.50 = (s32[]{:T(128)}, f32[10,64,128]{2,1,0:T(8,128)}, f32[10]{0:T(128)}, f32[2,256,10,64]{1,0,3,2:T(2,128)}, f32[2,256,10]{1,2,0:T(8,128)}, /*index=5*/f3...) while((s32[]{:T(128)}, f32[10,64,128]{2,1,0:T(8,128)}, ...), condition=%wide.region_7.8_spmd.clone, body=%wide.region_4.7_spmd.clone.sunk | while | flops 608640576 | bytes 10162316 | solution.py:62
  46.1 14.2 %dynamic_update_slice.32 = f32[2,256,10,64]{1,0,3,2:T(2,128)} dynamic-update-slice(f32[2,256,10,64]{1,0,3,2:T(2,128)} %get-tuple-element.623, f32[1,256,10,64]{1,0,3,2:T(1,128)} %copy.152, s32[]{:T(128)S(6)} %copy.162, s32[]{:T(128)} %constant.70.clone.1..sunk.1, s32[]{:T(128)} %constant.70.clone.1..sunk.1, s32[]{:T(128)} %constant.70.clone.1..sunk.1) | dynamic-update-slice | bytes 1310724 | tf_op jit(solution)/shard_map/while/body/jit(dynamic_update_index_in_dim)/dynamic_update_slice | solution.py:62
  77.4 14.2 %dynamic_update_slice.32 = f32[2,256,10,64]{1,0,3,2:T(2,128)} dynamic-update-slice(f32[2,256,10,64]{1,0,3,2:T(2,128)} %get-tuple-element.623, f32[1,256,10,64]{1,0,3,2:T(1,128)} %copy.152, s32[]{:T(128)S(6)} %copy.162, s32[]{:T(128)} %constant.70.clone.1..sunk.1, s32[]{:T(128)} %constant.70.clone.1..sunk.1, s32[]{:T(128)} %constant.70.clone.1..sunk.1) | dynamic-update-slice | bytes 1310724 | tf_op jit(solution)/shard_map/while/body/jit(dynamic_update_index_in_dim)/dynamic_update_slice | solution.py:62
  93.0 3.1 reshape.217
  98.3 62.3 %while.49 = (s32[]{:T(128)}, f32[10,64,128]{2,1,0:T(8,128)}, f32[10]{0:T(128)}, f32[2,256,10,64]{1,0,3,2:T(2,128)}, f32[2,256,10]{1,2,0:T(8,128)}, /*index=5*/f3...) while((s32[]{:T(128)}, f32[10,64,128]{2,1,0:T(8,128)}, ...), condition=%wide.region_3.4_spmd.clone, body=%wide.region_0.3_spmd.clone.sunk | while | flops 608640576 | bytes 10156172 | solution.py:62
  114.4 14.2 %dynamic_update_slice.30 = f32[2,256,10,64]{1,0,3,2:T(2,128)} dynamic-update-slice(f32[2,256,10,64]{1,0,3,2:T(2,128)} %get-tuple-element.662, f32[1,256,10,64]{1,0,3,2:T(1,128)} %copy.146, s32[]{:T(128)S(6)} %copy.177, s32[]{:T(128)} %constant.70.clone.1..sunk, s32[]{:T(128)} %constant.70.clone.1..sunk, s32[]{:T(128)} %constant.70.clone.1..sunk) | dynamic-update-slice | bytes 1310724 | tf_op jit(solution)/shard_map/while/body/jit(dynamic_update_index_in_dim)/dynamic_update_slice | solution.py:62
  146.5 14.2 %dynamic_update_slice.30 = f32[2,256,10,64]{1,0,3,2:T(2,128)} dynamic-update-slice(f32[2,256,10,64]{1,0,3,2:T(2,128)} %get-tuple-element.662, f32[1,256,10,64]{1,0,3,2:T(1,128)} %copy.146, s32[]{:T(128)S(6)} %copy.177, s32[]{:T(128)} %constant.70.clone.1..sunk, s32[]{:T(128)} %constant.70.clone.1..sunk, s32[]{:T(128)} %constant.70.clone.1..sunk) | dynamic-update-slice | bytes 1310724 | tf_op jit(solution)/shard_map/while/body/jit(dynamic_update_index_in_dim)/dynamic_update_slice | solution.py:62
  163.6 54.8 %while.48 = (s32[]{:T(128)}, f32[10,64,128]{2,1,0:T(8,128)}, f32[10,64,128]{2,1,0:T(8,128)}, f32[10,1,1]{0,2,1:T(1,128)S(1)}, f32[10,64,128]{2,1,0:T(8,128)}, /*...) while((s32[]{:T(128)}, f32[10,64,128]{2,1,0:T(8,128)}, f32[10,64,128]{2,1,0:T(8,128)}, ...), condition=%wide.region_9.10_spmd, body=%wide.region_8.9_spmd.sunk | while | flops 327682 | bytes 4587765 | solution.py:112
  165.5 5.7 %collective-permute-start = (f32[10,64,128]{2,1,0:T(8,128)}, f32[10,64,128]{2,1,0:T(8,128)}, u32[]{:S(2)}, u32[]{:S(2)}) collective-permute-start(f32[10,64,128]{2,1,0:T(8,128)} %multiply_add_fusion.4), channel_id=1, source_target_pairs={{0,4},{4,8},{8,12},{1,5},{5,9},{9,13},{2,6},{6,10},{10,14},{3,7},{... | collective-permute-start | bytes 983048 | tf_op jit(solution)/shard_map/while/body/eval_jaxpr/ppermute | solution.py:17
  174.4 3.3 collective-permute-done
  177.7 6.7 %collective-permute-done.1 = f32[10,64,128]{2,1,0:T(8,128)} collective-permute-done((f32[10,64,128]{2,1,0:T(8,128)}, f32[10,64,128]{2,1,0:T(8,128)}, u32[]{:S(2)}, u32[]{:S(2)}) %collective-permute-start.1) | collective-permute-done | bytes 327712 | tf_op jit(solution)/shard_map/while/body/eval_jaxpr/ppermute | solution.py:17
  186.3 3.5 collective-permute-start
  195.2 6.7 %collective-permute-done.1 = f32[10,64,128]{2,1,0:T(8,128)} collective-permute-done((f32[10,64,128]{2,1,0:T(8,128)}, f32[10,64,128]{2,1,0:T(8,128)}, u32[]{:S(2)}, u32[]{:S(2)}) %collective-permute-start.1) | collective-permute-done | bytes 327712 | tf_op jit(solution)/shard_map/while/body/eval_jaxpr/ppermute | solution.py:17
  203.8 3.5 collective-permute-start
  211.4 7.0 %collective-permute-done.1 = f32[10,64,128]{2,1,0:T(8,128)} collective-permute-done((f32[10,64,128]{2,1,0:T(8,128)}, f32[10,64,128]{2,1,0:T(8,128)}, u32[]{:S(2)}, u32[]{:S(2)}) %collective-permute-start.1) | collective-permute-done | bytes 327712 | tf_op jit(solution)/shard_map/while/body/eval_jaxpr/ppermute | solution.py:17
  218.5 3.2 fusion.73
  221.6 3.8 %rev.23 = f32[512,10,64]{0,2,1:T(8,128)} reverse(f32[512,10,64]{0,2,1:T(8,128)} %fusion.73), dimensions={0} | reverse | bytes 2621440 | tf_op jit(solution)/shard_map/rev | solution.py:124
  226.1 3.2 reshape.210
  229.2 3.9 %fusion.77 = f32[512,10,64]{0,2,1:T(8,128)} fusion(f32[512,10,64]{0,2,1:T(8,128)} %rev.23, f32[512,10,64]{0,2,1:T(8,128)} %reshape.210, f32[10,64,128]{2,1,0:T(8,128)} %get-tuple-element.204, bf16[512,10,64]{0,2,1:T(8,128)(2,1)} %bitcast.265, f32[10]{0:T(128)S(1)} %copy-done.9, f32[512,10]{0,1:T(8,128)} %bitcast.289, bf16[2,512,128]{2,1,0:T(8,128)(2,1)S(1)} %copy-done.7), kind=kOutput, calls=%fused_computation.115 | convolution fusion | flops 505282560 | bytes 5067264 | tf_op jit(solution)/shard_map/tn,hpn->thp/dot_general | solution.py:118
  238.0 6.4 %fusion.82 = f32[512,2560]{1,0:T(8,128)} fusion(bf16[640,2560]{1,0:T(8,128)(2,1)S(1)} %copy-done, f32[640]{0:T(1024)S(1)} %copy-done.12, f32[512]{0:T(512)S(1)} %add_rsqrt_fusion.1, f32[512,640]{1,0:T(8,128)} %copy.69, bf16[512,640]{1,0:T(8,128)(2,1)} %param.21), kind=kOutput, calls=%fused_computation.125 | convolution fusion | flops 1680670720 | bytes 10490368 | tf_op jit(solution)/shard_map/dot_general | solution.py:131
  247.1 100.9 %all-reduce.2.cloned.1.call-done = f32[512,2560]{1,0:T(8,128)} async-done(((f32[512,2560]{1,0:T(8,128)}), f32[512,2560]{1,0:T(8,128)}) %all-reduce.2.cloned.1.call-update) | async-done | bytes 5242896 | tf_op jit(solution)/shard_map/psum | solution.py:136
  347.9 3.1 multiply_reduce_fusion
  352.0 4.2 %convolution_convert_fusion = bf16[512,512]{1,0:T(8,128)(2,1)} fusion(bf16[2560,512]{1,0:T(8,128)(2,1)} %param.33, f32[512,2560]{1,0:T(8,128)S(1)} %copy-done.3, f32[2560]{0:T(1024)S(1)} %copy-done.11, f32[512]{0:T(512)S(1)} %add_rsqrt_fusion), kind=kOutput, calls=%fused_computation.123 | convolution fusion | flops 1346371584 | bytes 8400896 | tf_op jit(solution)/shard_map/dot_general | solution.py:143
  (177 shorter events, 122.7 us)
Async XLA Ops:
  7.2 230.9 %copy-start = (bf16[640,2560]{1,0:T(8,128)(2,1)S(1)}, bf16[640,2560]{1,0:T(8,128)(2,1)}, u32[]{:S(2)}) copy-start(bf16[640,2560]{1,0:T(8,128)(2,1)} %param.29) | copy-start | bytes 9830404
  7.2 340.8 %all-reduce.2.cloned.1.call-start = ((), (), s32[]{:S(2)}) async-start(), calls=%async_computation | async-start | bytes 10485760 | tf_op jit(solution)/shard_map/psum | solution.py:136
  26.4 2.1 copy-start.5
  38.1 4.5 %copy-start.2 = (bf16[2,256,10,64]{1,3,2,0:T(8,128)(2,1)S(1)}, bf16[2,256,10,64]{1,3,2,0:T(8,128)(2,1)}, u32[]{:S(2)}) copy-start(bf16[2,256,10,64]{1,3,2,0:T(8,128)(2,1)} %get-tuple-element.639) | copy-start | bytes 1966084 | tf_op jit(solution)/shard_map/while
  66.7 6.1 %copy-start.2 = (bf16[2,256,10,64]{1,3,2,0:T(8,128)(2,1)S(1)}, bf16[2,256,10,64]{1,3,2,0:T(8,128)(2,1)}, u32[]{:S(2)}) copy-start(bf16[2,256,10,64]{1,3,2,0:T(8,128)(2,1)} %get-tuple-element.639) | copy-start | bytes 1966084 | tf_op jit(solution)/shard_map/while
  96.1 2.2 copy-start.4
  104.8 6.0 %copy-start.1 = (bf16[2,256,10,64]{1,3,2,0:T(8,128)(2,1)S(1)}, bf16[2,256,10,64]{1,3,2,0:T(8,128)(2,1)}, u32[]{:S(2)}) copy-start(bf16[2,256,10,64]{1,3,2,0:T(8,128)(2,1)} %get-tuple-element.678) | copy-start | bytes 1966084 | tf_op jit(solution)/shard_map/while
  135.1 6.8 %copy-start.1 = (bf16[2,256,10,64]{1,3,2,0:T(8,128)(2,1)S(1)}, bf16[2,256,10,64]{1,3,2,0:T(8,128)(2,1)}, u32[]{:S(2)}) copy-start(bf16[2,256,10,64]{1,3,2,0:T(8,128)(2,1)} %get-tuple-element.678) | copy-start | bytes 1966084 | tf_op jit(solution)/shard_map/while
  163.6 54.8 %copy-start.8 = (f32[2,8,2,256]{3,1,2,0:T(8,128)S(1)}, f32[2,8,2,256]{3,1,2,0:T(8,128)}, u32[]{:S(2)}) copy-start(f32[2,8,2,256]{3,1,2,0:T(8,128)} %copy.85) | copy-start | bytes 98308
  165.5 12.2 %collective-permute-start = (f32[10,64,128]{2,1,0:T(8,128)}, f32[10,64,128]{2,1,0:T(8,128)}, u32[]{:S(2)}, u32[]{:S(2)}) collective-permute-start(f32[10,64,128]{2,1,0:T(8,128)} %multiply_add_fusion.4), channel_id=1, source_target_pairs={{0,4},{4,8},{8,12},{1,5},{5,9},{9,13},{2,6},{6,10},{10,14},{3,7},{... | collective-permute-start | bytes 983048 | tf_op jit(solution)/shard_map/while/body/eval_jaxpr/ppermute | solution.py:17
  173.1 11.4 %collective-permute-start.1 = (f32[10,64,128]{2,1,0:T(8,128)}, f32[10,64,128]{2,1,0:T(8,128)}, u32[]{:S(2)}, u32[]{:S(2)}) collective-permute-start(f32[10,64,128]{2,1,0:T(8,128)} %multiply_add_fusion.5), channel_id=1, source_target_pairs={{4,0},{8,4},{12,8},{5,1},{9,5},{13,9},{6,2},{10,6},{14,10},{7,3},{... | collective-permute-start | bytes 983048 | tf_op jit(solution)/shard_map/while/body/eval_jaxpr/ppermute | solution.py:17
  186.3 8.8 %collective-permute-start = (f32[10,64,128]{2,1,0:T(8,128)}, f32[10,64,128]{2,1,0:T(8,128)}, u32[]{:S(2)}, u32[]{:S(2)}) collective-permute-start(f32[10,64,128]{2,1,0:T(8,128)} %multiply_add_fusion.4), channel_id=1, source_target_pairs={{0,4},{4,8},{8,12},{1,5},{5,9},{9,13},{2,6},{6,10},{10,14},{3,7},{... | collective-permute-start | bytes 983048 | tf_op jit(solution)/shard_map/while/body/eval_jaxpr/ppermute | solution.py:17
  191.7 10.2 %collective-permute-start.1 = (f32[10,64,128]{2,1,0:T(8,128)}, f32[10,64,128]{2,1,0:T(8,128)}, u32[]{:S(2)}, u32[]{:S(2)}) collective-permute-start(f32[10,64,128]{2,1,0:T(8,128)} %multiply_add_fusion.5), channel_id=1, source_target_pairs={{4,0},{8,4},{12,8},{5,1},{9,5},{13,9},{6,2},{10,6},{14,10},{7,3},{... | collective-permute-start | bytes 983048 | tf_op jit(solution)/shard_map/while/body/eval_jaxpr/ppermute | solution.py:17
  203.8 7.6 %collective-permute-start = (f32[10,64,128]{2,1,0:T(8,128)}, f32[10,64,128]{2,1,0:T(8,128)}, u32[]{:S(2)}, u32[]{:S(2)}) collective-permute-start(f32[10,64,128]{2,1,0:T(8,128)} %multiply_add_fusion.4), channel_id=1, source_target_pairs={{0,4},{4,8},{8,12},{1,5},{5,9},{9,13},{2,6},{6,10},{10,14},{3,7},{... | collective-permute-start | bytes 983048 | tf_op jit(solution)/shard_map/while/body/eval_jaxpr/ppermute | solution.py:17
  209.2 9.3 %collective-permute-start.1 = (f32[10,64,128]{2,1,0:T(8,128)}, f32[10,64,128]{2,1,0:T(8,128)}, u32[]{:S(2)}, u32[]{:S(2)}) collective-permute-start(f32[10,64,128]{2,1,0:T(8,128)} %multiply_add_fusion.5), channel_id=1, source_target_pairs={{4,0},{8,4},{12,8},{5,1},{9,5},{13,9},{6,2},{10,6},{14,10},{7,3},{... | collective-permute-start | bytes 983048 | tf_op jit(solution)/shard_map/while/body/eval_jaxpr/ppermute | solution.py:17
  226.1 3.2 copy-start.7
  226.1 3.2 copy-start.9
  236.0 2.0 copy-start.12
  238.0 6.4 %copy-start.6 = (bf16[512,640]{1,0:T(8,128)(2,1)S(1)}, bf16[512,640]{1,0:T(8,128)(2,1)}, u32[]{:S(2)}) copy-start(bf16[512,640]{1,0:T(8,128)(2,1)} %param.30) | copy-start | bytes 1966084
  247.0 104.0 %copy-start.11 = (f32[2560]{0:T(1024)S(1)}, f32[2560]{0:T(1024)}, u32[]{:S(2)}) copy-start(f32[2560]{0:T(1024)} %param.31) | copy-start | bytes 30724
  347.9 4.0 %copy-start.3 = (f32[512,2560]{1,0:T(8,128)S(1)}, f32[512,2560]{1,0:T(8,128)}, u32[]{:S(2)}) copy-start(f32[512,2560]{1,0:T(8,128)} %all-reduce.2.cloned.1.call-done) | copy-start | bytes 15728644
  352.0 4.3 %copy-start.10 = (bf16[2560,512]{1,0:T(8,128)(2,1)S(1)}, bf16[2560,512]{1,0:T(8,128)(2,1)}, u32[]{:S(2)}) copy-start(bf16[2560,512]{1,0:T(8,128)(2,1)} %param.32) | copy-start | bytes 7864324
Sparse Core Ops, SparseCore 0:
  247.2 100.7 all-reduce.1
where the time goes:
time: 372 us; the launch traced here: 365 us
  local copies, waits for them, and re-layouts  128 us (34%)
  waiting for transfers between devices  128 us (34%)
  other arithmetic  41.7 us (11%)
  matrix products  37.3 us (10%)
  starting transfers between devices  16.5 us (4%)
  between operations  14.2 us (4%)
    psum x1, waiting for transfers between devices, per_device(): encoded = lax.psum(partial_value, 'head')  101 us
    dynamic_update_slice x8, local copies, waits for them, and re-layouts, local_blocks(): lax.scan(advance, initial, inputs)  62.7 us
    ppermute x6, waiting for transfers between devices, passed_along(): lax.ppermute(value, axis, [(source, source + steps) for source in range(f...  26.9 us
    ppermute x6, starting transfers between devices, passed_along(): lax.ppermute(value, axis, [(source, source + steps) for source in range(f...  16.5 us
    another operation x20, local copies, waits for them, and re-layouts  14 us
    another operation x12, other arithmetic  10.3 us
    dynamic_slice x12, local copies, waits for them, and re-layouts, local_blocks(): lax.scan(advance, initial, inputs)  8.28 us
  transfers between devices with their start and end apart: 7, of which 7 were waited for; matrix products, arithmetic and copies ran while one was open for 2% of the time, Pallas kernels for 0%

commit v1 on v0

v1 whole, which is shorter than its diff:
```python
import jax
import jax.numpy as jnp
from jax import lax
from jax.sharding import PartitionSpec as P

STRETCH = 256
NORM_GROUPS = 4


epsilon = 1e-05
highest = lax.Precision.HIGHEST


def passed_along(value, axis, steps):
    count = lax.axis_size(axis)
    first, last = (max(0, -steps), min(count, count - steps))
    if first >= last:
        return jnp.zeros_like(value)
    return lax.ppermute(value, axis, [(source, source + steps) for source in range(first, last)])


def block_parts(acts, writes, reads, steps, rates, reverse):
    tokens, heads, width = acts.shape
    count = tokens // STRETCH
    acts_b = acts.reshape(count, STRETCH, heads, width)
    writes_b = writes.reshape(count, STRETCH, -1)
    reads_b = reads.reshape(count, STRETCH, -1)
    steps_b = steps.reshape(count, STRETCH, heads)
    rates_b = rates.reshape(count, STRETCH, heads)
    cum_rate = lax.cumsum(rates_b, axis=1, reverse=reverse)
    block_total = cum_rate[:, 0] if reverse else cum_rate[:, -1]
    along = jnp.transpose(cum_rate, (0, 2, 1))
    position = jnp.arange(STRETCH)
    if reverse:
        causal = position[:, None] <= position[None, :]
    else:
        causal = position[:, None] >= position[None, :]
    spans = along[:, :, :, None] - along[:, :, None, :]
    decays = jnp.exp(jnp.where(causal[None, None], spans, -1e30))
    intersection = jnp.einsum("btn,bsn->bts", reads_b, writes_b, preferred_element_type=jnp.float32)
    weights = (
        intersection[:, None] * decays * jnp.transpose(steps_b, (0, 2, 1))[:, :, None, :]
    ).astype(jnp.bfloat16)
    within = jnp.einsum("bhts,bshp->bthp", weights, acts_b, preferred_element_type=jnp.float32)
    tail = jnp.exp(block_total[:, None, :] - cum_rate) * steps_b
    weighted = acts_b.astype(jnp.float32) * tail[:, :, :, None]
    ends = jnp.einsum(
        "bshp,bsn->bhpn", weighted, writes_b.astype(jnp.float32), precision=highest
    )
    return within, cum_rate, ends, jnp.exp(block_total)


def chain_blocks(ends, decays, reverse):
    count = ends.shape[0]
    order = range(count - 1, -1, -1) if reverse else range(count)
    state = jnp.zeros_like(ends[0])
    gain = jnp.ones_like(decays[0])
    starts = [None] * count
    gains = [None] * count
    for index in order:
        starts[index] = state
        gains[index] = gain
        state = decays[index][:, None, None] * state + ends[index]
        gain = gain * decays[index]
    return jnp.stack(starts), jnp.stack(gains), state, gain


def relay(state, gain, axis, steps):
    count = lax.axis_size(axis)
    distance = 1
    while distance < count:
        got_state = passed_along(state, axis, distance * steps)
        got_gain = passed_along(gain, axis, distance * steps)
        state = gain[:, None, None] * got_state + state
        gain = gain * got_gain
        distance *= 2
    return passed_along(state, axis, steps)


def direction_out(acts, writes, reads, steps, rates, reverse, axis):
    within, cum_rate, ends, decays = block_parts(acts, writes, reads, steps, rates, reverse)
    starts, gains, own_end, own_gain = chain_blocks(ends, decays, reverse)
    entering = relay(own_end, own_gain, axis, -1 if reverse else 1)
    block_states = starts + gains[:, :, None, None] * entering[None]
    count = within.shape[0]
    reads_b = reads.reshape(count, STRETCH, -1).astype(jnp.float32)
    carried = jnp.einsum("btn,bhpn->bthp", reads_b, block_states, precision=highest)
    outputs = within + jnp.exp(cum_rate)[:, :, :, None] * carried
    return outputs.reshape(acts.shape)


def per_device(
    inner_acts,
    gate_acts,
    write_map,
    read_map,
    step_raw,
    step_bias,
    decay_log,
    skip_gain,
    norm_gain,
    out_weight,
    residual,
    final_gain,
    key_weight,
    value_weight,
):
    tokens = inner_acts.shape[0]
    heads = step_bias.shape[0]
    width = inner_acts.shape[1] // heads
    acts = inner_acts.reshape(tokens, heads, width)
    decay_rate = -jnp.exp(decay_log)
    steps_fwd = jax.nn.softplus(step_raw[0] + step_bias[None, :])
    steps_bwd = jax.nn.softplus(step_raw[1] + step_bias[None, :])
    fwd_all = direction_out(
        acts, write_map[0], read_map[0], steps_fwd, steps_fwd * decay_rate[None, :], False, "seq"
    )
    bwd_all = direction_out(
        acts, write_map[1], read_map[1], steps_bwd, steps_bwd * decay_rate[None, :], True, "seq"
    )
    summed = fwd_all + bwd_all + skip_gain[None, :, None] * acts.astype(jnp.float32)
    gated = summed.reshape(tokens, heads * width) * jax.nn.silu(gate_acts.astype(jnp.float32))
    grouped = gated.reshape(tokens, NORM_GROUPS // lax.axis_size("head"), -1)
    scaled = grouped * lax.rsqrt(jnp.mean(grouped * grouped, axis=2, keepdims=True) + epsilon)
    mixed = (scaled.reshape(tokens, -1) * norm_gain[None, :]).astype(jnp.bfloat16)
    own_width = residual.shape[1]
    offset = lax.axis_index("head") * own_width
    partial_value = jnp.dot(mixed, out_weight, preferred_element_type=jnp.float32)
    own_cols = lax.dynamic_slice_in_dim(partial_value, offset, own_width, 1) + residual.astype(
        jnp.float32
    )
    partial_value = lax.dynamic_update_slice_in_dim(partial_value, own_cols, offset, 1)
    encoded = lax.psum_scatter(partial_value, "head", scatter_dimension=0, tiled=True)
    normed = (
        encoded
        * lax.rsqrt(jnp.mean(encoded * encoded, axis=1, keepdims=True) + epsilon)
        * final_gain[None, :]
    ).astype(jnp.bfloat16)
    normed = lax.all_gather(normed, "head", axis=0, tiled=True)
    key_sum = jnp.dot(normed, key_weight, preferred_element_type=jnp.float32)
    value_sum = jnp.dot(normed, value_weight, preferred_element_type=jnp.float32)
    return (key_sum.astype(jnp.bfloat16), value_sum.astype(jnp.bfloat16))


def solution(mesh):
    placed = (
        P(("groups", "seq"), "head"),
        P(("groups", "seq"), "head"),
        P(None, ("groups", "seq"), None),
        P(None, ("groups", "seq"), None),
        P(None, ("groups", "seq"), "head"),
        P("head"),
        P("head"),
        P("head"),
        P("head"),
        P("head", None),
        P(("groups", "seq"), "head"),
        P(),
        P(None, "head"),
        P(None, "head"),
    )
    return jax.shard_map(
        per_device,
        mesh=mesh,
        in_specs=placed,
        out_specs=(P(("groups", "seq"), "head"), P(("groups", "seq"), "head")),
        check_vma=False,
    )
```

time: 372 us -> 194 us (0.52); the launches traced: 365 us -> 193 us
  local copies, waits for them, and re-layouts: 128 us -> 13.8 us
  waiting for transfers between devices: 128 us -> 83.2 us
  other arithmetic: 41.7 us -> 25.4 us
  starting transfers between devices: 16.5 us -> 32.6 us
  matrix products: 37.3 us -> 23.4 us
    psum x1 -> x0, waiting for transfers between devices: 101 us -> none  [per_device(): encoded = lax.psum(partial_value, 'head')]
    dynamic_update_slice x8 -> x0, local copies, waits for them, and re-layouts: 62.7 us -> none  [local_blocks(): lax.scan(advance, initial, inputs)]
    reduce_scatter x0 -> x1, waiting for transfers between devices: none -> 51.5 us  [per_device(): lax.psum_scatter(partial_value, 'head', scatter_dimension=0, tiled=True)]
    all_gather x0 -> x1, waiting for transfers between devices: none -> 25.7 us  [per_device(): normed = lax.all_gather(normed, 'head', axis=0, tiled=True)]
    ppermute x6 -> x8, waiting for transfers between devices: 26.9 us -> 5.95 us  [passed_along(): lax.ppermute(value, axis, [(source, source + steps) for source in range(f...]
    reshape x10 -> x2, local copies, waits for them, and re-layouts: 16.3 us -> 0.03 us  [the longest x2 6.32 us: local_blocks(): results.reshape(tokens, heads, width)]
    ppermute x6 -> x8, starting transfers between devices: 16.5 us -> 32.5 us  [passed_along(): lax.ppermute(value, axis, [(source, source + steps) for source in range(f...]
    another operation x21 -> x14, local copies, waits for them, and re-layouts: 16.7 us -> 2.93 us  [the longest x1 2.68 us: block_parts(): acts_b = acts.reshape(count, STRETCH, heads, width)]
  transfers between devices with their start and end apart: 7 -> 10, of which waited for: 7 -> 7; matrix products, arithmetic and copies ran while one was open for 2% -> 16% of each run, Pallas kernels for 0% -> 0%
where the time goes in v1:
time: 194 us; the launch traced here: 193 us
  waiting for transfers between devices  83.2 us (43%)
  starting transfers between devices  32.6 us (17%)
  other arithmetic  25.4 us (13%)
  matrix products  23.4 us (12%)
  between operations  14.7 us (8%)
  local copies, waits for them, and re-layouts  13.8 us (7%)
    reduce_scatter x1, waiting for transfers between devices, per_device(): lax.psum_scatter(partial_value, 'head', scatter_dimension=0, tiled=True)  51.5 us
    ppermute x8, starting transfers between devices, passed_along(): lax.ppermute(value, axis, [(source, source + steps) for source in range(f...  32.5 us
    all_gather x1, waiting for transfers between devices, per_device(): normed = lax.all_gather(normed, 'head', axis=0, tiled=True)  25.7 us
    another operation x5, other arithmetic  7.66 us
    unnamed x67, local copies, waits for them, and re-layouts  6.37 us
    ppermute x8, waiting for transfers between devices, passed_along(): lax.ppermute(value, axis, [(source, source + steps) for source in range(f...  5.95 us
    dot_general x2, matrix products, block_parts(): jnp.einsum('bhts,bshp->bthp', weights, acts_b, preferred_element_type=jnp...  5.21 us
    dot_general x1, matrix products, per_device(): jnp.dot(normed, value_weight, preferred_element_type=jnp.float32)  4.99 us
  transfers between devices with their start and end apart: 10, of which 7 were waited for; matrix products, arithmetic and copies ran while one was open for 16% of the time, Pallas kernels for 0%

profile of v1, /device:TPU:0, one launch (start us, length us, event | category | flops | bytes accessed | tf_op | source)
XLA Modules:
  0.0 193.0 jit_solution(5765042596339423927)
XLA Ops:
  9.1 1.4 multiply_bitcast_fusion
  10.6 5.0 %reduce-window.16 = f32[2,10,2,128]{3,1,2,0:T(8,128)S(1)} reduce-window(f32[2,10,2,128]{3,1,2,0:T(8,128)S(1)} %copy.44, f32[]{:T(128)} %constant.10.clone.1), window={size=1x1x1x128 pad=0_0x0_0x0_0x0_127}, to_apply=%region_2.3 | reduce-window | flops 650240 | bytes 40964 | tf_op jit(solution)/shard_map/reduce-window.2
  20.2 6.1 %collective-permute-start = (f32[10]{0:T(128)}, f32[10]{0:T(128)}, u32[]{:S(2)}, u32[]{:S(2)}) collective-permute-start(f32[10]{0:T(128)} %get-tuple-element.28), channel_id=1, source_target_pairs={{0,4},{4,8},{8,12},{1,5},{5,9},{9,13},{2,6},{6,10},{10,14},{3,7},{... | collective-permute-start | bytes 128 | tf_op jit(solution)/shard_map/ppermute | solution.py:19
  28.0 2.2 %copy.38 = bf16[512,640]{0,1:T(8,128)(2,1)} copy(bf16[512,640]{1,0:T(8,128)(2,1)} %param.14) | data formatting | bytes 1310720 | tf_op args[0]
  30.2 2.7 %reshape_reshape.4 = bf16[2,256,10,64]{1,0,3,2:T(2,128)(2,1)} reshape(bf16[512,640]{0,1:T(8,128)(2,1)} %copy.38) | data formatting | bytes 1310720 | tf_op jit(solution)/shard_map/reshape;reshape | solution.py:25
  32.9 1.4 bitcast_exponential_fusion.1
  34.4 1.8 convert_multiply_fusion.1
  39.4 4.7 %collective-permute-start.1 = (f32[10,64,128]{2,1,0:T(8,128)S(1)}, f32[10,64,128]{2,1,0:T(8,128)S(1)}, u32[]{:S(2)}, u32[]{:S(2)}) collective-permute-start(f32[10,64,128]{2,1,0:T(8,128)S(1)} %fusion.41), channel_id=1, source_target_pairs={{0,4},{4,8},{8,12},{1,5},{5,9},{9,13},{2,6},{6,10},{10,14},{3,7},{... | collective-permute-start | bytes 983048 | tf_op jit(solution)/shard_map/ppermute | solution.py:19
  45.2 2.6 %fusion.14 = f32[2,256,10,64]{1,3,2,0:T(8,128)} fusion(f32[2,10,256]{2,1,0:T(8,128)S(1)} %copy.48, f32[2,10,256]{2,1,0:T(8,128)S(1)} %copy.46, f32[2,256,256]{2,1,0:T(8,128)S(1)} %fusion.58, pred[256,256]{1,0:T(8,128)(4,1)S(1)} %iota_compare_fusion, bf16[2,256,10,64]{1,0,3,2:T(2,128)(2,1)S(1)} %copy-done.3), kind=kOutput, calls=%fused_computation.20 | convolution fusion | flops 174325760 | bytes 2596864 | tf_op jit(solution)/shard_map/bhts,bshp->bthp/dot_general | solution.py:44
  47.8 2.6 %fusion.15 = f32[2,256,10,64]{1,3,2,0:T(8,128)} fusion(f32[2,10,256]{2,1,0:T(8,128)S(1)} %copy.37, f32[2,10,256]{2,1,0:T(8,128)S(1)} %copy.35, f32[2,256,256]{2,1,0:T(8,128)S(1)} %fusion.57, pred[256,256]{1,0:T(8,128)(4,1)S(1)} %iota_compare_fusion.1, bf16[2,256,10,64]{1,0,3,2:T(2,128)(2,1)S(1)} %copy-done.3), kind=kOutput, calls=%fused_computation.21 | convolution fusion | flops 174325760 | bytes 2596864 | tf_op jit(solution)/shard_map/bhts,bshp->bthp/dot_general | solution.py:44
  51.2 5.4 %collective-permute-start.2 = (f32[10,64,128]{2,1,0:T(8,128)S(1)}, f32[10,64,128]{2,1,0:T(8,128)S(1)}, u32[]{:S(2)}, u32[]{:S(2)}) collective-permute-start(f32[10,64,128]{2,1,0:T(8,128)S(1)} %multiply_add_fusion.3), channel_id=1, source_target_pairs={{0,8},{4,12},{1,9},{5,13},{2,10},{6,14},{3,11},{7,15},{16,24},{20,... | collective-permute-start | bytes 983048 | tf_op jit(solution)/shard_map/ppermute | solution.py:19
  62.9 11.1 %collective-permute-start.3 = (f32[10,64,128]{2,1,0:T(8,128)}, f32[10,64,128]{2,1,0:T(8,128)}, u32[]{:S(2)}, u32[]{:S(2)}) collective-permute-start(f32[10,64,128]{2,1,0:T(8,128)} %multiply_add_fusion.2), channel_id=1, source_target_pairs={{0,4},{4,8},{8,12},{1,5},{5,9},{9,13},{2,6},{6,10},{10,14},{3,7},{... | collective-permute-start | bytes 983048 | tf_op jit(solution)/shard_map/ppermute | solution.py:19
  75.8 1.5 collective-permute-start.7
  78.3 2.2 %copy.56 = bf16[512,640]{0,1:T(8,128)(2,1)} copy(bf16[512,640]{1,0:T(8,128)(2,1)} %param.15) | data formatting | bytes 1310720 | tf_op args[1]
  80.7 2.4 %fusion.20 = f32[2,256,10,64]{1,3,2,0:T(8,128)S(1)} fusion(f32[2,256,10,64]{1,3,2,0:T(8,128)} %fusion.15, bf16[2,256,128,1]{2,1,3,0:T(8,128)(2,1)S(1)} %bitcast.131, f32[1,10,64,128]{3,2,1,0:T(8,128)} %slice_add_fusion.1, f32[2,256,10]{1,2,0:T(8,128)S(1)} %copy.40, f32[10,64,128]{2,1,0:T(8,128)} %collective-permute-done.3, f32[2,10]{1,0:T(2,128)S(1)} %stack.15), kind=kOutput, calls=%fused_computation.28 | convolution fusion | flops 504299520 | bytes 3428432 | tf_op jit(solution)/shard_map/btn,bhpn->bthp/dot_general | solution.py:87
  83.2 3.5 %collective-permute-done.7 = f32[10,64,128]{2,1,0:T(8,128)} collective-permute-done((f32[10,64,128]{2,1,0:T(8,128)}, f32[10,64,128]{2,1,0:T(8,128)}, u32[]{:S(2)}, u32[]{:S(2)}) %collective-permute-start.7) | collective-permute-done | bytes 327712 | tf_op jit(solution)/shard_map/ppermute | solution.py:19
  86.7 1.8 fusion.18
  91.5 4.7 %fusion.29 = f32[512,2560]{1,0:T(8,128)} fusion(bf16[640,2560]{1,0:T(8,128)(2,1)S(1)} %copy-done, f32[512,640]{0,1:T(8,128)S(1)} %get-tuple-element.5, f32[640]{0:T(1024)S(1)} %copy-done.21, f32[512]{0:T(512)S(1)} %add_rsqrt_fusion), kind=kOutput, calls=%fused_computation.44 | convolution fusion | flops 1678704640 | bytes 9835008 | tf_op jit(solution)/shard_map/dot_general | solution.py:128
  96.2 2.6 %add_dynamic-update-slice_fusion = f32[512,2560]{1,0:T(8,128)} fusion(f32[512,2560]{1,0:T(8,128)} %fusion.29, s32[]{:T(128)S(6)} %select_n.26, bf16[512,640]{1,0:T(8,128)(2,1)S(1)} %copy-done.11), kind=kLoop, calls=%fused_computation.39 | loop fusion | flops 655360 | bytes 3276804 | tf_op jit(solution)/shard_map/dynamic_update_slice | solution.py:132
  98.9 51.5 %reduce-scatter.2.cloned.1.call-done = f32[128,2560]{1,0:T(8,128)} async-done(((f32[512,2560]{1,0:T(8,128)}), f32[128,2560]{1,0:T(8,128)}) %reduce-scatter.2.cloned.1.call-update) | async-done | bytes 1310736 | tf_op jit(solution)/shard_map/reduce_scatter | solution.py:133
  150.4 1.6 multiply_reduce_fusion
  153.1 25.7 %all-gather.2.cloned.1.call-done = bf16[512,2560]{1,0:T(8,128)(2,1)} async-done(((bf16[128,2560]{1,0:T(8,128)(2,1)}), bf16[512,2560]{1,0:T(8,128)(2,1)}) %all-gather.2.cloned.1.call-update) | async-done | bytes 2621456 | tf_op jit(solution)/shard_map/all_gather | solution.py:139
  178.8 5.0 %convolution_convert_fusion = bf16[512,512]{1,0:T(8,128)(2,1)} fusion(bf16[512,2560]{1,0:T(8,128)(2,1)} %all-gather.2.cloned.1.call-done, bf16[2560,512]{1,0:T(8,128)(2,1)} %param.27), kind=kOutput, calls=%fused_computation.42 | convolution fusion | flops 1342439424 | bytes 5767168 | tf_op jit(solution)/shard_map/dot_general | solution.py:141
  183.8 2.3 %convolution_convert_fusion.1 = bf16[512,512]{1,0:T(8,128)(2,1)} fusion(bf16[512,2560]{1,0:T(8,128)(2,1)S(1)} %copy-done.31, bf16[2560,512]{1,0:T(8,128)(2,1)S(1)} %copy-done.30), kind=kOutput, calls=%fused_computation.43 | convolution fusion | flops 1342439424 | bytes 5767168 | tf_op jit(solution)/shard_map/dot_general | solution.py:140
  (145 shorter events, 26.6 us)
Async XLA Ops:
  7.2 84.3 %copy-start = (bf16[640,2560]{1,0:T(8,128)(2,1)S(1)}, bf16[640,2560]{1,0:T(8,128)(2,1)}, u32[]{:S(2)}) copy-start(bf16[640,2560]{1,0:T(8,128)(2,1)} %param.23) | copy-start | bytes 9830404
  7.2 143.2 %reduce-scatter.2.cloned.1.call-start = ((), (), s32[]{:S(2)}) async-start(), calls=%async_computation.1 | async-start | bytes 6553600 | tf_op jit(solution)/shard_map/reduce_scatter | solution.py:133
  16.6 43.0 %collective-permute-start.4 = (f32[10]{0:T(128)}, f32[10]{0:T(128)}, u32[]{:S(2)}, u32[]{:S(2)}) collective-permute-start(f32[10]{0:T(128)} %get-tuple-element.22), channel_id=1, source_target_pairs={{4,0},{8,4},{12,8},{5,1},{9,5},{13,9},{6,2},{10,6},{14,10},{7,3},{... | collective-permute-start | bytes 128 | tf_op jit(solution)/shard_map/ppermute | solution.py:19
  19.4 7.5 %copy-start.15 = (f32[2,10,256]{2,0,1:T(2,128)}, f32[2,10,256]{2,0,1:T(2,128)S(1)}, u32[]{:S(2)}) copy-start(f32[2,10,256]{2,0,1:T(2,128)S(1)} %reduce_window_sum.45) | copy-start | bytes 61444
  19.6 7.2 %copy-start.23 = (f32[2,10]{1,0:T(2,128)}, f32[2,10]{1,0:T(2,128)S(1)}, u32[]{:S(2)}) copy-start(f32[2,10]{1,0:T(2,128)S(1)} %bitcast_exponential_fusion.2) | copy-start | bytes 244
  20.2 40.0 %collective-permute-start = (f32[10]{0:T(128)}, f32[10]{0:T(128)}, u32[]{:S(2)}, u32[]{:S(2)}) collective-permute-start(f32[10]{0:T(128)} %get-tuple-element.28), channel_id=1, source_target_pairs={{0,4},{4,8},{8,12},{1,5},{5,9},{9,13},{2,6},{6,10},{10,14},{3,7},{... | collective-permute-start | bytes 128 | tf_op jit(solution)/shard_map/ppermute | solution.py:19
  28.0 10.4 %copy-start.7 = (bf16[1,512,128]{2,1,0:T(8,128)(2,1)}, bf16[1,512,128]{2,1,0:T(8,128)(2,1)S(1)}, u32[]{:S(2)}) copy-start(bf16[1,512,128]{2,1,0:T(8,128)(2,1)S(1)} %get-tuple-element.13) | copy-start | bytes 393220
  37.1 19.5 %collective-permute-start.5 = (f32[10,64,128]{2,1,0:T(8,128)S(1)}, f32[10,64,128]{2,1,0:T(8,128)S(1)}, u32[]{:S(2)}, u32[]{:S(2)}) collective-permute-start(f32[10,64,128]{2,1,0:T(8,128)S(1)} %fusion.40), channel_id=1, source_target_pairs={{4,0},{8,4},{12,8},{5,1},{9,5},{13,9},{6,2},{10,6},{14,10},{7,3},{... | collective-permute-start | bytes 983048 | tf_op jit(solution)/shard_map/ppermute | solution.py:19
  38.5 5.8 %copy-start.12 = (bf16[2,512,128]{2,1,0:T(8,128)(2,1)S(1)}, bf16[2,512,128]{2,1,0:T(8,128)(2,1)}, u32[]{:S(2)}) copy-start(bf16[2,512,128]{2,1,0:T(8,128)(2,1)} %param.17) | copy-start | bytes 786436
  39.4 5.8 %copy-start.3 = (bf16[2,256,10,64]{1,0,3,2:T(2,128)(2,1)S(1)}, bf16[2,256,10,64]{1,0,3,2:T(2,128)(2,1)}, u32[]{:S(2)}) copy-start(bf16[2,256,10,64]{1,0,3,2:T(2,128)(2,1)} %reshape_reshape.4) | copy-start | bytes 1966084
  39.4 11.1 %collective-permute-start.1 = (f32[10,64,128]{2,1,0:T(8,128)S(1)}, f32[10,64,128]{2,1,0:T(8,128)S(1)}, u32[]{:S(2)}, u32[]{:S(2)}) collective-permute-start(f32[10,64,128]{2,1,0:T(8,128)S(1)} %fusion.41), channel_id=1, source_target_pairs={{0,4},{4,8},{8,12},{1,5},{5,9},{9,13},{2,6},{6,10},{10,14},{3,7},{... | collective-permute-start | bytes 983048 | tf_op jit(solution)/shard_map/ppermute | solution.py:19
  51.2 10.9 %collective-permute-start.2 = (f32[10,64,128]{2,1,0:T(8,128)S(1)}, f32[10,64,128]{2,1,0:T(8,128)S(1)}, u32[]{:S(2)}, u32[]{:S(2)}) collective-permute-start(f32[10,64,128]{2,1,0:T(8,128)S(1)} %multiply_add_fusion.3), channel_id=1, source_target_pairs={{0,8},{4,12},{1,9},{5,13},{2,10},{6,14},{3,11},{7,15},{16,24},{20,... | collective-permute-start | bytes 983048 | tf_op jit(solution)/shard_map/ppermute | solution.py:19
  57.5 17.5 %collective-permute-start.6 = (f32[10,64,128]{2,1,0:T(8,128)S(1)}, f32[10,64,128]{2,1,0:T(8,128)S(1)}, u32[]{:S(2)}, u32[]{:S(2)}) collective-permute-start(f32[10,64,128]{2,1,0:T(8,128)S(1)} %multiply_add_fusion.1), channel_id=1, source_target_pairs={{8,0},{12,4},{9,1},{13,5},{10,2},{14,6},{11,3},{15,7},{24,16},{28,... | collective-permute-start | bytes 983048 | tf_op jit(solution)/shard_map/ppermute | solution.py:19
  60.9 17.2 %copy-start.29 = (f32[10]{0:T(128)S(1)}, f32[10]{0:T(128)}, u32[]{:S(2)}) copy-start(f32[10]{0:T(128)} %param.21) | copy-start | bytes 124
  60.9 17.3 %copy-start.28 = (f32[1,10]{1,0:T(1,128)S(1)}, f32[1,10]{1,0:T(1,128)}, u32[]{:S(2)}) copy-start(f32[1,10]{1,0:T(1,128)} %get-tuple-element.20) | copy-start | bytes 124
  60.9 17.3 %copy-start.20 = (f32[2,256,10]{1,0,2:T(2,128)S(1)}, f32[2,256,10]{1,0,2:T(2,128)}, u32[]{:S(2)}) copy-start(f32[2,256,10]{1,0,2:T(2,128)} %get-tuple-element.16) | copy-start | bytes 61444
  60.9 17.3 %copy-start.19 = (f32[2,256,10]{1,0,2:T(2,128)S(1)}, f32[2,256,10]{1,0,2:T(2,128)}, u32[]{:S(2)}) copy-start(f32[2,256,10]{1,0,2:T(2,128)} %get-tuple-element.31) | copy-start | bytes 61444
  62.9 17.8 %collective-permute-start.3 = (f32[10,64,128]{2,1,0:T(8,128)}, f32[10,64,128]{2,1,0:T(8,128)}, u32[]{:S(2)}, u32[]{:S(2)}) collective-permute-start(f32[10,64,128]{2,1,0:T(8,128)} %multiply_add_fusion.2), channel_id=1, source_target_pairs={{0,4},{4,8},{8,12},{1,5},{5,9},{9,13},{2,6},{6,10},{10,14},{3,7},{... | collective-permute-start | bytes 983048 | tf_op jit(solution)/shard_map/ppermute | solution.py:19
  75.8 10.9 %collective-permute-start.7 = (f32[10,64,128]{2,1,0:T(8,128)}, f32[10,64,128]{2,1,0:T(8,128)}, u32[]{:S(2)}, u32[]{:S(2)}) collective-permute-start(f32[10,64,128]{2,1,0:T(8,128)} %multiply_add_fusion), channel_id=1, source_target_pairs={{4,0},{8,4},{12,8},{5,1},{9,5},{13,9},{6,2},{10,6},{14,10},{7,3},{... | collective-permute-start | bytes 983048 | tf_op jit(solution)/shard_map/ppermute | solution.py:19
  80.7 5.9 %copy-start.5 = (f32[2,256,10,64]{1,3,2,0:T(8,128)S(1)}, f32[2,256,10,64]{1,3,2,0:T(8,128)}, u32[]{:S(2)}) copy-start(f32[2,256,10,64]{1,3,2,0:T(8,128)} %fusion.14) | copy-start | bytes 3932164
  80.7 5.9 %copy-start.6 = (f32[1,10,64,128]{3,2,1,0:T(8,128)S(1)}, f32[1,10,64,128]{3,2,1,0:T(8,128)}, u32[]{:S(2)}) copy-start(f32[1,10,64,128]{3,2,1,0:T(8,128)} %slice_add_fusion) | copy-start | bytes 983044
  80.7 5.9 %copy-start.10 = (bf16[1,512,128]{2,1,0:T(8,128)(2,1)S(1)}, bf16[1,512,128]{2,1,0:T(8,128)(2,1)}, u32[]{:S(2)}) copy-start(bf16[1,512,128]{2,1,0:T(8,128)(2,1)} %copy-done.9) | copy-start | bytes 393220
  98.8 53.2 %copy-start.22 = (f32[2560]{0:T(1024)S(1)}, f32[2560]{0:T(1024)}, u32[]{:S(2)}) copy-start(f32[2560]{0:T(1024)} %param.25) | copy-start | bytes 30724
  98.8 80.0 %all-gather.2.cloned.1.call-start = ((), (), s32[]{:S(2)}) async-start(), calls=%async_computation.2 | async-start | bytes 3276800 | tf_op jit(solution)/shard_map/all_gather | solution.py:139
  (18 other events, 56.1 us)
Sparse Core Ops, SparseCore 0:
  99.0 51.3 reduce-scatter.1
  153.2 25.5 all-gather.1

commit v2 on v1

--- a/solution.py
+++ b/solution.py
@@ -1,7 +1,7 @@
 import jax
 import jax.numpy as jnp
 from jax import lax
-from jax.sharding import PartitionSpec as P
+from jax.sharding import Mesh, PartitionSpec as P
 
 STRETCH = 256
 NORM_GROUPS = 4
@@ -120,49 +120,61 @@
     )
     summed = fwd_all + bwd_all + skip_gain[None, :, None] * acts.astype(jnp.float32)
     gated = summed.reshape(tokens, heads * width) * jax.nn.silu(gate_acts.astype(jnp.float32))
-    grouped = gated.reshape(tokens, NORM_GROUPS // lax.axis_size("head"), -1)
+    grouped = gated.reshape(tokens, NORM_GROUPS // (lax.axis_size("head_chip") * lax.axis_size("head_core")), -1)
     scaled = grouped * lax.rsqrt(jnp.mean(grouped * grouped, axis=2, keepdims=True) + epsilon)
     mixed = (scaled.reshape(tokens, -1) * norm_gain[None, :]).astype(jnp.bfloat16)
     own_width = residual.shape[1]
-    offset = lax.axis_index("head") * own_width
+    offset = (lax.axis_index("head_chip") * lax.axis_size("head_core") + lax.axis_index("head_core")) * own_width
     partial_value = jnp.dot(mixed, out_weight, preferred_element_type=jnp.float32)
     own_cols = lax.dynamic_slice_in_dim(partial_value, offset, own_width, 1) + residual.astype(
         jnp.float32
     )
     partial_value = lax.dynamic_update_slice_in_dim(partial_value, own_cols, offset, 1)
-    encoded = lax.psum_scatter(partial_value, "head", scatter_dimension=0, tiled=True)
+    encoded = lax.psum_scatter(partial_value, "head_core", scatter_dimension=0, tiled=True)
+    encoded = lax.psum_scatter(encoded, "head_chip", scatter_dimension=0, tiled=True)
     normed = (
         encoded
         * lax.rsqrt(jnp.mean(encoded * encoded, axis=1, keepdims=True) + epsilon)
         * final_gain[None, :]
     ).astype(jnp.bfloat16)
-    normed = lax.all_gather(normed, "head", axis=0, tiled=True)
+    normed = lax.all_gather(normed, "head_chip", axis=0, tiled=True)
+    normed = lax.all_gather(normed, "head_core", axis=0, tiled=True)
     key_sum = jnp.dot(normed, key_weight, preferred_element_type=jnp.float32)
     value_sum = jnp.dot(normed, value_weight, preferred_element_type=jnp.float32)
     return (key_sum.astype(jnp.bfloat16), value_sum.astype(jnp.bfloat16))
 
 
+def split_head(mesh):
+    shape = dict(mesh.shape)
+    head = shape["head"]
+    cores = 2 if head % 2 == 0 else 1
+    devices = mesh.devices.reshape(shape["groups"], shape["seq"], head // cores, cores)
+    return Mesh(devices, ("groups", "seq", "head_chip", "head_core"))
+
+
 def solution(mesh):
+    mesh = split_head(mesh)
+    head = ("head_chip", "head_core")
     placed = (
-        P(("groups", "seq"), "head"),
-        P(("groups", "seq"), "head"),
+        P(("groups", "seq"), head),
+        P(("groups", "seq"), head),
         P(None, ("groups", "seq"), None),
         P(None, ("groups", "seq"), None),
-        P(None, ("groups", "seq"), "head"),
-        P("head"),
-        P("head"),
-        P("head"),
-        P("head"),
-        P("head", None),
-        P(("groups", "seq"), "head"),
+        P(None, ("groups", "seq"), head),
+        P(head),
+        P(head),
+        P(head),
+        P(head),
+        P(head, None),
+        P(("groups", "seq"), head),
         P(),
-        P(None, "head"),
-        P(None, "head"),
+        P(None, head),
+        P(None, head),
     )
     return jax.shard_map(
         per_device,
         mesh=mesh,
         in_specs=placed,
-        out_specs=(P(("groups", "seq"), "head"), P(("groups", "seq"), "head")),
+        out_specs=(P(("groups", "seq"), head), P(("groups", "seq"), head)),
         check_vma=False,
     )

time: 194 us -> 208 us (1.072)
  waiting for transfers between devices: 83.2 us -> 97.7 us
    all_gather x1 -> x2, waiting for transfers between devices: 25.7 us -> 37.1 us  [the longest x1 24.4 us: per_device(): normed = lax.all_gather(normed, 'head_chip', axis=0, tiled=True)]
    reduce_scatter x1 -> x2, waiting for transfers between devices: 51.5 us -> 54.5 us  [the longest x1 41.1 us: per_device(): lax.psum_scatter(encoded, 'head_chip', scatter_dimension=0, tiled=True)]
  transfers between devices with their start and end apart: 10 -> 12, of which waited for: 7 -> 8; matrix products, arithmetic and copies ran while one was open for 16% -> 15% of each run, Pallas kernels for 0% -> 0%
where the time goes in v2:
time: 208 us; the launch traced here: 207 us
  waiting for transfers between devices  97.7 us (47%)
  starting transfers between devices  32.7 us (16%)
  other arithmetic  25.1 us (12%)
  matrix products  23.4 us (11%)
  between operations  14.4 us (7%)
  local copies, waits for them, and re-layouts  13.8 us (7%)
    reduce_scatter x1, waiting for transfers between devices, per_device(): lax.psum_scatter(encoded, 'head_chip', scatter_dimension=0, tiled=True)  41.1 us
    ppermute x8, starting transfers between devices, passed_along(): lax.ppermute(value, axis, [(source, source + steps) for source in range(f...  32.6 us
    all_gather x1, waiting for transfers between devices, per_device(): normed = lax.all_gather(normed, 'head_chip', axis=0, tiled=True)  24.4 us
    reduce_scatter x1, waiting for transfers between devices, per_device(): lax.psum_scatter(partial_value, 'head_core', scatter_dimension=0, tiled=T...  13.4 us
    all_gather x1, waiting for transfers between devices, per_device(): normed = lax.all_gather(normed, 'head_core', axis=0, tiled=True)  12.8 us
    another operation x5, other arithmetic  7.66 us
    unnamed x67, local copies, waits for them, and re-layouts  6.38 us
    ppermute x8, waiting for transfers between devices, passed_along(): lax.ppermute(value, axis, [(source, source + steps) for source in range(f...  5.99 us
  transfers between devices with their start and end apart: 12, of which 8 were waited for; matrix products, arithmetic and copies ran while one was open for 15% of the time, Pallas kernels for 0%

profile of v2, /device:TPU:0, one launch (start us, length us, event | category | flops | bytes accessed | tf_op | source)
XLA Modules:
  0.0 207.2 jit_solution(6789798148636080469)
XLA Ops:
  10.6 5.0 %reduce-window.16 = f32[2,10,2,128]{3,1,2,0:T(8,128)S(1)} reduce-window(f32[2,10,2,128]{3,1,2,0:T(8,128)S(1)} %copy.44, f32[]{:T(128)} %constant.11.clone.1), window={size=1x1x1x128 pad=0_0x0_0x0_0x0_127}, to_apply=%region_2.3 | reduce-window | flops 650240 | bytes 40964 | tf_op jit(solution)/shard_map/reduce-window.2
  20.2 6.1 %collective-permute-start = (f32[10]{0:T(128)}, f32[10]{0:T(128)}, u32[]{:S(2)}, u32[]{:S(2)}) collective-permute-start(f32[10]{0:T(128)} %get-tuple-element.28), channel_id=1, source_target_pairs={{0,4},{4,8},{8,12},{1,5},{5,9},{9,13},{2,6},{6,10},{10,14},{3,7},{... | collective-permute-start | bytes 128 | tf_op jit(solution)/shard_map/ppermute | solution.py:19
  28.0 2.2 %copy.38 = bf16[512,640]{0,1:T(8,128)(2,1)} copy(bf16[512,640]{1,0:T(8,128)(2,1)} %param.14) | data formatting | bytes 1310720 | tf_op args[0]
  30.3 2.7 %reshape_reshape.4 = bf16[2,256,10,64]{1,0,3,2:T(2,128)(2,1)} reshape(bf16[512,640]{0,1:T(8,128)(2,1)} %copy.38) | data formatting | bytes 1310720 | tf_op jit(solution)/shard_map/reshape;reshape | solution.py:25
  34.3 1.8 convert_multiply_fusion.1
  39.4 4.7 %collective-permute-start.1 = (f32[10,64,128]{2,1,0:T(8,128)S(1)}, f32[10,64,128]{2,1,0:T(8,128)S(1)}, u32[]{:S(2)}, u32[]{:S(2)}) collective-permute-start(f32[10,64,128]{2,1,0:T(8,128)S(1)} %fusion.41), channel_id=1, source_target_pairs={{0,4},{4,8},{8,12},{1,5},{5,9},{9,13},{2,6},{6,10},{10,14},{3,7},{... | collective-permute-start | bytes 983048 | tf_op jit(solution)/shard_map/ppermute | solution.py:19
  45.2 2.6 %fusion.14 = f32[2,256,10,64]{1,3,2,0:T(8,128)} fusion(f32[2,10,256]{2,1,0:T(8,128)S(1)} %copy.48, f32[2,10,256]{2,1,0:T(8,128)S(1)} %copy.46, f32[2,256,256]{2,1,0:T(8,128)S(1)} %fusion.58, pred[256,256]{1,0:T(8,128)(4,1)S(1)} %iota_compare_fusion, bf16[2,256,10,64]{1,0,3,2:T(2,128)(2,1)S(1)} %copy-done.3), kind=kOutput, calls=%fused_computation.20 | convolution fusion | flops 174325760 | bytes 2596864 | tf_op jit(solution)/shard_map/bhts,bshp->bthp/dot_general | solution.py:44
  47.8 2.6 %fusion.15 = f32[2,256,10,64]{1,3,2,0:T(8,128)} fusion(f32[2,10,256]{2,1,0:T(8,128)S(1)} %copy.37, f32[2,10,256]{2,1,0:T(8,128)S(1)} %copy.35, f32[2,256,256]{2,1,0:T(8,128)S(1)} %fusion.57, pred[256,256]{1,0:T(8,128)(4,1)S(1)} %iota_compare_fusion.1, bf16[2,256,10,64]{1,0,3,2:T(2,128)(2,1)S(1)} %copy-done.3), kind=kOutput, calls=%fused_computation.21 | convolution fusion | flops 174325760 | bytes 2596864 | tf_op jit(solution)/shard_map/bhts,bshp->bthp/dot_general | solution.py:44
  51.2 5.4 %collective-permute-start.2 = (f32[10,64,128]{2,1,0:T(8,128)S(1)}, f32[10,64,128]{2,1,0:T(8,128)S(1)}, u32[]{:S(2)}, u32[]{:S(2)}) collective-permute-start(f32[10,64,128]{2,1,0:T(8,128)S(1)} %multiply_add_fusion.3), channel_id=1, source_target_pairs={{0,8},{4,12},{1,9},{5,13},{2,10},{6,14},{3,11},{7,15},{16,24},{20,... | collective-permute-start | bytes 983048 | tf_op jit(solution)/shard_map/ppermute | solution.py:19
  62.9 11.1 %collective-permute-start.3 = (f32[10,64,128]{2,1,0:T(8,128)}, f32[10,64,128]{2,1,0:T(8,128)}, u32[]{:S(2)}, u32[]{:S(2)}) collective-permute-start(f32[10,64,128]{2,1,0:T(8,128)} %multiply_add_fusion.2), channel_id=1, source_target_pairs={{0,4},{4,8},{8,12},{1,5},{5,9},{9,13},{2,6},{6,10},{10,14},{3,7},{... | collective-permute-start | bytes 983048 | tf_op jit(solution)/shard_map/ppermute | solution.py:19
  75.8 1.5 collective-permute-start.7
  78.3 2.2 %copy.56 = bf16[512,640]{0,1:T(8,128)(2,1)} copy(bf16[512,640]{1,0:T(8,128)(2,1)} %param.15) | data formatting | bytes 1310720 | tf_op args[1]
  80.7 2.4 %fusion.20 = f32[2,256,10,64]{1,3,2,0:T(8,128)S(1)} fusion(f32[2,256,10,64]{1,3,2,0:T(8,128)} %fusion.15, bf16[2,256,128,1]{2,1,3,0:T(8,128)(2,1)S(1)} %bitcast.131, f32[1,10,64,128]{3,2,1,0:T(8,128)} %slice_add_fusion.1, f32[2,256,10]{1,2,0:T(8,128)S(1)} %copy.40, f32[10,64,128]{2,1,0:T(8,128)} %collective-permute-done.3, f32[2,10]{1,0:T(2,128)S(1)} %stack.15), kind=kOutput, calls=%fused_computation.28 | convolution fusion | flops 504299520 | bytes 3428432 | tf_op jit(solution)/shard_map/btn,bhpn->bthp/dot_general | solution.py:87
  83.1 3.5 %collective-permute-done.7 = f32[10,64,128]{2,1,0:T(8,128)} collective-permute-done((f32[10,64,128]{2,1,0:T(8,128)}, f32[10,64,128]{2,1,0:T(8,128)}, u32[]{:S(2)}, u32[]{:S(2)}) %collective-permute-start.7) | collective-permute-done | bytes 327712 | tf_op jit(solution)/shard_map/ppermute | solution.py:19
  86.6 1.8 fusion.18
  91.5 4.7 %fusion.29 = f32[512,2560]{1,0:T(8,128)} fusion(bf16[640,2560]{1,0:T(8,128)(2,1)S(1)} %copy-done, f32[512,640]{0,1:T(8,128)S(1)} %get-tuple-element.5, f32[640]{0:T(1024)S(1)} %copy-done.21, f32[512]{0:T(512)S(1)} %add_rsqrt_fusion), kind=kOutput, calls=%fused_computation.44 | convolution fusion | flops 1678704640 | bytes 9835008 | tf_op jit(solution)/shard_map/dot_general | solution.py:128
  96.1 2.5 %add_dynamic-update-slice_fusion = f32[512,2560]{1,0:T(8,128)} fusion(f32[512,2560]{1,0:T(8,128)} %fusion.29, s32[]{:T(128)S(6)} %select_n.26, bf16[512,640]{1,0:T(8,128)(2,1)S(1)} %copy-done.11), kind=kLoop, calls=%fused_computation.39 | loop fusion | flops 655360 | bytes 3276804 | tf_op jit(solution)/shard_map/dynamic_update_slice | solution.py:132
  98.8 13.4 %reduce-scatter.3.cloned.1.call-done = f32[256,2560]{1,0:T(8,128)} async-done(((f32[512,2560]{1,0:T(8,128)}), f32[256,2560]{1,0:T(8,128)}) %reduce-scatter.3.cloned.1.call-update) | async-done | bytes 2621456 | tf_op jit(solution)/shard_map/reduce_scatter | solution.py:133
  112.3 41.1 %reduce-scatter.5.cloned.1.call-done = f32[128,2560]{1,0:T(8,128)} async-done(((f32[256,2560]{1,0:T(8,128)}), f32[128,2560]{1,0:T(8,128)}) %reduce-scatter.5.cloned.1.call-update) | async-done | bytes 1310736 | tf_op jit(solution)/shard_map/reduce_scatter | solution.py:134
  153.4 1.6 multiply_reduce_fusion
  156.2 24.4 %all-gather.3.cloned.1.call-done = bf16[256,2560]{1,0:T(8,128)(2,1)} async-done(((bf16[128,2560]{1,0:T(8,128)(2,1)}), bf16[256,2560]{1,0:T(8,128)(2,1)}) %all-gather.3.cloned.1.call-update) | async-done | bytes 1310736 | tf_op jit(solution)/shard_map/all_gather | solution.py:140
  180.6 12.8 %all-gather.5.cloned.1.call-done = bf16[512,2560]{1,0:T(8,128)(2,1)} async-done(((bf16[256,2560]{1,0:T(8,128)(2,1)}), bf16[512,2560]{1,0:T(8,128)(2,1)}) %all-gather.5.cloned.1.call-update) | async-done | bytes 2621456 | tf_op jit(solution)/shard_map/all_gather | solution.py:141
  193.3 5.0 %convolution_convert_fusion = bf16[512,512]{1,0:T(8,128)(2,1)} fusion(bf16[512,2560]{1,0:T(8,128)(2,1)} %all-gather.5.cloned.1.call-done, bf16[2560,512]{1,0:T(8,128)(2,1)} %param.27), kind=kOutput, calls=%fused_computation.42 | convolution fusion | flops 1342439424 | bytes 5767168 | tf_op jit(solution)/shard_map/dot_general | solution.py:143
  198.3 2.3 %convolution_convert_fusion.1 = bf16[512,512]{1,0:T(8,128)(2,1)} fusion(bf16[512,2560]{1,0:T(8,128)(2,1)S(1)} %copy-done.31, bf16[2560,512]{1,0:T(8,128)(2,1)S(1)} %copy-done.30), kind=kOutput, calls=%fused_computation.43 | convolution fusion | flops 1342439424 | bytes 5767168 | tf_op jit(solution)/shard_map/dot_general | solution.py:142
  (151 shorter events, 29.5 us)
Async XLA Ops:
  7.2 84.2 %copy-start = (bf16[640,2560]{1,0:T(8,128)(2,1)S(1)}, bf16[640,2560]{1,0:T(8,128)(2,1)}, u32[]{:S(2)}) copy-start(bf16[640,2560]{1,0:T(8,128)(2,1)} %param.23) | copy-start | bytes 9830404
  7.2 105.0 %reduce-scatter.3.cloned.1.call-start = ((), (), s32[]{:S(2)}) async-start(), calls=%async_computation.2 | async-start | bytes 7864320 | tf_op jit(solution)/shard_map/reduce_scatter | solution.py:133
  16.6 43.0 %collective-permute-start.4 = (f32[10]{0:T(128)}, f32[10]{0:T(128)}, u32[]{:S(2)}, u32[]{:S(2)}) collective-permute-start(f32[10]{0:T(128)} %get-tuple-element.22), channel_id=1, source_target_pairs={{4,0},{8,4},{12,8},{5,1},{9,5},{13,9},{6,2},{10,6},{14,10},{7,3},{... | collective-permute-start | bytes 128 | tf_op jit(solution)/shard_map/ppermute | solution.py:19
  19.4 7.5 %copy-start.15 = (f32[2,10,256]{2,0,1:T(2,128)}, f32[2,10,256]{2,0,1:T(2,128)S(1)}, u32[]{:S(2)}) copy-start(f32[2,10,256]{2,0,1:T(2,128)S(1)} %reduce_window_sum.45) | copy-start | bytes 61444
  19.6 7.2 %copy-start.23 = (f32[2,10]{1,0:T(2,128)}, f32[2,10]{1,0:T(2,128)S(1)}, u32[]{:S(2)}) copy-start(f32[2,10]{1,0:T(2,128)S(1)} %bitcast_exponential_fusion.2) | copy-start | bytes 244
  20.2 40.1 %collective-permute-start = (f32[10]{0:T(128)}, f32[10]{0:T(128)}, u32[]{:S(2)}, u32[]{:S(2)}) collective-permute-start(f32[10]{0:T(128)} %get-tuple-element.28), channel_id=1, source_target_pairs={{0,4},{4,8},{8,12},{1,5},{5,9},{9,13},{2,6},{6,10},{10,14},{3,7},{... | collective-permute-start | bytes 128 | tf_op jit(solution)/shard_map/ppermute | solution.py:19
  28.0 10.4 %copy-start.7 = (bf16[1,512,128]{2,1,0:T(8,128)(2,1)}, bf16[1,512,128]{2,1,0:T(8,128)(2,1)S(1)}, u32[]{:S(2)}) copy-start(bf16[1,512,128]{2,1,0:T(8,128)(2,1)S(1)} %get-tuple-element.13) | copy-start | bytes 393220
  37.1 19.5 %collective-permute-start.5 = (f32[10,64,128]{2,1,0:T(8,128)S(1)}, f32[10,64,128]{2,1,0:T(8,128)S(1)}, u32[]{:S(2)}, u32[]{:S(2)}) collective-permute-start(f32[10,64,128]{2,1,0:T(8,128)S(1)} %fusion.40), channel_id=1, source_target_pairs={{4,0},{8,4},{12,8},{5,1},{9,5},{13,9},{6,2},{10,6},{14,10},{7,3},{... | collective-permute-start | bytes 983048 | tf_op jit(solution)/shard_map/ppermute | solution.py:19
  39.4 11.1 %collective-permute-start.1 = (f32[10,64,128]{2,1,0:T(8,128)S(1)}, f32[10,64,128]{2,1,0:T(8,128)S(1)}, u32[]{:S(2)}, u32[]{:S(2)}) collective-permute-start(f32[10,64,128]{2,1,0:T(8,128)S(1)} %fusion.41), channel_id=1, source_target_pairs={{0,4},{4,8},{8,12},{1,5},{5,9},{9,13},{2,6},{6,10},{10,14},{3,7},{... | collective-permute-start | bytes 983048 | tf_op jit(solution)/shard_map/ppermute | solution.py:19
  51.2 10.9 %collective-permute-start.2 = (f32[10,64,128]{2,1,0:T(8,128)S(1)}, f32[10,64,128]{2,1,0:T(8,128)S(1)}, u32[]{:S(2)}, u32[]{:S(2)}) collective-permute-start(f32[10,64,128]{2,1,0:T(8,128)S(1)} %multiply_add_fusion.3), channel_id=1, source_target_pairs={{0,8},{4,12},{1,9},{5,13},{2,10},{6,14},{3,11},{7,15},{16,24},{20,... | collective-permute-start | bytes 983048 | tf_op jit(solution)/shard_map/ppermute | solution.py:19
  57.4 17.5 %collective-permute-start.6 = (f32[10,64,128]{2,1,0:T(8,128)S(1)}, f32[10,64,128]{2,1,0:T(8,128)S(1)}, u32[]{:S(2)}, u32[]{:S(2)}) collective-permute-start(f32[10,64,128]{2,1,0:T(8,128)S(1)} %multiply_add_fusion.1), channel_id=1, source_target_pairs={{8,0},{12,4},{9,1},{13,5},{10,2},{14,6},{11,3},{15,7},{24,16},{28,... | collective-permute-start | bytes 983048 | tf_op jit(solution)/shard_map/ppermute | solution.py:19
  60.8 17.2 %copy-start.29 = (f32[10]{0:T(128)S(1)}, f32[10]{0:T(128)}, u32[]{:S(2)}) copy-start(f32[10]{0:T(128)} %param.21) | copy-start | bytes 124
  60.8 17.3 %copy-start.28 = (f32[1,10]{1,0:T(1,128)S(1)}, f32[1,10]{1,0:T(1,128)}, u32[]{:S(2)}) copy-start(f32[1,10]{1,0:T(1,128)} %get-tuple-element.20) | copy-start | bytes 124
  60.8 17.4 %copy-start.20 = (f32[2,256,10]{1,0,2:T(2,128)S(1)}, f32[2,256,10]{1,0,2:T(2,128)}, u32[]{:S(2)}) copy-start(f32[2,256,10]{1,0,2:T(2,128)} %get-tuple-element.16) | copy-start | bytes 61444
  60.8 17.4 %copy-start.19 = (f32[2,256,10]{1,0,2:T(2,128)S(1)}, f32[2,256,10]{1,0,2:T(2,128)}, u32[]{:S(2)}) copy-start(f32[2,256,10]{1,0,2:T(2,128)} %get-tuple-element.31) | copy-start | bytes 61444
  62.9 17.8 %collective-permute-start.3 = (f32[10,64,128]{2,1,0:T(8,128)}, f32[10,64,128]{2,1,0:T(8,128)}, u32[]{:S(2)}, u32[]{:S(2)}) collective-permute-start(f32[10,64,128]{2,1,0:T(8,128)} %multiply_add_fusion.2), channel_id=1, source_target_pairs={{0,4},{4,8},{8,12},{1,5},{5,9},{9,13},{2,6},{6,10},{10,14},{3,7},{... | collective-permute-start | bytes 983048 | tf_op jit(solution)/shard_map/ppermute | solution.py:19
  75.8 10.9 %collective-permute-start.7 = (f32[10,64,128]{2,1,0:T(8,128)}, f32[10,64,128]{2,1,0:T(8,128)}, u32[]{:S(2)}, u32[]{:S(2)}) collective-permute-start(f32[10,64,128]{2,1,0:T(8,128)} %multiply_add_fusion), channel_id=1, source_target_pairs={{4,0},{8,4},{12,8},{5,1},{9,5},{13,9},{6,2},{10,6},{14,10},{7,3},{... | collective-permute-start | bytes 983048 | tf_op jit(solution)/shard_map/ppermute | solution.py:19
  80.7 5.9 %copy-start.5 = (f32[2,256,10,64]{1,3,2,0:T(8,128)S(1)}, f32[2,256,10,64]{1,3,2,0:T(8,128)}, u32[]{:S(2)}) copy-start(f32[2,256,10,64]{1,3,2,0:T(8,128)} %fusion.14) | copy-start | bytes 3932164
  80.7 5.9 %copy-start.6 = (f32[1,10,64,128]{3,2,1,0:T(8,128)S(1)}, f32[1,10,64,128]{3,2,1,0:T(8,128)}, u32[]{:S(2)}) copy-start(f32[1,10,64,128]{3,2,1,0:T(8,128)} %slice_add_fusion) | copy-start | bytes 983044
  80.7 5.9 %copy-start.10 = (bf16[1,512,128]{2,1,0:T(8,128)(2,1)S(1)}, bf16[1,512,128]{2,1,0:T(8,128)(2,1)}, u32[]{:S(2)}) copy-start(bf16[1,512,128]{2,1,0:T(8,128)(2,1)} %copy-done.9) | copy-start | bytes 393220
  98.7 54.6 %reduce-scatter.5.cloned.1.call-start = ((), (), s32[]{:S(2)}) async-start(), calls=%async_computation.3 | async-start | bytes 3932160 | tf_op jit(solution)/shard_map/reduce_scatter | solution.py:134
  112.2 42.8 %copy-start.22 = (f32[2560]{0:T(1024)S(1)}, f32[2560]{0:T(1024)}, u32[]{:S(2)}) copy-start(f32[2560]{0:T(1024)} %param.25) | copy-start | bytes 30724
  112.2 68.3 %all-gather.3.cloned.1.call-start = ((), (), s32[]{:S(2)}) async-start(), calls=%async_computation.4 | async-start | bytes 1966080 | tf_op jit(solution)/shard_map/all_gather | solution.py:140
  156.1 37.2 %all-gather.5.cloned.1.call-start = ((), (), s32[]{:S(2)}) async-start(), calls=%async_computation.5 | async-start | bytes 3932160 | tf_op jit(solution)/shard_map/all_gather | solution.py:141
  (20 other events, 67.7 us)
Sparse Core Ops, SparseCore 0:
  98.8 13.3 reduce-scatter.2
  114.5 38.7 reduce-scatter.4
  156.2 24.2 all-gather.2
  181.9 11.3 all-gather.4

commit v3 on v1

--- a/solution.py
+++ b/solution.py
@@ -67,6 +67,11 @@
 
 def relay(state, gain, axis, steps):
     count = lax.axis_size(axis)
+    if count <= 4:
+        entering = jnp.zeros_like(state)
+        for _ in range(count - 1):
+            entering = passed_along(gain[:, None, None] * entering + state, axis, steps)
+        return entering
     distance = 1
     while distance < count:
         got_state = passed_along(state, axis, distance * steps)

time: 194 us -> 178 us (0.918)
  starting transfers between devices: 32.6 us -> 19.4 us
  other arithmetic: 25.4 us -> 22 us
    ppermute x8 -> x6, starting transfers between devices: 32.5 us -> 19.3 us  [passed_along(): lax.ppermute(value, axis, [(source, source + steps) for source in range(f...]
    mul x4 -> x2, other arithmetic: 2.53 us -> 0.55 us  [relay(): entering = passed_along(gain[:, None, None] * entering + state, axis, steps)]
    ppermute x8 -> x6, waiting for transfers between devices: 5.95 us -> 6.89 us  [passed_along(): lax.ppermute(value, axis, [(source, source + steps) for source in range(f...]
    unnamed x67 -> x69, local copies, waits for them, and re-layouts: 6.37 us -> 6.95 us
  transfers between devices with their start and end apart: 10 -> 8, of which waited for: 7 -> 5; matrix products, arithmetic and copies ran while one was open for 16% -> 8% of each run, Pallas kernels for 0% -> 0%
where the time goes in v3:
time: 178 us; the launch traced here: 177 us
  waiting for transfers between devices  83.6 us (47%)
  matrix products  23.4 us (13%)
  other arithmetic  22 us (12%)
  starting transfers between devices  19.4 us (11%)
  between operations  14.7 us (8%)
  local copies, waits for them, and re-layouts  14.3 us (8%)
    reduce_scatter x1, waiting for transfers between devices, per_device(): lax.psum_scatter(partial_value, 'head', scatter_dimension=0, tiled=True)  51 us
    all_gather x1, waiting for transfers between devices, per_device(): normed = lax.all_gather(normed, 'head', axis=0, tiled=True)  25.7 us
    ppermute x6, starting transfers between devices, passed_along(): lax.ppermute(value, axis, [(source, source + steps) for source in range(f...  19.3 us
    another operation x5, other arithmetic  7.65 us
    unnamed x69, local copies, waits for them, and re-layouts  6.95 us
    ppermute x6, waiting for transfers between devices, passed_along(): lax.ppermute(value, axis, [(source, source + steps) for source in range(f...  6.89 us
    dot_general x2, matrix products, block_parts(): jnp.einsum('bhts,bshp->bthp', weights, acts_b, preferred_element_type=jnp...  5.22 us
    dot_general x1, matrix products, per_device(): jnp.dot(normed, value_weight, preferred_element_type=jnp.float32)  4.99 us
  transfers between devices with their start and end apart: 8, of which 5 were waited for; matrix products, arithmetic and copies ran while one was open for 8% of the time, Pallas kernels for 0%

profile of v3, /device:TPU:0, one launch (start us, length us, event | category | flops | bytes accessed | tf_op | source)
XLA Modules:
  0.0 177.4 jit_solution(18365593814081352419)
XLA Ops:
  9.1 1.4 multiply_bitcast_fusion
  10.6 5.0 %reduce-window.16 = f32[2,10,2,128]{3,1,2,0:T(8,128)S(1)} reduce-window(f32[2,10,2,128]{3,1,2,0:T(8,128)S(1)} %copy.44, f32[]{:T(128)} %constant.10.clone.1), window={size=1x1x1x128 pad=0_0x0_0x0_0x0_127}, to_apply=%region_2.3 | reduce-window | flops 650240 | bytes 40964 | tf_op jit(solution)/shard_map/reduce-window.2
  20.6 2.2 %copy.38 = bf16[512,640]{0,1:T(8,128)(2,1)} copy(bf16[512,640]{1,0:T(8,128)(2,1)} %param.14) | data formatting | bytes 1310720 | tf_op args[0]
  22.8 2.7 %reshape_reshape.4 = bf16[2,256,10,64]{1,0,3,2:T(2,128)(2,1)} reshape(bf16[512,640]{0,1:T(8,128)(2,1)} %copy.38) | data formatting | bytes 1310720 | tf_op jit(solution)/shard_map/reshape;reshape | solution.py:25
  25.5 1.4 bitcast_exponential_fusion.1
  26.9 1.8 %convert_multiply_fusion.1 = (f32[2,256,10,64]{1,0,3,2:T(2,128)S(1)}, f32[2,256,10,64]{1,0,3,2:T(2,128)S(1)}) fusion(bf16[2,256,10,64]{1,0,3,2:T(2,128)(2,1)} %reshape_reshape.4, f32[2,256,10]{1,0,2:T(2,128)S(1)} %get-tuple-element.25, f32[2,256,10]{1,0,2:T(2,128)S(1)} %get-tuple-element.36), kind=kLoop, calls=%fused_computation.18 | loop fusion | flops 983040 | bytes 3317760 | tf_op jit(solution)/shard_map/mul | solution.py:46
  32.0 5.7 %collective-permute-start = (f32[10,64,128]{2,1,0:T(8,128)S(1)}, f32[10,64,128]{2,1,0:T(8,128)S(1)}, u32[]{:S(2)}, u32[]{:S(2)}) collective-permute-start(f32[10,64,128]{2,1,0:T(8,128)S(1)} %get-tuple-element.12), channel_id=1, source_target_pairs={{0,4},{4,8},{8,12},{1,5},{5,9},{9,13},{2,6},{6,10},{10,14},{3,7},{... | collective-permute-start | bytes 983048 | tf_op jit(solution)/shard_map/ppermute | solution.py:19
  38.8 2.6 %fusion.14 = f32[2,256,10,64]{1,3,2,0:T(8,128)} fusion(f32[2,10,256]{2,1,0:T(8,128)S(1)} %copy.48, f32[2,10,256]{2,1,0:T(8,128)S(1)} %copy.46, f32[2,256,256]{2,1,0:T(8,128)S(1)} %fusion.60, pred[256,256]{1,0:T(8,128)(4,1)S(1)} %iota_compare_fusion, bf16[2,256,10,64]{1,0,3,2:T(2,128)(2,1)S(1)} %copy-done.3), kind=kOutput, calls=%fused_computation.20 | convolution fusion | flops 174325760 | bytes 2596864 | tf_op jit(solution)/shard_map/bhts,bshp->bthp/dot_general | solution.py:44
  41.4 2.6 %fusion.15 = f32[2,256,10,64]{1,3,2,0:T(8,128)} fusion(f32[2,10,256]{2,1,0:T(8,128)S(1)} %copy.37, f32[2,10,256]{2,1,0:T(8,128)S(1)} %copy.35, f32[2,256,256]{2,1,0:T(8,128)S(1)} %fusion.59, pred[256,256]{1,0:T(8,128)(4,1)S(1)} %iota_compare_fusion.1, bf16[2,256,10,64]{1,0,3,2:T(2,128)(2,1)S(1)} %copy-done.3), kind=kOutput, calls=%fused_computation.21 | convolution fusion | flops 174325760 | bytes 2596864 | tf_op jit(solution)/shard_map/bhts,bshp->bthp/dot_general | solution.py:44
  44.7 4.4 %collective-permute-start.1 = (f32[10,64,128]{2,1,0:T(8,128)S(1)}, f32[10,64,128]{2,1,0:T(8,128)S(1)}, u32[]{:S(2)}, u32[]{:S(2)}) collective-permute-start(f32[10,64,128]{2,1,0:T(8,128)S(1)} %multiply_add_fusion.3), channel_id=1, source_target_pairs={{0,4},{4,8},{8,12},{1,5},{5,9},{9,13},{2,6},{6,10},{10,14},{3,7},{... | collective-permute-start | bytes 983048 | tf_op jit(solution)/shard_map/ppermute | solution.py:19
  51.4 3.8 %collective-permute-done.1 = f32[10,64,128]{2,1,0:T(8,128)S(1)} collective-permute-done((f32[10,64,128]{2,1,0:T(8,128)S(1)}, f32[10,64,128]{2,1,0:T(8,128)S(1)}, u32[]{:S(2)}, u32[]{:S(2)}) %collective-permute-start.1) | collective-permute-done | bytes 327712 | tf_op jit(solution)/shard_map/ppermute | solution.py:19
  56.0 5.1 %collective-permute-start.2 = (f32[10,64,128]{2,1,0:T(8,128)}, f32[10,64,128]{2,1,0:T(8,128)}, u32[]{:S(2)}, u32[]{:S(2)}) collective-permute-start(f32[10,64,128]{2,1,0:T(8,128)} %multiply_add_fusion.2), channel_id=1, source_target_pairs={{0,4},{4,8},{8,12},{1,5},{5,9},{9,13},{2,6},{6,10},{10,14},{3,7},{... | collective-permute-start | bytes 983048 | tf_op jit(solution)/shard_map/ppermute | solution.py:19
  62.0 1.5 collective-permute-start.5
  64.5 2.2 %copy.56 = bf16[512,640]{0,1:T(8,128)(2,1)} copy(bf16[512,640]{1,0:T(8,128)(2,1)} %param.15) | data formatting | bytes 1310720 | tf_op args[1]
  66.6 2.4 %fusion.20 = f32[2,256,10,64]{1,3,2,0:T(8,128)S(1)} fusion(f32[2,256,10,64]{1,3,2,0:T(8,128)} %fusion.15, bf16[2,256,128,1]{2,1,3,0:T(8,128)(2,1)S(1)} %bitcast.131, f32[1,10,64,128]{3,2,1,0:T(8,128)} %slice_add_fusion.1, f32[2,256,10]{1,2,0:T(8,128)S(1)} %copy.40, f32[10,64,128]{2,1,0:T(8,128)} %collective-permute-done.2, f32[2,10]{1,0:T(2,128)S(1)} %stack.15), kind=kOutput, calls=%fused_computation.28 | convolution fusion | flops 504299520 | bytes 3428432 | tf_op jit(solution)/shard_map/btn,bhpn->bthp/dot_general | solution.py:92
  69.1 2.5 %collective-permute-done.5 = f32[10,64,128]{2,1,0:T(8,128)} collective-permute-done((f32[10,64,128]{2,1,0:T(8,128)}, f32[10,64,128]{2,1,0:T(8,128)}, u32[]{:S(2)}, u32[]{:S(2)}) %collective-permute-start.5) | collective-permute-done | bytes 327712 | tf_op jit(solution)/shard_map/ppermute | solution.py:19
  71.6 1.8 %fusion.18 = f32[2,256,10,64]{1,3,2,0:T(8,128)S(1)} fusion(f32[2,256,10,64]{1,3,2,0:T(8,128)S(1)} %fusion.20, f32[2,256,10,64]{1,3,2,0:T(8,128)S(1)} %copy-done.5, bf16[2,256,128,1]{2,1,3,0:T(8,128)(2,1)S(1)} %bitcast.137, f32[1,10,64,128]{3,2,1,0:T(8,128)S(1)} %copy-done.6, f32[2,256,10]{1,2,0:T(8,128)S(1)} %copy.50, ...), kind=kOutput, calls=%fused_computation.25 | convolution fusion | flops 504627200 | bytes 4739152 | tf_op jit(solution)/shard_map/btn,bhpn->bthp/dot_general | solution.py:92
  76.4 4.7 %fusion.29 = f32[512,2560]{1,0:T(8,128)} fusion(bf16[640,2560]{1,0:T(8,128)(2,1)S(1)} %copy-done, f32[512,640]{0,1:T(8,128)S(1)} %get-tuple-element.5, f32[640]{0:T(1024)S(1)} %copy-done.21, f32[512]{0:T(512)S(1)} %add_rsqrt_fusion), kind=kOutput, calls=%fused_computation.44 | convolution fusion | flops 1678704640 | bytes 9835008 | tf_op jit(solution)/shard_map/dot_general | solution.py:133
  81.1 2.6 %add_dynamic-update-slice_fusion = f32[512,2560]{1,0:T(8,128)} fusion(f32[512,2560]{1,0:T(8,128)} %fusion.29, s32[]{:T(128)S(6)} %select_n.26, bf16[512,640]{1,0:T(8,128)(2,1)S(1)} %copy-done.11), kind=kLoop, calls=%fused_computation.39 | loop fusion | flops 655360 | bytes 3276804 | tf_op jit(solution)/shard_map/dynamic_update_slice | solution.py:137
  83.8 51.0 %reduce-scatter.2.cloned.1.call-done = f32[128,2560]{1,0:T(8,128)} async-done(((f32[512,2560]{1,0:T(8,128)}), f32[128,2560]{1,0:T(8,128)}) %reduce-scatter.2.cloned.1.call-update) | async-done | bytes 1310736 | tf_op jit(solution)/shard_map/reduce_scatter | solution.py:138
  134.7 1.6 multiply_reduce_fusion
  137.5 25.7 %all-gather.2.cloned.1.call-done = bf16[512,2560]{1,0:T(8,128)(2,1)} async-done(((bf16[128,2560]{1,0:T(8,128)(2,1)}), bf16[512,2560]{1,0:T(8,128)(2,1)}) %all-gather.2.cloned.1.call-update) | async-done | bytes 2621456 | tf_op jit(solution)/shard_map/all_gather | solution.py:144
  163.2 5.0 %convolution_convert_fusion = bf16[512,512]{1,0:T(8,128)(2,1)} fusion(bf16[512,2560]{1,0:T(8,128)(2,1)} %all-gather.2.cloned.1.call-done, bf16[2560,512]{1,0:T(8,128)(2,1)} %param.27), kind=kOutput, calls=%fused_computation.42 | convolution fusion | flops 1342439424 | bytes 5767168 | tf_op jit(solution)/shard_map/dot_general | solution.py:146
  168.2 2.3 %convolution_convert_fusion.1 = bf16[512,512]{1,0:T(8,128)(2,1)} fusion(bf16[512,2560]{1,0:T(8,128)(2,1)S(1)} %copy-done.32, bf16[2560,512]{1,0:T(8,128)(2,1)S(1)} %copy-done.31), kind=kOutput, calls=%fused_computation.43 | convolution fusion | flops 1342439424 | bytes 5767168 | tf_op jit(solution)/shard_map/dot_general | solution.py:145
  (141 shorter events, 20.6 us)
Async XLA Ops:
  7.2 69.1 %copy-start = (bf16[640,2560]{1,0:T(8,128)(2,1)S(1)}, bf16[640,2560]{1,0:T(8,128)(2,1)}, u32[]{:S(2)}) copy-start(bf16[640,2560]{1,0:T(8,128)(2,1)} %param.23) | copy-start | bytes 9830404
  7.2 127.6 %reduce-scatter.2.cloned.1.call-start = ((), (), s32[]{:S(2)}) async-start(), calls=%async_computation.1 | async-start | bytes 6553600 | tf_op jit(solution)/shard_map/reduce_scatter | solution.py:138
  20.6 10.4 %copy-start.7 = (bf16[1,512,128]{2,1,0:T(8,128)(2,1)}, bf16[1,512,128]{2,1,0:T(8,128)(2,1)S(1)}, u32[]{:S(2)}) copy-start(bf16[1,512,128]{2,1,0:T(8,128)(2,1)S(1)} %get-tuple-element.21) | copy-start | bytes 393220
  29.7 19.5 %collective-permute-start.3 = (f32[10,64,128]{2,1,0:T(8,128)S(1)}, f32[10,64,128]{2,1,0:T(8,128)S(1)}, u32[]{:S(2)}, u32[]{:S(2)}) collective-permute-start(f32[10,64,128]{2,1,0:T(8,128)S(1)} %get-tuple-element.6), channel_id=1, source_target_pairs={{4,0},{8,4},{12,8},{5,1},{9,5},{13,9},{6,2},{10,6},{14,10},{7,3},{... | collective-permute-start | bytes 983048 | tf_op jit(solution)/shard_map/ppermute | solution.py:19
  31.0 6.7 %copy-start.16 = (f32[2,10,256]{2,0,1:T(2,128)S(1)}, f32[2,10,256]{2,0,1:T(2,128)}, u32[]{:S(2)}) copy-start(f32[2,10,256]{2,0,1:T(2,128)} %copy-done.15) | copy-start | bytes 61444
  31.0 6.8 %copy-start.14 = (f32[2,10,256]{2,0,1:T(2,128)S(1)}, f32[2,10,256]{2,0,1:T(2,128)}, u32[]{:S(2)}) copy-start(f32[2,10,256]{2,0,1:T(2,128)} %copy-done.13) | copy-start | bytes 61444
  31.0 6.8 %copy-start.18 = (f32[2,256,10]{1,0,2:T(2,128)S(1)}, f32[2,256,10]{1,0,2:T(2,128)}, u32[]{:S(2)}) copy-start(f32[2,256,10]{1,0,2:T(2,128)} %get-tuple-element.32) | copy-start | bytes 61444
  31.8 6.0 %copy-start.17 = (f32[2,256,10]{1,0,2:T(2,128)S(1)}, f32[2,256,10]{1,0,2:T(2,128)}, u32[]{:S(2)}) copy-start(f32[2,256,10]{1,0,2:T(2,128)} %get-tuple-element.11) | copy-start | bytes 61444
  31.8 6.1 %copy-start.12 = (bf16[2,512,128]{2,1,0:T(8,128)(2,1)S(1)}, bf16[2,512,128]{2,1,0:T(8,128)(2,1)}, u32[]{:S(2)}) copy-start(bf16[2,512,128]{2,1,0:T(8,128)(2,1)} %param.17) | copy-start | bytes 786436
  31.8 6.1 %copy-start.8 = (bf16[1,512,128]{2,1,0:T(8,128)(2,1)S(1)}, bf16[1,512,128]{2,1,0:T(8,128)(2,1)}, u32[]{:S(2)}) copy-start(bf16[1,512,128]{2,1,0:T(8,128)(2,1)} %copy-done.7) | copy-start | bytes 393220
  32.0 6.8 %copy-start.3 = (bf16[2,256,10,64]{1,0,3,2:T(2,128)(2,1)S(1)}, bf16[2,256,10,64]{1,0,3,2:T(2,128)(2,1)}, u32[]{:S(2)}) copy-start(bf16[2,256,10,64]{1,0,3,2:T(2,128)(2,1)} %reshape_reshape.4) | copy-start | bytes 1966084
  32.0 12.6 %collective-permute-start = (f32[10,64,128]{2,1,0:T(8,128)S(1)}, f32[10,64,128]{2,1,0:T(8,128)S(1)}, u32[]{:S(2)}, u32[]{:S(2)}) collective-permute-start(f32[10,64,128]{2,1,0:T(8,128)S(1)} %get-tuple-element.12), channel_id=1, source_target_pairs={{0,4},{4,8},{8,12},{1,5},{5,9},{9,13},{2,6},{6,10},{10,14},{3,7},{... | collective-permute-start | bytes 983048 | tf_op jit(solution)/shard_map/ppermute | solution.py:19
  41.4 7.7 %copy-start.25 = (f32[10]{0:T(128)S(1)}, f32[10]{0:T(128)}, u32[]{:S(2)}) copy-start(f32[10]{0:T(128)} %get-tuple-element.9) | copy-start | bytes 124
  44.7 10.5 %collective-permute-start.1 = (f32[10,64,128]{2,1,0:T(8,128)S(1)}, f32[10,64,128]{2,1,0:T(8,128)S(1)}, u32[]{:S(2)}, u32[]{:S(2)}) collective-permute-start(f32[10,64,128]{2,1,0:T(8,128)S(1)} %multiply_add_fusion.3), channel_id=1, source_target_pairs={{0,4},{4,8},{8,12},{1,5},{5,9},{9,13},{2,6},{6,10},{10,14},{3,7},{... | collective-permute-start | bytes 983048 | tf_op jit(solution)/shard_map/ppermute | solution.py:19
  49.3 11.9 %collective-permute-start.4 = (f32[10,64,128]{2,1,0:T(8,128)S(1)}, f32[10,64,128]{2,1,0:T(8,128)S(1)}, u32[]{:S(2)}, u32[]{:S(2)}) collective-permute-start(f32[10,64,128]{2,1,0:T(8,128)S(1)} %multiply_add_fusion.1), channel_id=1, source_target_pairs={{4,0},{8,4},{12,8},{5,1},{9,5},{13,9},{6,2},{10,6},{14,10},{7,3},{... | collective-permute-start | bytes 983048 | tf_op jit(solution)/shard_map/ppermute | solution.py:19
  51.4 12.9 %copy-start.30 = (f32[10]{0:T(128)S(1)}, f32[10]{0:T(128)}, u32[]{:S(2)}) copy-start(f32[10]{0:T(128)} %param.21) | copy-start | bytes 124
  51.4 13.0 %copy-start.29 = (f32[1,10]{1,0:T(1,128)S(1)}, f32[1,10]{1,0:T(1,128)}, u32[]{:S(2)}) copy-start(f32[1,10]{1,0:T(1,128)} %get-tuple-element.28) | copy-start | bytes 124
  51.4 13.1 %copy-start.20 = (f32[2,256,10]{1,0,2:T(2,128)S(1)}, f32[2,256,10]{1,0,2:T(2,128)}, u32[]{:S(2)}) copy-start(f32[2,256,10]{1,0,2:T(2,128)} %get-tuple-element.24) | copy-start | bytes 61444
  51.4 13.1 %copy-start.19 = (f32[2,256,10]{1,0,2:T(2,128)S(1)}, f32[2,256,10]{1,0,2:T(2,128)}, u32[]{:S(2)}) copy-start(f32[2,256,10]{1,0,2:T(2,128)} %get-tuple-element.37) | copy-start | bytes 61444
  56.0 10.6 %collective-permute-start.2 = (f32[10,64,128]{2,1,0:T(8,128)}, f32[10,64,128]{2,1,0:T(8,128)}, u32[]{:S(2)}, u32[]{:S(2)}) collective-permute-start(f32[10,64,128]{2,1,0:T(8,128)} %multiply_add_fusion.2), channel_id=1, source_target_pairs={{0,4},{4,8},{8,12},{1,5},{5,9},{9,13},{2,6},{6,10},{10,14},{3,7},{... | collective-permute-start | bytes 983048 | tf_op jit(solution)/shard_map/ppermute | solution.py:19
  62.0 9.6 %collective-permute-start.5 = (f32[10,64,128]{2,1,0:T(8,128)}, f32[10,64,128]{2,1,0:T(8,128)}, u32[]{:S(2)}, u32[]{:S(2)}) collective-permute-start(f32[10,64,128]{2,1,0:T(8,128)} %multiply_add_fusion), channel_id=1, source_target_pairs={{4,0},{8,4},{12,8},{5,1},{9,5},{13,9},{6,2},{10,6},{14,10},{7,3},{... | collective-permute-start | bytes 983048 | tf_op jit(solution)/shard_map/ppermute | solution.py:19
  83.7 52.7 %copy-start.22 = (f32[2560]{0:T(1024)S(1)}, f32[2560]{0:T(1024)}, u32[]{:S(2)}) copy-start(f32[2560]{0:T(1024)} %param.25) | copy-start | bytes 30724
  83.7 79.5 %all-gather.2.cloned.1.call-start = ((), (), s32[]{:S(2)}) async-start(), calls=%async_computation.2 | async-start | bytes 3276800 | tf_op jit(solution)/shard_map/all_gather | solution.py:144
  163.2 5.0 %copy-start.32 = (bf16[512,2560]{1,0:T(8,128)(2,1)S(1)}, bf16[512,2560]{1,0:T(8,128)(2,1)}, u32[]{:S(2)}) copy-start(bf16[512,2560]{1,0:T(8,128)(2,1)} %all-gather.2.cloned.1.call-done) | copy-start | bytes 7864324
  (17 other events, 36.9 us)
Sparse Core Ops, SparseCore 0:
  83.8 50.8 reduce-scatter.1
  137.6 25.5 all-gather.1

commit v4 on v3

--- a/solution.py
+++ b/solution.py
@@ -27,14 +27,16 @@
     reads_b = reads.reshape(count, STRETCH, -1)
     steps_b = steps.reshape(count, STRETCH, heads)
     rates_b = rates.reshape(count, STRETCH, heads)
-    cum_rate = lax.cumsum(rates_b, axis=1, reverse=reverse)
-    block_total = cum_rate[:, 0] if reverse else cum_rate[:, -1]
-    along = jnp.transpose(cum_rate, (0, 2, 1))
     position = jnp.arange(STRETCH)
     if reverse:
         causal = position[:, None] <= position[None, :]
     else:
         causal = position[:, None] >= position[None, :]
+    cum_rate = jnp.einsum(
+        "ts,bsh->bth", causal.astype(jnp.float32), rates_b, precision=highest
+    )
+    block_total = cum_rate[:, 0] if reverse else cum_rate[:, -1]
+    along = jnp.transpose(cum_rate, (0, 2, 1))
     spans = along[:, :, :, None] - along[:, :, None, :]
     decays = jnp.exp(jnp.where(causal[None, None], spans, -1e30))
     intersection = jnp.einsum("btn,bsn->bts", reads_b, writes_b, preferred_element_type=jnp.float32)
@@ -130,21 +132,28 @@
     mixed = (scaled.reshape(tokens, -1) * norm_gain[None, :]).astype(jnp.bfloat16)
     own_width = residual.shape[1]
     offset = lax.axis_index("head") * own_width
-    partial_value = jnp.dot(mixed, out_weight, preferred_element_type=jnp.float32)
-    own_cols = lax.dynamic_slice_in_dim(partial_value, offset, own_width, 1) + residual.astype(
-        jnp.float32
-    )
-    partial_value = lax.dynamic_update_slice_in_dim(partial_value, own_cols, offset, 1)
-    encoded = lax.psum_scatter(partial_value, "head", scatter_dimension=0, tiled=True)
-    normed = (
-        encoded
-        * lax.rsqrt(jnp.mean(encoded * encoded, axis=1, keepdims=True) + epsilon)
-        * final_gain[None, :]
-    ).astype(jnp.bfloat16)
-    normed = lax.all_gather(normed, "head", axis=0, tiled=True)
-    key_sum = jnp.dot(normed, key_weight, preferred_element_type=jnp.float32)
-    value_sum = jnp.dot(normed, value_weight, preferred_element_type=jnp.float32)
-    return (key_sum.astype(jnp.bfloat16), value_sum.astype(jnp.bfloat16))
+    chunks = 2 if tokens % (2 * lax.axis_size("head")) == 0 else 1
+    rows = tokens // chunks
+    keys, values = [], []
+    for chunk in range(chunks):
+        part = slice(chunk * rows, (chunk + 1) * rows)
+        partial_value = jnp.dot(mixed[part], out_weight, preferred_element_type=jnp.float32)
+        own_cols = lax.dynamic_slice_in_dim(partial_value, offset, own_width, 1) + residual[
+            part
+        ].astype(jnp.float32)
+        partial_value = lax.dynamic_update_slice_in_dim(partial_value, own_cols, offset, 1)
+        encoded = lax.psum_scatter(partial_value, "head", scatter_dimension=0, tiled=True)
+        normed = (
+            encoded
+            * lax.rsqrt(jnp.mean(encoded * encoded, axis=1, keepdims=True) + epsilon)
+            * final_gain[None, :]
+        ).astype(jnp.bfloat16)
+        normed = lax.all_gather(normed, "head", axis=0, tiled=True)
+        keys.append(jnp.dot(normed, key_weight, preferred_element_type=jnp.float32).astype(jnp.bfloat16))
+        values.append(
+            jnp.dot(normed, value_weight, preferred_element_type=jnp.float32).astype(jnp.bfloat16)
+        )
+    return (jnp.concatenate(keys, axis=0), jnp.concatenate(values, axis=0))
 
 
 def solution(mesh):

time: 178 us -> 206 us (1.16)
  waiting for transfers between devices: 83.6 us -> 113 us
  other arithmetic: 22 us -> 17.6 us
  matrix products: 23.4 us -> 26.6 us
    reduce_scatter x1 -> x2, waiting for transfers between devices: 51 us -> 69.7 us  [per_device(): lax.psum_scatter(partial_value, 'head', scatter_dimension=0, tiled=True)]
    all_gather x1 -> x2, waiting for transfers between devices: 25.7 us -> 35 us  [per_device(): normed = lax.all_gather(normed, 'head', axis=0, tiled=True)]
    another operation x7 -> x0, other arithmetic: 7.8 us -> none
    dot_general x2 -> x6, matrix products: 6.99 us -> 13.5 us  [the longest x2 6.1 us: per_device(): jnp.dot(normed, key_weight, preferred_element_type=jnp.float32)]
    dot_general x1 -> x2, matrix products: 4.99 us -> 1.67 us  [per_device(): jnp.dot(normed, value_weight, preferred_element_type=jnp.float32)]
    unnamed x69 -> x59, local copies, waits for them, and re-layouts: 6.95 us -> 6.51 us
  transfers between devices with their start and end apart: 8 -> 10, of which waited for: 5 -> 7; matrix products, arithmetic and copies ran while one was open for 8% -> 9% of each run, Pallas kernels for 0% -> 0%
where the time goes in v4:
time: 206 us
  waiting for transfers between devices  113 us (55%)
  matrix products  26.6 us (13%)
  starting transfers between devices  19.6 us (10%)
  other arithmetic  17.6 us (9%)
  local copies, waits for them, and re-layouts  14.5 us (7%)
  between operations  14.3 us (7%)
    reduce_scatter x2, waiting for transfers between devices, per_device(): lax.psum_scatter(partial_value, 'head', scatter_dimension=0, tiled=True)  69.7 us
    all_gather x2, waiting for transfers between devices, per_device(): normed = lax.all_gather(normed, 'head', axis=0, tiled=True)  35 us
    ppermute x6, starting transfers between devices, passed_along(): lax.ppermute(value, axis, [(source, source + steps) for source in range(f...  19.4 us
    ppermute x6, waiting for transfers between devices, passed_along(): lax.ppermute(value, axis, [(source, source + steps) for source in range(f...  7.18 us
    unnamed x59, local copies, waits for them, and re-layouts  6.51 us
    dot_general x2, matrix products, per_device(): jnp.dot(normed, key_weight, preferred_element_type=jnp.float32)  6.1 us
    dot_general x2, matrix products, per_device(): jnp.dot(mixed[part], out_weight, preferred_element_type=jnp.float32)  5.47 us
    dot_general x2, matrix products, block_parts(): jnp.einsum('bhts,bshp->bthp', weights, acts_b, preferred_element_type=jnp...  5.25 us
  transfers between devices with their start and end apart: 10, of which 7 were waited for; matrix products, arithmetic and copies ran while one was open for 9% of the time, Pallas kernels for 0%

profile of v4, /device:TPU:0, one launch (start us, length us, event | category | flops | bytes accessed | tf_op | source)
XLA Modules:
  0.0 205.7 jit_solution(16849655217689260363)
XLA Ops:
  15.6 2.2 %copy.20 = bf16[512,640]{0,1:T(8,128)(2,1)} copy(bf16[512,640]{1,0:T(8,128)(2,1)} %param.14) | data formatting | bytes 1310720 | tf_op args[0]
  17.8 2.7 %reshape_reshape.4 = bf16[2,256,10,64]{1,0,3,2:T(2,128)(2,1)} reshape(bf16[512,640]{0,1:T(8,128)(2,1)} %copy.20) | data formatting | bytes 1310720 | tf_op jit(solution)/shard_map/reshape;reshape | solution.py:25
  20.4 1.8 convert_multiply_fusion.1
  25.4 5.7 %collective-permute-start = (f32[10,64,128]{2,1,0:T(8,128)S(1)}, f32[10,64,128]{2,1,0:T(8,128)S(1)}, u32[]{:S(2)}, u32[]{:S(2)}) collective-permute-start(f32[10,64,128]{2,1,0:T(8,128)S(1)} %get-tuple-element.10), channel_id=1, source_target_pairs={{0,4},{4,8},{8,12},{1,5},{5,9},{9,13},{2,6},{6,10},{10,14},{3,7},{... | collective-permute-start | bytes 983048 | tf_op jit(solution)/shard_map/ppermute | solution.py:19
  31.9 2.6 %fusion.14 = f32[2,256,10,64]{1,3,2,0:T(8,128)} fusion(f32[2,10,256]{2,1,0:T(8,128)S(1)} %copy-done.19, f32[2,10,256]{2,1,0:T(8,128)S(1)} %copy-done.15, f32[2,256,256]{2,1,0:T(8,128)S(1)} %fusion.83, pred[256,256]{1,0:T(8,128)(4,1)S(1)} %iota_compare_fusion, bf16[2,256,10,64]{1,0,3,2:T(2,128)(2,1)S(1)} %copy-done.2), kind=kOutput, calls=%fused_computation.20 | convolution fusion | flops 174325760 | bytes 2596864 | tf_op jit(solution)/shard_map/bhts,bshp->bthp/dot_general | solution.py:46
  34.6 2.6 %fusion.15 = f32[2,256,10,64]{1,3,2,0:T(8,128)} fusion(f32[2,10,256]{2,1,0:T(8,128)S(1)} %copy-done.18, f32[2,10,256]{2,1,0:T(8,128)S(1)} %copy-done.17, f32[2,256,256]{2,1,0:T(8,128)S(1)} %fusion.82, pred[256,256]{1,0:T(8,128)(4,1)S(1)} %iota_compare_fusion.1, bf16[2,256,10,64]{1,0,3,2:T(2,128)(2,1)S(1)} %copy-done.2), kind=kOutput, calls=%fused_computation.21 | convolution fusion | flops 174325760 | bytes 2596864 | tf_op jit(solution)/shard_map/bhts,bshp->bthp/dot_general | solution.py:46
  38.2 4.4 %collective-permute-start.1 = (f32[10,64,128]{2,1,0:T(8,128)S(1)}, f32[10,64,128]{2,1,0:T(8,128)S(1)}, u32[]{:S(2)}, u32[]{:S(2)}) collective-permute-start(f32[10,64,128]{2,1,0:T(8,128)S(1)} %multiply_add_fusion.3), channel_id=1, source_target_pairs={{0,4},{4,8},{8,12},{1,5},{5,9},{9,13},{2,6},{6,10},{10,14},{3,7},{... | collective-permute-start | bytes 983048 | tf_op jit(solution)/shard_map/ppermute | solution.py:19
  44.9 3.8 %collective-permute-done.1 = f32[10,64,128]{2,1,0:T(8,128)S(1)} collective-permute-done((f32[10,64,128]{2,1,0:T(8,128)S(1)}, f32[10,64,128]{2,1,0:T(8,128)S(1)}, u32[]{:S(2)}, u32[]{:S(2)}) %collective-permute-start.1) | collective-permute-done | bytes 327712 | tf_op jit(solution)/shard_map/ppermute | solution.py:19
  49.5 5.2 %collective-permute-start.2 = (f32[10,64,128]{2,1,0:T(8,128)}, f32[10,64,128]{2,1,0:T(8,128)}, u32[]{:S(2)}, u32[]{:S(2)}) collective-permute-start(f32[10,64,128]{2,1,0:T(8,128)} %multiply_add_fusion.2), channel_id=1, source_target_pairs={{0,4},{4,8},{8,12},{1,5},{5,9},{9,13},{2,6},{6,10},{10,14},{3,7},{... | collective-permute-start | bytes 983048 | tf_op jit(solution)/shard_map/ppermute | solution.py:19
  55.6 1.5 collective-permute-start.5
  58.0 2.2 %copy.30 = bf16[512,640]{0,1:T(8,128)(2,1)} copy(bf16[512,640]{1,0:T(8,128)(2,1)} %param.15) | data formatting | bytes 1310720 | tf_op args[1]
  60.3 2.4 %fusion.20 = f32[2,256,10,64]{1,3,2,0:T(8,128)S(1)} fusion(f32[2,256,10,64]{1,3,2,0:T(8,128)} %fusion.15, bf16[2,256,128,1]{2,1,3,0:T(8,128)(2,1)S(1)} %bitcast.128, f32[1,10,64,128]{3,2,1,0:T(8,128)} %slice_add_fusion.1, f32[2,256,10]{1,2,0:T(8,128)S(1)} %copy-done.12, f32[10,64,128]{2,1,0:T(8,128)} %collective-permute-done.2, f32[2,10]{1,0:T(2,128)S(1)} %stack.15), kind=kOutput, calls=%fused_computation.28 | convolution fusion | flops 504299520 | bytes 3428432 | tf_op jit(solution)/shard_map/btn,bhpn->bthp/dot_general | solution.py:94
  62.7 2.5 %collective-permute-done.5 = f32[10,64,128]{2,1,0:T(8,128)} collective-permute-done((f32[10,64,128]{2,1,0:T(8,128)}, f32[10,64,128]{2,1,0:T(8,128)}, u32[]{:S(2)}, u32[]{:S(2)}) %collective-permute-start.5) | collective-permute-done | bytes 327712 | tf_op jit(solution)/shard_map/ppermute | solution.py:19
  65.2 1.8 fusion.18
  70.2 2.8 %fusion.37 = f32[256,2560]{1,0:T(8,128)} fusion(bf16[640,2560]{1,0:T(8,128)(2,1)S(1)} %copy-done, bf16[512,640]{0,1:T(8,128)(2,1)S(1)} %multiply_convert_fusion.8), kind=kOutput, calls=%fused_computation.59 | convolution fusion | flops 838860800 | bytes 6225920 | tf_op jit(solution)/shard_map/dot_general | solution.py:140
  73.0 2.7 %fusion.39 = f32[256,2560]{1,0:T(8,128)} fusion(bf16[640,2560]{1,0:T(8,128)(2,1)S(1)} %copy-done, bf16[512,640]{0,1:T(8,128)(2,1)S(1)} %multiply_convert_fusion.8), kind=kOutput, calls=%fused_computation.61 | convolution fusion | flops 838860800 | bytes 6225920 | tf_op jit(solution)/shard_map/dot_general | solution.py:140
  75.7 2.6 %add_dynamic-update-slice_fusion.1 = (f32[256,2560]{1,0:T(8,128)}, f32[256,2560]{1,0:T(8,128)}) fusion(f32[256,2560]{1,0:T(8,128)} %fusion.39, s32[]{:T(128)S(6)} %select_n.28, bf16[512,640]{1,0:T(8,128)(2,1)S(1)} %copy-done.10, f32[256,2560]{1,0:T(8,128)} %fusion.37), kind=kLoop, calls=%fused_computation.48 | loop fusion | flops 655360 | bytes 3276804 | tf_op jit(solution)/shard_map/dynamic_update_slice | solution.py:144
  79.1 33.5 %reduce-scatter.5.cloned.1.call-done = f32[64,2560]{1,0:T(8,128)} async-done(((f32[256,2560]{1,0:T(8,128)}), f32[64,2560]{1,0:T(8,128)}) %reduce-scatter.5.cloned.1.call-update) | async-done | bytes 655376 | tf_op jit(solution)/shard_map/reduce_scatter | solution.py:145
  113.9 36.2 %reduce-scatter.3.cloned.1.call-done = f32[64,2560]{1,0:T(8,128)} async-done(((f32[256,2560]{1,0:T(8,128)}), f32[64,2560]{1,0:T(8,128)}) %reduce-scatter.3.cloned.1.call-update) | async-done | bytes 655376 | tf_op jit(solution)/shard_map/reduce_scatter | solution.py:145
  151.3 2.3 %multiply_convert_fusion.10 = (bf16[64,2560]{1,0:T(8,128)(2,1)}, bf16[64,2560]{1,0:T(8,128)(2,1)}) fusion(f32[64,2560]{1,0:T(8,128)} %reduce-scatter.3.cloned.1.call-done, f32[2560]{0:T(1024)S(1)} %copy-done.20, f32[64]{0:T(128)S(1)} %add_rsqrt_fusion.2, f32[64,2560]{1,0:T(8,128)} %reduce-scatter.5.cloned.1.call-done, f32[64]{0:T(128)S(1)} %add_rsqrt_fusion.1), kind=kLoop, calls=%fused_computation.46 | loop fusion | flops 983040 | bytes 1976832 | tf_op jit(solution)/shard_map/convert_element_type | solution.py:150
  154.2 17.8 %all-gather.5.cloned.1.call-done = bf16[256,2560]{1,0:T(8,128)(2,1)} async-done(((bf16[64,2560]{1,0:T(8,128)(2,1)}), bf16[256,2560]{1,0:T(8,128)(2,1)}) %all-gather.5.cloned.1.call-update) | async-done | bytes 1310736 | tf_op jit(solution)/shard_map/all_gather | solution.py:151
  172.0 3.0 %convolution_convert_fusion.2 = bf16[256,512]{1,0:T(8,128)(2,1)S(1)} fusion(bf16[256,2560]{1,0:T(8,128)(2,1)} %all-gather.5.cloned.1.call-done, bf16[2560,512]{1,0:T(8,128)(2,1)} %param.26), kind=kOutput, calls=%fused_computation.41 | convolution fusion | flops 671219712 | bytes 4194304 | tf_op jit(solution)/shard_map/dot_general | solution.py:152
  175.0 17.2 %all-gather.3.cloned.1.call-done = bf16[256,2560]{1,0:T(8,128)(2,1)} async-done(((bf16[64,2560]{1,0:T(8,128)(2,1)}), bf16[256,2560]{1,0:T(8,128)(2,1)}) %all-gather.3.cloned.1.call-update) | async-done | bytes 1310736 | tf_op jit(solution)/shard_map/all_gather | solution.py:151
  192.2 3.1 %convolution_convert_fusion.3 = bf16[256,512]{1,0:T(8,128)(2,1)S(1)} fusion(bf16[256,2560]{1,0:T(8,128)(2,1)} %all-gather.3.cloned.1.call-done, bf16[2560,512]{1,0:T(8,128)(2,1)} %param.26), kind=kOutput, calls=%fused_computation.42 | convolution fusion | flops 671219712 | bytes 4194304 | tf_op jit(solution)/shard_map/dot_general | solution.py:152
  (120 shorter events, 28.8 us)
Async XLA Ops:
  7.2 63.0 %copy-start = (bf16[640,2560]{1,0:T(8,128)(2,1)S(1)}, bf16[640,2560]{1,0:T(8,128)(2,1)}, u32[]{:S(2)}) copy-start(bf16[640,2560]{1,0:T(8,128)(2,1)} %param.23) | copy-start | bytes 9830404
  7.2 105.5 %reduce-scatter.5.cloned.1.call-start = ((), (), s32[]{:S(2)}) async-start(), calls=%async_computation.4 | async-start | bytes 3276800 | tf_op jit(solution)/shard_map/reduce_scatter | solution.py:145
  15.5 9.0 %copy-start.6 = (bf16[1,512,128]{2,1,0:T(8,128)(2,1)}, bf16[1,512,128]{2,1,0:T(8,128)(2,1)S(1)}, u32[]{:S(2)}) copy-start(bf16[1,512,128]{2,1,0:T(8,128)(2,1)S(1)} %get-tuple-element.19) | copy-start | bytes 393220
  23.2 19.4 %collective-permute-start.3 = (f32[10,64,128]{2,1,0:T(8,128)S(1)}, f32[10,64,128]{2,1,0:T(8,128)S(1)}, u32[]{:S(2)}, u32[]{:S(2)}) collective-permute-start(f32[10,64,128]{2,1,0:T(8,128)S(1)} %get-tuple-element.6), channel_id=1, source_target_pairs={{4,0},{8,4},{12,8},{5,1},{9,5},{13,9},{6,2},{10,6},{14,10},{7,3},{... | collective-permute-start | bytes 983048 | tf_op jit(solution)/shard_map/ppermute | solution.py:19
  24.5 6.7 %copy-start.11 = (bf16[2,512,128]{2,1,0:T(8,128)(2,1)S(1)}, bf16[2,512,128]{2,1,0:T(8,128)(2,1)}, u32[]{:S(2)}) copy-start(bf16[2,512,128]{2,1,0:T(8,128)(2,1)} %param.17) | copy-start | bytes 786436
  25.3 6.0 %copy-start.7 = (bf16[1,512,128]{2,1,0:T(8,128)(2,1)S(1)}, bf16[1,512,128]{2,1,0:T(8,128)(2,1)}, u32[]{:S(2)}) copy-start(bf16[1,512,128]{2,1,0:T(8,128)(2,1)} %copy-done.6) | copy-start | bytes 393220
  25.4 6.5 %copy-start.2 = (bf16[2,256,10,64]{1,0,3,2:T(2,128)(2,1)S(1)}, bf16[2,256,10,64]{1,0,3,2:T(2,128)(2,1)}, u32[]{:S(2)}) copy-start(bf16[2,256,10,64]{1,0,3,2:T(2,128)(2,1)} %reshape_reshape.4) | copy-start | bytes 1966084
  25.4 6.5 %copy-start.15 = (f32[2,10,256]{2,1,0:T(8,128)S(1)}, f32[2,10,256]{2,1,0:T(8,128)}, u32[]{:S(2)}) copy-start(f32[2,10,256]{2,1,0:T(8,128)} %copy-done.14) | copy-start | bytes 61444
  25.4 6.5 %copy-start.19 = (f32[2,10,256]{2,1,0:T(8,128)S(1)}, f32[2,10,256]{2,1,0:T(8,128)}, u32[]{:S(2)}) copy-start(f32[2,10,256]{2,1,0:T(8,128)} %get-tuple-element.27) | copy-start | bytes 61444
  25.4 12.6 %collective-permute-start = (f32[10,64,128]{2,1,0:T(8,128)S(1)}, f32[10,64,128]{2,1,0:T(8,128)S(1)}, u32[]{:S(2)}, u32[]{:S(2)}) collective-permute-start(f32[10,64,128]{2,1,0:T(8,128)S(1)} %get-tuple-element.10), channel_id=1, source_target_pairs={{0,4},{4,8},{8,12},{1,5},{5,9},{9,13},{2,6},{6,10},{10,14},{3,7},{... | collective-permute-start | bytes 983048 | tf_op jit(solution)/shard_map/ppermute | solution.py:19
  38.2 10.5 %collective-permute-start.1 = (f32[10,64,128]{2,1,0:T(8,128)S(1)}, f32[10,64,128]{2,1,0:T(8,128)S(1)}, u32[]{:S(2)}, u32[]{:S(2)}) collective-permute-start(f32[10,64,128]{2,1,0:T(8,128)S(1)} %multiply_add_fusion.3), channel_id=1, source_target_pairs={{0,4},{4,8},{8,12},{1,5},{5,9},{9,13},{2,6},{6,10},{10,14},{3,7},{... | collective-permute-start | bytes 983048 | tf_op jit(solution)/shard_map/ppermute | solution.py:19
  42.7 12.0 %collective-permute-start.4 = (f32[10,64,128]{2,1,0:T(8,128)S(1)}, f32[10,64,128]{2,1,0:T(8,128)S(1)}, u32[]{:S(2)}, u32[]{:S(2)}) collective-permute-start(f32[10,64,128]{2,1,0:T(8,128)S(1)} %multiply_add_fusion.1), channel_id=1, source_target_pairs={{4,0},{8,4},{12,8},{5,1},{9,5},{13,9},{6,2},{10,6},{14,10},{7,3},{... | collective-permute-start | bytes 983048 | tf_op jit(solution)/shard_map/ppermute | solution.py:19
  44.9 13.0 %copy-start.24 = (f32[10]{0:T(128)S(1)}, f32[10]{0:T(128)}, u32[]{:S(2)}) copy-start(f32[10]{0:T(128)} %param.21) | copy-start | bytes 124
  44.9 13.2 %copy-start.23 = (f32[1,10]{1,0:T(1,128)S(1)}, f32[1,10]{1,0:T(1,128)}, u32[]{:S(2)}) copy-start(f32[1,10]{1,0:T(1,128)} %get-tuple-element.30) | copy-start | bytes 124
  49.5 10.7 %copy-start.12 = (f32[2,256,10]{1,2,0:T(8,128)S(1)}, f32[2,256,10]{1,2,0:T(8,128)}, u32[]{:S(2)}) copy-start(f32[2,256,10]{1,2,0:T(8,128)} %get-tuple-element.38) | copy-start | bytes 61444
  49.5 10.7 %collective-permute-start.2 = (f32[10,64,128]{2,1,0:T(8,128)}, f32[10,64,128]{2,1,0:T(8,128)}, u32[]{:S(2)}, u32[]{:S(2)}) collective-permute-start(f32[10,64,128]{2,1,0:T(8,128)} %multiply_add_fusion.2), channel_id=1, source_target_pairs={{0,4},{4,8},{8,12},{1,5},{5,9},{9,13},{2,6},{6,10},{10,14},{3,7},{... | collective-permute-start | bytes 983048 | tf_op jit(solution)/shard_map/ppermute | solution.py:19
  55.6 9.6 %collective-permute-start.5 = (f32[10,64,128]{2,1,0:T(8,128)}, f32[10,64,128]{2,1,0:T(8,128)}, u32[]{:S(2)}, u32[]{:S(2)}) collective-permute-start(f32[10,64,128]{2,1,0:T(8,128)} %multiply_add_fusion), channel_id=1, source_target_pairs={{4,0},{8,4},{12,8},{5,1},{9,5},{13,9},{6,2},{10,6},{14,10},{7,3},{... | collective-permute-start | bytes 983048 | tf_op jit(solution)/shard_map/ppermute | solution.py:19
  60.2 4.9 %copy-start.4 = (f32[2,256,10,64]{1,3,2,0:T(8,128)S(1)}, f32[2,256,10,64]{1,3,2,0:T(8,128)}, u32[]{:S(2)}) copy-start(f32[2,256,10,64]{1,3,2,0:T(8,128)} %fusion.14) | copy-start | bytes 3932164
  60.2 4.9 %copy-start.5 = (f32[1,10,64,128]{3,2,1,0:T(8,128)S(1)}, f32[1,10,64,128]{3,2,1,0:T(8,128)}, u32[]{:S(2)}) copy-start(f32[1,10,64,128]{3,2,1,0:T(8,128)} %slice_add_fusion) | copy-start | bytes 983044
  60.2 4.9 %copy-start.9 = (bf16[1,512,128]{2,1,0:T(8,128)(2,1)S(1)}, bf16[1,512,128]{2,1,0:T(8,128)(2,1)}, u32[]{:S(2)}) copy-start(bf16[1,512,128]{2,1,0:T(8,128)(2,1)} %copy-done.8) | copy-start | bytes 393220
  78.3 71.8 %reduce-scatter.3.cloned.1.call-start = ((), (), s32[]{:S(2)}) async-start(), calls=%async_computation.2 | async-start | bytes 3276800 | tf_op jit(solution)/shard_map/reduce_scatter | solution.py:145
  79.1 72.3 %copy-start.20 = (f32[2560]{0:T(1024)S(1)}, f32[2560]{0:T(1024)}, u32[]{:S(2)}) copy-start(f32[2560]{0:T(1024)} %param.25) | copy-start | bytes 30724
  79.1 92.9 %all-gather.5.cloned.1.call-start = ((), (), s32[]{:S(2)}) async-start(), calls=%async_computation.5 | async-start | bytes 1638400 | tf_op jit(solution)/shard_map/all_gather | solution.py:151
  153.6 38.6 %all-gather.3.cloned.1.call-start = ((), (), s32[]{:S(2)}) async-start(), calls=%async_computation.3 | async-start | bytes 1638400 | tf_op jit(solution)/shard_map/all_gather | solution.py:151
  (14 other events, 33.3 us)
Sparse Core Ops, SparseCore 0:
  78.4 34.1 reduce-scatter.4
  115.4 34.6 reduce-scatter.2
  153.8 18.1 all-gather.4
  174.0 18.1 all-gather.2

commit v5 on v3

--- a/solution.py
+++ b/solution.py
@@ -27,14 +27,16 @@
     reads_b = reads.reshape(count, STRETCH, -1)
     steps_b = steps.reshape(count, STRETCH, heads)
     rates_b = rates.reshape(count, STRETCH, heads)
-    cum_rate = lax.cumsum(rates_b, axis=1, reverse=reverse)
-    block_total = cum_rate[:, 0] if reverse else cum_rate[:, -1]
-    along = jnp.transpose(cum_rate, (0, 2, 1))
     position = jnp.arange(STRETCH)
     if reverse:
         causal = position[:, None] <= position[None, :]
     else:
         causal = position[:, None] >= position[None, :]
+    cum_rate = jnp.einsum(
+        "ts,bsh->bth", causal.astype(jnp.float32), rates_b, precision=highest
+    )
+    block_total = cum_rate[:, 0] if reverse else cum_rate[:, -1]
+    along = jnp.transpose(cum_rate, (0, 2, 1))
     spans = along[:, :, :, None] - along[:, :, None, :]
     decays = jnp.exp(jnp.where(causal[None, None], spans, -1e30))
     intersection = jnp.einsum("btn,bsn->bts", reads_b, writes_b, preferred_element_type=jnp.float32)
@@ -129,12 +131,10 @@
     scaled = grouped * lax.rsqrt(jnp.mean(grouped * grouped, axis=2, keepdims=True) + epsilon)
     mixed = (scaled.reshape(tokens, -1) * norm_gain[None, :]).astype(jnp.bfloat16)
     own_width = residual.shape[1]
-    offset = lax.axis_index("head") * own_width
+    own_block = jnp.arange(out_weight.shape[1]) // own_width == lax.axis_index("head")
+    spread = jnp.tile(residual.astype(jnp.float32), (1, out_weight.shape[1] // own_width))
     partial_value = jnp.dot(mixed, out_weight, preferred_element_type=jnp.float32)
-    own_cols = lax.dynamic_slice_in_dim(partial_value, offset, own_width, 1) + residual.astype(
-        jnp.float32
-    )
-    partial_value = lax.dynamic_update_slice_in_dim(partial_value, own_cols, offset, 1)
+    partial_value = partial_value + jnp.where(own_block[None, :], spread, 0.0)
     encoded = lax.psum_scatter(partial_value, "head", scatter_dimension=0, tiled=True)
     normed = (
         encoded

time: 178 us -> 174 us (0.978)
  other arithmetic: 22 us -> 14.7 us
  local copies, waits for them, and re-layouts: 14.3 us -> 17.2 us
    another operation x7 -> x0, other arithmetic: 7.8 us -> none
    add x6, other arithmetic: 2.11 us -> 5.74 us  [relay(): entering = passed_along(gain[:, None, None] * entering + state, axis, steps)]
    ppermute x6, waiting for transfers between devices: 6.89 us -> 3.29 us  [passed_along(): lax.ppermute(value, axis, [(source, source + steps) for source in range(f...]
    dynamic_update_slice x1 -> x0, other arithmetic: 2.6 us -> none  [per_device(): lax.dynamic_update_slice_in_dim(partial_value, own_cols, offset, 1)]
    dot_general x0 -> x2, matrix products: none -> 1.89 us  [block_parts(): jnp.einsum('ts,bsh->bth', causal.astype(jnp.float32), rates_b, precision=...]
    reduce_scatter x1, waiting for transfers between devices: 51 us -> 52.9 us  [per_device(): lax.psum_scatter(partial_value, 'head', scatter_dimension=0, tiled=True)]
    unnamed x69 -> x66, local copies, waits for them, and re-layouts: 6.95 us -> 7.49 us
  transfers between devices with their start and end apart: 8 -> 8, of which waited for: 5 -> 5; matrix products, arithmetic and copies ran while one was open for 8% -> 12% of each run, Pallas kernels for 0% -> 0%
where the time goes in v5:
time: 174 us; the launch traced here: 173 us
  waiting for transfers between devices  81.9 us (47%)
  matrix products  24.8 us (14%)
  starting transfers between devices  20.2 us (12%)
  local copies, waits for them, and re-layouts  17.2 us (10%)
  other arithmetic  14.7 us (8%)
  between operations  14.5 us (8%)
    reduce_scatter x1, waiting for transfers between devices, per_device(): lax.psum_scatter(partial_value, 'head', scatter_dimension=0, tiled=True)  52.9 us
    all_gather x1, waiting for transfers between devices, per_device(): normed = lax.all_gather(normed, 'head', axis=0, tiled=True)  25.7 us
    ppermute x6, starting transfers between devices, passed_along(): lax.ppermute(value, axis, [(source, source + steps) for source in range(f...  20.1 us
    unnamed x66, local copies, waits for them, and re-layouts  7.49 us
    add x6, other arithmetic, relay(): entering = passed_along(gain[:, None, None] * entering + state, axis, steps)  5.74 us
    dot_general x2, matrix products, block_parts(): jnp.einsum('bhts,bshp->bthp', weights, acts_b, preferred_element_type=jnp...  5.24 us
    dot_general x1, matrix products, per_device(): jnp.dot(normed, value_weight, preferred_element_type=jnp.float32)  4.99 us
    dot_general x1, matrix products, per_device(): jnp.dot(mixed, out_weight, preferred_element_type=jnp.float32)  4.79 us
  transfers between devices with their start and end apart: 8, of which 5 were waited for; matrix products, arithmetic and copies ran while one was open for 12% of the time, Pallas kernels for 0%

profile of v5, /device:TPU:0, one launch (start us, length us, event | category | flops | bytes accessed | tf_op | source)
XLA Modules:
  0.0 173.4 jit_solution(11358810491944874681)
XLA Ops:
  11.9 1.4 bitcast_exponential_fusion
  15.5 2.2 %copy.20 = bf16[512,640]{0,1:T(8,128)(2,1)} copy(bf16[512,640]{1,0:T(8,128)(2,1)} %param.14) | data formatting | bytes 1310720 | tf_op args[0]
  17.7 2.7 %reshape_reshape.4 = bf16[2,256,10,64]{1,0,3,2:T(2,128)(2,1)} reshape(bf16[512,640]{0,1:T(8,128)(2,1)} %copy.20) | data formatting | bytes 1310720 | tf_op jit(solution)/shard_map/reshape;reshape | solution.py:25
  20.4 1.8 %convert_multiply_fusion.1 = (f32[2,256,10,64]{1,0,3,2:T(2,128)S(1)}, f32[2,256,10,64]{1,0,3,2:T(2,128)S(1)}) fusion(bf16[2,256,10,64]{1,0,3,2:T(2,128)(2,1)} %reshape_reshape.4, f32[2,256,10]{1,0,2:T(2,128)} %copy.26, f32[2,256,10]{1,0,2:T(2,128)} %copy.22), kind=kLoop, calls=%fused_computation.19 | loop fusion | flops 983040 | bytes 3317760 | tf_op jit(solution)/shard_map/mul | solution.py:48
  25.4 5.7 %collective-permute-start = (f32[10,64,128]{2,1,0:T(8,128)S(1)}, f32[10,64,128]{2,1,0:T(8,128)S(1)}, u32[]{:S(2)}, u32[]{:S(2)}) collective-permute-start(f32[10,64,128]{2,1,0:T(8,128)S(1)} %get-tuple-element.10), channel_id=1, source_target_pairs={{0,4},{4,8},{8,12},{1,5},{5,9},{9,13},{2,6},{6,10},{10,14},{3,7},{... | collective-permute-start | bytes 983048 | tf_op jit(solution)/shard_map/ppermute | solution.py:19
  32.0 2.6 %fusion.14 = f32[2,256,10,64]{1,3,2,0:T(8,128)} fusion(f32[2,10,256]{2,1,0:T(8,128)S(1)} %copy-done.23, f32[2,10,256]{2,1,0:T(8,128)S(1)} %copy-done.19, f32[2,256,256]{2,1,0:T(8,128)S(1)} %fusion.85, pred[256,256]{1,0:T(8,128)(4,1)S(1)} %iota_compare_fusion, bf16[2,256,10,64]{1,0,3,2:T(2,128)(2,1)S(1)} %copy-done.5), kind=kOutput, calls=%fused_computation.21 | convolution fusion | flops 174325760 | bytes 2596864 | tf_op jit(solution)/shard_map/bhts,bshp->bthp/dot_general | solution.py:46
  34.6 2.6 %fusion.15 = f32[2,256,10,64]{1,3,2,0:T(8,128)} fusion(f32[2,10,256]{2,1,0:T(8,128)S(1)} %copy-done.22, f32[2,10,256]{2,1,0:T(8,128)S(1)} %copy-done.21, f32[2,256,256]{2,1,0:T(8,128)S(1)} %fusion.84, pred[256,256]{1,0:T(8,128)(4,1)S(1)} %iota_compare_fusion.1, bf16[2,256,10,64]{1,0,3,2:T(2,128)(2,1)S(1)} %copy-done.5), kind=kOutput, calls=%fused_computation.22 | convolution fusion | flops 174325760 | bytes 2596864 | tf_op jit(solution)/shard_map/bhts,bshp->bthp/dot_general | solution.py:46
  38.9 5.1 %collective-permute-start.1 = (f32[10,64,128]{2,1,0:T(8,128)}, f32[10,64,128]{2,1,0:T(8,128)}, u32[]{:S(2)}, u32[]{:S(2)}) collective-permute-start(f32[10,64,128]{2,1,0:T(8,128)} %multiply_add_fusion.3), channel_id=1, source_target_pairs={{0,4},{4,8},{8,12},{1,5},{5,9},{9,13},{2,6},{6,10},{10,14},{3,7},{... | collective-permute-start | bytes 983048 | tf_op jit(solution)/shard_map/ppermute | solution.py:19
  44.9 1.4 collective-permute-start.4
  47.1 2.6 %collective-permute-done.1 = f32[10,64,128]{2,1,0:T(8,128)} collective-permute-done((f32[10,64,128]{2,1,0:T(8,128)}, f32[10,64,128]{2,1,0:T(8,128)}, u32[]{:S(2)}, u32[]{:S(2)}) %collective-permute-start.1) | collective-permute-done | bytes 327712 | tf_op jit(solution)/shard_map/ppermute | solution.py:19
  49.7 1.9 %multiply_add_fusion.2 = f32[10,64,128]{2,1,0:T(8,128)} fusion(f32[10,64,128]{2,1,0:T(8,128)} %copy-done.4, f32[10,64,128]{2,1,0:T(8,128)} %collective-permute-done.1, f32[10]{0:T(128)S(1)} %get-tuple-element.13), kind=kLoop, calls=%fused_computation.67 | loop fusion | flops 163840 | bytes 983080 | tf_op jit(solution)/shard_map/add | solution.py:75
  51.6 5.1 %collective-permute-start.2 = (f32[10,64,128]{2,1,0:T(8,128)}, f32[10,64,128]{2,1,0:T(8,128)}, u32[]{:S(2)}, u32[]{:S(2)}) collective-permute-start(f32[10,64,128]{2,1,0:T(8,128)} %multiply_add_fusion.2), channel_id=1, source_target_pairs={{0,4},{4,8},{8,12},{1,5},{5,9},{9,13},{2,6},{6,10},{10,14},{3,7},{... | collective-permute-start | bytes 983048 | tf_op jit(solution)/shard_map/ppermute | solution.py:19
  56.7 1.9 %multiply_add_fusion = f32[10,64,128]{2,1,0:T(8,128)} fusion(f32[10,64,128]{2,1,0:T(8,128)} %copy-done.3, f32[10,64,128]{2,1,0:T(8,128)} %collective-permute-done.4, f32[10]{0:T(128)S(1)} %get-tuple-element.9), kind=kLoop, calls=%fused_computation.63 | loop fusion | flops 163840 | bytes 983080 | tf_op jit(solution)/shard_map/add | solution.py:75
  58.6 1.5 collective-permute-start.5
  60.3 2.2 %copy.30 = bf16[512,640]{0,1:T(8,128)(2,1)} copy(bf16[512,640]{1,0:T(8,128)(2,1)} %param.15) | data formatting | bytes 1310720 | tf_op args[1]
  62.5 1.8 %tile.4 = f32[512,4,640]{2,1,0:T(4,128)S(1)} broadcast(bf16[512,640]{1,0:T(8,128)(2,1)} %param.24), dimensions={0,2} | broadcast | bytes 5898240 | tf_op jit(solution)/shard_map/tile | solution.py:135
  65.6 1.9 %fusion.20 = f32[2,256,10,64]{1,3,2,0:T(8,128)S(1)} fusion(f32[2,256,10,64]{1,3,2,0:T(8,128)S(1)} %copy-done.7, bf16[2,256,128,1]{2,1,3,0:T(8,128)(2,1)S(1)} %bitcast.127, f32[1,10,64,128]{3,2,1,0:T(8,128)S(1)} %copy-done.8, f32[2,256,10]{1,2,0:T(8,128)S(1)} %copy-done.16, f32[10,64,128]{2,1,0:T(8,128)} %collective-permute-done.2, f32[2,10]{1,0:T(2,128)S(1)} %stack.15), kind=kOutput, calls=%fused_computation.29 | convolution fusion | flops 504299520 | bytes 3428432 | tf_op jit(solution)/shard_map/btn,bhpn->bthp/dot_general | solution.py:94
  68.2 1.8 %fusion.18 = f32[2,256,10,64]{1,3,2,0:T(8,128)S(1)} fusion(f32[2,256,10,64]{1,3,2,0:T(8,128)S(1)} %fusion.20, f32[2,256,10,64]{1,3,2,0:T(8,128)S(1)} %copy-done.9, bf16[2,256,128,1]{2,1,3,0:T(8,128)(2,1)S(1)} %bitcast.133, f32[1,10,64,128]{3,2,1,0:T(8,128)S(1)} %copy-done.10, f32[2,256,10]{1,2,0:T(8,128)S(1)} %copy-done.17, ...), kind=kOutput, calls=%fused_computation.26 | convolution fusion | flops 504627200 | bytes 4739152 | tf_op jit(solution)/shard_map/btn,bhpn->bthp/dot_general | solution.py:94
  73.1 4.8 %select_add_fusion = f32[512,2560]{1,0:T(8,128)} fusion(f32[512,2560]{1,0:T(8,128)S(1)} %bitcast.123, bf16[640,2560]{1,0:T(8,128)(2,1)S(1)} %copy-done, pred[2560]{0:T(1024)(128)(4,1)S(1)} %fusion.67, f32[512,640]{0,1:T(8,128)S(1)} %get-tuple-element.5, f32[640]{0:T(1024)S(1)} %copy-done.24, f32[512]{0:T(512)S(1)} %add_rsqrt_fusion), kind=kOutput, calls=%fused_computation | convolution fusion | flops 1681326080 | bytes 15080448 | tf_op jit(solution)/shard_map/dot_general | solution.py:136
  77.9 52.9 %reduce-scatter.2.cloned.1.call-done = f32[128,2560]{1,0:T(8,128)} async-done(((f32[512,2560]{1,0:T(8,128)}), f32[128,2560]{1,0:T(8,128)}) %reduce-scatter.2.cloned.1.call-update) | async-done | bytes 1310736 | tf_op jit(solution)/shard_map/reduce_scatter | solution.py:138
  130.8 1.6 multiply_reduce_fusion
  133.5 25.7 %all-gather.2.cloned.1.call-done = bf16[512,2560]{1,0:T(8,128)(2,1)} async-done(((bf16[128,2560]{1,0:T(8,128)(2,1)}), bf16[512,2560]{1,0:T(8,128)(2,1)}) %all-gather.2.cloned.1.call-update) | async-done | bytes 2621456 | tf_op jit(solution)/shard_map/all_gather | solution.py:144
  159.3 5.0 %convolution_convert_fusion = bf16[512,512]{1,0:T(8,128)(2,1)} fusion(bf16[512,2560]{1,0:T(8,128)(2,1)} %all-gather.2.cloned.1.call-done, bf16[2560,512]{1,0:T(8,128)(2,1)} %param.27), kind=kOutput, calls=%fused_computation.42 | convolution fusion | flops 1342439424 | bytes 5767168 | tf_op jit(solution)/shard_map/dot_general | solution.py:146
  164.3 2.3 %convolution_convert_fusion.1 = bf16[512,512]{1,0:T(8,128)(2,1)} fusion(bf16[512,2560]{1,0:T(8,128)(2,1)S(1)} %copy-done.30, bf16[2560,512]{1,0:T(8,128)(2,1)S(1)} %copy-done.29), kind=kOutput, calls=%fused_computation.43 | convolution fusion | flops 1342439424 | bytes 5767168 | tf_op jit(solution)/shard_map/dot_general | solution.py:145
  (114 shorter events, 20.4 us)
Async XLA Ops:
  7.2 65.8 %copy-start = (bf16[640,2560]{1,0:T(8,128)(2,1)S(1)}, bf16[640,2560]{1,0:T(8,128)(2,1)}, u32[]{:S(2)}) copy-start(bf16[640,2560]{1,0:T(8,128)(2,1)} %param.23) | copy-start | bytes 9830404
  7.2 123.6 %reduce-scatter.2.cloned.1.call-start = ((), (), s32[]{:S(2)}) async-start(), calls=%async_computation.1 | async-start | bytes 6553600 | tf_op jit(solution)/shard_map/reduce_scatter | solution.py:138
  10.1 3.8 %copy-start.18 = (f32[2,10,256]{2,1,0:T(8,128)}, f32[2,10,256]{2,1,0:T(8,128)S(1)}, u32[]{:S(2)}) copy-start(f32[2,10,256]{2,1,0:T(8,128)S(1)} %fusion.47) | copy-start | bytes 61444
  11.7 2.8 %copy-start.20 = (f32[2,10,256]{2,1,0:T(8,128)}, f32[2,10,256]{2,1,0:T(8,128)S(1)}, u32[]{:S(2)}) copy-start(f32[2,10,256]{2,1,0:T(8,128)S(1)} %fusion.49) | copy-start | bytes 61444
  15.5 9.0 %copy-start.11 = (bf16[1,512,128]{2,1,0:T(8,128)(2,1)}, bf16[1,512,128]{2,1,0:T(8,128)(2,1)S(1)}, u32[]{:S(2)}) copy-start(bf16[1,512,128]{2,1,0:T(8,128)(2,1)S(1)} %get-tuple-element.17) | copy-start | bytes 393220
  23.2 20.9 %copy-start.3 = (f32[10,64,128]{2,1,0:T(8,128)}, f32[10,64,128]{2,1,0:T(8,128)S(1)}, u32[]{:S(2)}) copy-start(f32[10,64,128]{2,1,0:T(8,128)S(1)} %get-tuple-element.7) | copy-start | bytes 983044
  23.2 20.9 %collective-permute-start.3 = (f32[10,64,128]{2,1,0:T(8,128)S(1)}, f32[10,64,128]{2,1,0:T(8,128)S(1)}, u32[]{:S(2)}, u32[]{:S(2)}) collective-permute-start(f32[10,64,128]{2,1,0:T(8,128)S(1)} %get-tuple-element.6), channel_id=1, source_target_pairs={{4,0},{8,4},{12,8},{5,1},{9,5},{13,9},{6,2},{10,6},{14,10},{7,3},{... | collective-permute-start | bytes 983048 | tf_op jit(solution)/shard_map/ppermute | solution.py:19
  24.5 6.7 %copy-start.15 = (bf16[2,512,128]{2,1,0:T(8,128)(2,1)S(1)}, bf16[2,512,128]{2,1,0:T(8,128)(2,1)}, u32[]{:S(2)}) copy-start(bf16[2,512,128]{2,1,0:T(8,128)(2,1)} %param.17) | copy-start | bytes 786436
  25.3 6.0 %copy-start.12 = (bf16[1,512,128]{2,1,0:T(8,128)(2,1)S(1)}, bf16[1,512,128]{2,1,0:T(8,128)(2,1)}, u32[]{:S(2)}) copy-start(bf16[1,512,128]{2,1,0:T(8,128)(2,1)} %copy-done.11) | copy-start | bytes 393220
  25.4 12.7 %copy-start.4 = (f32[10,64,128]{2,1,0:T(8,128)}, f32[10,64,128]{2,1,0:T(8,128)S(1)}, u32[]{:S(2)}) copy-start(f32[10,64,128]{2,1,0:T(8,128)S(1)} %get-tuple-element.11) | copy-start | bytes 983044
  25.4 6.5 %copy-start.5 = (bf16[2,256,10,64]{1,0,3,2:T(2,128)(2,1)S(1)}, bf16[2,256,10,64]{1,0,3,2:T(2,128)(2,1)}, u32[]{:S(2)}) copy-start(bf16[2,256,10,64]{1,0,3,2:T(2,128)(2,1)} %reshape_reshape.4) | copy-start | bytes 1966084
  25.4 6.5 %copy-start.19 = (f32[2,10,256]{2,1,0:T(8,128)S(1)}, f32[2,10,256]{2,1,0:T(8,128)}, u32[]{:S(2)}) copy-start(f32[2,10,256]{2,1,0:T(8,128)} %copy-done.18) | copy-start | bytes 61444
  25.4 6.5 %copy-start.23 = (f32[2,10,256]{2,1,0:T(8,128)S(1)}, f32[2,10,256]{2,1,0:T(8,128)}, u32[]{:S(2)}) copy-start(f32[2,10,256]{2,1,0:T(8,128)} %get-tuple-element.25) | copy-start | bytes 61444
  25.4 12.6 %collective-permute-start = (f32[10,64,128]{2,1,0:T(8,128)S(1)}, f32[10,64,128]{2,1,0:T(8,128)S(1)}, u32[]{:S(2)}, u32[]{:S(2)}) collective-permute-start(f32[10,64,128]{2,1,0:T(8,128)S(1)} %get-tuple-element.10), channel_id=1, source_target_pairs={{0,4},{4,8},{8,12},{1,5},{5,9},{9,13},{2,6},{6,10},{10,14},{3,7},{... | collective-permute-start | bytes 983048 | tf_op jit(solution)/shard_map/ppermute | solution.py:19
  38.9 10.8 %collective-permute-start.1 = (f32[10,64,128]{2,1,0:T(8,128)}, f32[10,64,128]{2,1,0:T(8,128)}, u32[]{:S(2)}, u32[]{:S(2)}) collective-permute-start(f32[10,64,128]{2,1,0:T(8,128)} %multiply_add_fusion.3), channel_id=1, source_target_pairs={{0,4},{4,8},{8,12},{1,5},{5,9},{9,13},{2,6},{6,10},{10,14},{3,7},{... | collective-permute-start | bytes 983048 | tf_op jit(solution)/shard_map/ppermute | solution.py:19
  44.9 15.2 %copy-start.28 = (f32[10]{0:T(128)S(1)}, f32[10]{0:T(128)}, u32[]{:S(2)}) copy-start(f32[10]{0:T(128)} %param.21) | copy-start | bytes 124
  44.9 15.4 %copy-start.27 = (f32[1,10]{1,0:T(1,128)S(1)}, f32[1,10]{1,0:T(1,128)}, u32[]{:S(2)}) copy-start(f32[1,10]{1,0:T(1,128)} %get-tuple-element.26) | copy-start | bytes 124
  44.9 11.8 %collective-permute-start.4 = (f32[10,64,128]{2,1,0:T(8,128)}, f32[10,64,128]{2,1,0:T(8,128)}, u32[]{:S(2)}, u32[]{:S(2)}) collective-permute-start(f32[10,64,128]{2,1,0:T(8,128)} %multiply_add_fusion.1), channel_id=1, source_target_pairs={{4,0},{8,4},{12,8},{5,1},{9,5},{13,9},{6,2},{10,6},{14,10},{7,3},{... | collective-permute-start | bytes 983048 | tf_op jit(solution)/shard_map/ppermute | solution.py:19
  51.6 13.0 %collective-permute-start.2 = (f32[10,64,128]{2,1,0:T(8,128)}, f32[10,64,128]{2,1,0:T(8,128)}, u32[]{:S(2)}, u32[]{:S(2)}) collective-permute-start(f32[10,64,128]{2,1,0:T(8,128)} %multiply_add_fusion.2), channel_id=1, source_target_pairs={{0,4},{4,8},{8,12},{1,5},{5,9},{9,13},{2,6},{6,10},{10,14},{3,7},{... | collective-permute-start | bytes 983048 | tf_op jit(solution)/shard_map/ppermute | solution.py:19
  58.6 9.6 %collective-permute-start.5 = (f32[10,64,128]{2,1,0:T(8,128)}, f32[10,64,128]{2,1,0:T(8,128)}, u32[]{:S(2)}, u32[]{:S(2)}) collective-permute-start(f32[10,64,128]{2,1,0:T(8,128)} %multiply_add_fusion), channel_id=1, source_target_pairs={{4,0},{8,4},{12,8},{5,1},{9,5},{13,9},{6,2},{10,6},{14,10},{7,3},{... | collective-permute-start | bytes 983048 | tf_op jit(solution)/shard_map/ppermute | solution.py:19
  77.9 54.5 %copy-start.25 = (f32[2560]{0:T(1024)S(1)}, f32[2560]{0:T(1024)}, u32[]{:S(2)}) copy-start(f32[2560]{0:T(1024)} %param.25) | copy-start | bytes 30724
  77.9 81.4 %all-gather.2.cloned.1.call-start = ((), (), s32[]{:S(2)}) async-start(), calls=%async_computation.2 | async-start | bytes 3276800 | tf_op jit(solution)/shard_map/all_gather | solution.py:144
  159.3 5.0 %copy-start.29 = (bf16[2560,512]{1,0:T(8,128)(2,1)S(1)}, bf16[2560,512]{1,0:T(8,128)(2,1)}, u32[]{:S(2)}) copy-start(bf16[2560,512]{1,0:T(8,128)(2,1)} %param.26) | copy-start | bytes 7864324
  159.3 5.0 %copy-start.30 = (bf16[512,2560]{1,0:T(8,128)(2,1)S(1)}, bf16[512,2560]{1,0:T(8,128)(2,1)}, u32[]{:S(2)}) copy-start(bf16[512,2560]{1,0:T(8,128)(2,1)} %all-gather.2.cloned.1.call-done) | copy-start | bytes 7864324
  (15 other events, 25.9 us)
Sparse Core Ops, SparseCore 0:
  78.0 52.7 reduce-scatter.1
  133.7 25.5 all-gather.1

commit v6 on v5

--- a/solution.py
+++ b/solution.py
@@ -45,11 +45,12 @@
     ).astype(jnp.bfloat16)
     within = jnp.einsum("bhts,bshp->bthp", weights, acts_b, preferred_element_type=jnp.float32)
     tail = jnp.exp(block_total[:, None, :] - cum_rate) * steps_b
-    weighted = acts_b.astype(jnp.float32) * tail[:, :, :, None]
+    weighted = (acts_b.astype(jnp.float32) * tail[:, :, :, None]).reshape(count, STRETCH, -1)
     ends = jnp.einsum(
-        "bshp,bsn->bhpn", weighted, writes_b.astype(jnp.float32), precision=highest
+        "bsn,bsc->bnc", writes_b.astype(jnp.float32), weighted, precision=highest
     )
-    return within, cum_rate, ends, jnp.exp(block_total)
+    spread = jnp.repeat(jnp.exp(block_total), width, axis=1)
+    return within, cum_rate, ends, spread
 
 
 def chain_blocks(ends, decays, reverse):
@@ -62,7 +63,7 @@
     for index in order:
         starts[index] = state
         gains[index] = gain
-        state = decays[index][:, None, None] * state + ends[index]
+        state = decays[index][None, :] * state + ends[index]
         gain = gain * decays[index]
     return jnp.stack(starts), jnp.stack(gains), state, gain
 
@@ -72,13 +73,13 @@
     if count <= 4:
         entering = jnp.zeros_like(state)
         for _ in range(count - 1):
-            entering = passed_along(gain[:, None, None] * entering + state, axis, steps)
+            entering = passed_along(gain[None, :] * entering + state, axis, steps)
         return entering
     distance = 1
     while distance < count:
         got_state = passed_along(state, axis, distance * steps)
         got_gain = passed_along(gain, axis, distance * steps)
-        state = gain[:, None, None] * got_state + state
+        state = gain[None, :] * got_state + state
         gain = gain * got_gain
         distance *= 2
     return passed_along(state, axis, steps)
@@ -88,10 +89,11 @@
     within, cum_rate, ends, decays = block_parts(acts, writes, reads, steps, rates, reverse)
     starts, gains, own_end, own_gain = chain_blocks(ends, decays, reverse)
     entering = relay(own_end, own_gain, axis, -1 if reverse else 1)
-    block_states = starts + gains[:, :, None, None] * entering[None]
-    count = within.shape[0]
+    block_states = starts + gains[:, None, :] * entering[None]
+    count, _, heads, width = within.shape
     reads_b = reads.reshape(count, STRETCH, -1).astype(jnp.float32)
-    carried = jnp.einsum("btn,bhpn->bthp", reads_b, block_states, precision=highest)
+    carried = jnp.einsum("btn,bnc->btc", reads_b, block_states, precision=highest)
+    carried = carried.reshape(count, STRETCH, heads, width)
     outputs = within + jnp.exp(cum_rate)[:, :, :, None] * carried
     return outputs.reshape(acts.shape)
 

time: 174 us -> 191 us (1.098)
  local copies, waits for them, and re-layouts: 17.2 us -> 28.2 us
  waiting for transfers between devices: 81.9 us -> 86.9 us
  other arithmetic: 14.7 us -> 18.8 us
  matrix products: 24.8 us -> 21.5 us
    ppermute x6, waiting for transfers between devices: 3.29 us -> 7.95 us  [passed_along(): lax.ppermute(value, axis, [(source, source + steps) for source in range(f...]
    broadcast_in_dim x0 -> x10, local copies, waits for them, and re-layouts: none -> 3.72 us  [block_parts(): spread = jnp.repeat(jnp.exp(block_total), width, axis=1)]
    dot_general x4, matrix products: 5.18 us -> 2.98 us  [the longest x2 1.53 us: block_parts(): jnp.einsum('bsn,bsc->bnc', writes_b.astype(jnp.float32), weighted, precis...]
    slice x5, local copies, waits for them, and re-layouts: 2.61 us -> 4.79 us  [the longest x1 1.65 us: per_device(): steps_fwd = jax.nn.softplus(step_raw[0] + step_bias[None, :])]
    unnamed x66 -> x86, local copies, waits for them, and re-layouts: 7.49 us -> 9.54 us
    dot_general x2, matrix products: 5.24 us -> 3.29 us  [block_parts(): jnp.einsum('bhts,bshp->bthp', weights, acts_b, preferred_element_type=jnp...]
  transfers between devices with their start and end apart: 8 -> 8, of which waited for: 5 -> 5; matrix products, arithmetic and copies ran while one was open for 12% -> 17% of each run, Pallas kernels for 0% -> 0%
where the time goes in v6:
time: 191 us; the launch traced here: 189 us
  waiting for transfers between devices  86.9 us (45%)
  local copies, waits for them, and re-layouts  28.2 us (15%)
  matrix products  21.5 us (11%)
  starting transfers between devices  19.4 us (10%)
  other arithmetic  18.8 us (10%)
  between operations  14.7 us (8%)
    reduce_scatter x1, waiting for transfers between devices, per_device(): lax.psum_scatter(partial_value, 'head', scatter_dimension=0, tiled=True)  53.2 us
    all_gather x1, waiting for transfers between devices, per_device(): normed = lax.all_gather(normed, 'head', axis=0, tiled=True)  25.7 us
    ppermute x6, starting transfers between devices, passed_along(): lax.ppermute(value, axis, [(source, source + steps) for source in range(f...  19.3 us
    unnamed x86, local copies, waits for them, and re-layouts  9.54 us
    ppermute x6, waiting for transfers between devices, passed_along(): lax.ppermute(value, axis, [(source, source + steps) for source in range(f...  7.95 us
    dot_general x1, matrix products, per_device(): jnp.dot(normed, value_weight, preferred_element_type=jnp.float32)  4.99 us
    add x6, other arithmetic, relay(): entering = passed_along(gain[None, :] * entering + state, axis, steps)  4.91 us
    dot_general x1, matrix products, per_device(): jnp.dot(mixed, out_weight, preferred_element_type=jnp.float32)  4.76 us
  transfers between devices with their start and end apart: 8, of which 5 were waited for; matrix products, arithmetic and copies ran while one was open for 17% of the time, Pallas kernels for 0%

profile of v6, /device:TPU:0, one launch (start us, length us, event | category | flops | bytes accessed | tf_op | source)
XLA Modules:
  0.0 189.5 jit_solution(2821289944322304766)
XLA Ops:
  8.0 1.7 slice_reduce_fusion.1
  13.4 2.2 %copy.21 = bf16[512,640]{0,1:T(8,128)(2,1)} copy(bf16[512,640]{1,0:T(8,128)(2,1)} %param.14) | data formatting | bytes 1310720 | tf_op args[0]
  21.7 1.4 squeeze.28
  24.7 1.4 bitcast_exponential_fusion.1
  28.8 1.4 broadcast_multiply_fusion.2
  33.9 6.3 %collective-permute-start = (f32[128,640]{0,1:T(8,128)}, f32[128,640]{0,1:T(8,128)}, u32[]{:S(2)}, u32[]{:S(2)}) collective-permute-start(f32[128,640]{0,1:T(8,128)} %get-tuple-element.6), channel_id=1, source_target_pairs={{0,4},{4,8},{8,12},{1,5},{5,9},{9,13},{2,6},{6,10},{10,14},{3,7},{... | collective-permute-start | bytes 983048 | tf_op jit(solution)/shard_map/ppermute | solution.py:19
  41.4 2.7 %reshape_reshape.4 = bf16[2,256,10,64]{1,0,3,2:T(2,128)(2,1)} reshape(bf16[512,640]{0,1:T(8,128)(2,1)} %copy.21) | data formatting | bytes 1310720 | tf_op jit(solution)/shard_map/reshape;reshape | solution.py:25
  44.1 1.8 slice_add_fusion
  46.0 1.8 slice_add_fusion.1
  49.9 1.6 fusion.83
  53.3 2.2 %copy.29 = bf16[512,640]{0,1:T(8,128)(2,1)} copy(bf16[512,640]{1,0:T(8,128)(2,1)} %param.15) | data formatting | bytes 1310720 | tf_op args[1]
  55.4 1.8 tile.4
  62.1 4.6 %collective-permute-start.1 = (f32[128,640]{0,1:T(8,128)S(1)}, f32[128,640]{0,1:T(8,128)S(1)}, u32[]{:S(2)}, u32[]{:S(2)}) collective-permute-start(f32[128,640]{0,1:T(8,128)S(1)} %multiply_add_fusion.3), channel_id=1, source_target_pairs={{0,4},{4,8},{8,12},{1,5},{5,9},{9,13},{2,6},{6,10},{10,14},{3,7},{... | collective-permute-start | bytes 983048 | tf_op jit(solution)/shard_map/ppermute | solution.py:19
  66.6 3.9 %collective-permute-done.4 = f32[128,640]{0,1:T(8,128)S(1)} collective-permute-done((f32[128,640]{0,1:T(8,128)S(1)}, f32[128,640]{0,1:T(8,128)S(1)}, u32[]{:S(2)}, u32[]{:S(2)}) %collective-permute-start.4) | collective-permute-done | bytes 327712 | tf_op jit(solution)/shard_map/ppermute | solution.py:19
  73.2 4.6 %collective-permute-start.2 = (f32[128,640]{0,1:T(8,128)S(1)}, f32[128,640]{0,1:T(8,128)S(1)}, u32[]{:S(2)}, u32[]{:S(2)}) collective-permute-start(f32[128,640]{0,1:T(8,128)S(1)} %multiply_add_fusion.2), channel_id=1, source_target_pairs={{0,4},{4,8},{8,12},{1,5},{5,9},{9,13},{2,6},{6,10},{10,14},{3,7},{... | collective-permute-start | bytes 983048 | tf_op jit(solution)/shard_map/ppermute | solution.py:19
  77.8 3.1 %collective-permute-done.5 = f32[128,640]{0,1:T(8,128)S(1)} collective-permute-done((f32[128,640]{0,1:T(8,128)S(1)}, f32[128,640]{0,1:T(8,128)S(1)}, u32[]{:S(2)}, u32[]{:S(2)}) %collective-permute-start.5) | collective-permute-done | bytes 327712 | tf_op jit(solution)/shard_map/ppermute | solution.py:19
  81.7 1.6 fusion.18
  84.1 1.7 fusion.17
  88.8 4.8 %select_add_fusion = f32[512,2560]{1,0:T(8,128)} fusion(f32[512,2560]{1,0:T(8,128)S(1)} %bitcast.111, bf16[640,2560]{1,0:T(8,128)(2,1)S(1)} %copy-done, pred[2560]{0:T(1024)(128)(4,1)S(1)} %fusion.69, f32[512,640]{0,1:T(8,128)S(1)} %get-tuple-element.5, f32[640]{0:T(1024)S(1)} %copy-done.33, f32[512]{0:T(512)S(1)} %add_rsqrt_fusion), kind=kOutput, calls=%fused_computation | convolution fusion | flops 1681326080 | bytes 15080448 | tf_op jit(solution)/shard_map/dot_general | solution.py:138
  93.6 53.2 %reduce-scatter.2.cloned.1.call-done = f32[128,2560]{1,0:T(8,128)} async-done(((f32[512,2560]{1,0:T(8,128)}), f32[128,2560]{1,0:T(8,128)}) %reduce-scatter.2.cloned.1.call-update) | async-done | bytes 1310736 | tf_op jit(solution)/shard_map/reduce_scatter | solution.py:140
  146.9 1.6 multiply_reduce_fusion
  149.6 25.7 %all-gather.2.cloned.1.call-done = bf16[512,2560]{1,0:T(8,128)(2,1)} async-done(((bf16[128,2560]{1,0:T(8,128)(2,1)}), bf16[512,2560]{1,0:T(8,128)(2,1)}) %all-gather.2.cloned.1.call-update) | async-done | bytes 2621456 | tf_op jit(solution)/shard_map/all_gather | solution.py:146
  175.3 5.0 %convolution_convert_fusion = bf16[512,512]{1,0:T(8,128)(2,1)} fusion(bf16[512,2560]{1,0:T(8,128)(2,1)} %all-gather.2.cloned.1.call-done, bf16[2560,512]{1,0:T(8,128)(2,1)} %param.27), kind=kOutput, calls=%fused_computation.36 | convolution fusion | flops 1342439424 | bytes 5767168 | tf_op jit(solution)/shard_map/dot_general | solution.py:148
  180.3 2.3 %convolution_convert_fusion.1 = bf16[512,512]{1,0:T(8,128)(2,1)} fusion(bf16[512,2560]{1,0:T(8,128)(2,1)S(1)} %copy-done.39, bf16[2560,512]{1,0:T(8,128)(2,1)S(1)} %copy-done.38), kind=kOutput, calls=%fused_computation.37 | convolution fusion | flops 1342439424 | bytes 5767168 | tf_op jit(solution)/shard_map/dot_general | solution.py:147
  (145 shorter events, 36.5 us)
Async XLA Ops:
  7.2 81.5 %copy-start = (bf16[640,2560]{1,0:T(8,128)(2,1)S(1)}, bf16[640,2560]{1,0:T(8,128)(2,1)}, u32[]{:S(2)}) copy-start(bf16[640,2560]{1,0:T(8,128)(2,1)} %param.23) | copy-start | bytes 9830404
  7.2 139.7 %reduce-scatter.2.cloned.1.call-start = ((), (), s32[]{:S(2)}) async-start(), calls=%async_computation.1 | async-start | bytes 6553600 | tf_op jit(solution)/shard_map/reduce_scatter | solution.py:140
  8.0 4.3 %copy-start.40 = (f32[10]{0:T(128)}, f32[10]{0:T(128)S(1)}, u32[]{:S(2)}) copy-start(f32[10]{0:T(128)S(1)} %exponential_negate_fusion) | copy-start | bytes 124
  18.4 4.7 %copy-start.36 = (f32[10]{0:T(128)S(1)}, f32[10]{0:T(128)}, u32[]{:S(2)}) copy-start(f32[10]{0:T(128)} %param.19) | copy-start | bytes 124
  20.4 38.0 %collective-permute-start.3 = (f32[128,640]{0,1:T(8,128)}, f32[128,640]{0,1:T(8,128)}, u32[]{:S(2)}, u32[]{:S(2)}) collective-permute-start(f32[128,640]{0,1:T(8,128)} %get-tuple-element.10), channel_id=1, source_target_pairs={{4,0},{8,4},{12,8},{5,1},{9,5},{13,9},{6,2},{10,6},{14,10},{7,3},{... | collective-permute-start | bytes 983048 | tf_op jit(solution)/shard_map/ppermute | solution.py:19
  33.9 27.0 %collective-permute-start = (f32[128,640]{0,1:T(8,128)}, f32[128,640]{0,1:T(8,128)}, u32[]{:S(2)}, u32[]{:S(2)}) collective-permute-start(f32[128,640]{0,1:T(8,128)} %get-tuple-element.6), channel_id=1, source_target_pairs={{0,4},{4,8},{8,12},{1,5},{5,9},{9,13},{2,6},{6,10},{10,14},{3,7},{... | collective-permute-start | bytes 983048 | tf_op jit(solution)/shard_map/ppermute | solution.py:19
  40.8 3.4 %copy-start.25 = (f32[640]{0:T(1024)S(1)}, f32[640]{0:T(1024)}, u32[]{:S(2)}) copy-start(f32[640]{0:T(1024)} %copy-done.24) | copy-start | bytes 7684
  40.8 5.2 %copy-start.27 = (f32[640]{0:T(1024)S(1)}, f32[640]{0:T(1024)}, u32[]{:S(2)}) copy-start(f32[640]{0:T(1024)} %copy-done.26) | copy-start | bytes 7684
  41.4 6.4 %copy-start.37 = (f32[10]{0:T(128)S(1)}, f32[10]{0:T(128)}, u32[]{:S(2)}) copy-start(f32[10]{0:T(128)} %param.21) | copy-start | bytes 124
  59.5 11.1 %collective-permute-start.4 = (f32[128,640]{0,1:T(8,128)S(1)}, f32[128,640]{0,1:T(8,128)S(1)}, u32[]{:S(2)}, u32[]{:S(2)}) collective-permute-start(f32[128,640]{0,1:T(8,128)S(1)} %multiply_add_fusion.1), channel_id=1, source_target_pairs={{4,0},{8,4},{12,8},{5,1},{9,5},{13,9},{6,2},{10,6},{14,10},{7,3},{... | collective-permute-start | bytes 983048 | tf_op jit(solution)/shard_map/ppermute | solution.py:19
  60.9 20.0 %copy-start.11 = (f32[1,128,640]{1,2,0:T(8,128)S(1)}, f32[1,128,640]{1,2,0:T(8,128)}, u32[]{:S(2)}) copy-start(f32[1,128,640]{1,2,0:T(8,128)} %slice_add_fusion) | copy-start | bytes 983044
  60.9 20.0 %copy-start.14 = (bf16[1,512,128]{2,1,0:T(8,128)(2,1)S(1)}, bf16[1,512,128]{2,1,0:T(8,128)(2,1)}, u32[]{:S(2)}) copy-start(bf16[1,512,128]{2,1,0:T(8,128)(2,1)} %copy-done.13) | copy-start | bytes 393220
  62.1 10.9 %collective-permute-start.1 = (f32[128,640]{0,1:T(8,128)S(1)}, f32[128,640]{0,1:T(8,128)S(1)}, u32[]{:S(2)}, u32[]{:S(2)}) collective-permute-start(f32[128,640]{0,1:T(8,128)S(1)} %multiply_add_fusion.3), channel_id=1, source_target_pairs={{0,4},{4,8},{8,12},{1,5},{5,9},{9,13},{2,6},{6,10},{10,14},{3,7},{... | collective-permute-start | bytes 983048 | tf_op jit(solution)/shard_map/ppermute | solution.py:19
  70.7 10.1 %collective-permute-start.5 = (f32[128,640]{0,1:T(8,128)S(1)}, f32[128,640]{0,1:T(8,128)S(1)}, u32[]{:S(2)}, u32[]{:S(2)}) collective-permute-start(f32[128,640]{0,1:T(8,128)S(1)} %multiply_add_fusion), channel_id=1, source_target_pairs={{4,0},{8,4},{12,8},{5,1},{9,5},{13,9},{6,2},{10,6},{14,10},{7,3},{... | collective-permute-start | bytes 983048 | tf_op jit(solution)/shard_map/ppermute | solution.py:19
  72.0 9.6 %copy-start.15 = (bf16[2,256,10,64]{1,0,3,2:T(2,128)(2,1)S(1)}, bf16[2,256,10,64]{1,0,3,2:T(2,128)(2,1)}, u32[]{:S(2)}) copy-start(bf16[2,256,10,64]{1,0,3,2:T(2,128)(2,1)} %reshape_reshape.4) | copy-start | bytes 1966084
  72.0 9.6 %copy-start.16 = (f32[2,256,256]{2,1,0:T(8,128)S(1)}, f32[2,256,256]{2,1,0:T(8,128)}, u32[]{:S(2)}) copy-start(f32[2,256,256]{2,1,0:T(8,128)} %fusion.85) | copy-start | bytes 1572868
  72.1 9.6 %copy-start.19 = (f32[2,10,256]{2,1,0:T(8,128)S(1)}, f32[2,10,256]{2,1,0:T(8,128)}, u32[]{:S(2)}) copy-start(f32[2,10,256]{2,1,0:T(8,128)} %copy-done.18) | copy-start | bytes 61444
  72.1 9.6 %copy-start.29 = (f32[2,256,10]{1,2,0:T(8,128)S(1)}, f32[2,256,10]{1,2,0:T(8,128)}, u32[]{:S(2)}) copy-start(f32[2,256,10]{1,2,0:T(8,128)} %get-tuple-element.20) | copy-start | bytes 61444
  72.1 9.6 %copy-start.30 = (f32[2,10,256]{2,1,0:T(8,128)S(1)}, f32[2,10,256]{2,1,0:T(8,128)}, u32[]{:S(2)}) copy-start(f32[2,10,256]{2,1,0:T(8,128)} %get-tuple-element.22) | copy-start | bytes 61444
  73.2 10.2 %collective-permute-start.2 = (f32[128,640]{0,1:T(8,128)S(1)}, f32[128,640]{0,1:T(8,128)S(1)}, u32[]{:S(2)}, u32[]{:S(2)}) collective-permute-start(f32[128,640]{0,1:T(8,128)S(1)} %multiply_add_fusion.2), channel_id=1, source_target_pairs={{0,4},{4,8},{8,12},{1,5},{5,9},{9,13},{2,6},{6,10},{10,14},{3,7},{... | collective-permute-start | bytes 983048 | tf_op jit(solution)/shard_map/ppermute | solution.py:19
  93.5 54.9 %copy-start.35 = (f32[2560]{0:T(1024)S(1)}, f32[2560]{0:T(1024)}, u32[]{:S(2)}) copy-start(f32[2560]{0:T(1024)} %param.25) | copy-start | bytes 30724
  93.6 81.7 %all-gather.2.cloned.1.call-start = ((), (), s32[]{:S(2)}) async-start(), calls=%async_computation.2 | async-start | bytes 3276800 | tf_op jit(solution)/shard_map/all_gather | solution.py:146
  175.3 5.0 %copy-start.38 = (bf16[2560,512]{1,0:T(8,128)(2,1)S(1)}, bf16[2560,512]{1,0:T(8,128)(2,1)}, u32[]{:S(2)}) copy-start(bf16[2560,512]{1,0:T(8,128)(2,1)} %param.26) | copy-start | bytes 7864324
  175.3 5.0 %copy-start.39 = (bf16[512,2560]{1,0:T(8,128)(2,1)S(1)}, bf16[512,2560]{1,0:T(8,128)(2,1)}, u32[]{:S(2)}) copy-start(bf16[512,2560]{1,0:T(8,128)(2,1)} %all-gather.2.cloned.1.call-done) | copy-start | bytes 7864324
  (25 other events, 34.2 us)
Sparse Core Ops, SparseCore 0:
  93.7 53.1 reduce-scatter.1
  149.7 25.5 all-gather.1

commit v7 on v5

--- a/solution.py
+++ b/solution.py
@@ -84,10 +84,29 @@
     return passed_along(state, axis, steps)
 
 
+def gathered_entry(state, gain, axis):
+    count = lax.axis_size(axis)
+    me = lax.axis_index(axis)
+    heads = state.shape[0]
+    flat = state.reshape(heads, -1)
+    packed = jnp.concatenate([flat, jnp.broadcast_to(gain[:, None], (heads, 128))], axis=1)
+    every = lax.all_gather(packed, axis)
+    total = jnp.zeros_like(flat)
+    carry = jnp.ones_like(gain)
+    for source in range(count - 1, -1, -1):
+        take = source < me
+        total = total + jnp.where(take, carry, 0.0)[:, None] * every[source, :, : flat.shape[1]]
+        carry = jnp.where(take, carry * every[source, :, flat.shape[1]], carry)
+    return total.reshape(state.shape)
+
+
 def direction_out(acts, writes, reads, steps, rates, reverse, axis):
     within, cum_rate, ends, decays = block_parts(acts, writes, reads, steps, rates, reverse)
     starts, gains, own_end, own_gain = chain_blocks(ends, decays, reverse)
-    entering = relay(own_end, own_gain, axis, -1 if reverse else 1)
+    if reverse:
+        entering = relay(own_end, own_gain, axis, -1)
+    else:
+        entering = gathered_entry(own_end, own_gain, axis)
     block_states = starts + gains[:, :, None, None] * entering[None]
     count = within.shape[0]
     reads_b = reads.reshape(count, STRETCH, -1).astype(jnp.float32)

time: 174 us -> 203 us (1.17)
  waiting for transfers between devices: 81.9 us -> 119 us
  starting transfers between devices: 20.2 us -> 4.15 us
  local copies, waits for them, and re-layouts: 17.2 us -> 22.6 us
  other arithmetic: 14.7 us -> 18.9 us
    ppermute x6 -> x3, waiting for transfers between devices: 3.29 us -> 24.3 us  [passed_along(): lax.ppermute(value, axis, [(source, source + steps) for source in range(f...]
    ppermute x6 -> x3, starting transfers between devices: 20.1 us -> 4.03 us  [passed_along(): lax.ppermute(value, axis, [(source, source + steps) for source in range(f...]
    all_gather x0 -> x1, waiting for transfers between devices: none -> 13.3 us  [gathered_entry(): every = lax.all_gather(packed, axis)]
    unnamed x66 -> x80, local copies, waits for them, and re-layouts: 7.49 us -> 11.1 us
    add x6 -> x3, other arithmetic: 5.74 us -> 2.97 us  [relay(): entering = passed_along(gain[:, None, None] * entering + state, axis, steps)]
    reduce_scatter x1, waiting for transfers between devices: 52.9 us -> 55.4 us  [per_device(): lax.psum_scatter(partial_value, 'head', scatter_dimension=0, tiled=True)]
  transfers between devices with their start and end apart: 8 -> 6, of which waited for: 5 -> 4; matrix products, arithmetic and copies ran while one was open for 12% -> 13% of each run, Pallas kernels for 0% -> 0%
where the time goes in v7:
time: 203 us; the launch traced here: 202 us
  waiting for transfers between devices  119 us (59%)
  matrix products  23.8 us (12%)
  local copies, waits for them, and re-layouts  22.6 us (11%)
  other arithmetic  18.9 us (9%)
  between operations  14.3 us (7%)
  starting transfers between devices  4.15 us (2%)
    reduce_scatter x1, waiting for transfers between devices, per_device(): lax.psum_scatter(partial_value, 'head', scatter_dimension=0, tiled=True)  55.4 us
    all_gather x1, waiting for transfers between devices, per_device(): normed = lax.all_gather(normed, 'head', axis=0, tiled=True)  25.7 us
    ppermute x3, waiting for transfers between devices, passed_along(): lax.ppermute(value, axis, [(source, source + steps) for source in range(f...  24.3 us
    all_gather x1, waiting for transfers between devices, gathered_entry(): every = lax.all_gather(packed, axis)  13.3 us
    unnamed x80, local copies, waits for them, and re-layouts  11.1 us
    dot_general x2, matrix products, block_parts(): jnp.einsum('bhts,bshp->bthp', weights, acts_b, preferred_element_type=jnp...  5.24 us
    dot_general x1, matrix products, per_device(): jnp.dot(normed, value_weight, preferred_element_type=jnp.float32)  4.99 us
    dot_general x1, matrix products, per_device(): jnp.dot(mixed, out_weight, preferred_element_type=jnp.float32)  4.66 us
  transfers between devices with their start and end apart: 6, of which 4 were waited for; matrix products, arithmetic and copies ran while one was open for 13% of the time, Pallas kernels for 0%

profile of v7, /device:TPU:0, one launch (start us, length us, event | category | flops | bytes accessed | tf_op | source)
XLA Modules:
  0.0 202.5 jit_solution(16910689234568676502)
XLA Ops:
  12.4 1.4 bitcast_exponential_fusion
  16.0 2.2 %copy.56 = bf16[512,640]{0,1:T(8,128)(2,1)} copy(bf16[512,640]{1,0:T(8,128)(2,1)} %param.14) | data formatting | bytes 1310720 | tf_op args[0]
  18.2 2.7 %reshape_reshape.4 = bf16[2,256,10,64]{1,0,3,2:T(2,128)(2,1)} reshape(bf16[512,640]{0,1:T(8,128)(2,1)} %copy.56) | data formatting | bytes 1310720 | tf_op jit(solution)/shard_map/reshape;reshape | solution.py:25
  20.9 2.3 %convert_multiply_fusion.1 = (f32[2,256,10,64]{1,0,3,2:T(2,128)S(1)}, f32[2,256,10,64]{1,0,3,2:T(2,128)S(1)}) fusion(bf16[2,256,10,64]{1,0,3,2:T(2,128)(2,1)} %reshape_reshape.4, f32[2,256,10]{1,0,2:T(2,128)} %copy.62, f32[2,256,10]{1,0,2:T(2,128)} %copy.58), kind=kLoop, calls=%fused_computation.19 | loop fusion | flops 983040 | bytes 3317760 | tf_op jit(solution)/shard_map/mul | solution.py:48
  24.9 1.3 collective-permute-start
  31.5 1.8 slice_add_fusion
  34.7 2.2 %copy.66 = bf16[512,640]{0,1:T(8,128)(2,1)} copy(bf16[512,640]{1,0:T(8,128)(2,1)} %param.15) | data formatting | bytes 1310720 | tf_op args[1]
  36.9 1.8 tile.4
  38.7 2.7 %copy.78 = f32[64,8,4,640]{3,1,2,0:T(8,128)} copy(f32[64,8,4,640]{3,2,1,0:T(4,128)S(1)} %bitcast.136) | data formatting | bytes 10485760
  42.6 2.7 %fusion.14 = f32[2,256,10,64]{1,3,2,0:T(8,128)} fusion(f32[2,10,256]{2,1,0:T(8,128)S(1)} %copy-done.25, f32[2,10,256]{2,1,0:T(8,128)S(1)} %copy-done.21, f32[2,256,256]{2,1,0:T(8,128)S(1)} %fusion.86, pred[256,256]{1,0:T(8,128)(4,1)S(1)} %copy-done.23, bf16[2,256,10,64]{1,0,3,2:T(2,128)(2,1)S(1)} %copy-done.5), kind=kOutput, calls=%fused_computation.21 | convolution fusion | flops 174325760 | bytes 2596864 | tf_op jit(solution)/shard_map/bhts,bshp->bthp/dot_general | solution.py:46
  45.3 1.1 multiply_add_fusion.2
  46.4 1.3 collective-permute-start.1
  47.7 2.6 %fusion.15 = f32[2,256,10,64]{1,3,2,0:T(8,128)} fusion(f32[2,10,256]{2,1,0:T(8,128)S(1)} %copy-done.24, f32[2,10,256]{2,1,0:T(8,128)S(1)} %copy-done.19, f32[2,256,256]{2,1,0:T(8,128)S(1)} %fusion.85, pred[256,256]{1,0:T(8,128)(4,1)S(1)} %copy-done.22, bf16[2,256,10,64]{1,0,3,2:T(2,128)(2,1)S(1)} %copy-done.5), kind=kOutput, calls=%fused_computation.22 | convolution fusion | flops 174325760 | bytes 2596864 | tf_op jit(solution)/shard_map/bhts,bshp->bthp/dot_general | solution.py:46
  50.3 24.3 %collective-permute-done.1 = f32[10,64,128]{2,1,0:T(8,128)S(1)} collective-permute-done((f32[10,64,128]{2,1,0:T(8,128)S(1)}, f32[10,64,128]{2,1,0:T(8,128)S(1)}, u32[]{:S(2)}, u32[]{:S(2)}) %collective-permute-start.1) | collective-permute-done | bytes 327712 | tf_op jit(solution)/shard_map/ppermute | solution.py:19
  75.4 1.5 collective-permute-start.2
  76.9 13.3 %all-gather.7.cloned.1.call-done = f32[4,10,8320]{2,1,0:T(8,128)} async-done(((f32[1,10,8320]{2,1,0:T(8,128)}), f32[4,10,8320]{2,1,0:T(8,128)}) %all-gather.7.cloned.1.call-update) | async-done | bytes 1331216 | tf_op jit(solution)/shard_map/all_gather | solution.py:93
  90.1 1.7 slice_multiply_fusion
  95.0 2.0 fusion.18
  100.0 4.7 %select_add_fusion = f32[512,2560]{1,0:T(8,128)} fusion(f32[512,2560]{1,0:T(8,128)S(1)} %bitcast.139, bf16[640,2560]{1,0:T(8,128)(2,1)S(1)} %copy-done, pred[2560]{0:T(1024)(128)(4,1)S(1)} %fusion.68, f32[512,640]{0,1:T(8,128)S(1)} %get-tuple-element.8, f32[640]{0:T(1024)S(1)} %copy-done.26, f32[512]{0:T(512)S(1)} %add_rsqrt_fusion), kind=kOutput, calls=%fused_computation | convolution fusion | flops 1681326080 | bytes 15080448 | tf_op jit(solution)/shard_map/dot_general | solution.py:155
  104.8 55.4 %reduce-scatter.2.cloned.1.call-done = f32[128,2560]{1,0:T(8,128)} async-done(((f32[512,2560]{1,0:T(8,128)}), f32[128,2560]{1,0:T(8,128)}) %reduce-scatter.2.cloned.1.call-update) | async-done | bytes 1310736 | tf_op jit(solution)/shard_map/reduce_scatter | solution.py:157
  160.2 1.6 multiply_reduce_fusion
  162.9 25.7 %all-gather.5.cloned.1.call-done = bf16[512,2560]{1,0:T(8,128)(2,1)} async-done(((bf16[128,2560]{1,0:T(8,128)(2,1)}), bf16[512,2560]{1,0:T(8,128)(2,1)}) %all-gather.5.cloned.1.call-update) | async-done | bytes 2621456 | tf_op jit(solution)/shard_map/all_gather | solution.py:163
  188.6 5.0 %convolution_convert_fusion = bf16[512,512]{1,0:T(8,128)(2,1)} fusion(bf16[512,2560]{1,0:T(8,128)(2,1)} %all-gather.5.cloned.1.call-done, bf16[2560,512]{1,0:T(8,128)(2,1)} %param.27), kind=kOutput, calls=%fused_computation.42 | convolution fusion | flops 1342439424 | bytes 5767168 | tf_op jit(solution)/shard_map/dot_general | solution.py:165
  193.6 2.3 %convolution_convert_fusion.1 = bf16[512,512]{1,0:T(8,128)(2,1)} fusion(bf16[512,2560]{1,0:T(8,128)(2,1)S(1)} %copy-done.31, bf16[2560,512]{1,0:T(8,128)(2,1)S(1)} %copy-done.30), kind=kOutput, calls=%fused_computation.43 | convolution fusion | flops 1342439424 | bytes 5767168 | tf_op jit(solution)/shard_map/dot_general | solution.py:164
  (130 shorter events, 25.0 us)
Async XLA Ops:
  7.2 92.8 %copy-start = (bf16[640,2560]{1,0:T(8,128)(2,1)S(1)}, bf16[640,2560]{1,0:T(8,128)(2,1)}, u32[]{:S(2)}) copy-start(bf16[640,2560]{1,0:T(8,128)(2,1)} %param.23) | copy-start | bytes 9830404
  7.2 83.0 %all-gather.7.cloned.1.call-start = ((), (), s32[]{:S(2)}) async-start(), calls=%async_computation.3 | async-start | bytes 2662400 | tf_op jit(solution)/shard_map/all_gather | solution.py:93
  10.1 4.3 %copy-start.20 = (f32[2,10,256]{2,1,0:T(8,128)}, f32[2,10,256]{2,1,0:T(8,128)S(1)}, u32[]{:S(2)}) copy-start(f32[2,10,256]{2,1,0:T(8,128)S(1)} %fusion.48) | copy-start | bytes 61444
  12.2 2.8 %copy-start.18 = (f32[2,10,256]{2,1,0:T(8,128)}, f32[2,10,256]{2,1,0:T(8,128)S(1)}, u32[]{:S(2)}) copy-start(f32[2,10,256]{2,1,0:T(8,128)S(1)} %fusion.50) | copy-start | bytes 61444
  23.9 3.7 %copy-start.3 = (f32[2,10,64,128]{3,2,1,0:T(8,128)}, f32[2,10,64,128]{3,2,1,0:T(8,128)S(1)}, u32[]{:S(2)}) copy-start(f32[2,10,64,128]{3,2,1,0:T(8,128)S(1)} %fusion.25) | copy-start | bytes 1966084
  24.9 20.3 %collective-permute-start = (f32[10,64,128]{2,1,0:T(8,128)}, f32[10,64,128]{2,1,0:T(8,128)}, u32[]{:S(2)}, u32[]{:S(2)}) collective-permute-start(f32[10,64,128]{2,1,0:T(8,128)} %get-tuple-element.9), channel_id=1, source_target_pairs={{4,0},{8,4},{12,8},{5,1},{9,5},{13,9},{6,2},{10,6},{14,10},{7,3},{... | collective-permute-start | bytes 983048 | tf_op jit(solution)/shard_map/ppermute | solution.py:19
  29.2 4.1 %copy-start.29 = (f32[10]{0:T(128)S(1)}, f32[10]{0:T(128)}, u32[]{:S(2)}) copy-start(f32[10]{0:T(128)} %param.21) | copy-start | bytes 124
  30.2 130.0 %reduce-scatter.2.cloned.1.call-start = ((), (), s32[]{:S(2)}) async-start(), calls=%async_computation.1 | async-start | bytes 6553600 | tf_op jit(solution)/shard_map/reduce_scatter | solution.py:157
  38.7 2.7 %copy-start.15 = (bf16[2,512,128]{2,1,0:T(8,128)(2,1)S(1)}, bf16[2,512,128]{2,1,0:T(8,128)(2,1)}, u32[]{:S(2)}) copy-start(bf16[2,512,128]{2,1,0:T(8,128)(2,1)} %param.17) | copy-start | bytes 786436
  42.6 2.7 %copy-start.4 = (f32[10,64,128]{2,1,0:T(8,128)S(1)}, f32[10,64,128]{2,1,0:T(8,128)}, u32[]{:S(2)}) copy-start(f32[10,64,128]{2,1,0:T(8,128)} %get-tuple-element.10) | copy-start | bytes 983044
  42.6 2.7 %copy-start.28 = (f32[10]{0:T(128)S(1)}, f32[10]{0:T(128)}, u32[]{:S(2)}) copy-start(f32[10]{0:T(128)} %get-tuple-element.12) | copy-start | bytes 124
  42.6 5.1 %copy-start.19 = (f32[2,10,256]{2,1,0:T(8,128)S(1)}, f32[2,10,256]{2,1,0:T(8,128)}, u32[]{:S(2)}) copy-start(f32[2,10,256]{2,1,0:T(8,128)} %copy-done.18) | copy-start | bytes 61444
  42.6 5.1 %copy-start.22 = (pred[256,256]{1,0:T(8,128)(4,1)S(1)}, pred[256,256]{1,0:T(8,128)(4,1)}, u32[]{:S(2)}) copy-start(pred[256,256]{1,0:T(8,128)(4,1)} %iota_compare_fusion.1) | copy-start | bytes 196612
  42.6 5.1 %copy-start.24 = (f32[2,10,256]{2,1,0:T(8,128)S(1)}, f32[2,10,256]{2,1,0:T(8,128)}, u32[]{:S(2)}) copy-start(f32[2,10,256]{2,1,0:T(8,128)} %get-tuple-element.42) | copy-start | bytes 61444
  46.4 28.2 %collective-permute-start.1 = (f32[10,64,128]{2,1,0:T(8,128)S(1)}, f32[10,64,128]{2,1,0:T(8,128)S(1)}, u32[]{:S(2)}, u32[]{:S(2)}) collective-permute-start(f32[10,64,128]{2,1,0:T(8,128)S(1)} %multiply_add_fusion.2), channel_id=1, source_target_pairs={{4,0},{8,4},{12,8},{5,1},{9,5},{13,9},{6,2},{10,6},{14,10},{7,3},{... | collective-permute-start | bytes 983048 | tf_op jit(solution)/shard_map/ppermute | solution.py:19
  75.4 19.0 %collective-permute-start.2 = (f32[10,64,128]{2,1,0:T(8,128)}, f32[10,64,128]{2,1,0:T(8,128)}, u32[]{:S(2)}, u32[]{:S(2)}) collective-permute-start(f32[10,64,128]{2,1,0:T(8,128)} %multiply_add_fusion.1), channel_id=1, source_target_pairs={{4,0},{8,4},{12,8},{5,1},{9,5},{13,9},{6,2},{10,6},{14,10},{7,3},{... | collective-permute-start | bytes 983048 | tf_op jit(solution)/shard_map/ppermute | solution.py:19
  92.2 1.4 copy-start.12
  95.0 4.9 %slice-start = ((s8[5242880]{0:T(1024)(128)(4,1)}), s8[4194304]{0:T(1024)(128)(4,1)S(1)}, s32[]{:S(2)}) async-start(s8[5242880]{0:T(1024)(128)(4,1)} %bitcast.137), calls=%async_computation.4 | async-start | bytes 8388608
  97.0 2.9 %slice-start.1 = ((s8[5242880]{0:T(1024)(128)(4,1)}), s8[1048576]{0:T(1024)(128)(4,1)S(1)}, s32[]{:S(2)}) async-start(s8[5242880]{0:T(1024)(128)(4,1)} %bitcast.137), calls=%async_computation.5 | async-start | bytes 2097152
  104.7 57.1 %copy-start.27 = (f32[2560]{0:T(1024)S(1)}, f32[2560]{0:T(1024)}, u32[]{:S(2)}) copy-start(f32[2560]{0:T(1024)} %param.25) | copy-start | bytes 30724
  104.7 83.9 %all-gather.5.cloned.1.call-start = ((), (), s32[]{:S(2)}) async-start(), calls=%async_computation.2 | async-start | bytes 3276800 | tf_op jit(solution)/shard_map/all_gather | solution.py:163
  160.2 1.7 copy-start.2
  188.6 5.0 %copy-start.30 = (bf16[2560,512]{1,0:T(8,128)(2,1)S(1)}, bf16[2560,512]{1,0:T(8,128)(2,1)}, u32[]{:S(2)}) copy-start(bf16[2560,512]{1,0:T(8,128)(2,1)} %param.26) | copy-start | bytes 7864324
  188.6 5.0 %copy-start.31 = (bf16[512,2560]{1,0:T(8,128)(2,1)S(1)}, bf16[512,2560]{1,0:T(8,128)(2,1)}, u32[]{:S(2)}) copy-start(bf16[512,2560]{1,0:T(8,128)(2,1)} %all-gather.5.cloned.1.call-done) | copy-start | bytes 7864324
  (16 other events, 19.0 us)
Sparse Core Ops, SparseCore 0:
  30.3 59.8 all-gather.6
  104.8 55.2 reduce-scatter.1
  163.0 25.5 all-gather.4

commit v8 on v5

--- a/solution.py
+++ b/solution.py
@@ -43,7 +43,12 @@
     weights = (
         intersection[:, None] * decays * jnp.transpose(steps_b, (0, 2, 1))[:, :, None, :]
     ).astype(jnp.bfloat16)
-    within = jnp.einsum("bhts,bshp->bthp", weights, acts_b, preferred_element_type=jnp.float32)
+    weights = jnp.transpose(weights, (0, 2, 1, 3)).reshape(count, STRETCH, heads * STRETCH)
+    same_head = jnp.arange(heads)[:, None, None, None] == jnp.arange(heads)[None, None, :, None]
+    diagonal = jnp.where(same_head[None], acts_b[:, None], jnp.zeros((), acts_b.dtype))
+    diagonal = diagonal.reshape(count, heads * STRETCH, heads * width)
+    within = jnp.einsum("btk,bkc->btc", weights, diagonal, preferred_element_type=jnp.float32)
+    within = within.reshape(count, STRETCH, heads, width)
     tail = jnp.exp(block_total[:, None, :] - cum_rate) * steps_b
     weighted = acts_b.astype(jnp.float32) * tail[:, :, :, None]
     ends = jnp.einsum(

time: 174 us -> 222 us (1.28)
  local copies, waits for them, and re-layouts: 17.2 us -> 47.6 us
  other arithmetic: 14.7 us -> 26.2 us
  matrix products: 24.8 us -> 30.3 us
    broadcast_in_dim x0 -> x7, local copies, waits for them, and re-layouts: none -> 25.3 us  [the longest x5 24.1 us: block_parts(): jnp.where(same_head[None], acts_b[:, None], jnp.zeros((), acts_b.dtype))]
    convert_element_type x0 -> x2, other arithmetic: none -> 5.06 us  [block_parts(): weights = (intersection[:, None] * decays * jnp.transpose(steps_b, (0, 2,...]
    unnamed x66 -> x87, local copies, waits for them, and re-layouts: 7.49 us -> 11.9 us
    dot_general x2, matrix products: 5.24 us -> 8.88 us  [block_parts(): jnp.einsum('btk,bkc->btc', weights, diagonal, preferred_element_type=jnp....]
    add x6, other arithmetic: 5.74 us -> 9.37 us  [relay(): entering = passed_along(gain[:, None, None] * entering + state, axis, steps)]
    another operation x1 -> x0, local copies, waits for them, and re-layouts: 2.67 us -> none  [block_parts(): acts_b = acts.reshape(count, STRETCH, heads, width)]
  transfers between devices with their start and end apart: 8 -> 8, of which waited for: 5 -> 4; matrix products, arithmetic and copies ran while one was open for 12% -> 30% of each run, Pallas kernels for 0% -> 0%
where the time goes in v8:
time: 222 us; the launch traced here: 221 us
  waiting for transfers between devices  81.3 us (37%)
  local copies, waits for them, and re-layouts  47.6 us (21%)
  matrix products  30.3 us (14%)
  other arithmetic  26.2 us (12%)
  starting transfers between devices  20.6 us (9%)
  between operations  14.7 us (7%)
    reduce_scatter x1, waiting for transfers between devices, per_device(): lax.psum_scatter(partial_value, 'head', scatter_dimension=0, tiled=True)  52.4 us
    all_gather x1, waiting for transfers between devices, per_device(): normed = lax.all_gather(normed, 'head', axis=0, tiled=True)  25.7 us
    broadcast_in_dim x5, local copies, waits for them, and re-layouts, block_parts(): jnp.where(same_head[None], acts_b[:, None], jnp.zeros((), acts_b.dtype))  24.1 us
    ppermute x6, starting transfers between devices, passed_along(): lax.ppermute(value, axis, [(source, source + steps) for source in range(f...  20.5 us
    unnamed x87, local copies, waits for them, and re-layouts  11.9 us
    add x6, other arithmetic, relay(): entering = passed_along(gain[:, None, None] * entering + state, axis, steps)  9.37 us
    dot_general x2, matrix products, block_parts(): jnp.einsum('btk,bkc->btc', weights, diagonal, preferred_element_type=jnp....  8.88 us
    convert_element_type x2, other arithmetic, block_parts(): weights = (intersection[:, None] * decays * jnp.transpose(steps_b, (0, 2,...  5.06 us
  transfers between devices with their start and end apart: 8, of which 4 were waited for; matrix products, arithmetic and copies ran while one was open for 30% of the time, Pallas kernels for 0%

profile of v8, /device:TPU:0, one launch (start us, length us, event | category | flops | bytes accessed | tf_op | source)
XLA Modules:
  0.0 220.5 jit_solution(17103588195765972750)
XLA Ops:
  13.7 2.2 copy.24
  15.9 2.7 %broadcast_in_dim.124 = bf16[2,256,10,64]{1,0,3,2:T(2,128)(2,1)} reshape(bf16[512,640]{0,1:T(8,128)(2,1)} %copy.24) | data formatting | bytes 1310720 | tf_op jit(solution)/shard_map/jit(_where)/broadcast_in_dim | solution.py:48
  19.6 2.3 %convert_multiply_fusion.1 = (f32[2,256,10,64]{1,0,3,2:T(2,128)S(1)}, f32[2,256,10,64]{1,0,3,2:T(2,128)S(1)}) fusion(bf16[2,256,10,64]{1,0,3,2:T(2,128)(2,1)} %broadcast_in_dim.124, f32[2,256,10]{1,0,2:T(2,128)S(1)} %copy.37, f32[2,256,10]{1,0,2:T(2,128)S(1)} %copy.29), kind=kLoop, calls=%fused_computation.20 | loop fusion | flops 983040 | bytes 3317760 | tf_op jit(solution)/shard_map/mul | solution.py:53
  23.6 5.8 %collective-permute-start = (f32[10,64,128]{2,1,0:T(8,128)}, f32[10,64,128]{2,1,0:T(8,128)}, u32[]{:S(2)}, u32[]{:S(2)}) collective-permute-start(f32[10,64,128]{2,1,0:T(8,128)} %get-tuple-element.10), channel_id=1, source_target_pairs={{0,4},{4,8},{8,12},{1,5},{5,9},{9,13},{2,6},{6,10},{10,14},{3,7},{... | collective-permute-start | bytes 983048 | tf_op jit(solution)/shard_map/ppermute | solution.py:19
  39.0 6.1 %broadcast_in_dim.125 = bf16[2,10,256,10,64]{2,1,4,3,0:T(8,128)(2,1)} broadcast(bf16[2,256,10,64]{1,3,2,0:T(8,128)(2,1)} %copy.25), dimensions={0,2,3,4} | broadcast | bytes 7208960 | tf_op jit(solution)/shard_map/jit(_where)/broadcast_in_dim | solution.py:48
  45.1 13.7 %broadcast_in_dim.126 = bf16[2,2560,640]{1,2,0:T(8,128)(2,1)} reshape(bf16[2,10,256,10,64]{2,1,4,3,0:T(8,128)(2,1)} %broadcast_in_dim.125) | data formatting | bytes 13107200 | tf_op jit(solution)/shard_map/jit(_where)/broadcast_in_dim | solution.py:48
  59.6 2.9 %copy.54 = pred[80,8,10,256]{3,1,2,0:T(8,128)(4,1)} copy(pred[80,8,10,256]{3,2,1,0:T(8,128)(4,1)S(1)} %bitcast.169) | data formatting | bytes 3276800
  68.7 3.3 %fusion.9 = bf16[2,256,2560]{1,2,0:T(8,128)(2,1)S(1)} fusion(f32[2,2560]{1,0:T(2,128)} %bitcast.194, f32[2,2560]{1,0:T(2,128)} %bitcast.195, f32[2,256,10]{1,2,0:T(8,128)} %bitcast.190, f32[2,256,256]{1,2,0:T(8,128)S(1)} %fusion.80, pred[256,2560]{0,1:T(8,128)(4,1)S(1)} %bitcast.174), kind=kLoop, calls=%fused_computation.12 | loop fusion | flops 6553600 | bytes 3862528 | tf_op jit(solution)/shard_map/convert_element_type | solution.py:45
  72.1 6.0 %fusion.10 = f32[2,256,640]{1,2,0:T(8,128)} fusion(bf16[2,256,2560]{1,2,0:T(8,128)(2,1)S(1)} %fusion.9, bf16[2,2560,640]{1,2,0:T(8,128)(2,1)} %broadcast_in_dim.126, pred[2560,640]{0,1:T(8,128)(4,1)S(1)} %bitcast.176), kind=kOutput, calls=%fused_computation.14 | convolution fusion | flops 1680998400 | bytes 12124160 | tf_op jit(solution)/shard_map/btk,bkc->btc/dot_general | solution.py:50
  80.1 2.9 %fusion.11 = f32[2,256,640]{1,2,0:T(8,128)} fusion(bf16[2,256,2560]{1,2,0:T(8,128)(2,1)S(1)} %fusion.4, bf16[2,2560,640]{1,2,0:T(8,128)(2,1)S(1)} %bitcast.171, pred[2560,640]{0,1:T(8,128)(4,1)S(1)} %bitcast.177), kind=kOutput, calls=%fused_computation.15 | convolution fusion | flops 1680998400 | bytes 12124160 | tf_op jit(solution)/shard_map/btk,bkc->btc/dot_general | solution.py:50
  83.9 1.8 multiply_add_fusion.3
  85.7 5.4 %collective-permute-start.1 = (f32[10,64,128]{2,1,0:T(8,128)}, f32[10,64,128]{2,1,0:T(8,128)}, u32[]{:S(2)}, u32[]{:S(2)}) collective-permute-start(f32[10,64,128]{2,1,0:T(8,128)} %multiply_add_fusion.3), channel_id=1, source_target_pairs={{0,4},{4,8},{8,12},{1,5},{5,9},{9,13},{2,6},{6,10},{10,14},{3,7},{... | collective-permute-start | bytes 983048 | tf_op jit(solution)/shard_map/ppermute | solution.py:19
  95.0 2.1 collective-permute-done.1
  97.1 1.9 multiply_add_fusion.2
  98.9 5.1 %collective-permute-start.2 = (f32[10,64,128]{2,1,0:T(8,128)}, f32[10,64,128]{2,1,0:T(8,128)}, u32[]{:S(2)}, u32[]{:S(2)}) collective-permute-start(f32[10,64,128]{2,1,0:T(8,128)} %multiply_add_fusion.2), channel_id=1, source_target_pairs={{0,4},{4,8},{8,12},{1,5},{5,9},{9,13},{2,6},{6,10},{10,14},{3,7},{... | collective-permute-start | bytes 983048 | tf_op jit(solution)/shard_map/ppermute | solution.py:19
  104.1 1.9 multiply_add_fusion
  107.5 2.2 copy.41
  115.9 1.8 fusion.16
  119.6 4.8 %select_add_fusion = f32[512,2560]{1,0:T(8,128)} fusion(f32[512,2560]{1,0:T(8,128)S(1)} %bitcast.168, bf16[640,2560]{1,0:T(8,128)(2,1)S(1)} %copy-done, pred[2560]{0:T(1024)(128)(4,1)S(1)} %fusion.63, f32[512,640]{0,1:T(8,128)S(1)} %get-tuple-element.5, f32[640]{0:T(1024)S(1)} %copy-done.28, f32[512]{0:T(512)S(1)} %add_rsqrt_fusion), kind=kOutput, calls=%fused_computation.13 | convolution fusion | flops 1681326080 | bytes 15080448 | tf_op jit(solution)/shard_map/dot_general | solution.py:141
  124.5 52.4 %reduce-scatter.2.cloned.1.call-done = f32[128,2560]{1,0:T(8,128)} async-done(((f32[512,2560]{1,0:T(8,128)}), f32[128,2560]{1,0:T(8,128)}) %reduce-scatter.2.cloned.1.call-update) | async-done | bytes 1310736 | tf_op jit(solution)/shard_map/reduce_scatter | solution.py:143
  178.3 2.3 %multiply_convert_fusion = bf16[128,2560]{1,0:T(8,128)(2,1)} fusion(f32[128,2560]{1,0:T(8,128)} %reduce-scatter.2.cloned.1.call-done, f32[2560]{0:T(1024)S(1)} %copy-done.29, f32[128]{0:T(128)S(1)} %add_rsqrt_fusion.1), kind=kLoop, calls=%fused_computation.37 | loop fusion | flops 983040 | bytes 1976832 | tf_op jit(solution)/shard_map/convert_element_type | solution.py:148
  180.7 25.7 %all-gather.2.cloned.1.call-done = bf16[512,2560]{1,0:T(8,128)(2,1)} async-done(((bf16[128,2560]{1,0:T(8,128)(2,1)}), bf16[512,2560]{1,0:T(8,128)(2,1)}) %all-gather.2.cloned.1.call-update) | async-done | bytes 2621456 | tf_op jit(solution)/shard_map/all_gather | solution.py:149
  206.4 5.0 %convolution_convert_fusion = bf16[512,512]{1,0:T(8,128)(2,1)} fusion(bf16[512,2560]{1,0:T(8,128)(2,1)} %all-gather.2.cloned.1.call-done, bf16[2560,512]{1,0:T(8,128)(2,1)} %param.27), kind=kOutput, calls=%fused_computation.41 | convolution fusion | flops 1342439424 | bytes 5767168 | tf_op jit(solution)/shard_map/dot_general | solution.py:151
  211.4 2.3 %convolution_convert_fusion.1 = bf16[512,512]{1,0:T(8,128)(2,1)} fusion(bf16[512,2560]{1,0:T(8,128)(2,1)S(1)} %copy-done.36, bf16[2560,512]{1,0:T(8,128)(2,1)S(1)} %copy-done.35), kind=kOutput, calls=%fused_computation.42 | convolution fusion | flops 1342439424 | bytes 5767168 | tf_op jit(solution)/shard_map/dot_general | solution.py:150
  (147 shorter events, 43.5 us)
Async XLA Ops:
  7.2 112.4 %copy-start = (bf16[640,2560]{1,0:T(8,128)(2,1)S(1)}, bf16[640,2560]{1,0:T(8,128)(2,1)}, u32[]{:S(2)}) copy-start(bf16[640,2560]{1,0:T(8,128)(2,1)} %param.23) | copy-start | bytes 9830404
  7.2 169.6 %reduce-scatter.2.cloned.1.call-start = ((), (), s32[]{:S(2)}) async-start(), calls=%async_computation.1 | async-start | bytes 6553600 | tf_op jit(solution)/shard_map/reduce_scatter | solution.py:143
  9.9 26.2 %copy-start.17 = (f32[2,10,256]{2,1,0:T(8,128)}, f32[2,10,256]{2,1,0:T(8,128)S(1)}, u32[]{:S(2)}) copy-start(f32[2,10,256]{2,1,0:T(8,128)S(1)} %fusion.45) | copy-start | bytes 61444
  22.6 7.4 %copy-start.5 = (f32[2,10,64,128]{3,2,1,0:T(8,128)}, f32[2,10,64,128]{3,2,1,0:T(8,128)S(1)}, u32[]{:S(2)}) copy-start(f32[2,10,64,128]{3,2,1,0:T(8,128)S(1)} %fusion.25) | copy-start | bytes 1966084
  22.6 11.3 %copy-start.1 = (bf16[2,256,10,64]{1,0,3,2:T(2,128)(2,1)S(1)}, bf16[2,256,10,64]{1,0,3,2:T(2,128)(2,1)}, u32[]{:S(2)}) copy-start(bf16[2,256,10,64]{1,0,3,2:T(2,128)(2,1)} %broadcast_in_dim.124) | copy-start | bytes 1966084
  23.6 13.1 %copy-start.21 = (bf16[2,512,128]{2,1,0:T(8,128)(2,1)S(1)}, bf16[2,512,128]{2,1,0:T(8,128)(2,1)}, u32[]{:S(2)}) copy-start(bf16[2,512,128]{2,1,0:T(8,128)(2,1)} %param.17) | copy-start | bytes 786436
  23.6 60.3 %collective-permute-start = (f32[10,64,128]{2,1,0:T(8,128)}, f32[10,64,128]{2,1,0:T(8,128)}, u32[]{:S(2)}, u32[]{:S(2)}) collective-permute-start(f32[10,64,128]{2,1,0:T(8,128)} %get-tuple-element.10), channel_id=1, source_target_pairs={{0,4},{4,8},{8,12},{1,5},{5,9},{9,13},{2,6},{6,10},{10,14},{3,7},{... | collective-permute-start | bytes 983048 | tf_op jit(solution)/shard_map/ppermute | solution.py:19
  31.8 59.3 %collective-permute-start.3 = (f32[10,64,128]{2,1,0:T(8,128)}, f32[10,64,128]{2,1,0:T(8,128)}, u32[]{:S(2)}, u32[]{:S(2)}) collective-permute-start(f32[10,64,128]{2,1,0:T(8,128)} %get-tuple-element.6), channel_id=1, source_target_pairs={{4,0},{8,4},{12,8},{5,1},{9,5},{13,9},{6,2},{10,6},{14,10},{7,3},{... | collective-permute-start | bytes 983048 | tf_op jit(solution)/shard_map/ppermute | solution.py:19
  72.0 8.0 %slice-start = ((s8[6553600]{0:T(1024)(128)(4,1)}), s8[4194304]{0:T(1024)(128)(4,1)S(1)}, s32[]{:S(2)}) async-start(s8[6553600]{0:T(1024)(128)(4,1)} %bitcast.170), calls=%async_computation.3 | async-start | bytes 8388608
  72.0 6.2 %copy-start.20 = (f32[2,10,256]{2,1,0:T(8,128)S(1)}, f32[2,10,256]{2,1,0:T(8,128)}, u32[]{:S(2)}) copy-start(f32[2,10,256]{2,1,0:T(8,128)} %copy-done.18) | copy-start | bytes 61444
  72.0 6.2 %copy-start.26 = (f32[1,2,10,256]{3,1,2,0:T(2,128)S(1)}, f32[1,2,10,256]{3,1,2,0:T(2,128)}, u32[]{:S(2)}) copy-start(f32[1,2,10,256]{3,1,2,0:T(2,128)} %copy.58) | copy-start | bytes 61444
  72.1 8.0 %slice-start.1 = ((s8[6553600]{0:T(1024)(128)(4,1)}), s8[2359296]{0:T(1024)(128)(4,1)S(1)}, s32[]{:S(2)}) async-start(s8[6553600]{0:T(1024)(128)(4,1)} %bitcast.170), calls=%async_computation.4 | async-start | bytes 4718592
  80.1 11.0 %copy-start.8 = (f32[10,64,128]{2,1,0:T(8,128)S(1)}, f32[10,64,128]{2,1,0:T(8,128)}, u32[]{:S(2)}) copy-start(f32[10,64,128]{2,1,0:T(8,128)} %get-tuple-element.7) | copy-start | bytes 983044
  83.0 11.1 %copy-start.4 = (f32[2,10,64,128]{3,2,1,0:T(8,128)S(1)}, f32[2,10,64,128]{3,2,1,0:T(8,128)}, u32[]{:S(2)}) copy-start(f32[2,10,64,128]{3,2,1,0:T(8,128)} %copy-done.3) | copy-start | bytes 1966084
  83.0 11.1 %copy-start.31 = (f32[10]{0:T(128)S(1)}, f32[10]{0:T(128)}, u32[]{:S(2)}) copy-start(f32[10]{0:T(128)} %copy-done.30) | copy-start | bytes 124
  83.0 24.5 %copy-start.32 = (f32[1,10]{1,0:T(1,128)S(1)}, f32[1,10]{1,0:T(1,128)}, u32[]{:S(2)}) copy-start(f32[1,10]{1,0:T(1,128)} %get-tuple-element.29) | copy-start | bytes 124
  83.0 24.5 %copy-start.33 = (f32[1,10]{1,0:T(1,128)S(1)}, f32[1,10]{1,0:T(1,128)}, u32[]{:S(2)}) copy-start(f32[1,10]{1,0:T(1,128)} %get-tuple-element.26) | copy-start | bytes 124
  85.7 24.0 %copy-start.34 = (f32[10]{0:T(128)S(1)}, f32[10]{0:T(128)}, u32[]{:S(2)}) copy-start(f32[10]{0:T(128)} %param.21) | copy-start | bytes 124
  85.7 11.4 %collective-permute-start.1 = (f32[10,64,128]{2,1,0:T(8,128)}, f32[10,64,128]{2,1,0:T(8,128)}, u32[]{:S(2)}, u32[]{:S(2)}) collective-permute-start(f32[10,64,128]{2,1,0:T(8,128)} %multiply_add_fusion.3), channel_id=1, source_target_pairs={{0,4},{4,8},{8,12},{1,5},{5,9},{9,13},{2,6},{6,10},{10,14},{3,7},{... | collective-permute-start | bytes 983048 | tf_op jit(solution)/shard_map/ppermute | solution.py:19
  92.9 11.2 %collective-permute-start.4 = (f32[10,64,128]{2,1,0:T(8,128)}, f32[10,64,128]{2,1,0:T(8,128)}, u32[]{:S(2)}, u32[]{:S(2)}) collective-permute-start(f32[10,64,128]{2,1,0:T(8,128)} %multiply_add_fusion.1), channel_id=1, source_target_pairs={{4,0},{8,4},{12,8},{5,1},{9,5},{13,9},{6,2},{10,6},{14,10},{7,3},{... | collective-permute-start | bytes 983048 | tf_op jit(solution)/shard_map/ppermute | solution.py:19
  98.9 13.1 %collective-permute-start.2 = (f32[10,64,128]{2,1,0:T(8,128)}, f32[10,64,128]{2,1,0:T(8,128)}, u32[]{:S(2)}, u32[]{:S(2)}) collective-permute-start(f32[10,64,128]{2,1,0:T(8,128)} %multiply_add_fusion.2), channel_id=1, source_target_pairs={{0,4},{4,8},{8,12},{1,5},{5,9},{9,13},{2,6},{6,10},{10,14},{3,7},{... | collective-permute-start | bytes 983048 | tf_op jit(solution)/shard_map/ppermute | solution.py:19
  106.0 9.9 %collective-permute-start.5 = (f32[10,64,128]{2,1,0:T(8,128)}, f32[10,64,128]{2,1,0:T(8,128)}, u32[]{:S(2)}, u32[]{:S(2)}) collective-permute-start(f32[10,64,128]{2,1,0:T(8,128)} %multiply_add_fusion), channel_id=1, source_target_pairs={{4,0},{8,4},{12,8},{5,1},{9,5},{13,9},{6,2},{10,6},{14,10},{7,3},{... | collective-permute-start | bytes 983048 | tf_op jit(solution)/shard_map/ppermute | solution.py:19
  124.4 53.9 %copy-start.29 = (f32[2560]{0:T(1024)S(1)}, f32[2560]{0:T(1024)}, u32[]{:S(2)}) copy-start(f32[2560]{0:T(1024)} %param.25) | copy-start | bytes 30724
  124.4 82.0 %all-gather.2.cloned.1.call-start = ((), (), s32[]{:S(2)}) async-start(), calls=%async_computation.2 | async-start | bytes 3276800 | tf_op jit(solution)/shard_map/all_gather | solution.py:149
  (23 other events, 75.8 us)
Sparse Core Ops, SparseCore 0:
  124.5 52.2 reduce-scatter.1
  180.8 25.5 all-gather.1

commit v9 on v5

--- a/solution.py
+++ b/solution.py
@@ -19,35 +19,40 @@
     return lax.ppermute(value, axis, [(source, source + steps) for source in range(first, last)])
 
 
-def block_parts(acts, writes, reads, steps, rates, reverse):
+def block_parts(acts, writes, reads, steps, rates):
     tokens, heads, width = acts.shape
     count = tokens // STRETCH
     acts_b = acts.reshape(count, STRETCH, heads, width)
-    writes_b = writes.reshape(count, STRETCH, -1)
-    reads_b = reads.reshape(count, STRETCH, -1)
-    steps_b = steps.reshape(count, STRETCH, heads)
-    rates_b = rates.reshape(count, STRETCH, heads)
+    writes_b = writes.reshape(2, count, STRETCH, -1)
+    reads_b = reads.reshape(2, count, STRETCH, -1)
+    steps_b = steps.reshape(2, count, STRETCH, heads)
+    rates_b = rates.reshape(2, count, STRETCH, heads)
     position = jnp.arange(STRETCH)
-    if reverse:
-        causal = position[:, None] <= position[None, :]
-    else:
-        causal = position[:, None] >= position[None, :]
+    causal = jnp.stack(
+        [position[:, None] >= position[None, :], position[:, None] <= position[None, :]]
+    )
     cum_rate = jnp.einsum(
-        "ts,bsh->bth", causal.astype(jnp.float32), rates_b, precision=highest
+        "dts,dbsh->dbth", causal.astype(jnp.float32), rates_b, precision=highest
     )
-    block_total = cum_rate[:, 0] if reverse else cum_rate[:, -1]
-    along = jnp.transpose(cum_rate, (0, 2, 1))
-    spans = along[:, :, :, None] - along[:, :, None, :]
-    decays = jnp.exp(jnp.where(causal[None, None], spans, -1e30))
-    intersection = jnp.einsum("btn,bsn->bts", reads_b, writes_b, preferred_element_type=jnp.float32)
+    block_total = jnp.stack([cum_rate[0, :, -1], cum_rate[1, :, 0]])
+    along = jnp.transpose(cum_rate, (0, 1, 3, 2))
+    spans = along[..., :, None] - along[..., None, :]
+    decays = jnp.exp(jnp.where(causal[:, None, None], spans, -1e30))
+    intersection = jnp.einsum(
+        "dbtn,dbsn->dbts", reads_b, writes_b, preferred_element_type=jnp.float32
+    )
     weights = (
-        intersection[:, None] * decays * jnp.transpose(steps_b, (0, 2, 1))[:, :, None, :]
+        intersection[:, :, None]
+        * decays
+        * jnp.transpose(steps_b, (0, 1, 3, 2))[:, :, :, None, :]
     ).astype(jnp.bfloat16)
-    within = jnp.einsum("bhts,bshp->bthp", weights, acts_b, preferred_element_type=jnp.float32)
-    tail = jnp.exp(block_total[:, None, :] - cum_rate) * steps_b
-    weighted = acts_b.astype(jnp.float32) * tail[:, :, :, None]
+    within = jnp.einsum(
+        "dbhts,bshp->dbthp", weights, acts_b, preferred_element_type=jnp.float32
+    )
+    tail = jnp.exp(block_total[:, :, None, :] - cum_rate) * steps_b
+    weighted = acts_b.astype(jnp.float32)[None] * tail[..., None]
     ends = jnp.einsum(
-        "bshp,bsn->bhpn", weighted, writes_b.astype(jnp.float32), precision=highest
+        "dbshp,dbsn->dbhpn", weighted, writes_b.astype(jnp.float32), precision=highest
     )
     return within, cum_rate, ends, jnp.exp(block_total)
 
@@ -84,16 +89,19 @@
     return passed_along(state, axis, steps)
 
 
-def direction_out(acts, writes, reads, steps, rates, reverse, axis):
-    within, cum_rate, ends, decays = block_parts(acts, writes, reads, steps, rates, reverse)
-    starts, gains, own_end, own_gain = chain_blocks(ends, decays, reverse)
-    entering = relay(own_end, own_gain, axis, -1 if reverse else 1)
-    block_states = starts + gains[:, :, None, None] * entering[None]
-    count = within.shape[0]
-    reads_b = reads.reshape(count, STRETCH, -1).astype(jnp.float32)
-    carried = jnp.einsum("btn,bhpn->bthp", reads_b, block_states, precision=highest)
-    outputs = within + jnp.exp(cum_rate)[:, :, :, None] * carried
-    return outputs.reshape(acts.shape)
+def both_directions(acts, writes, reads, steps, rates, axis):
+    within, cum_rate, ends, decays = block_parts(acts, writes, reads, steps, rates)
+    block_states = []
+    for direction, reverse in ((0, False), (1, True)):
+        starts, gains, own_end, own_gain = chain_blocks(ends[direction], decays[direction], reverse)
+        entering = relay(own_end, own_gain, axis, -1 if reverse else 1)
+        block_states.append(starts + gains[:, :, None, None] * entering[None])
+    block_states = jnp.stack(block_states)
+    count = within.shape[1]
+    reads_b = reads.reshape(2, count, STRETCH, -1).astype(jnp.float32)
+    carried = jnp.einsum("dbtn,dbhpn->dbthp", reads_b, block_states, precision=highest)
+    outputs = within + jnp.exp(cum_rate)[..., None] * carried
+    return outputs.reshape((2,) + acts.shape)
 
 
 def per_device(
@@ -117,15 +125,11 @@
     width = inner_acts.shape[1] // heads
     acts = inner_acts.reshape(tokens, heads, width)
     decay_rate = -jnp.exp(decay_log)
-    steps_fwd = jax.nn.softplus(step_raw[0] + step_bias[None, :])
-    steps_bwd = jax.nn.softplus(step_raw[1] + step_bias[None, :])
-    fwd_all = direction_out(
-        acts, write_map[0], read_map[0], steps_fwd, steps_fwd * decay_rate[None, :], False, "seq"
+    steps_both = jax.nn.softplus(step_raw + step_bias[None, None, :])
+    outputs = both_directions(
+        acts, write_map, read_map, steps_both, steps_both * decay_rate[None, None, :], "seq"
     )
-    bwd_all = direction_out(
-        acts, write_map[1], read_map[1], steps_bwd, steps_bwd * decay_rate[None, :], True, "seq"
-    )
-    summed = fwd_all + bwd_all + skip_gain[None, :, None] * acts.astype(jnp.float32)
+    summed = outputs[0] + outputs[1] + skip_gain[None, :, None] * acts.astype(jnp.float32)
     gated = summed.reshape(tokens, heads * width) * jax.nn.silu(gate_acts.astype(jnp.float32))
     grouped = gated.reshape(tokens, NORM_GROUPS // lax.axis_size("head"), -1)
     scaled = grouped * lax.rsqrt(jnp.mean(grouped * grouped, axis=2, keepdims=True) + epsilon)

time: 174 us -> 179 us (1.029)
  waiting for transfers between devices: 81.9 us -> 90 us
  matrix products: 24.8 us -> 20.5 us
  local copies, waits for them, and re-layouts: 17.2 us -> 19 us
    ppermute x6, waiting for transfers between devices: 3.29 us -> 12.6 us  [passed_along(): lax.ppermute(value, axis, [(source, source + steps) for source in range(f...]
    dot_general x10 -> x5, matrix products: 12.8 us -> 8.44 us  [the longest x1 3.25 us: block_parts(): jnp.einsum('dbhts,bshp->dbthp', weights, acts_b, preferred_element_type=j...]
    slice x5 -> x1, local copies, waits for them, and re-layouts: 2.29 us -> 0.14 us  [block_parts(): block_total = jnp.stack([cum_rate[0, :, -1], cum_rate[1, :, 0]])]
    reshape x0 -> x2, local copies, waits for them, and re-layouts: none -> 2.11 us  [the longest x1 1.44 us: block_parts(): steps_b = steps.reshape(2, count, STRETCH, heads)]
    add x6 -> x5, other arithmetic: 5.74 us -> 3.64 us  [relay(): entering = passed_along(gain[:, None, None] * entering + state, axis, steps)]
    unnamed x66 -> x56, local copies, waits for them, and re-layouts: 7.49 us -> 6.24 us
  transfers between devices with their start and end apart: 8 -> 8, of which waited for: 5 -> 6; matrix products, arithmetic and copies ran while one was open for 12% -> 7% of each run, Pallas kernels for 0% -> 0%
where the time goes in v9:
time: 179 us; the launch traced here: 178 us
  waiting for transfers between devices  90 us (50%)
  matrix products  20.5 us (11%)
  local copies, waits for them, and re-layouts  19 us (11%)
  starting transfers between devices  18.9 us (11%)
  other arithmetic  14.7 us (8%)
  between operations  14.5 us (8%)
    reduce_scatter x1, waiting for transfers between devices, per_device(): lax.psum_scatter(partial_value, 'head', scatter_dimension=0, tiled=True)  51.7 us
    all_gather x1, waiting for transfers between devices, per_device(): normed = lax.all_gather(normed, 'head', axis=0, tiled=True)  25.7 us
    ppermute x6, starting transfers between devices, passed_along(): lax.ppermute(value, axis, [(source, source + steps) for source in range(f...  18.8 us
    ppermute x6, waiting for transfers between devices, passed_along(): lax.ppermute(value, axis, [(source, source + steps) for source in range(f...  12.6 us
    unnamed x56, local copies, waits for them, and re-layouts  6.24 us
    dot_general x1, matrix products, per_device(): jnp.dot(normed, value_weight, preferred_element_type=jnp.float32)  4.99 us
    dot_general x1, matrix products, per_device(): jnp.dot(mixed, out_weight, preferred_element_type=jnp.float32)  4.78 us
    add x5, other arithmetic, relay(): entering = passed_along(gain[:, None, None] * entering + state, axis, steps)  3.64 us
  transfers between devices with their start and end apart: 8, of which 6 were waited for; matrix products, arithmetic and copies ran while one was open for 7% of the time, Pallas kernels for 0%

profile of v9, /device:TPU:0, one launch (start us, length us, event | category | flops | bytes accessed | tf_op | source)
XLA Modules:
  0.0 177.6 jit_solution(11238247663256087188)
XLA Ops:
  8.9 1.6 broadcast_multiply_fusion
  14.4 1.4 reshape.191
  15.8 2.2 %copy.28 = bf16[512,640]{0,1:T(8,128)(2,1)} copy(bf16[512,640]{1,0:T(8,128)(2,1)} %param.14) | data formatting | bytes 1310720 | tf_op args[0]
  18.0 2.7 %reshape_reshape.3 = bf16[2,256,10,64]{1,0,3,2:T(2,128)(2,1)} reshape(bf16[512,640]{0,1:T(8,128)(2,1)} %copy.28) | data formatting | bytes 1310720 | tf_op jit(solution)/shard_map/reshape;reshape | solution.py:25
  21.9 1.5 bitcast_exponential_fusion
  23.4 1.4 fusion.3
  26.1 5.7 %collective-permute-start = (f32[10,64,128]{2,1,0:T(8,128)}, f32[10,64,128]{2,1,0:T(8,128)}, u32[]{:S(2)}, u32[]{:S(2)}) collective-permute-start(f32[10,64,128]{2,1,0:T(8,128)} %get-tuple-element.6), channel_id=1, source_target_pairs={{0,4},{4,8},{8,12},{1,5},{5,9},{9,13},{2,6},{6,10},{10,14},{3,7},{... | collective-permute-start | bytes 983048 | tf_op jit(solution)/shard_map/ppermute | solution.py:19
  38.5 2.2 %copy.36 = bf16[512,640]{0,1:T(8,128)(2,1)} copy(bf16[512,640]{1,0:T(8,128)(2,1)} %param.15) | data formatting | bytes 1310720 | tf_op args[1]
  40.7 1.8 tile.4
  44.6 4.6 %collective-permute-start.1 = (f32[10,64,128]{2,1,0:T(8,128)S(1)}, f32[10,64,128]{2,1,0:T(8,128)S(1)}, u32[]{:S(2)}, u32[]{:S(2)}) collective-permute-start(f32[10,64,128]{2,1,0:T(8,128)S(1)} %multiply_add_fusion.3), channel_id=1, source_target_pairs={{0,4},{4,8},{8,12},{1,5},{5,9},{9,13},{2,6},{6,10},{10,14},{3,7},{... | collective-permute-start | bytes 983048 | tf_op jit(solution)/shard_map/ppermute | solution.py:19
  50.3 1.4 collective-permute-start.4
  51.8 3.8 %collective-permute-done.1 = f32[10,64,128]{2,1,0:T(8,128)S(1)} collective-permute-done((f32[10,64,128]{2,1,0:T(8,128)S(1)}, f32[10,64,128]{2,1,0:T(8,128)S(1)}, u32[]{:S(2)}, u32[]{:S(2)}) %collective-permute-start.1) | collective-permute-done | bytes 327712 | tf_op jit(solution)/shard_map/ppermute | solution.py:19
  55.6 4.4 %collective-permute-start.2 = (f32[10,64,128]{2,1,0:T(8,128)S(1)}, f32[10,64,128]{2,1,0:T(8,128)S(1)}, u32[]{:S(2)}, u32[]{:S(2)}) collective-permute-start(f32[10,64,128]{2,1,0:T(8,128)S(1)} %multiply_add_fusion.2), channel_id=1, source_target_pairs={{0,4},{4,8},{8,12},{1,5},{5,9},{9,13},{2,6},{6,10},{10,14},{3,7},{... | collective-permute-start | bytes 983048 | tf_op jit(solution)/shard_map/ppermute | solution.py:19
  61.0 1.5 collective-permute-start.5
  62.5 3.0 %collective-permute-done.2 = f32[10,64,128]{2,1,0:T(8,128)S(1)} collective-permute-done((f32[10,64,128]{2,1,0:T(8,128)S(1)}, f32[10,64,128]{2,1,0:T(8,128)S(1)}, u32[]{:S(2)}, u32[]{:S(2)}) %collective-permute-start.2) | collective-permute-done | bytes 327712 | tf_op jit(solution)/shard_map/ppermute | solution.py:19
  65.6 5.0 %collective-permute-done.5 = f32[10,64,128]{2,1,0:T(8,128)S(1)} collective-permute-done((f32[10,64,128]{2,1,0:T(8,128)S(1)}, f32[10,64,128]{2,1,0:T(8,128)S(1)}, u32[]{:S(2)}, u32[]{:S(2)}) %collective-permute-start.5) | collective-permute-done | bytes 327712 | tf_op jit(solution)/shard_map/ppermute | solution.py:19
  72.0 3.3 %fusion.2 = f32[2,2,256,10,64]{2,4,0,3,1:T(8,128)S(1)} fusion(f32[2,2,10,64,256]{4,3,0,2,1:T(8,128)S(1)} %fusion.9, f32[2,2,10,256]{3,0,2,1:T(2,128)S(1)} %copy.27, f32[2,2,10,256]{3,0,2,1:T(2,128)S(1)} %copy.25, f32[2,2,256,256]{3,2,0,1:T(8,128)S(1)} %copy-done.8, pred[2,256,256]{2,1,0:T(8,128)(4,1)S(1)} %pad_add_fusion, f32[2,2,256,10]{2,0,3,1:T(2,128)S(1)} %copy.30, ...), kind=kOutput, calls=%fused_computation.5 | convolution fusion | flops 349962240 | bytes 7200768 | tf_op jit(solution)/shard_map/dbhts,bshp->dbthp/dot_general | solution.py:49
  77.3 4.8 %select_add_fusion = f32[512,2560]{1,0:T(8,128)} fusion(f32[512,2560]{1,0:T(8,128)S(1)} %bitcast.100, bf16[640,2560]{1,0:T(8,128)(2,1)S(1)} %copy-done, pred[2560]{0:T(1024)(128)(4,1)S(1)} %fusion.27, f32[512,640]{0,1:T(8,128)S(1)} %get-tuple-element.5, f32[640]{0:T(1024)S(1)} %copy-done.16, f32[512]{0:T(512)S(1)} %add_rsqrt_fusion), kind=kOutput, calls=%fused_computation.1 | convolution fusion | flops 1681326080 | bytes 15080448 | tf_op jit(solution)/shard_map/dot_general | solution.py:140
  82.2 51.7 %reduce-scatter.2.cloned.1.call-done = f32[128,2560]{1,0:T(8,128)} async-done(((f32[512,2560]{1,0:T(8,128)}), f32[128,2560]{1,0:T(8,128)}) %reduce-scatter.2.cloned.1.call-update) | async-done | bytes 1310736 | tf_op jit(solution)/shard_map/reduce_scatter | solution.py:142
  133.9 1.5 multiply_reduce_fusion
  135.4 2.3 %multiply_convert_fusion.4 = bf16[128,2560]{1,0:T(8,128)(2,1)} fusion(f32[128,2560]{1,0:T(8,128)} %reduce-scatter.2.cloned.1.call-done, f32[2560]{0:T(1024)S(1)} %copy-done.17, f32[128]{0:T(128)S(1)} %add_rsqrt_fusion.1), kind=kLoop, calls=%fused_computation.18 | loop fusion | flops 983040 | bytes 1976832 | tf_op jit(solution)/shard_map/convert_element_type | solution.py:147
  137.8 25.7 %all-gather.2.cloned.1.call-done = bf16[512,2560]{1,0:T(8,128)(2,1)} async-done(((bf16[128,2560]{1,0:T(8,128)(2,1)}), bf16[512,2560]{1,0:T(8,128)(2,1)}) %all-gather.2.cloned.1.call-update) | async-done | bytes 2621456 | tf_op jit(solution)/shard_map/all_gather | solution.py:148
  163.5 5.0 %convolution_convert_fusion = bf16[512,512]{1,0:T(8,128)(2,1)} fusion(bf16[512,2560]{1,0:T(8,128)(2,1)} %all-gather.2.cloned.1.call-done, bf16[2560,512]{1,0:T(8,128)(2,1)} %param.27), kind=kOutput, calls=%fused_computation.24 | convolution fusion | flops 1342439424 | bytes 5767168 | tf_op jit(solution)/shard_map/dot_general | solution.py:150
  168.5 2.3 %convolution_convert_fusion.1 = bf16[512,512]{1,0:T(8,128)(2,1)} fusion(bf16[512,2560]{1,0:T(8,128)(2,1)S(1)} %copy-done.25, bf16[2560,512]{1,0:T(8,128)(2,1)S(1)} %copy-done.24), kind=kOutput, calls=%fused_computation.25 | convolution fusion | flops 1342439424 | bytes 5767168 | tf_op jit(solution)/shard_map/dot_general | solution.py:149
  (95 shorter events, 22.6 us)
Async XLA Ops:
  7.2 70.2 %copy-start = (bf16[640,2560]{1,0:T(8,128)(2,1)S(1)}, bf16[640,2560]{1,0:T(8,128)(2,1)}, u32[]{:S(2)}) copy-start(bf16[640,2560]{1,0:T(8,128)(2,1)} %param.23) | copy-start | bytes 9830404
  7.2 126.7 %reduce-scatter.2.cloned.1.call-start = ((), (), s32[]{:S(2)}) async-start(), calls=%async_computation.1 | async-start | bytes 6553600 | tf_op jit(solution)/shard_map/reduce_scatter | solution.py:142
  11.1 12.3 %copy-start.9 = (bf16[2,512,128]{2,1,0:T(8,128)(2,1)S(1)}, bf16[2,512,128]{2,1,0:T(8,128)(2,1)}, u32[]{:S(2)}) copy-start(bf16[2,512,128]{2,1,0:T(8,128)(2,1)} %param.16) | copy-start | bytes 786436
  20.7 4.2 %copy-start.22 = (f32[10]{0:T(128)S(1)}, f32[10]{0:T(128)}, u32[]{:S(2)}) copy-start(f32[10]{0:T(128)} %get-tuple-element.24) | copy-start | bytes 124
  20.7 4.2 %copy-start.23 = (f32[10]{0:T(128)S(1)}, f32[10]{0:T(128)}, u32[]{:S(2)}) copy-start(f32[10]{0:T(128)} %get-tuple-element.25) | copy-start | bytes 124
  23.4 9.7 %copy-start.10 = (bf16[2,512,128]{2,1,0:T(8,128)(2,1)S(1)}, bf16[2,512,128]{2,1,0:T(8,128)(2,1)}, u32[]{:S(2)}) copy-start(bf16[2,512,128]{2,1,0:T(8,128)(2,1)} %param.17) | copy-start | bytes 786436
  24.9 10.4 %copy-start.13 = (f32[2,2,10,256]{3,2,1,0:T(8,128)S(1)}, f32[2,2,10,256]{3,2,1,0:T(8,128)}, u32[]{:S(2)}) copy-start(f32[2,2,10,256]{3,2,1,0:T(8,128)} %copy-done.12) | copy-start | bytes 122884
  24.9 12.8 %copy-start.19 = (f32[1,10]{1,0:T(1,128)S(1)}, f32[1,10]{1,0:T(1,128)}, u32[]{:S(2)}) copy-start(f32[1,10]{1,0:T(1,128)} %get-tuple-element.23) | copy-start | bytes 124
  26.1 16.8 %collective-permute-start = (f32[10,64,128]{2,1,0:T(8,128)}, f32[10,64,128]{2,1,0:T(8,128)}, u32[]{:S(2)}, u32[]{:S(2)}) collective-permute-start(f32[10,64,128]{2,1,0:T(8,128)} %get-tuple-element.6), channel_id=1, source_target_pairs={{0,4},{4,8},{8,12},{1,5},{5,9},{9,13},{2,6},{6,10},{10,14},{3,7},{... | collective-permute-start | bytes 983048 | tf_op jit(solution)/shard_map/ppermute | solution.py:19
  31.8 17.4 %collective-permute-start.3 = (f32[10,64,128]{2,1,0:T(8,128)}, f32[10,64,128]{2,1,0:T(8,128)}, u32[]{:S(2)}, u32[]{:S(2)}) collective-permute-start(f32[10,64,128]{2,1,0:T(8,128)} %get-tuple-element.16), channel_id=1, source_target_pairs={{4,0},{8,4},{12,8},{5,1},{9,5},{13,9},{6,2},{10,6},{14,10},{7,3},{... | collective-permute-start | bytes 983048 | tf_op jit(solution)/shard_map/ppermute | solution.py:19
  42.5 6.7 %copy-start.2 = (f32[10,64,128]{2,1,0:T(8,128)S(1)}, f32[10,64,128]{2,1,0:T(8,128)}, u32[]{:S(2)}) copy-start(f32[10,64,128]{2,1,0:T(8,128)} %get-tuple-element.17) | copy-start | bytes 983044
  42.5 9.2 %copy-start.14 = (pred[1,256,256]{2,1,0:T(32,128)(4,1)S(1)}, pred[1,256,256]{2,1,0:T(32,128)(4,1)}, u32[]{:S(2)}) copy-start(pred[1,256,256]{2,1,0:T(32,128)(4,1)} %get-tuple-element.32) | copy-start | bytes 196612
  42.5 9.2 %copy-start.15 = (pred[1,256,256]{2,1,0:T(32,128)(4,1)S(1)}, pred[1,256,256]{2,1,0:T(32,128)(4,1)}, u32[]{:S(2)}) copy-start(pred[1,256,256]{2,1,0:T(32,128)(4,1)} %get-tuple-element.33) | copy-start | bytes 196612
  42.9 22.6 %copy-start.7 = (f32[1,10,64,128]{3,2,1,0:T(8,128)S(1)}, f32[1,10,64,128]{3,2,1,0:T(8,128)}, u32[]{:S(2)}) copy-start(f32[1,10,64,128]{3,2,1,0:T(8,128)} %get-tuple-element.18) | copy-start | bytes 983044
  43.5 27.1 %copy-start.6 = (f32[1,10,64,128]{3,2,1,0:T(8,128)S(1)}, f32[1,10,64,128]{3,2,1,0:T(8,128)}, u32[]{:S(2)}) copy-start(f32[1,10,64,128]{3,2,1,0:T(8,128)} %get-tuple-element.19) | copy-start | bytes 983044
  44.6 10.9 %collective-permute-start.1 = (f32[10,64,128]{2,1,0:T(8,128)S(1)}, f32[10,64,128]{2,1,0:T(8,128)S(1)}, u32[]{:S(2)}, u32[]{:S(2)}) collective-permute-start(f32[10,64,128]{2,1,0:T(8,128)S(1)} %multiply_add_fusion.3), channel_id=1, source_target_pairs={{0,4},{4,8},{8,12},{1,5},{5,9},{9,13},{2,6},{6,10},{10,14},{3,7},{... | collective-permute-start | bytes 983048 | tf_op jit(solution)/shard_map/ppermute | solution.py:19
  50.3 20.5 %copy-start.11 = (bf16[2,512,128]{2,1,0:T(8,128)(2,1)S(1)}, bf16[2,512,128]{2,1,0:T(8,128)(2,1)}, u32[]{:S(2)}) copy-start(bf16[2,512,128]{2,1,0:T(8,128)(2,1)} %param.17) | copy-start | bytes 786436
  50.3 10.6 %collective-permute-start.4 = (f32[10,64,128]{2,1,0:T(8,128)S(1)}, f32[10,64,128]{2,1,0:T(8,128)S(1)}, u32[]{:S(2)}, u32[]{:S(2)}) collective-permute-start(f32[10,64,128]{2,1,0:T(8,128)S(1)} %multiply_add_fusion.1), channel_id=1, source_target_pairs={{4,0},{8,4},{12,8},{5,1},{9,5},{13,9},{6,2},{10,6},{14,10},{7,3},{... | collective-permute-start | bytes 983048 | tf_op jit(solution)/shard_map/ppermute | solution.py:19
  55.6 9.9 %collective-permute-start.2 = (f32[10,64,128]{2,1,0:T(8,128)S(1)}, f32[10,64,128]{2,1,0:T(8,128)S(1)}, u32[]{:S(2)}, u32[]{:S(2)}) collective-permute-start(f32[10,64,128]{2,1,0:T(8,128)S(1)} %multiply_add_fusion.2), channel_id=1, source_target_pairs={{0,4},{4,8},{8,12},{1,5},{5,9},{9,13},{2,6},{6,10},{10,14},{3,7},{... | collective-permute-start | bytes 983048 | tf_op jit(solution)/shard_map/ppermute | solution.py:19
  61.0 9.6 %collective-permute-start.5 = (f32[10,64,128]{2,1,0:T(8,128)S(1)}, f32[10,64,128]{2,1,0:T(8,128)S(1)}, u32[]{:S(2)}, u32[]{:S(2)}) collective-permute-start(f32[10,64,128]{2,1,0:T(8,128)S(1)} %multiply_add_fusion), channel_id=1, source_target_pairs={{4,0},{8,4},{12,8},{5,1},{9,5},{13,9},{6,2},{10,6},{14,10},{7,3},{... | collective-permute-start | bytes 983048 | tf_op jit(solution)/shard_map/ppermute | solution.py:19
  82.1 53.3 %copy-start.17 = (f32[2560]{0:T(1024)S(1)}, f32[2560]{0:T(1024)}, u32[]{:S(2)}) copy-start(f32[2560]{0:T(1024)} %param.25) | copy-start | bytes 30724
  82.2 81.3 %all-gather.2.cloned.1.call-start = ((), (), s32[]{:S(2)}) async-start(), calls=%async_computation.2 | async-start | bytes 3276800 | tf_op jit(solution)/shard_map/all_gather | solution.py:148
  163.5 5.0 %copy-start.24 = (bf16[2560,512]{1,0:T(8,128)(2,1)S(1)}, bf16[2560,512]{1,0:T(8,128)(2,1)}, u32[]{:S(2)}) copy-start(bf16[2560,512]{1,0:T(8,128)(2,1)} %param.26) | copy-start | bytes 7864324
  163.5 5.0 %copy-start.25 = (bf16[512,2560]{1,0:T(8,128)(2,1)S(1)}, bf16[512,2560]{1,0:T(8,128)(2,1)}, u32[]{:S(2)}) copy-start(bf16[512,2560]{1,0:T(8,128)(2,1)} %all-gather.2.cloned.1.call-done) | copy-start | bytes 7864324
  (10 other events, 20.1 us)
Sparse Core Ops, SparseCore 0:
  82.3 51.5 reduce-scatter.1
  137.9 25.5 all-gather.1

commit v10 on v9

--- a/solution.py
+++ b/solution.py
@@ -19,22 +19,37 @@
     return lax.ppermute(value, axis, [(source, source + steps) for source in range(first, last)])
 
 
-def block_parts(acts, writes, reads, steps, rates):
+def block_ends(acts, writes, steps, rates):
+    tokens, heads, width = acts.shape
+    count = tokens // STRETCH
+    writes_b = writes.reshape(2, count, STRETCH, -1)
+    steps_b = steps.reshape(2, count, STRETCH, heads)
+    rates_b = rates.reshape(2, count, STRETCH, heads)
+    position = jnp.arange(STRETCH)
+    causal = jnp.stack(
+        [position[:, None] >= position[None, :], position[:, None] <= position[None, :]]
+    )
+    cum_rate = jnp.einsum(
+        "dts,dbsh->dbth", causal.astype(jnp.float32), rates_b, precision=highest
+    )
+    block_total = jnp.stack([cum_rate[0, :, -1], cum_rate[1, :, 0]])
+    tail = jnp.exp(block_total[:, :, None, :] - cum_rate) * steps_b
+    acts_b = acts.reshape(count, STRETCH, heads, width).astype(jnp.float32)
+    weighted = (acts_b[None] * tail[..., None]).reshape(2, count, STRETCH, heads * width)
+    ends = jnp.einsum(
+        "dbsn,dbsc->dbnc", writes_b.astype(jnp.float32), weighted, precision=highest
+    )
+    spread = jnp.repeat(jnp.exp(block_total), width, axis=2)
+    return causal, cum_rate, ends, spread
+
+
+def block_within(causal, cum_rate, acts, writes, reads, steps):
     tokens, heads, width = acts.shape
     count = tokens // STRETCH
     acts_b = acts.reshape(count, STRETCH, heads, width)
     writes_b = writes.reshape(2, count, STRETCH, -1)
     reads_b = reads.reshape(2, count, STRETCH, -1)
     steps_b = steps.reshape(2, count, STRETCH, heads)
-    rates_b = rates.reshape(2, count, STRETCH, heads)
-    position = jnp.arange(STRETCH)
-    causal = jnp.stack(
-        [position[:, None] >= position[None, :], position[:, None] <= position[None, :]]
-    )
-    cum_rate = jnp.einsum(
-        "dts,dbsh->dbth", causal.astype(jnp.float32), rates_b, precision=highest
-    )
-    block_total = jnp.stack([cum_rate[0, :, -1], cum_rate[1, :, 0]])
     along = jnp.transpose(cum_rate, (0, 1, 3, 2))
     spans = along[..., :, None] - along[..., None, :]
     decays = jnp.exp(jnp.where(causal[:, None, None], spans, -1e30))
@@ -46,15 +61,7 @@
         * decays
         * jnp.transpose(steps_b, (0, 1, 3, 2))[:, :, :, None, :]
     ).astype(jnp.bfloat16)
-    within = jnp.einsum(
-        "dbhts,bshp->dbthp", weights, acts_b, preferred_element_type=jnp.float32
-    )
-    tail = jnp.exp(block_total[:, :, None, :] - cum_rate) * steps_b
-    weighted = acts_b.astype(jnp.float32)[None] * tail[..., None]
-    ends = jnp.einsum(
-        "dbshp,dbsn->dbhpn", weighted, writes_b.astype(jnp.float32), precision=highest
-    )
-    return within, cum_rate, ends, jnp.exp(block_total)
+    return jnp.einsum("dbhts,bshp->dbthp", weights, acts_b, preferred_element_type=jnp.float32)
 
 
 def chain_blocks(ends, decays, reverse):
@@ -67,39 +74,66 @@
     for index in order:
         starts[index] = state
         gains[index] = gain
-        state = decays[index][:, None, None] * state + ends[index]
+        state = decays[index][None, :] * state + ends[index]
         gain = gain * decays[index]
     return jnp.stack(starts), jnp.stack(gains), state, gain
 
 
-def relay(state, gain, axis, steps):
+def relay_pair(states, gains, axis, first_round):
     count = lax.axis_size(axis)
+    directions = (1, -1)
     if count <= 4:
-        entering = jnp.zeros_like(state)
-        for _ in range(count - 1):
-            entering = passed_along(gain[:, None, None] * entering + state, axis, steps)
+        entering = [jnp.zeros_like(state) for state in states]
+        for turn in range(count - 1):
+            entering = [
+                passed_along(gain[None, :] * enter + state, axis, steps)
+                for enter, state, gain, steps in zip(entering, states, gains, directions)
+            ]
+            if turn == 0:
+                entering = first_round(entering)
+        if count == 1:
+            entering = first_round(entering)
         return entering
-    distance = 1
-    while distance < count:
-        got_state = passed_along(state, axis, distance * steps)
-        got_gain = passed_along(gain, axis, distance * steps)
-        state = gain[:, None, None] * got_state + state
-        gain = gain * got_gain
-        distance *= 2
-    return passed_along(state, axis, steps)
+    result = []
+    for state, gain, steps in zip(states, gains, directions):
+        distance = 1
+        while distance < count:
+            got_state = passed_along(state, axis, distance * steps)
+            got_gain = passed_along(gain, axis, distance * steps)
+            state = gain[None, :] * got_state + state
+            gain = gain * got_gain
+            distance *= 2
+        result.append(passed_along(state, axis, steps))
+    return first_round(result)
 
 
 def both_directions(acts, writes, reads, steps, rates, axis):
-    within, cum_rate, ends, decays = block_parts(acts, writes, reads, steps, rates)
-    block_states = []
+    causal, cum_rate, ends, decays = block_ends(acts, writes, steps, rates)
+    starts, gains, own_ends, own_gains = [], [], [], []
     for direction, reverse in ((0, False), (1, True)):
-        starts, gains, own_end, own_gain = chain_blocks(ends[direction], decays[direction], reverse)
-        entering = relay(own_end, own_gain, axis, -1 if reverse else 1)
-        block_states.append(starts + gains[:, :, None, None] * entering[None])
-    block_states = jnp.stack(block_states)
+        start, gain, own_end, own_gain = chain_blocks(ends[direction], decays[direction], reverse)
+        starts.append(start)
+        gains.append(gain)
+        own_ends.append(own_end)
+        own_gains.append(own_gain)
+    held = {}
+
+    def first_round(entering):
+        entering, held["inputs"] = lax.optimization_barrier(
+            (entering, (causal, cum_rate, acts, writes, reads, steps))
+        )
+        return entering
+
+    entering = relay_pair(own_ends, own_gains, axis, first_round)
+    within = block_within(*held["inputs"])
+    block_states = jnp.stack(
+        [start + gain[:, None, :] * enter[None] for start, gain, enter in zip(starts, gains, entering)]
+    )
     count = within.shape[1]
+    heads, width = acts.shape[1], acts.shape[2]
     reads_b = reads.reshape(2, count, STRETCH, -1).astype(jnp.float32)
-    carried = jnp.einsum("dbtn,dbhpn->dbthp", reads_b, block_states, precision=highest)
+    carried = jnp.einsum("dbtn,dbnc->dbtc", reads_b, block_states, precision=highest)
+    carried = carried.reshape(2, count, STRETCH, heads, width)
     outputs = within + jnp.exp(cum_rate)[..., None] * carried
     return outputs.reshape((2,) + acts.shape)
 

time: 179 us -> 184 us (1.028)
  waiting for transfers between devices: 90 us -> 81.2 us
  local copies, waits for them, and re-layouts: 19 us -> 27.5 us
  other arithmetic: 14.7 us -> 20.6 us
    ppermute x6, waiting for transfers between devices: 12.6 us -> 4.16 us  [passed_along(): lax.ppermute(value, axis, [(source, source + steps) for source in range(f...]
    broadcast_in_dim x0 -> x10, local copies, waits for them, and re-layouts: none -> 4.21 us  [block_ends(): spread = jnp.repeat(jnp.exp(block_total), width, axis=2)]
    another operation x3, other arithmetic: 0.28 us -> 3.43 us  [the longest x2 2.73 us: both_directions(): jnp.stack([start + gain[:, None, :] * enter[None] for start, gain, enter...]
    unnamed x56 -> x88, local copies, waits for them, and re-layouts: 6.24 us -> 9.18 us
    reshape x2 -> x4, local copies, waits for them, and re-layouts: 2.11 us -> 4.87 us  [the longest x1 2.71 us: block_within(): acts_b = acts.reshape(count, STRETCH, heads, width)]
    another operation x1 -> x0, local copies, waits for them, and re-layouts: 2.68 us -> none  [block_parts(): acts_b = acts.reshape(count, STRETCH, heads, width)]
    add x6, other arithmetic: 4.58 us -> 6.77 us  [the longest x5 5.7 us: relay_pair(): gain[None, :] * enter + state]
  transfers between devices with their start and end apart: 8 -> 8, of which waited for: 6 -> 4; matrix products, arithmetic and copies ran while one was open for 7% -> 14% of each run, Pallas kernels for 0% -> 0%
where the time goes in v10:
time: 184 us; the launch traced here: 183 us
  waiting for transfers between devices  81.2 us (44%)
  local copies, waits for them, and re-layouts  27.5 us (15%)
  other arithmetic  20.6 us (11%)
  starting transfers between devices  20 us (11%)
  matrix products  19.4 us (11%)
  between operations  14.7 us (8%)
    reduce_scatter x1, waiting for transfers between devices, per_device(): lax.psum_scatter(partial_value, 'head', scatter_dimension=0, tiled=True)  51.3 us
    all_gather x1, waiting for transfers between devices, per_device(): normed = lax.all_gather(normed, 'head', axis=0, tiled=True)  25.7 us
    ppermute x6, starting transfers between devices, passed_along(): lax.ppermute(value, axis, [(source, source + steps) for source in range(f...  19.9 us
    unnamed x88, local copies, waits for them, and re-layouts  9.18 us
    add x5, other arithmetic, relay_pair(): gain[None, :] * enter + state  5.7 us
    dot_general x1, matrix products, per_device(): jnp.dot(normed, value_weight, preferred_element_type=jnp.float32)  4.99 us
    dot_general x1, matrix products, per_device(): jnp.dot(mixed, out_weight, preferred_element_type=jnp.float32)  4.68 us
    broadcast_in_dim x10, local copies, waits for them, and re-layouts, block_ends(): spread = jnp.repeat(jnp.exp(block_total), width, axis=2)  4.21 us
  transfers between devices with their start and end apart: 8, of which 4 were waited for; matrix products, arithmetic and copies ran while one was open for 14% of the time, Pallas kernels for 0%

profile of v10, /device:TPU:0, one launch (start us, length us, event | category | flops | bytes accessed | tf_op | source)
XLA Modules:
  0.0 183.4 jit_solution(10482065679952670770)
XLA Ops:
  14.5 2.2 %copy.23 = bf16[512,640]{0,1:T(8,128)(2,1)} copy(bf16[512,640]{1,0:T(8,128)(2,1)} %param.14) | data formatting | bytes 1310720 | tf_op args[0]
  20.3 1.4 convolution_bitcast_fusion
  22.8 1.6 broadcast_add_fusion.1
  24.4 5.7 %collective-permute-start = (f32[128,640]{0,1:T(8,128)}, f32[128,640]{0,1:T(8,128)}, u32[]{:S(2)}, u32[]{:S(2)}) collective-permute-start(f32[128,640]{0,1:T(8,128)} %get-tuple-element.26), channel_id=1, source_target_pairs={{0,4},{4,8},{8,12},{1,5},{5,9},{9,13},{2,6},{6,10},{10,14},{3,7},{... | collective-permute-start | bytes 983048 | tf_op jit(solution)/shard_map/ppermute | solution.py:19
  35.4 1.5 copy.31
  36.8 2.2 %copy.34 = bf16[512,640]{0,1:T(8,128)(2,1)} copy(bf16[512,640]{1,0:T(8,128)(2,1)} %param.15) | data formatting | bytes 1310720 | tf_op args[1]
  39.1 1.8 tile.4
  40.9 2.7 %copy.43 = f32[64,8,4,640]{3,1,2,0:T(8,128)} copy(f32[64,8,4,640]{3,2,1,0:T(4,128)S(1)} %bitcast.93) | data formatting | bytes 10485760
  49.0 5.2 %collective-permute-start.2 = (f32[128,640]{0,1:T(8,128)S(1)}, f32[128,640]{0,1:T(8,128)S(1)}, u32[]{:S(2)}, u32[]{:S(2)}) collective-permute-start(f32[128,640]{0,1:T(8,128)S(1)} %multiply_add_fusion.3), channel_id=1, source_target_pairs={{0,4},{4,8},{8,12},{1,5},{5,9},{9,13},{2,6},{6,10},{10,14},{3,7},{... | collective-permute-start | bytes 983048 | tf_op jit(solution)/shard_map/ppermute | solution.py:19
  54.2 4.0 %collective-permute-done.4 = f32[128,640]{0,1:T(8,128)S(1)} collective-permute-done((f32[128,640]{0,1:T(8,128)S(1)}, f32[128,640]{0,1:T(8,128)S(1)}, u32[]{:S(2)}, u32[]{:S(2)}) %collective-permute-start.4) | collective-permute-done | bytes 327712 | tf_op jit(solution)/shard_map/ppermute | solution.py:19
  61.5 5.1 %collective-permute-start.3 = (f32[128,640]{0,1:T(8,128)}, f32[128,640]{0,1:T(8,128)}, u32[]{:S(2)}, u32[]{:S(2)}) collective-permute-start(f32[128,640]{0,1:T(8,128)} %multiply_add_fusion.2), channel_id=1, source_target_pairs={{0,4},{4,8},{8,12},{1,5},{5,9},{9,13},{2,6},{6,10},{10,14},{3,7},{... | collective-permute-start | bytes 983048 | tf_op jit(solution)/shard_map/ppermute | solution.py:19
  68.6 1.4 reshape.316
  70.0 1.4 copy.29
  71.4 2.7 %reshape.313 = bf16[2,256,10,64]{1,0,3,2:T(2,128)(2,1)} reshape(bf16[512,10,64]{0,2,1:T(8,128)(2,1)} %bitcast.97) | data formatting | bytes 1310720 | tf_op jit(solution)/shard_map/reshape | solution.py:49
  74.1 1.3 add_bitcast_fusion
  75.5 1.4 add_bitcast_fusion.1
  78.2 3.2 %bitcast_add_fusion = f32[2,2,256,10,64]{2,4,0,3,1:T(8,128)S(1)} fusion(f32[2,2,256,10,64]{2,4,3,1,0:T(8,128)S(1)} %bitcast.102, f32[2,2,10,256]{3,0,2,1:T(2,128)S(1)} %copy-done.24, f32[2,2,10,256]{3,0,2,1:T(2,128)S(1)} %copy-done.23, f32[2,2,256,256]{3,2,0,1:T(8,128)S(1)} %copy-done.7, pred[2,256,256]{2,1,0:T(8,128)(4,1)S(1)} %copy-done.21, ...), kind=kOutput, calls=%fused_computation.4 | convolution fusion | flops 349962240 | bytes 7200768 | tf_op jit(solution)/shard_map/dbhts,bshp->dbthp/dot_general | solution.py:64
  83.6 4.7 %select_add_fusion = f32[512,2560]{1,0:T(8,128)} fusion(f32[512,2560]{1,0:T(8,128)S(1)} %bitcast.96, bf16[640,2560]{1,0:T(8,128)(2,1)S(1)} %copy-done, pred[2560]{0:T(1024)(128)(4,1)S(1)} %fusion.22, f32[512,640]{0,1:T(8,128)S(1)} %get-tuple-element.21, f32[640]{0:T(1024)S(1)} %copy-done.33, f32[512]{0:T(512)S(1)} %add_rsqrt_fusion), kind=kOutput, calls=%fused_computation.1 | convolution fusion | flops 1681326080 | bytes 15080448 | tf_op jit(solution)/shard_map/dot_general | solution.py:174
  88.4 51.3 %reduce-scatter.2.cloned.1.call-done = f32[128,2560]{1,0:T(8,128)} async-done(((f32[512,2560]{1,0:T(8,128)}), f32[128,2560]{1,0:T(8,128)}) %reduce-scatter.2.cloned.1.call-update) | async-done | bytes 1310736 | tf_op jit(solution)/shard_map/reduce_scatter | solution.py:176
  139.7 1.5 multiply_reduce_fusion
  141.2 2.3 %multiply_convert_fusion.4 = bf16[128,2560]{1,0:T(8,128)(2,1)} fusion(f32[128,2560]{1,0:T(8,128)} %reduce-scatter.2.cloned.1.call-done, f32[2560]{0:T(1024)S(1)} %copy-done.36, f32[128]{0:T(128)S(1)} %add_rsqrt_fusion.1), kind=kLoop, calls=%fused_computation.20 | loop fusion | flops 983040 | bytes 1976832 | tf_op jit(solution)/shard_map/convert_element_type | solution.py:181
  143.6 25.7 %all-gather.2.cloned.1.call-done = bf16[512,2560]{1,0:T(8,128)(2,1)} async-done(((bf16[128,2560]{1,0:T(8,128)(2,1)}), bf16[512,2560]{1,0:T(8,128)(2,1)}) %all-gather.2.cloned.1.call-update) | async-done | bytes 2621456 | tf_op jit(solution)/shard_map/all_gather | solution.py:182
  169.3 5.0 %convolution_convert_fusion = bf16[512,512]{1,0:T(8,128)(2,1)} fusion(bf16[512,2560]{1,0:T(8,128)(2,1)} %all-gather.2.cloned.1.call-done, bf16[2560,512]{1,0:T(8,128)(2,1)} %param.27), kind=kOutput, calls=%fused_computation.24 | convolution fusion | flops 1342439424 | bytes 5767168 | tf_op jit(solution)/shard_map/dot_general | solution.py:184
  174.3 2.3 %convolution_convert_fusion.1 = bf16[512,512]{1,0:T(8,128)(2,1)} fusion(bf16[512,2560]{1,0:T(8,128)(2,1)S(1)} %copy-done.39, bf16[2560,512]{1,0:T(8,128)(2,1)S(1)} %copy-done.38), kind=kOutput, calls=%fused_computation.25 | convolution fusion | flops 1342439424 | bytes 5767168 | tf_op jit(solution)/shard_map/dot_general | solution.py:183
  (142 shorter events, 31.0 us)
Async XLA Ops:
  7.2 76.4 %copy-start = (bf16[640,2560]{1,0:T(8,128)(2,1)S(1)}, bf16[640,2560]{1,0:T(8,128)(2,1)}, u32[]{:S(2)}) copy-start(bf16[640,2560]{1,0:T(8,128)(2,1)} %param.23) | copy-start | bytes 9830404
  7.2 132.5 %reduce-scatter.2.cloned.1.call-start = ((), (), s32[]{:S(2)}) async-start(), calls=%async_computation.1 | async-start | bytes 6553600 | tf_op jit(solution)/shard_map/reduce_scatter | solution.py:176
  7.3 10.8 %copy-start.16 = (pred[1,256,256]{2,1,0:T(32,128)(4,1)}, pred[1,256,256]{2,1,0:T(32,128)(4,1)S(1)}, u32[]{:S(2)}) copy-start(pred[1,256,256]{2,1,0:T(32,128)(4,1)S(1)} %get-tuple-element.46) | copy-start | bytes 196612
  7.3 10.8 %copy-start.18 = (pred[1,256,256]{2,1,0:T(32,128)(4,1)}, pred[1,256,256]{2,1,0:T(32,128)(4,1)S(1)}, u32[]{:S(2)}) copy-start(pred[1,256,256]{2,1,0:T(32,128)(4,1)S(1)} %get-tuple-element.47) | copy-start | bytes 196612
  9.2 8.9 %copy-start.15 = (f32[2,512,10]{1,0,2:T(2,128)}, f32[2,512,10]{1,0,2:T(2,128)S(1)}, u32[]{:S(2)}) copy-start(f32[2,512,10]{1,0,2:T(2,128)S(1)} %get-tuple-element.15) | copy-start | bytes 122884
  24.4 21.0 %collective-permute-start = (f32[128,640]{0,1:T(8,128)}, f32[128,640]{0,1:T(8,128)}, u32[]{:S(2)}, u32[]{:S(2)}) collective-permute-start(f32[128,640]{0,1:T(8,128)} %get-tuple-element.26), channel_id=1, source_target_pairs={{0,4},{4,8},{8,12},{1,5},{5,9},{9,13},{2,6},{6,10},{10,14},{3,7},{... | collective-permute-start | bytes 983048 | tf_op jit(solution)/shard_map/ppermute | solution.py:19
  30.1 15.3 %collective-permute-start.1 = (f32[128,640]{0,1:T(8,128)}, f32[128,640]{0,1:T(8,128)}, u32[]{:S(2)}, u32[]{:S(2)}) collective-permute-start(f32[128,640]{0,1:T(8,128)} %get-tuple-element.34), channel_id=1, source_target_pairs={{4,0},{8,4},{12,8},{5,1},{9,5},{13,9},{6,2},{10,6},{14,10},{7,3},{... | collective-permute-start | bytes 983048 | tf_op jit(solution)/shard_map/ppermute | solution.py:19
  40.9 4.5 %copy-start.5 = (f32[128,640]{0,1:T(8,128)S(1)}, f32[128,640]{0,1:T(8,128)}, u32[]{:S(2)}) copy-start(f32[128,640]{0,1:T(8,128)} %get-tuple-element.35) | copy-start | bytes 983044
  40.9 4.5 %copy-start.26 = (f32[640]{0:T(1024)S(1)}, f32[640]{0:T(1024)}, u32[]{:S(2)}) copy-start(f32[640]{0:T(1024)} %get-tuple-element.25) | copy-start | bytes 7684
  40.9 7.0 %copy-start.25 = (f32[640]{0:T(1024)S(1)}, f32[640]{0:T(1024)}, u32[]{:S(2)}) copy-start(f32[640]{0:T(1024)} %get-tuple-element.29) | copy-start | bytes 7684
  43.6 4.3 %copy-start.4 = (f32[128,640]{0,1:T(8,128)S(1)}, f32[128,640]{0,1:T(8,128)}, u32[]{:S(2)}) copy-start(f32[128,640]{0,1:T(8,128)} %get-tuple-element.27) | copy-start | bytes 983044
  44.3 22.3 %copy-start.9 = (bf16[2,512,128]{2,1,0:T(8,128)(2,1)S(1)}, bf16[2,512,128]{2,1,0:T(8,128)(2,1)}, u32[]{:S(2)}) copy-start(bf16[2,512,128]{2,1,0:T(8,128)(2,1)} %param.17) | copy-start | bytes 786436
  45.4 22.5 %copy-start.14 = (f32[2,2,256,10]{2,3,1,0:T(8,128)S(1)}, f32[2,2,256,10]{2,3,1,0:T(8,128)}, u32[]{:S(2)}) copy-start(f32[2,2,256,10]{2,3,1,0:T(8,128)} %copy-done.12) | copy-start | bytes 122884
  46.6 11.7 %collective-permute-start.4 = (f32[128,640]{0,1:T(8,128)S(1)}, f32[128,640]{0,1:T(8,128)S(1)}, u32[]{:S(2)}, u32[]{:S(2)}) collective-permute-start(f32[128,640]{0,1:T(8,128)S(1)} %multiply_add_fusion.1), channel_id=1, source_target_pairs={{4,0},{8,4},{12,8},{5,1},{9,5},{13,9},{6,2},{10,6},{14,10},{7,3},{... | collective-permute-start | bytes 983048 | tf_op jit(solution)/shard_map/ppermute | solution.py:19
  49.0 11.6 %collective-permute-start.2 = (f32[128,640]{0,1:T(8,128)S(1)}, f32[128,640]{0,1:T(8,128)S(1)}, u32[]{:S(2)}, u32[]{:S(2)}) collective-permute-start(f32[128,640]{0,1:T(8,128)S(1)} %multiply_add_fusion.3), channel_id=1, source_target_pairs={{0,4},{4,8},{8,12},{1,5},{5,9},{9,13},{2,6},{6,10},{10,14},{3,7},{... | collective-permute-start | bytes 983048 | tf_op jit(solution)/shard_map/ppermute | solution.py:19
  59.2 15.0 %collective-permute-start.5 = (f32[128,640]{0,1:T(8,128)}, f32[128,640]{0,1:T(8,128)}, u32[]{:S(2)}, u32[]{:S(2)}) collective-permute-start(f32[128,640]{0,1:T(8,128)} %multiply_add_fusion), channel_id=1, source_target_pairs={{4,0},{8,4},{12,8},{5,1},{9,5},{13,9},{6,2},{10,6},{14,10},{7,3},{... | collective-permute-start | bytes 983048 | tf_op jit(solution)/shard_map/ppermute | solution.py:19
  61.5 14.0 %collective-permute-start.3 = (f32[128,640]{0,1:T(8,128)}, f32[128,640]{0,1:T(8,128)}, u32[]{:S(2)}, u32[]{:S(2)}) collective-permute-start(f32[128,640]{0,1:T(8,128)} %multiply_add_fusion.2), channel_id=1, source_target_pairs={{0,4},{4,8},{8,12},{1,5},{5,9},{9,13},{2,6},{6,10},{10,14},{3,7},{... | collective-permute-start | bytes 983048 | tf_op jit(solution)/shard_map/ppermute | solution.py:19
  67.9 9.0 %copy-start.10 = (bf16[2,512,128]{2,1,0:T(8,128)(2,1)S(1)}, bf16[2,512,128]{2,1,0:T(8,128)(2,1)}, u32[]{:S(2)}) copy-start(bf16[2,512,128]{2,1,0:T(8,128)(2,1)} %param.17) | copy-start | bytes 786436
  78.2 5.4 %slice-start = ((s8[5242880]{0:T(1024)(128)(4,1)}), s8[4194304]{0:T(1024)(128)(4,1)S(1)}, s32[]{:S(2)}) async-start(s8[5242880]{0:T(1024)(128)(4,1)} %bitcast.94), calls=%async_computation.3 | async-start | bytes 8388608
  78.2 5.4 %slice-start.1 = ((s8[5242880]{0:T(1024)(128)(4,1)}), s8[1048576]{0:T(1024)(128)(4,1)S(1)}, s32[]{:S(2)}) async-start(s8[5242880]{0:T(1024)(128)(4,1)} %bitcast.94), calls=%async_computation.4 | async-start | bytes 2097152
  88.3 52.9 %copy-start.36 = (f32[2560]{0:T(1024)S(1)}, f32[2560]{0:T(1024)}, u32[]{:S(2)}) copy-start(f32[2560]{0:T(1024)} %param.25) | copy-start | bytes 30724
  88.3 81.0 %all-gather.2.cloned.1.call-start = ((), (), s32[]{:S(2)}) async-start(), calls=%async_computation.2 | async-start | bytes 3276800 | tf_op jit(solution)/shard_map/all_gather | solution.py:182
  169.3 5.0 %copy-start.38 = (bf16[2560,512]{1,0:T(8,128)(2,1)S(1)}, bf16[2560,512]{1,0:T(8,128)(2,1)}, u32[]{:S(2)}) copy-start(bf16[2560,512]{1,0:T(8,128)(2,1)} %param.26) | copy-start | bytes 7864324
  169.3 5.0 %copy-start.39 = (bf16[512,2560]{1,0:T(8,128)(2,1)S(1)}, bf16[512,2560]{1,0:T(8,128)(2,1)}, u32[]{:S(2)}) copy-start(bf16[512,2560]{1,0:T(8,128)(2,1)} %all-gather.2.cloned.1.call-done) | copy-start | bytes 7864324
  (26 other events, 59.6 us)
Sparse Core Ops, SparseCore 0:
  88.4 51.2 reduce-scatter.1
  143.7 25.5 all-gather.1

commit v11 on v2

--- a/solution.py
+++ b/solution.py
@@ -27,14 +27,16 @@
     reads_b = reads.reshape(count, STRETCH, -1)
     steps_b = steps.reshape(count, STRETCH, heads)
     rates_b = rates.reshape(count, STRETCH, heads)
-    cum_rate = lax.cumsum(rates_b, axis=1, reverse=reverse)
-    block_total = cum_rate[:, 0] if reverse else cum_rate[:, -1]
-    along = jnp.transpose(cum_rate, (0, 2, 1))
     position = jnp.arange(STRETCH)
     if reverse:
         causal = position[:, None] <= position[None, :]
     else:
         causal = position[:, None] >= position[None, :]
+    cum_rate = jnp.einsum(
+        "ts,bsh->bth", causal.astype(jnp.float32), rates_b, precision=highest
+    )
+    block_total = cum_rate[:, 0] if reverse else cum_rate[:, -1]
+    along = jnp.transpose(cum_rate, (0, 2, 1))
     spans = along[:, :, :, None] - along[:, :, None, :]
     decays = jnp.exp(jnp.where(causal[None, None], spans, -1e30))
     intersection = jnp.einsum("btn,bsn->bts", reads_b, writes_b, preferred_element_type=jnp.float32)
@@ -67,6 +69,11 @@
 
 def relay(state, gain, axis, steps):
     count = lax.axis_size(axis)
+    if count <= 4:
+        entering = jnp.zeros_like(state)
+        for _ in range(count - 1):
+            entering = passed_along(gain[:, None, None] * entering + state, axis, steps)
+        return entering
     distance = 1
     while distance < count:
         got_state = passed_along(state, axis, distance * steps)
@@ -87,6 +94,52 @@
     carried = jnp.einsum("btn,bhpn->bthp", reads_b, block_states, precision=highest)
     outputs = within + jnp.exp(cum_rate)[:, :, :, None] * carried
     return outputs.reshape(acts.shape)
+
+
+def swapped(value, axis):
+    count = lax.axis_size(axis)
+    return lax.ppermute(value, axis, [(source, count - 1 - source) for source in range(count)])
+
+
+def pick(values, index):
+    chosen = values[0]
+    for position in range(1, len(values)):
+        chosen = jnp.where(index == position, values[position], chosen)
+    return chosen
+
+
+def owned_rows(partial_value):
+    chips, cores = lax.axis_size("head_chip"), lax.axis_size("head_core")
+    chip, core = lax.axis_index("head_chip"), lax.axis_index("head_core")
+    rows = partial_value.shape[0] // (chips * cores)
+    blocks = partial_value.reshape(chips, cores, rows, -1)
+    if cores == 2:
+        keep = lax.dynamic_index_in_dim(blocks, core, axis=1, keepdims=False)
+        give = lax.dynamic_index_in_dim(blocks, 1 - core, axis=1, keepdims=False)
+        blocks = keep + swapped(give, "head_core")
+    else:
+        blocks = blocks[:, 0]
+    if chips == 2:
+        keep = lax.dynamic_index_in_dim(blocks, chip, axis=0, keepdims=False)
+        give = lax.dynamic_index_in_dim(blocks, 1 - chip, axis=0, keepdims=False)
+        return keep + swapped(give, "head_chip")
+    return lax.psum_scatter(blocks, "head_chip", scatter_dimension=0, tiled=True)[0]
+
+
+def all_rows(own):
+    chips, cores = lax.axis_size("head_chip"), lax.axis_size("head_core")
+    chip, core = lax.axis_index("head_chip"), lax.axis_index("head_core")
+    if chips == 2:
+        other = swapped(own, "head_chip")
+        pair = pick([jnp.stack([own, other]), jnp.stack([other, own])], chip)
+    else:
+        pair = lax.all_gather(own, "head_chip")
+    if cores == 2:
+        other = swapped(pair, "head_core")
+        whole = pick([jnp.stack([pair, other], axis=1), jnp.stack([other, pair], axis=1)], core)
+    else:
+        whole = pair[:, None]
+    return whole.reshape(-1, own.shape[-1])
 
 
 def per_device(
@@ -124,21 +177,17 @@
     scaled = grouped * lax.rsqrt(jnp.mean(grouped * grouped, axis=2, keepdims=True) + epsilon)
     mixed = (scaled.reshape(tokens, -1) * norm_gain[None, :]).astype(jnp.bfloat16)
     own_width = residual.shape[1]
-    offset = (lax.axis_index("head_chip") * lax.axis_size("head_core") + lax.axis_index("head_core")) * own_width
+    own_block = jnp.arange(out_weight.shape[1]) // own_width == (lax.axis_index("head_chip") * lax.axis_size("head_core") + lax.axis_index("head_core"))
+    spread = jnp.tile(residual.astype(jnp.float32), (1, out_weight.shape[1] // own_width))
     partial_value = jnp.dot(mixed, out_weight, preferred_element_type=jnp.float32)
-    own_cols = lax.dynamic_slice_in_dim(partial_value, offset, own_width, 1) + residual.astype(
-        jnp.float32
-    )
-    partial_value = lax.dynamic_update_slice_in_dim(partial_value, own_cols, offset, 1)
-    encoded = lax.psum_scatter(partial_value, "head_core", scatter_dimension=0, tiled=True)
-    encoded = lax.psum_scatter(encoded, "head_chip", scatter_dimension=0, tiled=True)
+    partial_value = partial_value + jnp.where(own_block[None, :], spread, 0.0)
+    encoded = owned_rows(partial_value)
     normed = (
         encoded
         * lax.rsqrt(jnp.mean(encoded * encoded, axis=1, keepdims=True) + epsilon)
         * final_gain[None, :]
     ).astype(jnp.bfloat16)
-    normed = lax.all_gather(normed, "head_chip", axis=0, tiled=True)
-    normed = lax.all_gather(normed, "head_core", axis=0, tiled=True)
+    normed = all_rows(normed)
     key_sum = jnp.dot(normed, key_weight, preferred_element_type=jnp.float32)
     value_sum = jnp.dot(normed, value_weight, preferred_element_type=jnp.float32)
     return (key_sum.astype(jnp.bfloat16), value_sum.astype(jnp.bfloat16))

time: 208 us -> 146 us (0.70)
  waiting for transfers between devices: 97.7 us -> 55.5 us
  between operations: 14.4 us -> 1.15 us
  local copies, waits for them, and re-layouts: 13.8 us -> 24.2 us
  starting transfers between devices: 32.7 us -> 22.8 us
  other arithmetic: 25.1 us -> 21.8 us
  matrix products: 23.4 us -> 20.4 us
    reduce_scatter x2 -> x0, waiting for transfers between devices: 54.5 us -> none  [the longest x1 41.1 us: per_device(): lax.psum_scatter(encoded, 'head_chip', scatter_dimension=0, tiled=True)]
    ppermute x0 -> x4, waiting for transfers between devices: none -> 52.6 us  [swapped(): lax.ppermute(value, axis, [(source, count - 1 - source) for source in ran...]
    all_gather x2 -> x0, waiting for transfers between devices: 37.1 us -> none  [the longest x1 24.4 us: per_device(): normed = lax.all_gather(normed, 'head_chip', axis=0, tiled=True)]
    ppermute x8 -> x6, starting transfers between devices: 32.6 us -> 20.1 us  [passed_along(): lax.ppermute(value, axis, [(source, source + steps) for source in range(f...]
    another operation x7 -> x0, other arithmetic: 7.81 us -> none
    add x4 -> x7, other arithmetic: 3.2 us -> 8.55 us  [the longest x6 5.71 us: relay(): entering = passed_along(gain[:, None, None] * entering + state, axis, steps)]
    unnamed x67 -> x62, local copies, waits for them, and re-layouts: 6.38 us -> 11.2 us
    select_n x0 -> x3, other arithmetic: none -> 3.54 us  [pick(): chosen = jnp.where(index == position, values[position], chosen)]
  transfers between devices with their start and end apart: 12 -> 10, of which waited for: 8 -> 6; matrix products, arithmetic and copies ran while one was open for 15% -> 18% of each run, Pallas kernels for 0% -> 0%
where the time goes in v11:
time: 146 us
  waiting for transfers between devices  55.5 us (38%)
  local copies, waits for them, and re-layouts  24.2 us (17%)
  starting transfers between devices  22.8 us (16%)
  other arithmetic  21.8 us (15%)
  matrix products  20.4 us (14%)
    ppermute x4, waiting for transfers between devices, swapped(): lax.ppermute(value, axis, [(source, count - 1 - source) for source in ran...  52.6 us
    ppermute x6, starting transfers between devices, passed_along(): lax.ppermute(value, axis, [(source, source + steps) for source in range(f...  20.1 us
    unnamed x62, local copies, waits for them, and re-layouts  11.2 us
    add x6, other arithmetic, relay(): entering = passed_along(gain[:, None, None] * entering + state, axis, steps)  5.71 us
    dot_general x2, matrix products, block_parts(): jnp.einsum('bhts,bshp->bthp', weights, acts_b, preferred_element_type=jnp...  5.25 us
    dot_general x2, matrix products, direction_out(): jnp.einsum('btn,bhpn->bthp', reads_b, block_states, precision=highest)  4.4 us
    select_n x3, other arithmetic, pick(): chosen = jnp.where(index == position, values[position], chosen)  3.54 us
  transfers between devices with their start and end apart: 10, of which 6 were waited for; matrix products, arithmetic and copies ran while one was open for 18% of the time, Pallas kernels for 0%

profile of v11, /device:TPU:0, one launch (start us, length us, event | category | flops | bytes accessed | tf_op | source)
XLA Modules:
  0.0 145.8 jit_solution(4088124529172122741)
XLA Ops:
  7.8 2.3 %copy.20 = bf16[512,640]{0,1:T(8,128)(2,1)} copy(bf16[512,640]{1,0:T(8,128)(2,1)} %param.14) | data formatting | bytes 1310720 | tf_op args[0]
  10.1 2.7 %reshape_reshape.4 = bf16[2,256,10,64]{1,0,3,2:T(2,128)(2,1)} reshape(bf16[512,640]{0,1:T(8,128)(2,1)} %copy.20) | data formatting | bytes 1310720 | tf_op jit(solution)/shard_map/reshape;reshape | solution.py:25
  12.7 2.3 %convert_multiply_fusion.1 = (f32[2,256,10,64]{1,0,3,2:T(2,128)S(1)}, f32[2,256,10,64]{1,0,3,2:T(2,128)S(1)}) fusion(bf16[2,256,10,64]{1,0,3,2:T(2,128)(2,1)} %reshape_reshape.4, f32[2,256,10]{1,0,2:T(2,128)} %copy.26, f32[2,256,10]{1,0,2:T(2,128)} %copy.22), kind=kLoop, calls=%fused_computation.22 | loop fusion | flops 983040 | bytes 3317760 | tf_op jit(solution)/shard_map/mul | solution.py:48
  18.7 5.7 %collective-permute-start = (f32[10,64,128]{2,1,0:T(8,128)S(1)}, f32[10,64,128]{2,1,0:T(8,128)S(1)}, u32[]{:S(2)}, u32[]{:S(2)}) collective-permute-start(f32[10,64,128]{2,1,0:T(8,128)S(1)} %get-tuple-element.10), channel_id=1, source_target_pairs={{0,4},{4,8},{8,12},{1,5},{5,9},{9,13},{2,6},{6,10},{10,14},{3,7},{... | collective-permute-start | bytes 983048 | tf_op jit(solution)/shard_map/ppermute | solution.py:19
  25.0 2.7 %fusion.15 = f32[2,256,10,64]{1,3,2,0:T(8,128)} fusion(f32[2,10,256]{2,1,0:T(8,128)S(1)} %copy-done.18, f32[2,10,256]{2,1,0:T(8,128)S(1)} %copy-done.16, f32[2,256,256]{2,1,0:T(8,128)S(1)} %fusion.84, pred[256,256]{1,0:T(8,128)(4,1)S(1)} %iota_compare_fusion.1, bf16[2,256,10,64]{1,0,3,2:T(2,128)(2,1)S(1)} %copy-done.6), kind=kOutput, calls=%fused_computation.25 | convolution fusion | flops 174325760 | bytes 2596864 | tf_op jit(solution)/shard_map/bhts,bshp->bthp/dot_general | solution.py:46
  27.7 2.6 %fusion.14 = f32[2,256,10,64]{1,3,2,0:T(8,128)} fusion(f32[2,10,256]{2,1,0:T(8,128)S(1)} %copy-done.17, f32[2,10,256]{2,1,0:T(8,128)S(1)} %copy-done.14, f32[2,256,256]{2,1,0:T(8,128)S(1)} %fusion.85, pred[256,256]{1,0:T(8,128)(4,1)S(1)} %iota_compare_fusion, bf16[2,256,10,64]{1,0,3,2:T(2,128)(2,1)S(1)} %copy-done.6), kind=kOutput, calls=%fused_computation.24 | convolution fusion | flops 174325760 | bytes 2596864 | tf_op jit(solution)/shard_map/bhts,bshp->bthp/dot_general | solution.py:46
  32.1 5.1 %collective-permute-start.1 = (f32[10,64,128]{2,1,0:T(8,128)}, f32[10,64,128]{2,1,0:T(8,128)}, u32[]{:S(2)}, u32[]{:S(2)}) collective-permute-start(f32[10,64,128]{2,1,0:T(8,128)} %multiply_add_fusion.3), channel_id=1, source_target_pairs={{0,4},{4,8},{8,12},{1,5},{5,9},{9,13},{2,6},{6,10},{10,14},{3,7},{... | collective-permute-start | bytes 983048 | tf_op jit(solution)/shard_map/ppermute | solution.py:19
  40.3 2.6 %collective-permute-done.1 = f32[10,64,128]{2,1,0:T(8,128)} collective-permute-done((f32[10,64,128]{2,1,0:T(8,128)}, f32[10,64,128]{2,1,0:T(8,128)}, u32[]{:S(2)}, u32[]{:S(2)}) %collective-permute-start.1) | collective-permute-done | bytes 327712 | tf_op jit(solution)/shard_map/ppermute | solution.py:19
  44.8 5.1 %collective-permute-start.2 = (f32[10,64,128]{2,1,0:T(8,128)}, f32[10,64,128]{2,1,0:T(8,128)}, u32[]{:S(2)}, u32[]{:S(2)}) collective-permute-start(f32[10,64,128]{2,1,0:T(8,128)} %multiply_add_fusion.2), channel_id=1, source_target_pairs={{0,4},{4,8},{8,12},{1,5},{5,9},{9,13},{2,6},{6,10},{10,14},{3,7},{... | collective-permute-start | bytes 983048 | tf_op jit(solution)/shard_map/ppermute | solution.py:19
  49.9 1.9 %multiply_add_fusion = f32[10,64,128]{2,1,0:T(8,128)} fusion(f32[10,64,128]{2,1,0:T(8,128)} %copy-done.4, f32[10,64,128]{2,1,0:T(8,128)} %collective-permute-done.4, f32[10]{0:T(128)S(1)} %get-tuple-element.9), kind=kLoop, calls=%fused_computation.70 | loop fusion | flops 163840 | bytes 983080 | tf_op jit(solution)/shard_map/add | solution.py:75
  55.1 2.2 %copy.30 = bf16[512,640]{0,1:T(8,128)(2,1)} copy(bf16[512,640]{1,0:T(8,128)(2,1)} %param.15) | data formatting | bytes 1310720 | tf_op args[1]
  59.9 2.7 %copy.36 = f32[64,8,4,640]{3,1,2,0:T(8,128)} copy(f32[64,8,4,640]{3,2,1,0:T(4,128)S(1)} %bitcast.141) | data formatting | bytes 10485760
  62.6 2.4 %fusion.20 = f32[2,256,10,64]{1,3,2,0:T(8,128)S(1)} fusion(f32[2,256,10,64]{1,3,2,0:T(8,128)} %fusion.15, bf16[2,256,128,1]{2,1,3,0:T(8,128)(2,1)S(1)} %bitcast.156, f32[1,10,64,128]{3,2,1,0:T(8,128)} %slice_add_fusion.1, f32[2,256,10]{1,2,0:T(8,128)} %get-tuple-element.34, f32[10,64,128]{2,1,0:T(8,128)} %collective-permute-done.2, f32[2,10]{1,0:T(2,128)S(1)} %copy-done.21), kind=kOutput, calls=%fused_computation.32 | convolution fusion | flops 504299520 | bytes 3428432 | tf_op jit(solution)/shard_map/btn,bhpn->bthp/dot_general | solution.py:94
  65.1 2.0 %fusion.18 = f32[2,256,10,64]{1,3,2,0:T(8,128)S(1)} fusion(f32[2,256,10,64]{1,3,2,0:T(8,128)S(1)} %fusion.20, f32[2,256,10,64]{1,3,2,0:T(8,128)S(1)} %copy-done.8, bf16[2,256,128,1]{2,1,3,0:T(8,128)(2,1)S(1)} %bitcast.162, f32[1,10,64,128]{3,2,1,0:T(8,128)S(1)} %copy-done.9, f32[2,256,10]{1,2,0:T(8,128)S(1)} %copy-done.12, ...), kind=kOutput, calls=%fused_computation.29 | convolution fusion | flops 504627200 | bytes 4739152 | tf_op jit(solution)/shard_map/btn,bhpn->bthp/dot_general | solution.py:94
  70.1 2.3 %select_add_fusion = f32[512,2560]{1,0:T(8,128)S(1)} fusion(f32[512,2560]{1,0:T(8,128)S(1)} %bitcast.144, bf16[640,2560]{1,0:T(8,128)(2,1)S(1)} %copy-done, pred[2560]{0:T(1024)(128)(4,1)S(1)} %fusion.67, f32[512,640]{0,1:T(8,128)S(1)} %get-tuple-element.5, f32[640]{0:T(1024)S(1)} %copy-done.19, f32[512]{0:T(512)S(1)} %add_rsqrt_fusion), kind=kOutput, calls=%fused_computation | convolution fusion | flops 1681326080 | bytes 15080448 | tf_op jit(solution)/shard_map/dot_general | solution.py:182
  72.6 2.1 %copy-done.2 = f32[512,2560]{1,0:T(8,128)} copy-done((f32[512,2560]{1,0:T(8,128)}, f32[512,2560]{1,0:T(8,128)S(1)}, u32[]{:S(2)}) %copy-start.2) | copy-done | bytes 5242904
  74.7 5.0 %collective-permute-done.6 = f32[2,128,2560]{2,1,0:T(8,128)} collective-permute-done((f32[2,128,2560]{2,1,0:T(8,128)S(1)}, f32[2,128,2560]{2,1,0:T(8,128)}, u32[]{:S(2)}, u32[]{:S(2)}) %collective-permute-start.6) | collective-permute-done | bytes 2621472 | tf_op jit(solution)/shard_map/ppermute | solution.py:101
  79.8 2.8 %bitcast_add_fusion = f32[2,128,2560]{2,1,0:T(8,128)S(1)} fusion(f32[2,128,2560]{2,1,0:T(8,128)} %collective-permute-done.6, f32[2,2,128,2560]{3,2,1,0:T(8,128)} %bitcast.146, s32[]{:T(128)S(6)} %select_n.84), kind=kLoop, calls=%fused_computation.6 | loop fusion | flops 655360 | bytes 7864324 | tf_op jit(solution)/shard_map/add | solution.py:119
  85.1 29.8 %collective-permute-done.7 = f32[128,2560]{1,0:T(8,128)} collective-permute-done((f32[128,2560]{1,0:T(8,128)}, f32[128,2560]{1,0:T(8,128)}, u32[]{:S(2)}, u32[]{:S(2)}) %collective-permute-start.7) | collective-permute-done | bytes 1310752 | tf_op jit(solution)/shard_map/ppermute | solution.py:101
  119.4 14.6 %collective-permute-done.8 = bf16[128,2560]{1,0:T(8,128)(2,1)S(1)} collective-permute-done((bf16[128,2560]{1,0:T(8,128)(2,1)S(1)}, bf16[128,2560]{1,0:T(8,128)(2,1)S(1)}, u32[]{:S(2)}, u32[]{:S(2)}) %collective-permute-start.8) | collective-permute-done | bytes 655392 | tf_op jit(solution)/shard_map/ppermute | solution.py:101
  135.5 3.2 %collective-permute-done.9 = bf16[2,128,2560]{2,1,0:T(8,128)(2,1)} collective-permute-done((bf16[2,128,2560]{2,1,0:T(8,128)(2,1)}, bf16[2,128,2560]{2,1,0:T(8,128)(2,1)}, u32[]{:S(2)}, u32[]{:S(2)}) %collective-permute-start.9) | collective-permute-done | bytes 1310752 | tf_op jit(solution)/shard_map/ppermute | solution.py:101
  138.7 2.0 %maximum_select_fusion = bf16[2,2,128,2560]{3,2,1,0:T(8,128)(2,1)S(1)} fusion(bf16[2,1,128,2560]{3,2,1,0:T(8,128)(2,1)S(1)} %maximum_select_fusion.2, bf16[2,1,128,2560]{3,2,1,0:T(8,128)(2,1)} %bitcast.37, pred[]{:T(512)S(6)} %eq.16), kind=kLoop, calls=%fused_computation.5 | loop fusion | flops 3932160 | bytes 5242881 | tf_op jit(solution)/shard_map/jit(_where)/select_n | solution.py:107
  141.2 2.3 %convolution_convert_fusion = bf16[512,512]{1,0:T(8,128)(2,1)} fusion(bf16[512,2560]{1,0:T(8,128)(2,1)S(1)} %bitcast.151, bf16[2560,512]{1,0:T(8,128)(2,1)S(1)} %copy-done.25), kind=kOutput, calls=%fused_computation.49 | convolution fusion | flops 1342439424 | bytes 5767168 | tf_op jit(solution)/shard_map/dot_general | solution.py:192
  143.5 2.3 %convolution_convert_fusion.1 = bf16[512,512]{1,0:T(8,128)(2,1)} fusion(bf16[512,2560]{1,0:T(8,128)(2,1)S(1)} %bitcast.152, bf16[2560,512]{1,0:T(8,128)(2,1)S(1)} %copy-done.26), kind=kOutput, calls=%fused_computation.50 | convolution fusion | flops 1342439424 | bytes 5767168 | tf_op jit(solution)/shard_map/dot_general | solution.py:191
  (119 shorter events, 35.9 us)
Async XLA Ops:
  0.6 69.3 %copy-start = (bf16[640,2560]{1,0:T(8,128)(2,1)S(1)}, bf16[640,2560]{1,0:T(8,128)(2,1)}, u32[]{:S(2)}) copy-start(bf16[640,2560]{1,0:T(8,128)(2,1)} %param.23) | copy-start | bytes 9830404
  3.3 3.8 %copy-start.13 = (f32[2,10,256]{2,1,0:T(8,128)}, f32[2,10,256]{2,1,0:T(8,128)S(1)}, u32[]{:S(2)}) copy-start(f32[2,10,256]{2,1,0:T(8,128)S(1)} %fusion.47) | copy-start | bytes 61444
  7.8 4.9 %copy-start.10 = (bf16[2,512,128]{2,1,0:T(8,128)(2,1)S(1)}, bf16[2,512,128]{2,1,0:T(8,128)(2,1)}, u32[]{:S(2)}) copy-start(bf16[2,512,128]{2,1,0:T(8,128)(2,1)} %param.16) | copy-start | bytes 786436
  15.9 21.3 %copy-start.4 = (f32[10,64,128]{2,1,0:T(8,128)}, f32[10,64,128]{2,1,0:T(8,128)S(1)}, u32[]{:S(2)}) copy-start(f32[10,64,128]{2,1,0:T(8,128)S(1)} %get-tuple-element.7) | copy-start | bytes 983044
  15.9 21.3 %collective-permute-start.3 = (f32[10,64,128]{2,1,0:T(8,128)S(1)}, f32[10,64,128]{2,1,0:T(8,128)S(1)}, u32[]{:S(2)}, u32[]{:S(2)}) collective-permute-start(f32[10,64,128]{2,1,0:T(8,128)S(1)} %get-tuple-element.6), channel_id=1, source_target_pairs={{4,0},{8,4},{12,8},{5,1},{9,5},{13,9},{6,2},{10,6},{14,10},{7,3},{... | collective-permute-start | bytes 983048 | tf_op jit(solution)/shard_map/ppermute | solution.py:19
  17.8 6.7 %copy-start.11 = (bf16[2,512,128]{2,1,0:T(8,128)(2,1)S(1)}, bf16[2,512,128]{2,1,0:T(8,128)(2,1)}, u32[]{:S(2)}) copy-start(bf16[2,512,128]{2,1,0:T(8,128)(2,1)} %param.17) | copy-start | bytes 786436
  18.6 12.7 %copy-start.5 = (f32[10,64,128]{2,1,0:T(8,128)}, f32[10,64,128]{2,1,0:T(8,128)S(1)}, u32[]{:S(2)}) copy-start(f32[10,64,128]{2,1,0:T(8,128)S(1)} %get-tuple-element.11) | copy-start | bytes 983044
  18.6 6.3 %copy-start.6 = (bf16[2,256,10,64]{1,0,3,2:T(2,128)(2,1)S(1)}, bf16[2,256,10,64]{1,0,3,2:T(2,128)(2,1)}, u32[]{:S(2)}) copy-start(bf16[2,256,10,64]{1,0,3,2:T(2,128)(2,1)} %reshape_reshape.4) | copy-start | bytes 1966084
  18.6 6.3 %copy-start.16 = (f32[2,10,256]{2,1,0:T(8,128)S(1)}, f32[2,10,256]{2,1,0:T(8,128)}, u32[]{:S(2)}) copy-start(f32[2,10,256]{2,1,0:T(8,128)} %copy-done.15) | copy-start | bytes 61444
  18.7 6.3 %copy-start.18 = (f32[2,10,256]{2,1,0:T(8,128)S(1)}, f32[2,10,256]{2,1,0:T(8,128)}, u32[]{:S(2)}) copy-start(f32[2,10,256]{2,1,0:T(8,128)} %get-tuple-element.32) | copy-start | bytes 61444
  18.7 12.7 %collective-permute-start = (f32[10,64,128]{2,1,0:T(8,128)S(1)}, f32[10,64,128]{2,1,0:T(8,128)S(1)}, u32[]{:S(2)}, u32[]{:S(2)}) collective-permute-start(f32[10,64,128]{2,1,0:T(8,128)S(1)} %get-tuple-element.10), channel_id=1, source_target_pairs={{0,4},{4,8},{8,12},{1,5},{5,9},{9,13},{2,6},{6,10},{10,14},{3,7},{... | collective-permute-start | bytes 983048 | tf_op jit(solution)/shard_map/ppermute | solution.py:19
  32.1 10.8 %collective-permute-start.1 = (f32[10,64,128]{2,1,0:T(8,128)}, f32[10,64,128]{2,1,0:T(8,128)}, u32[]{:S(2)}, u32[]{:S(2)}) collective-permute-start(f32[10,64,128]{2,1,0:T(8,128)} %multiply_add_fusion.3), channel_id=1, source_target_pairs={{0,4},{4,8},{8,12},{1,5},{5,9},{9,13},{2,6},{6,10},{10,14},{3,7},{... | collective-permute-start | bytes 983048 | tf_op jit(solution)/shard_map/ppermute | solution.py:19
  38.1 16.4 %copy-start.24 = (f32[1,10]{1,0:T(1,128)S(1)}, f32[1,10]{1,0:T(1,128)}, u32[]{:S(2)}) copy-start(f32[1,10]{1,0:T(1,128)} %get-tuple-element.26) | copy-start | bytes 124
  38.1 11.9 %collective-permute-start.4 = (f32[10,64,128]{2,1,0:T(8,128)}, f32[10,64,128]{2,1,0:T(8,128)}, u32[]{:S(2)}, u32[]{:S(2)}) collective-permute-start(f32[10,64,128]{2,1,0:T(8,128)} %multiply_add_fusion.1), channel_id=1, source_target_pairs={{4,0},{8,4},{12,8},{5,1},{9,5},{13,9},{6,2},{10,6},{14,10},{7,3},{... | collective-permute-start | bytes 983048 | tf_op jit(solution)/shard_map/ppermute | solution.py:19
  44.8 17.7 %collective-permute-start.2 = (f32[10,64,128]{2,1,0:T(8,128)}, f32[10,64,128]{2,1,0:T(8,128)}, u32[]{:S(2)}, u32[]{:S(2)}) collective-permute-start(f32[10,64,128]{2,1,0:T(8,128)} %multiply_add_fusion.2), channel_id=1, source_target_pairs={{0,4},{4,8},{8,12},{1,5},{5,9},{9,13},{2,6},{6,10},{10,14},{3,7},{... | collective-permute-start | bytes 983048 | tf_op jit(solution)/shard_map/ppermute | solution.py:19
  51.9 13.2 %collective-permute-start.5 = (f32[10,64,128]{2,1,0:T(8,128)}, f32[10,64,128]{2,1,0:T(8,128)}, u32[]{:S(2)}, u32[]{:S(2)}) collective-permute-start(f32[10,64,128]{2,1,0:T(8,128)} %multiply_add_fusion), channel_id=1, source_target_pairs={{4,0},{8,4},{12,8},{5,1},{9,5},{13,9},{6,2},{10,6},{14,10},{7,3},{... | collective-permute-start | bytes 983048 | tf_op jit(solution)/shard_map/ppermute | solution.py:19
  59.9 2.7 %copy-start.21 = (f32[2,10]{1,0:T(2,128)S(1)}, f32[2,10]{1,0:T(2,128)}, u32[]{:S(2)}) copy-start(f32[2,10]{1,0:T(2,128)} %stack.49) | copy-start | bytes 244
  65.1 4.9 %slice-start = ((s8[5242880]{0:T(1024)(128)(4,1)}), s8[4194304]{0:T(1024)(128)(4,1)S(1)}, s32[]{:S(2)}) async-start(s8[5242880]{0:T(1024)(128)(4,1)} %bitcast.142), calls=%async_computation | async-start | bytes 8388608
  67.1 2.9 %slice-start.1 = ((s8[5242880]{0:T(1024)(128)(4,1)}), s8[1048576]{0:T(1024)(128)(4,1)S(1)}, s32[]{:S(2)}) async-start(s8[5242880]{0:T(1024)(128)(4,1)} %bitcast.142), calls=%async_computation.1 | async-start | bytes 2097152
  74.7 5.0 %collective-permute-start.6 = (f32[2,128,2560]{2,1,0:T(8,128)S(1)}, f32[2,128,2560]{2,1,0:T(8,128)}, u32[]{:S(2)}, u32[]{:S(2)}) collective-permute-start(f32[2,128,2560]{2,1,0:T(8,128)S(1)} %dynamic-slice_bitcast_fusion), channel_id=1, source_target_pairs={{0,1},{1,0},{2,3},{3,2},{4,5},{5,4},{6,7},{7,6},{8,9},{9,8},{10,11... | collective-permute-start | bytes 7864328 | tf_op jit(solution)/shard_map/ppermute | solution.py:101
  83.8 31.1 %collective-permute-start.7 = (f32[128,2560]{1,0:T(8,128)}, f32[128,2560]{1,0:T(8,128)}, u32[]{:S(2)}, u32[]{:S(2)}) collective-permute-start(f32[128,2560]{1,0:T(8,128)} %dynamic-slice_bitcast_fusion.1), channel_id=1, source_target_pairs={{0,2},{2,0},{1,3},{3,1},{4,6},{6,4},{5,7},{7,5},{8,10},{10,8},{9,1... | collective-permute-start | bytes 3932168 | tf_op jit(solution)/shard_map/ppermute | solution.py:101
  85.1 31.4 %copy-start.20 = (f32[2560]{0:T(1024)S(1)}, f32[2560]{0:T(1024)}, u32[]{:S(2)}) copy-start(f32[2560]{0:T(1024)} %param.25) | copy-start | bytes 30724
  118.0 16.0 %collective-permute-start.8 = (bf16[128,2560]{1,0:T(8,128)(2,1)S(1)}, bf16[128,2560]{1,0:T(8,128)(2,1)S(1)}, u32[]{:S(2)}, u32[]{:S(2)}) collective-permute-start(bf16[128,2560]{1,0:T(8,128)(2,1)S(1)} %multiply_convert_fusion.8), channel_id=1, source_target_pairs={{0,2},{2,0},{1,3},{3,1},{4,6},{6,4},{5,7},{7,5},{8,10},{10,8},{9,1... | collective-permute-start | bytes 1966088 | tf_op jit(solution)/shard_map/ppermute | solution.py:101
  135.3 3.4 %collective-permute-start.9 = (bf16[2,128,2560]{2,1,0:T(8,128)(2,1)}, bf16[2,128,2560]{2,1,0:T(8,128)(2,1)}, u32[]{:S(2)}, u32[]{:S(2)}) collective-permute-start(bf16[2,128,2560]{2,1,0:T(8,128)(2,1)} %maximum_select_fusion.1), channel_id=1, source_target_pairs={{0,1},{1,0},{2,3},{3,2},{4,5},{5,4},{6,7},{7,6},{8,9},{9,8},{10,11... | collective-permute-start | bytes 3932168 | tf_op jit(solution)/shard_map/ppermute | solution.py:101
  (15 other events, 30.7 us)

commit v12 on v11

--- a/solution.py
+++ b/solution.py
@@ -108,38 +108,46 @@
     return chosen
 
 
+def block_at(blocks, chip, core):
+    rows, width = blocks.shape[2], blocks.shape[3]
+    return lax.dynamic_slice(blocks, (chip, core, 0, 0), (1, 1, rows, width))[0, 0]
+
+
 def owned_rows(partial_value):
     chips, cores = lax.axis_size("head_chip"), lax.axis_size("head_core")
+    if chips != 2 or cores != 2:
+        return lax.psum_scatter(partial_value, ("head_chip", "head_core"), scatter_dimension=0, tiled=True)
     chip, core = lax.axis_index("head_chip"), lax.axis_index("head_core")
-    rows = partial_value.shape[0] // (chips * cores)
-    blocks = partial_value.reshape(chips, cores, rows, -1)
-    if cores == 2:
-        keep = lax.dynamic_index_in_dim(blocks, core, axis=1, keepdims=False)
-        give = lax.dynamic_index_in_dim(blocks, 1 - core, axis=1, keepdims=False)
-        blocks = keep + swapped(give, "head_core")
-    else:
-        blocks = blocks[:, 0]
-    if chips == 2:
-        keep = lax.dynamic_index_in_dim(blocks, chip, axis=0, keepdims=False)
-        give = lax.dynamic_index_in_dim(blocks, 1 - chip, axis=0, keepdims=False)
-        return keep + swapped(give, "head_chip")
-    return lax.psum_scatter(blocks, "head_chip", scatter_dimension=0, tiled=True)[0]
-
-
-def all_rows(own):
+    blocks = partial_value.reshape(chips, cores, partial_value.shape[0] // 4, -1)
+    far = block_at(blocks, 1 - chip, core) + swapped(block_at(blocks, 1 - chip, 1 - core), "head_core")
+    arrived = swapped(far, "head_chip")
+    near = block_at(blocks, chip, core) + swapped(block_at(blocks, chip, 1 - core), "head_core")
+    return near + arrived
+
+
+def project_all_rows(own, key_weight, value_weight):
+    def project(rows):
+        return (
+            jnp.dot(rows, key_weight, preferred_element_type=jnp.float32).astype(jnp.bfloat16),
+            jnp.dot(rows, value_weight, preferred_element_type=jnp.float32).astype(jnp.bfloat16),
+        )
+
     chips, cores = lax.axis_size("head_chip"), lax.axis_size("head_core")
+    if chips != 2 or cores != 2:
+        return project(lax.all_gather(own, ("head_chip", "head_core"), axis=0, tiled=True))
     chip, core = lax.axis_index("head_chip"), lax.axis_index("head_core")
-    if chips == 2:
-        other = swapped(own, "head_chip")
-        pair = pick([jnp.stack([own, other]), jnp.stack([other, own])], chip)
-    else:
-        pair = lax.all_gather(own, "head_chip")
-    if cores == 2:
-        other = swapped(pair, "head_core")
-        whole = pick([jnp.stack([pair, other], axis=1), jnp.stack([other, pair], axis=1)], core)
-    else:
-        whole = pair[:, None]
-    return whole.reshape(-1, own.shape[-1])
+    other = swapped(own, "head_chip")
+    partner = swapped(own, "head_core")
+    partner_other = swapped(other, "head_core")
+    results = [project(rows) for rows in (own, partner, other, partner_other)]
+    assembled = []
+    for which in range(2):
+        own_p, partner_p, other_p, partner_other_p = (result[which] for result in results)
+        near = pick([jnp.stack([own_p, partner_p]), jnp.stack([partner_p, own_p])], core)
+        far = pick([jnp.stack([other_p, partner_other_p]), jnp.stack([partner_other_p, other_p])], core)
+        whole = pick([jnp.stack([near, far]), jnp.stack([far, near])], chip)
+        assembled.append(whole.reshape(-1, whole.shape[-1]))
+    return tuple(assembled)
 
 
 def per_device(
@@ -187,10 +195,7 @@
         * lax.rsqrt(jnp.mean(encoded * encoded, axis=1, keepdims=True) + epsilon)
         * final_gain[None, :]
     ).astype(jnp.bfloat16)
-    normed = all_rows(normed)
-    key_sum = jnp.dot(normed, key_weight, preferred_element_type=jnp.float32)
-    value_sum = jnp.dot(normed, value_weight, preferred_element_type=jnp.float32)
-    return (key_sum.astype(jnp.bfloat16), value_sum.astype(jnp.bfloat16))
+    return project_all_rows(normed, key_weight, value_weight)
 
 
 def split_head(mesh):

time: 146 us -> 139 us (0.952)
  waiting for transfers between devices: 55.5 us -> 46.5 us
  matrix products: 20.4 us -> 25.2 us
  other arithmetic: 21.8 us -> 18.4 us
    ppermute x4 -> x6, waiting for transfers between devices: 52.6 us -> 43.6 us  [swapped(): lax.ppermute(value, axis, [(source, count - 1 - source) for source in ran...]
    dot_general x2 -> x8, matrix products: 4.62 us -> 9.4 us  [the longest x4 5.05 us: project(): jnp.dot(rows, value_weight, preferred_element_type=jnp.float32)]
    select_n x3 -> x6, other arithmetic: 3.54 us -> 1.84 us  [pick(): chosen = jnp.where(index == position, values[position], chosen)]
    unnamed x62 -> x60, local copies, waits for them, and re-layouts: 11.2 us -> 10 us
    ppermute x4 -> x6, starting transfers between devices: 2.71 us -> 3.22 us  [swapped(): lax.ppermute(value, axis, [(source, count - 1 - source) for source in ran...]
  transfers between devices with their start and end apart: 10 -> 12, of which waited for: 6 -> 6; matrix products, arithmetic and copies ran while one was open for 18% -> 26% of each run, Pallas kernels for 0% -> 0%
where the time goes in v12:
time: 139 us; the launch traced here: 138 us
  waiting for transfers between devices  46.5 us (33%)
  matrix products  25.2 us (18%)
  local copies, waits for them, and re-layouts  23.6 us (17%)
  starting transfers between devices  23.4 us (17%)
  other arithmetic  18.4 us (13%)
    ppermute x6, waiting for transfers between devices, swapped(): lax.ppermute(value, axis, [(source, count - 1 - source) for source in ran...  43.6 us
    ppermute x6, starting transfers between devices, passed_along(): lax.ppermute(value, axis, [(source, source + steps) for source in range(f...  20.1 us
    unnamed x60, local copies, waits for them, and re-layouts  10 us
    add x6, other arithmetic, relay(): entering = passed_along(gain[:, None, None] * entering + state, axis, steps)  5.72 us
    dot_general x2, matrix products, block_parts(): jnp.einsum('bhts,bshp->bthp', weights, acts_b, preferred_element_type=jnp...  5.25 us
    dot_general x4, matrix products, project(): jnp.dot(rows, value_weight, preferred_element_type=jnp.float32)  5.05 us
    dot_general x2, matrix products, direction_out(): jnp.einsum('btn,bhpn->bthp', reads_b, block_states, precision=highest)  4.4 us
    dot_general x4, matrix products, project(): jnp.dot(rows, key_weight, preferred_element_type=jnp.float32)  4.35 us
  transfers between devices with their start and end apart: 12, of which 6 were waited for; matrix products, arithmetic and copies ran while one was open for 26% of the time, Pallas kernels for 0%

profile of v12, /device:TPU:0, one launch (start us, length us, event | category | flops | bytes accessed | tf_op | source)
XLA Modules:
  0.0 138.3 jit_solution(14458065080109674759)
XLA Ops:
  7.8 2.2 %copy.20 = bf16[512,640]{0,1:T(8,128)(2,1)} copy(bf16[512,640]{1,0:T(8,128)(2,1)} %param.14) | data formatting | bytes 1310720 | tf_op args[0]
  10.0 2.7 %reshape_reshape.4 = bf16[2,256,10,64]{1,0,3,2:T(2,128)(2,1)} reshape(bf16[512,640]{0,1:T(8,128)(2,1)} %copy.20) | data formatting | bytes 1310720 | tf_op jit(solution)/shard_map/reshape;reshape | solution.py:25
  12.7 1.8 %convert_multiply_fusion.1 = (f32[2,256,10,64]{1,0,3,2:T(2,128)S(1)}, f32[2,256,10,64]{1,0,3,2:T(2,128)S(1)}) fusion(bf16[2,256,10,64]{1,0,3,2:T(2,128)(2,1)} %reshape_reshape.4, f32[2,256,10]{1,0,2:T(2,128)} %copy.26, f32[2,256,10]{1,0,2:T(2,128)} %copy.22), kind=kLoop, calls=%fused_computation.19 | loop fusion | flops 983040 | bytes 3317760 | tf_op jit(solution)/shard_map/mul | solution.py:48
  18.3 5.7 %collective-permute-start = (f32[10,64,128]{2,1,0:T(8,128)S(1)}, f32[10,64,128]{2,1,0:T(8,128)S(1)}, u32[]{:S(2)}, u32[]{:S(2)}) collective-permute-start(f32[10,64,128]{2,1,0:T(8,128)S(1)} %get-tuple-element.12), channel_id=1, source_target_pairs={{0,4},{4,8},{8,12},{1,5},{5,9},{9,13},{2,6},{6,10},{10,14},{3,7},{... | collective-permute-start | bytes 983048 | tf_op jit(solution)/shard_map/ppermute | solution.py:19
  24.7 2.7 %fusion.15 = f32[2,256,10,64]{1,3,2,0:T(8,128)} fusion(f32[2,10,256]{2,1,0:T(8,128)S(1)} %copy-done.19, f32[2,10,256]{2,1,0:T(8,128)S(1)} %copy-done.17, f32[2,256,256]{2,1,0:T(8,128)S(1)} %fusion.94, pred[256,256]{1,0:T(8,128)(4,1)S(1)} %iota_compare_fusion.1, bf16[2,256,10,64]{1,0,3,2:T(2,128)(2,1)S(1)} %copy-done.7), kind=kOutput, calls=%fused_computation.22 | convolution fusion | flops 174325760 | bytes 2596864 | tf_op jit(solution)/shard_map/bhts,bshp->bthp/dot_general | solution.py:46
  27.3 2.6 %fusion.14 = f32[2,256,10,64]{1,3,2,0:T(8,128)} fusion(f32[2,10,256]{2,1,0:T(8,128)S(1)} %copy-done.18, f32[2,10,256]{2,1,0:T(8,128)S(1)} %copy-done.15, f32[2,256,256]{2,1,0:T(8,128)S(1)} %fusion.95, pred[256,256]{1,0:T(8,128)(4,1)S(1)} %iota_compare_fusion, bf16[2,256,10,64]{1,0,3,2:T(2,128)(2,1)S(1)} %copy-done.7), kind=kOutput, calls=%fused_computation.21 | convolution fusion | flops 174325760 | bytes 2596864 | tf_op jit(solution)/shard_map/bhts,bshp->bthp/dot_general | solution.py:46
  31.8 5.1 %collective-permute-start.1 = (f32[10,64,128]{2,1,0:T(8,128)}, f32[10,64,128]{2,1,0:T(8,128)}, u32[]{:S(2)}, u32[]{:S(2)}) collective-permute-start(f32[10,64,128]{2,1,0:T(8,128)} %multiply_add_fusion.3), channel_id=1, source_target_pairs={{0,4},{4,8},{8,12},{1,5},{5,9},{9,13},{2,6},{6,10},{10,14},{3,7},{... | collective-permute-start | bytes 983048 | tf_op jit(solution)/shard_map/ppermute | solution.py:19
  40.0 2.6 %collective-permute-done.1 = f32[10,64,128]{2,1,0:T(8,128)} collective-permute-done((f32[10,64,128]{2,1,0:T(8,128)}, f32[10,64,128]{2,1,0:T(8,128)}, u32[]{:S(2)}, u32[]{:S(2)}) %collective-permute-start.1) | collective-permute-done | bytes 327712 | tf_op jit(solution)/shard_map/ppermute | solution.py:19
  42.6 1.9 %multiply_add_fusion.2 = f32[10,64,128]{2,1,0:T(8,128)} fusion(f32[10,64,128]{2,1,0:T(8,128)} %copy-done.6, f32[10,64,128]{2,1,0:T(8,128)} %collective-permute-done.1, f32[10]{0:T(128)S(1)} %get-tuple-element.15), kind=kLoop, calls=%fused_computation.88 | loop fusion | flops 163840 | bytes 983080 | tf_op jit(solution)/shard_map/add | solution.py:75
  44.5 5.1 %collective-permute-start.2 = (f32[10,64,128]{2,1,0:T(8,128)}, f32[10,64,128]{2,1,0:T(8,128)}, u32[]{:S(2)}, u32[]{:S(2)}) collective-permute-start(f32[10,64,128]{2,1,0:T(8,128)} %multiply_add_fusion.2), channel_id=1, source_target_pairs={{0,4},{4,8},{8,12},{1,5},{5,9},{9,13},{2,6},{6,10},{10,14},{3,7},{... | collective-permute-start | bytes 983048 | tf_op jit(solution)/shard_map/ppermute | solution.py:19
  49.6 1.9 %multiply_add_fusion = f32[10,64,128]{2,1,0:T(8,128)} fusion(f32[10,64,128]{2,1,0:T(8,128)} %copy-done.5, f32[10,64,128]{2,1,0:T(8,128)} %collective-permute-done.4, f32[10]{0:T(128)S(1)} %get-tuple-element.11), kind=kLoop, calls=%fused_computation.84 | loop fusion | flops 163840 | bytes 983080 | tf_op jit(solution)/shard_map/add | solution.py:75
  54.8 2.2 %copy.30 = bf16[512,640]{0,1:T(8,128)(2,1)} copy(bf16[512,640]{1,0:T(8,128)(2,1)} %param.15) | data formatting | bytes 1310720 | tf_op args[1]
  57.8 1.8 %tile.4 = f32[512,4,640]{2,1,0:T(4,128)S(1)} broadcast(bf16[512,640]{1,0:T(8,128)(2,1)} %param.24), dimensions={0,2} | broadcast | bytes 5898240 | tf_op jit(solution)/shard_map/tile | solution.py:189
  59.6 2.7 %copy.36 = f32[64,8,4,640]{3,1,2,0:T(8,128)} copy(f32[64,8,4,640]{3,2,1,0:T(4,128)S(1)} %bitcast.164) | data formatting | bytes 10485760
  62.3 2.4 %fusion.20 = f32[2,256,10,64]{1,3,2,0:T(8,128)S(1)} fusion(f32[2,256,10,64]{1,3,2,0:T(8,128)} %fusion.15, bf16[2,256,128,1]{2,1,3,0:T(8,128)(2,1)S(1)} %bitcast.174, f32[1,10,64,128]{3,2,1,0:T(8,128)} %slice_add_fusion.1, f32[2,256,10]{1,2,0:T(8,128)} %get-tuple-element.38, f32[10,64,128]{2,1,0:T(8,128)} %collective-permute-done.2, f32[2,10]{1,0:T(2,128)S(1)} %copy-done.22), kind=kOutput, calls=%fused_computation.29 | convolution fusion | flops 504299520 | bytes 3428432 | tf_op jit(solution)/shard_map/btn,bhpn->bthp/dot_general | solution.py:94
  64.8 2.0 %fusion.18 = f32[2,256,10,64]{1,3,2,0:T(8,128)S(1)} fusion(f32[2,256,10,64]{1,3,2,0:T(8,128)S(1)} %fusion.20, f32[2,256,10,64]{1,3,2,0:T(8,128)S(1)} %copy-done.9, bf16[2,256,128,1]{2,1,3,0:T(8,128)(2,1)S(1)} %bitcast.180, f32[1,10,64,128]{3,2,1,0:T(8,128)S(1)} %copy-done.10, f32[2,256,10]{1,2,0:T(8,128)S(1)} %copy-done.13, ...), kind=kOutput, calls=%fused_computation.26 | convolution fusion | flops 504627200 | bytes 4739152 | tf_op jit(solution)/shard_map/btn,bhpn->bthp/dot_general | solution.py:94
  69.8 2.3 %select_add_fusion = f32[512,2560]{1,0:T(8,128)S(1)} fusion(f32[512,2560]{1,0:T(8,128)S(1)} %bitcast.167, bf16[640,2560]{1,0:T(8,128)(2,1)S(1)} %copy-done, pred[2560]{0:T(1024)(128)(4,1)S(1)} %fusion.76, f32[512,640]{0,1:T(8,128)S(1)} %get-tuple-element.7, f32[640]{0:T(1024)S(1)} %copy-done.20, f32[512]{0:T(512)S(1)} %add_rsqrt_fusion), kind=kOutput, calls=%fused_computation | convolution fusion | flops 1681326080 | bytes 15080448 | tf_op jit(solution)/shard_map/dot_general | solution.py:190
  72.1 1.8 %dynamic-slice_bitcast_fusion.1 = (f32[128,2560]{1,0:T(8,128)}, f32[128,2560]{1,0:T(8,128)}) fusion(f32[2,2,128,2560]{3,2,1,0:T(8,128)S(1)} %bitcast.168, s32[]{:T(128)S(6)} %select_n.123, s32[]{:T(128)S(6)} %select_n.125, s32[]{:T(128)S(6)} %select_n.126), kind=kLoop, calls=%fused_computation.44 | loop fusion | bytes 5242892 | tf_op jit(solution)/shard_map/squeeze | solution.py:113
  75.7 4.7 %collective-permute-done.7 = f32[128,2560]{1,0:T(8,128)} collective-permute-done((f32[128,2560]{1,0:T(8,128)}, f32[128,2560]{1,0:T(8,128)}, u32[]{:S(2)}, u32[]{:S(2)}) %collective-permute-start.7) | collective-permute-done | bytes 1310752 | tf_op jit(solution)/shard_map/ppermute | solution.py:101
  80.4 1.9 %bitcast_add_fusion = f32[128,2560]{1,0:T(8,128)S(1)} fusion(f32[128,2560]{1,0:T(8,128)} %collective-permute-done.7, f32[2,2,128,2560]{3,2,1,0:T(8,128)} %bitcast.169, s32[]{:T(128)S(6)} %select_n.126, s32[]{:T(128)S(6)} %select_n.124), kind=kLoop, calls=%fused_computation.34 | loop fusion | flops 327680 | bytes 3932168 | tf_op jit(solution)/shard_map/add | solution.py:122
  83.7 29.5 %collective-permute-done.8 = f32[128,2560]{1,0:T(8,128)S(1)} collective-permute-done((f32[128,2560]{1,0:T(8,128)S(1)}, f32[128,2560]{1,0:T(8,128)S(1)}, u32[]{:S(2)}, u32[]{:S(2)}) %collective-permute-start.8) | collective-permute-done | bytes 1310752 | tf_op jit(solution)/shard_map/ppermute | solution.py:101
  117.3 2.4 %fusion.37 = bf16[1,1,128,512]{3,2,1,0:T(8,128)(2,1)S(1)} fusion(bf16[128,2560]{1,0:T(8,128)(2,1)} %multiply_convert_fusion.8, bf16[2560,512]{1,0:T(8,128)(2,1)} %param.27), kind=kOutput, calls=%fused_computation.62 | convolution fusion | flops 335609856 | bytes 3407872 | tf_op jit(solution)/shard_map/dot_general | solution.py:132
  119.8 1.7 %fusion.33 = bf16[1,1,128,512]{3,2,1,0:T(8,128)(2,1)S(1)} fusion(bf16[128,2560]{1,0:T(8,128)(2,1)} %multiply_convert_fusion.8, bf16[2560,512]{1,0:T(8,128)(2,1)S(1)} %copy-done.2), kind=kOutput, calls=%fused_computation.58 | convolution fusion | flops 335609856 | bytes 3407872 | tf_op jit(solution)/shard_map/dot_general | solution.py:131
  124.9 8.4 %collective-permute-done.9 = bf16[128,2560]{1,0:T(8,128)(2,1)S(1)} collective-permute-done((bf16[128,2560]{1,0:T(8,128)(2,1)}, bf16[128,2560]{1,0:T(8,128)(2,1)S(1)}, u32[]{:S(2)}, u32[]{:S(2)}) %collective-permute-start.9) | collective-permute-done | bytes 655392 | tf_op jit(solution)/shard_map/ppermute | solution.py:101
  (129 shorter events, 38.8 us)
Async XLA Ops:
  0.6 69.0 %copy-start = (bf16[640,2560]{1,0:T(8,128)(2,1)S(1)}, bf16[640,2560]{1,0:T(8,128)(2,1)}, u32[]{:S(2)}) copy-start(bf16[640,2560]{1,0:T(8,128)(2,1)} %param.23) | copy-start | bytes 9830404
  3.3 3.8 %copy-start.14 = (f32[2,10,256]{2,1,0:T(8,128)}, f32[2,10,256]{2,1,0:T(8,128)S(1)}, u32[]{:S(2)}) copy-start(f32[2,10,256]{2,1,0:T(8,128)S(1)} %fusion.56) | copy-start | bytes 61444
  7.8 4.9 %copy-start.11 = (bf16[2,512,128]{2,1,0:T(8,128)(2,1)S(1)}, bf16[2,512,128]{2,1,0:T(8,128)(2,1)}, u32[]{:S(2)}) copy-start(bf16[2,512,128]{2,1,0:T(8,128)(2,1)} %param.16) | copy-start | bytes 786436
  15.5 21.4 %copy-start.5 = (f32[10,64,128]{2,1,0:T(8,128)}, f32[10,64,128]{2,1,0:T(8,128)S(1)}, u32[]{:S(2)}) copy-start(f32[10,64,128]{2,1,0:T(8,128)S(1)} %get-tuple-element.9) | copy-start | bytes 983044
  15.5 21.4 %collective-permute-start.3 = (f32[10,64,128]{2,1,0:T(8,128)S(1)}, f32[10,64,128]{2,1,0:T(8,128)S(1)}, u32[]{:S(2)}, u32[]{:S(2)}) collective-permute-start(f32[10,64,128]{2,1,0:T(8,128)S(1)} %get-tuple-element.8), channel_id=1, source_target_pairs={{4,0},{8,4},{12,8},{5,1},{9,5},{13,9},{6,2},{10,6},{14,10},{7,3},{... | collective-permute-start | bytes 983048 | tf_op jit(solution)/shard_map/ppermute | solution.py:19
  17.4 6.7 %copy-start.12 = (bf16[2,512,128]{2,1,0:T(8,128)(2,1)S(1)}, bf16[2,512,128]{2,1,0:T(8,128)(2,1)}, u32[]{:S(2)}) copy-start(bf16[2,512,128]{2,1,0:T(8,128)(2,1)} %param.17) | copy-start | bytes 786436
  18.3 12.7 %copy-start.6 = (f32[10,64,128]{2,1,0:T(8,128)}, f32[10,64,128]{2,1,0:T(8,128)S(1)}, u32[]{:S(2)}) copy-start(f32[10,64,128]{2,1,0:T(8,128)S(1)} %get-tuple-element.13) | copy-start | bytes 983044
  18.3 6.3 %copy-start.7 = (bf16[2,256,10,64]{1,0,3,2:T(2,128)(2,1)S(1)}, bf16[2,256,10,64]{1,0,3,2:T(2,128)(2,1)}, u32[]{:S(2)}) copy-start(bf16[2,256,10,64]{1,0,3,2:T(2,128)(2,1)} %reshape_reshape.4) | copy-start | bytes 1966084
  18.3 6.3 %copy-start.17 = (f32[2,10,256]{2,1,0:T(8,128)S(1)}, f32[2,10,256]{2,1,0:T(8,128)}, u32[]{:S(2)}) copy-start(f32[2,10,256]{2,1,0:T(8,128)} %copy-done.16) | copy-start | bytes 61444
  18.3 6.3 %copy-start.19 = (f32[2,10,256]{2,1,0:T(8,128)S(1)}, f32[2,10,256]{2,1,0:T(8,128)}, u32[]{:S(2)}) copy-start(f32[2,10,256]{2,1,0:T(8,128)} %get-tuple-element.36) | copy-start | bytes 61444
  18.3 12.7 %collective-permute-start = (f32[10,64,128]{2,1,0:T(8,128)S(1)}, f32[10,64,128]{2,1,0:T(8,128)S(1)}, u32[]{:S(2)}, u32[]{:S(2)}) collective-permute-start(f32[10,64,128]{2,1,0:T(8,128)S(1)} %get-tuple-element.12), channel_id=1, source_target_pairs={{0,4},{4,8},{8,12},{1,5},{5,9},{9,13},{2,6},{6,10},{10,14},{3,7},{... | collective-permute-start | bytes 983048 | tf_op jit(solution)/shard_map/ppermute | solution.py:19
  31.8 10.8 %collective-permute-start.1 = (f32[10,64,128]{2,1,0:T(8,128)}, f32[10,64,128]{2,1,0:T(8,128)}, u32[]{:S(2)}, u32[]{:S(2)}) collective-permute-start(f32[10,64,128]{2,1,0:T(8,128)} %multiply_add_fusion.3), channel_id=1, source_target_pairs={{0,4},{4,8},{8,12},{1,5},{5,9},{9,13},{2,6},{6,10},{10,14},{3,7},{... | collective-permute-start | bytes 983048 | tf_op jit(solution)/shard_map/ppermute | solution.py:19
  37.8 16.5 %copy-start.25 = (f32[1,10]{1,0:T(1,128)S(1)}, f32[1,10]{1,0:T(1,128)}, u32[]{:S(2)}) copy-start(f32[1,10]{1,0:T(1,128)} %get-tuple-element.30) | copy-start | bytes 124
  37.8 11.8 %collective-permute-start.4 = (f32[10,64,128]{2,1,0:T(8,128)}, f32[10,64,128]{2,1,0:T(8,128)}, u32[]{:S(2)}, u32[]{:S(2)}) collective-permute-start(f32[10,64,128]{2,1,0:T(8,128)} %multiply_add_fusion.1), channel_id=1, source_target_pairs={{4,0},{8,4},{12,8},{5,1},{9,5},{13,9},{6,2},{10,6},{14,10},{7,3},{... | collective-permute-start | bytes 983048 | tf_op jit(solution)/shard_map/ppermute | solution.py:19
  44.5 17.8 %collective-permute-start.2 = (f32[10,64,128]{2,1,0:T(8,128)}, f32[10,64,128]{2,1,0:T(8,128)}, u32[]{:S(2)}, u32[]{:S(2)}) collective-permute-start(f32[10,64,128]{2,1,0:T(8,128)} %multiply_add_fusion.2), channel_id=1, source_target_pairs={{0,4},{4,8},{8,12},{1,5},{5,9},{9,13},{2,6},{6,10},{10,14},{3,7},{... | collective-permute-start | bytes 983048 | tf_op jit(solution)/shard_map/ppermute | solution.py:19
  51.5 13.2 %collective-permute-start.5 = (f32[10,64,128]{2,1,0:T(8,128)}, f32[10,64,128]{2,1,0:T(8,128)}, u32[]{:S(2)}, u32[]{:S(2)}) collective-permute-start(f32[10,64,128]{2,1,0:T(8,128)} %multiply_add_fusion), channel_id=1, source_target_pairs={{4,0},{8,4},{12,8},{5,1},{9,5},{13,9},{6,2},{10,6},{14,10},{7,3},{... | collective-permute-start | bytes 983048 | tf_op jit(solution)/shard_map/ppermute | solution.py:19
  64.7 4.9 %slice-start = ((s8[5242880]{0:T(1024)(128)(4,1)}), s8[4194304]{0:T(1024)(128)(4,1)S(1)}, s32[]{:S(2)}) async-start(s8[5242880]{0:T(1024)(128)(4,1)} %bitcast.165), calls=%async_computation | async-start | bytes 8388608
  75.2 5.2 %collective-permute-start.7 = (f32[128,2560]{1,0:T(8,128)}, f32[128,2560]{1,0:T(8,128)}, u32[]{:S(2)}, u32[]{:S(2)}) collective-permute-start(f32[128,2560]{1,0:T(8,128)} %get-tuple-element.17), channel_id=1, source_target_pairs={{0,1},{1,0},{2,3},{3,2},{4,5},{5,4},{6,7},{7,6},{8,9},{9,8},{10,11... | collective-permute-start | bytes 3932168 | tf_op jit(solution)/shard_map/ppermute | solution.py:101
  75.2 8.5 %collective-permute-start.6 = (f32[128,2560]{1,0:T(8,128)}, f32[128,2560]{1,0:T(8,128)S(1)}, u32[]{:S(2)}, u32[]{:S(2)}) collective-permute-start(f32[128,2560]{1,0:T(8,128)} %get-tuple-element.16), channel_id=1, source_target_pairs={{0,1},{1,0},{2,3},{3,2},{4,5},{5,4},{6,7},{7,6},{8,9},{9,8},{10,11... | collective-permute-start | bytes 3932168 | tf_op jit(solution)/shard_map/ppermute | solution.py:101
  82.3 32.6 %copy-start.21 = (f32[2560]{0:T(1024)S(1)}, f32[2560]{0:T(1024)}, u32[]{:S(2)}) copy-start(f32[2560]{0:T(1024)} %param.25) | copy-start | bytes 30724
  82.3 30.9 %collective-permute-start.8 = (f32[128,2560]{1,0:T(8,128)S(1)}, f32[128,2560]{1,0:T(8,128)S(1)}, u32[]{:S(2)}, u32[]{:S(2)}) collective-permute-start(f32[128,2560]{1,0:T(8,128)S(1)} %bitcast_add_fusion), channel_id=1, source_target_pairs={{0,2},{2,0},{1,3},{3,1},{4,6},{6,4},{5,7},{7,5},{8,10},{10,8},{9,1... | collective-permute-start | bytes 3932168 | tf_op jit(solution)/shard_map/ppermute | solution.py:101
  116.0 5.6 %collective-permute-start.11 = (bf16[128,2560]{1,0:T(8,128)(2,1)}, bf16[128,2560]{1,0:T(8,128)(2,1)}, u32[]{:S(2)}, u32[]{:S(2)}) collective-permute-start(bf16[128,2560]{1,0:T(8,128)(2,1)} %multiply_convert_fusion.8), channel_id=1, source_target_pairs={{0,1},{1,0},{2,3},{3,2},{4,5},{5,4},{6,7},{7,6},{8,9},{9,8},{10,11... | collective-permute-start | bytes 1966088 | tf_op jit(solution)/shard_map/ppermute | solution.py:101
  116.0 17.4 %collective-permute-start.9 = (bf16[128,2560]{1,0:T(8,128)(2,1)}, bf16[128,2560]{1,0:T(8,128)(2,1)S(1)}, u32[]{:S(2)}, u32[]{:S(2)}) collective-permute-start(bf16[128,2560]{1,0:T(8,128)(2,1)} %multiply_convert_fusion.8), channel_id=1, source_target_pairs={{0,2},{2,0},{1,3},{3,1},{4,6},{6,4},{5,7},{7,5},{8,10},{10,8},{9,1... | collective-permute-start | bytes 1966088 | tf_op jit(solution)/shard_map/ppermute | solution.py:101
  133.3 2.1 %collective-permute-start.10 = (bf16[128,2560]{1,0:T(8,128)(2,1)S(1)}, bf16[128,2560]{1,0:T(8,128)(2,1)S(1)}, u32[]{:S(2)}, u32[]{:S(2)}) collective-permute-start(bf16[128,2560]{1,0:T(8,128)(2,1)S(1)} %collective-permute-done.9), channel_id=1, source_target_pairs={{0,1},{1,0},{2,3},{3,2},{4,5},{5,4},{6,7},{7,6},{8,9},{9,8},{10,11... | collective-permute-start | bytes 1966088 | tf_op jit(solution)/shard_map/ppermute | solution.py:101
  (16 other events, 35.7 us)

commit v13 on v12

--- a/solution.py
+++ b/solution.py
@@ -113,15 +113,33 @@
     return lax.dynamic_slice(blocks, (chip, core, 0, 0), (1, 1, rows, width))[0, 0]
 
 
-def owned_rows(partial_value):
+def owned_rows(mixed, out_weight, residual):
     chips, cores = lax.axis_size("head_chip"), lax.axis_size("head_core")
+    own_width = residual.shape[1]
+    index = lax.axis_index("head_chip") * cores + lax.axis_index("head_core")
+    own_block = jnp.arange(out_weight.shape[1]) // own_width == index
+    repeats = out_weight.shape[1] // own_width
+
+    def partial_of(rows, extra):
+        value = jnp.dot(rows, out_weight, preferred_element_type=jnp.float32)
+        spread = jnp.tile(extra.astype(jnp.float32), (1, repeats))
+        return value + jnp.where(own_block[None, :], spread, 0.0)
+
     if chips != 2 or cores != 2:
-        return lax.psum_scatter(partial_value, ("head_chip", "head_core"), scatter_dimension=0, tiled=True)
+        return lax.psum_scatter(
+            partial_of(mixed, residual), ("head_chip", "head_core"), scatter_dimension=0, tiled=True
+        )
     chip, core = lax.axis_index("head_chip"), lax.axis_index("head_core")
-    blocks = partial_value.reshape(chips, cores, partial_value.shape[0] // 4, -1)
-    far = block_at(blocks, 1 - chip, core) + swapped(block_at(blocks, 1 - chip, 1 - core), "head_core")
+    rows = mixed.shape[0] // 4
+    mixed4 = mixed.reshape(chips, cores, rows, -1)
+    residual4 = residual.reshape(chips, cores, rows, -1)
+
+    def part(at_chip, at_core):
+        return partial_of(block_at(mixed4, at_chip, at_core), block_at(residual4, at_chip, at_core))
+
+    far = part(1 - chip, core) + swapped(part(1 - chip, 1 - core), "head_core")
     arrived = swapped(far, "head_chip")
-    near = block_at(blocks, chip, core) + swapped(block_at(blocks, chip, 1 - core), "head_core")
+    near = part(chip, core) + swapped(part(chip, 1 - core), "head_core")
     return near + arrived
 
 
@@ -184,12 +202,7 @@
     grouped = gated.reshape(tokens, NORM_GROUPS // (lax.axis_size("head_chip") * lax.axis_size("head_core")), -1)
     scaled = grouped * lax.rsqrt(jnp.mean(grouped * grouped, axis=2, keepdims=True) + epsilon)
     mixed = (scaled.reshape(tokens, -1) * norm_gain[None, :]).astype(jnp.bfloat16)
-    own_width = residual.shape[1]
-    own_block = jnp.arange(out_weight.shape[1]) // own_width == (lax.axis_index("head_chip") * lax.axis_size("head_core") + lax.axis_index("head_core"))
-    spread = jnp.tile(residual.astype(jnp.float32), (1, out_weight.shape[1] // own_width))
-    partial_value = jnp.dot(mixed, out_weight, preferred_element_type=jnp.float32)
-    partial_value = partial_value + jnp.where(own_block[None, :], spread, 0.0)
-    encoded = owned_rows(partial_value)
+    encoded = owned_rows(mixed, out_weight, residual)
     normed = (
         encoded
         * lax.rsqrt(jnp.mean(encoded * encoded, axis=1, keepdims=True) + epsilon)

time: 139 us -> 133 us (0.957)
  waiting for transfers between devices: 46.5 us -> 41.1 us
    ppermute x6, waiting for transfers between devices: 43.6 us -> 38.5 us  [swapped(): lax.ppermute(value, axis, [(source, count - 1 - source) for source in ran...]
    reshape x0 -> x1, local copies, waits for them, and re-layouts: none -> 2.8 us  [per_device(): scaled.reshape(tokens, -1) * norm_gain[None, :]]
    convert_element_type x0 -> x2, other arithmetic: none -> 2.6 us  [the longest x1 1.51 us: per_device(): (scaled.reshape(tokens, -1) * norm_gain[None, :]).astype(jnp.bfloat16)]
    add x1 -> x0, other arithmetic: 1.85 us -> none  [owned_rows(): block_at(blocks, 1 - chip, core)]
    squeeze x1 -> x0, local copies, waits for them, and re-layouts: 1.83 us -> none  [block_at(): lax.dynamic_slice(blocks, (chip, core, 0, 0), (1, 1, rows, width))[0, 0]]
    reduce_sum x1 -> x0, other arithmetic: 1.73 us -> none  [per_device(): jnp.mean(encoded * encoded, axis=1, keepdims=True) + epsilon]
    unnamed x60 -> x73, local copies, waits for them, and re-layouts: 10 us -> 9.24 us
    dot_general x1 -> x4, matrix products: 2.32 us -> 3.02 us  [partial_of(): value = jnp.dot(rows, out_weight, preferred_element_type=jnp.float32)]
  transfers between devices with their start and end apart: 12 -> 12, of which waited for: 6 -> 5; matrix products, arithmetic and copies ran while one was open for 26% -> 25% of each run, Pallas kernels for 0% -> 0%
where the time goes in v13:
time: 133 us; the launch traced here: 132 us
  waiting for transfers between devices  41.1 us (31%)
  matrix products  25.2 us (19%)
  local copies, waits for them, and re-layouts  22.8 us (17%)
  starting transfers between devices  22.4 us (17%)
  other arithmetic  19.4 us (15%)
    ppermute x6, waiting for transfers between devices, swapped(): lax.ppermute(value, axis, [(source, count - 1 - source) for source in ran...  38.5 us
    ppermute x6, starting transfers between devices, passed_along(): lax.ppermute(value, axis, [(source, source + steps) for source in range(f...  18.9 us
    unnamed x73, local copies, waits for them, and re-layouts  9.24 us
    add x6, other arithmetic, relay(): entering = passed_along(gain[:, None, None] * entering + state, axis, steps)  6.07 us
    dot_general x2, matrix products, block_parts(): jnp.einsum('bhts,bshp->bthp', weights, acts_b, preferred_element_type=jnp...  5.25 us
    dot_general x4, matrix products, project(): jnp.dot(rows, value_weight, preferred_element_type=jnp.float32)  5.05 us
    dot_general x4, matrix products, project(): jnp.dot(rows, key_weight, preferred_element_type=jnp.float32)  4.36 us
    dot_general x2, matrix products, direction_out(): jnp.einsum('btn,bhpn->bthp', reads_b, block_states, precision=highest)  3.7 us
  transfers between devices with their start and end apart: 12, of which 5 were waited for; matrix products, arithmetic and copies ran while one was open for 25% of the time, Pallas kernels for 0%

profile of v13, /device:TPU:0, one launch (start us, length us, event | category | flops | bytes accessed | tf_op | source)
XLA Modules:
  0.0 132.2 jit_solution(18394640341722996623)
XLA Ops:
  5.2 1.4 %bitcast_exponential_fusion = (f32[2,256,10]{1,2,0:T(8,128)}, f32[2,256,10]{1,2,0:T(8,128)S(1)}, f32[2,10,256]{2,1,0:T(8,128)}, f32[2,10,256]{2,1,0:T(8,128)}, f...) fusion(f32[2,10,256]{2,1,0:T(8,128)S(1)} %fusion.56, f32[10]{0:T(128)} %param.19, f32[2,256,10]{1,0,2:T(2,128)S(1)} %squeeze.53, ...), kind=kLoop, calls=%fused_computation.166 | loop fusion | flops 92160 | bytes 205000 | tf_op jit(solution)/shard_map/exp | solution.py:95
  7.8 2.2 %copy.32 = bf16[512,640]{0,1:T(8,128)(2,1)} copy(bf16[512,640]{1,0:T(8,128)(2,1)} %param.14) | data formatting | bytes 1310720 | tf_op args[0]
  10.1 2.7 %reshape_reshape.4 = bf16[2,256,10,64]{1,0,3,2:T(2,128)(2,1)} reshape(bf16[512,640]{0,1:T(8,128)(2,1)} %copy.32) | data formatting | bytes 1310720 | tf_op jit(solution)/shard_map/reshape;reshape | solution.py:25
  12.8 2.3 %convert_multiply_fusion.1 = (f32[2,256,10,64]{1,0,3,2:T(2,128)S(1)}, f32[2,256,10,64]{1,0,3,2:T(2,128)S(1)}) fusion(bf16[2,256,10,64]{1,0,3,2:T(2,128)(2,1)} %reshape_reshape.4, f32[2,256,10]{1,0,2:T(2,128)} %copy.38, f32[2,256,10]{1,0,2:T(2,128)} %copy.34), kind=kLoop, calls=%fused_computation.25 | loop fusion | flops 983040 | bytes 3317760 | tf_op jit(solution)/shard_map/mul | solution.py:48
  19.8 6.4 %collective-permute-start = (f32[10,64,128]{2,1,0:T(8,128)}, f32[10,64,128]{2,1,0:T(8,128)}, u32[]{:S(2)}, u32[]{:S(2)}) collective-permute-start(f32[10,64,128]{2,1,0:T(8,128)} %get-tuple-element.10), channel_id=1, source_target_pairs={{0,4},{4,8},{8,12},{1,5},{5,9},{9,13},{2,6},{6,10},{10,14},{3,7},{... | collective-permute-start | bytes 983048 | tf_op jit(solution)/shard_map/ppermute | solution.py:19
  26.8 2.6 %fusion.18 = f32[2,256,10,64]{1,3,2,0:T(8,128)} fusion(f32[2,10,256]{2,1,0:T(8,128)S(1)} %copy-done.26, f32[2,10,256]{2,1,0:T(8,128)S(1)} %copy-done.24, f32[2,256,256]{2,1,0:T(8,128)S(1)} %fusion.105, pred[256,256]{1,0:T(8,128)(4,1)S(1)} %iota_compare_fusion.1, bf16[2,256,10,64]{1,0,3,2:T(2,128)(2,1)S(1)} %copy-done.7), kind=kOutput, calls=%fused_computation.28 | convolution fusion | flops 174325760 | bytes 2596864 | tf_op jit(solution)/shard_map/bhts,bshp->bthp/dot_general | solution.py:46
  29.5 2.6 %fusion.17 = f32[2,256,10,64]{1,3,2,0:T(8,128)} fusion(f32[2,10,256]{2,1,0:T(8,128)S(1)} %copy-done.25, f32[2,10,256]{2,1,0:T(8,128)S(1)} %copy-done.22, f32[2,256,256]{2,1,0:T(8,128)S(1)} %fusion.106, pred[256,256]{1,0:T(8,128)(4,1)S(1)} %iota_compare_fusion, bf16[2,256,10,64]{1,0,3,2:T(2,128)(2,1)S(1)} %copy-done.7), kind=kOutput, calls=%fused_computation.27 | convolution fusion | flops 174325760 | bytes 2596864 | tf_op jit(solution)/shard_map/bhts,bshp->bthp/dot_general | solution.py:46
  35.0 3.3 %collective-permute-start.1 = (f32[10,64,128]{2,1,0:T(8,128)S(1)}, f32[10,64,128]{2,1,0:T(8,128)S(1)}, u32[]{:S(2)}, u32[]{:S(2)}) collective-permute-start(f32[10,64,128]{2,1,0:T(8,128)S(1)} %multiply_add_fusion.3), channel_id=1, source_target_pairs={{0,4},{4,8},{8,12},{1,5},{5,9},{9,13},{2,6},{6,10},{10,14},{3,7},{... | collective-permute-start | bytes 983048 | tf_op jit(solution)/shard_map/ppermute | solution.py:19
  42.0 2.6 %collective-permute-done.1 = f32[10,64,128]{2,1,0:T(8,128)S(1)} collective-permute-done((f32[10,64,128]{2,1,0:T(8,128)S(1)}, f32[10,64,128]{2,1,0:T(8,128)S(1)}, u32[]{:S(2)}, u32[]{:S(2)}) %collective-permute-start.1) | collective-permute-done | bytes 327712 | tf_op jit(solution)/shard_map/ppermute | solution.py:19
  45.5 5.1 %collective-permute-start.2 = (f32[10,64,128]{2,1,0:T(8,128)}, f32[10,64,128]{2,1,0:T(8,128)}, u32[]{:S(2)}, u32[]{:S(2)}) collective-permute-start(f32[10,64,128]{2,1,0:T(8,128)} %multiply_add_fusion.2), channel_id=1, source_target_pairs={{0,4},{4,8},{8,12},{1,5},{5,9},{9,13},{2,6},{6,10},{10,14},{3,7},{... | collective-permute-start | bytes 983048 | tf_op jit(solution)/shard_map/ppermute | solution.py:19
  51.4 1.5 %collective-permute-start.5 = (f32[10,64,128]{2,1,0:T(8,128)}, f32[10,64,128]{2,1,0:T(8,128)}, u32[]{:S(2)}, u32[]{:S(2)}) collective-permute-start(f32[10,64,128]{2,1,0:T(8,128)} %multiply_add_fusion), channel_id=1, source_target_pairs={{4,0},{8,4},{12,8},{5,1},{9,5},{13,9},{6,2},{10,6},{14,10},{7,3},{... | collective-permute-start | bytes 983048 | tf_op jit(solution)/shard_map/ppermute | solution.py:19
  54.0 2.2 %copy.42 = bf16[512,640]{0,1:T(8,128)(2,1)} copy(bf16[512,640]{1,0:T(8,128)(2,1)} %param.15) | data formatting | bytes 1310720 | tf_op args[1]
  60.1 1.9 %fusion.23 = f32[2,256,10,64]{1,3,2,0:T(8,128)S(1)} fusion(f32[2,256,10,64]{1,3,2,0:T(8,128)S(1)} %copy-done.9, bf16[2,256,128,1]{2,1,3,0:T(8,128)(2,1)S(1)} %bitcast.201, f32[1,10,64,128]{3,2,1,0:T(8,128)S(1)} %copy-done.10, f32[2,256,10]{1,2,0:T(8,128)S(1)} %copy-done.19, f32[10,64,128]{2,1,0:T(8,128)} %collective-permute-done.2, f32[2,10]{1,0:T(2,128)S(1)} %copy-done.28), kind=kOutput, calls=%fused_computation.35 | convolution fusion | flops 504299520 | bytes 3428432 | tf_op jit(solution)/shard_map/btn,bhpn->bthp/dot_general | solution.py:94
  62.0 1.8 %fusion.21 = f32[2,256,10,64]{1,3,2,0:T(8,128)S(1)} fusion(f32[2,256,10,64]{1,3,2,0:T(8,128)S(1)} %fusion.23, f32[2,256,10,64]{1,3,2,0:T(8,128)S(1)} %copy-done.11, bf16[2,256,128,1]{2,1,3,0:T(8,128)(2,1)S(1)} %bitcast.207, f32[1,10,64,128]{3,2,1,0:T(8,128)S(1)} %copy-done.15, f32[2,256,10]{1,2,0:T(8,128)S(1)} %copy-done.20, ...), kind=kOutput, calls=%fused_computation.32 | convolution fusion | flops 504627200 | bytes 4739152 | tf_op jit(solution)/shard_map/btn,bhpn->bthp/dot_general | solution.py:94
  68.0 2.8 %copy.48 = f32[512,640]{1,0:T(8,128)} copy(f32[512,640]{0,1:T(8,128)} %broadcast_multiply_fusion) | data formatting | bytes 2621440 | tf_op jit(solution)/shard_map/reshape | solution.py:204
  70.8 1.5 %multiply_convert_fusion.9 = bf16[2,2,128,640]{3,2,1,0:T(8,128)(2,1)S(1)} fusion(f32[2,2,128,640]{3,2,1,0:T(8,128)} %bitcast.193, f32[640]{0:T(1024)S(1)} %copy-done.29), kind=kLoop, calls=%fused_computation.46 | loop fusion | flops 655360 | bytes 1968640 | tf_op jit(solution)/shard_map/convert_element_type | solution.py:204
  77.1 1.6 %collective-permute-start.8 = (f32[128,2560]{1,0:T(8,128)S(1)}, f32[128,2560]{1,0:T(8,128)S(1)}, u32[]{:S(2)}, u32[]{:S(2)}) collective-permute-start(f32[128,2560]{1,0:T(8,128)S(1)} %fusion), channel_id=1, source_target_pairs={{0,2},{2,0},{1,3},{3,1},{4,6},{6,4},{5,7},{7,5},{8,10},{10,8},{9,1... | collective-permute-start | bytes 3932168 | tf_op jit(solution)/shard_map/ppermute | solution.py:101
  79.0 29.0 %collective-permute-done.8 = f32[128,2560]{1,0:T(8,128)S(1)} collective-permute-done((f32[128,2560]{1,0:T(8,128)S(1)}, f32[128,2560]{1,0:T(8,128)S(1)}, u32[]{:S(2)}, u32[]{:S(2)}) %collective-permute-start.8) | collective-permute-done | bytes 1310752 | tf_op jit(solution)/shard_map/ppermute | solution.py:101
  109.9 1.5 %collective-permute-start.9 = (bf16[128,2560]{1,0:T(8,128)(2,1)}, bf16[128,2560]{1,0:T(8,128)(2,1)S(1)}, u32[]{:S(2)}, u32[]{:S(2)}) collective-permute-start(bf16[128,2560]{1,0:T(8,128)(2,1)} %multiply_convert_fusion.8), channel_id=1, source_target_pairs={{0,2},{2,0},{1,3},{3,1},{4,6},{6,4},{5,7},{7,5},{8,10},{10,8},{9,1... | collective-permute-start | bytes 1966088 | tf_op jit(solution)/shard_map/ppermute | solution.py:101
  111.4 2.5 %fusion.39 = bf16[1,1,128,512]{3,2,1,0:T(8,128)(2,1)S(1)} fusion(bf16[128,2560]{1,0:T(8,128)(2,1)} %multiply_convert_fusion.8, bf16[2560,512]{1,0:T(8,128)(2,1)} %param.27), kind=kOutput, calls=%fused_computation.63 | convolution fusion | flops 335609856 | bytes 3407872 | tf_op jit(solution)/shard_map/dot_general | solution.py:150
  113.9 1.7 %fusion.35 = bf16[1,1,128,512]{3,2,1,0:T(8,128)(2,1)S(1)} fusion(bf16[128,2560]{1,0:T(8,128)(2,1)} %multiply_convert_fusion.8, bf16[2560,512]{1,0:T(8,128)(2,1)S(1)} %copy-done.2), kind=kOutput, calls=%fused_computation.59 | convolution fusion | flops 335609856 | bytes 3407872 | tf_op jit(solution)/shard_map/dot_general | solution.py:149
  115.8 1.6 %fusion.38 = bf16[1,1,128,512]{3,2,1,0:T(8,128)(2,1)S(1)} fusion(bf16[128,2560]{1,0:T(8,128)(2,1)} %collective-permute-done.11, bf16[2560,512]{1,0:T(8,128)(2,1)S(1)} %copy-done.1), kind=kOutput, calls=%fused_computation.62 | convolution fusion | flops 335609856 | bytes 3407872 | tf_op jit(solution)/shard_map/dot_general | solution.py:150
  117.4 1.6 %fusion.34 = bf16[1,1,128,512]{3,2,1,0:T(8,128)(2,1)S(1)} fusion(bf16[128,2560]{1,0:T(8,128)(2,1)} %collective-permute-done.11, bf16[2560,512]{1,0:T(8,128)(2,1)S(1)} %copy-done.2), kind=kOutput, calls=%fused_computation.58 | convolution fusion | flops 335609856 | bytes 3407872 | tf_op jit(solution)/shard_map/dot_general | solution.py:149
  119.0 8.2 %collective-permute-done.9 = bf16[128,2560]{1,0:T(8,128)(2,1)S(1)} collective-permute-done((bf16[128,2560]{1,0:T(8,128)(2,1)}, bf16[128,2560]{1,0:T(8,128)(2,1)S(1)}, u32[]{:S(2)}, u32[]{:S(2)}) %collective-permute-start.9) | collective-permute-done | bytes 655392 | tf_op jit(solution)/shard_map/ppermute | solution.py:101
  (148 shorter events, 40.3 us)
Async XLA Ops:
  0.6 71.7 %copy-start = (bf16[640,2560]{1,0:T(8,128)(2,1)S(1)}, bf16[640,2560]{1,0:T(8,128)(2,1)}, u32[]{:S(2)}) copy-start(bf16[640,2560]{1,0:T(8,128)(2,1)} %param.23) | copy-start | bytes 9830404
  3.3 3.9 %copy-start.21 = (f32[2,10,256]{2,1,0:T(8,128)}, f32[2,10,256]{2,1,0:T(8,128)S(1)}, u32[]{:S(2)}) copy-start(f32[2,10,256]{2,1,0:T(8,128)S(1)} %fusion.56) | copy-start | bytes 61444
  7.8 4.9 %copy-start.17 = (bf16[2,512,128]{2,1,0:T(8,128)(2,1)S(1)}, bf16[2,512,128]{2,1,0:T(8,128)(2,1)}, u32[]{:S(2)}) copy-start(bf16[2,512,128]{2,1,0:T(8,128)(2,1)} %param.16) | copy-start | bytes 786436
  16.8 21.6 %collective-permute-start.3 = (f32[10,64,128]{2,1,0:T(8,128)}, f32[10,64,128]{2,1,0:T(8,128)}, u32[]{:S(2)}, u32[]{:S(2)}) collective-permute-start(f32[10,64,128]{2,1,0:T(8,128)} %get-tuple-element.6), channel_id=1, source_target_pairs={{4,0},{8,4},{12,8},{5,1},{9,5},{13,9},{6,2},{10,6},{14,10},{7,3},{... | collective-permute-start | bytes 983048 | tf_op jit(solution)/shard_map/ppermute | solution.py:19
  18.1 8.2 %copy-start.18 = (bf16[2,512,128]{2,1,0:T(8,128)(2,1)S(1)}, bf16[2,512,128]{2,1,0:T(8,128)(2,1)}, u32[]{:S(2)}) copy-start(bf16[2,512,128]{2,1,0:T(8,128)(2,1)} %param.17) | copy-start | bytes 786436
  19.8 7.0 %copy-start.7 = (bf16[2,256,10,64]{1,0,3,2:T(2,128)(2,1)S(1)}, bf16[2,256,10,64]{1,0,3,2:T(2,128)(2,1)}, u32[]{:S(2)}) copy-start(bf16[2,256,10,64]{1,0,3,2:T(2,128)(2,1)} %reshape_reshape.4) | copy-start | bytes 1966084
  19.8 7.0 %copy-start.24 = (f32[2,10,256]{2,1,0:T(8,128)S(1)}, f32[2,10,256]{2,1,0:T(8,128)}, u32[]{:S(2)}) copy-start(f32[2,10,256]{2,1,0:T(8,128)} %copy-done.23) | copy-start | bytes 61444
  19.8 7.0 %copy-start.26 = (f32[2,10,256]{2,1,0:T(8,128)S(1)}, f32[2,10,256]{2,1,0:T(8,128)}, u32[]{:S(2)}) copy-start(f32[2,10,256]{2,1,0:T(8,128)} %get-tuple-element.38) | copy-start | bytes 61444
  19.8 14.0 %collective-permute-start = (f32[10,64,128]{2,1,0:T(8,128)}, f32[10,64,128]{2,1,0:T(8,128)}, u32[]{:S(2)}, u32[]{:S(2)}) collective-permute-start(f32[10,64,128]{2,1,0:T(8,128)} %get-tuple-element.10), channel_id=1, source_target_pairs={{0,4},{4,8},{8,12},{1,5},{5,9},{9,13},{2,6},{6,10},{10,14},{3,7},{... | collective-permute-start | bytes 983048 | tf_op jit(solution)/shard_map/ppermute | solution.py:19
  33.7 7.1 %copy-start.16 = (bf16[512,640]{1,0:T(8,128)(2,1)S(1)}, bf16[512,640]{1,0:T(8,128)(2,1)}, u32[]{:S(2)}) copy-start(bf16[512,640]{1,0:T(8,128)(2,1)} %param.24) | copy-start | bytes 1966084
  35.0 9.6 %collective-permute-start.1 = (f32[10,64,128]{2,1,0:T(8,128)S(1)}, f32[10,64,128]{2,1,0:T(8,128)S(1)}, u32[]{:S(2)}, u32[]{:S(2)}) collective-permute-start(f32[10,64,128]{2,1,0:T(8,128)S(1)} %multiply_add_fusion.3), channel_id=1, source_target_pairs={{0,4},{4,8},{8,12},{1,5},{5,9},{9,13},{2,6},{6,10},{10,14},{3,7},{... | collective-permute-start | bytes 983048 | tf_op jit(solution)/shard_map/ppermute | solution.py:19
  38.4 6.2 %copy-start.6 = (f32[10,64,128]{2,1,0:T(8,128)S(1)}, f32[10,64,128]{2,1,0:T(8,128)}, u32[]{:S(2)}) copy-start(f32[10,64,128]{2,1,0:T(8,128)} %get-tuple-element.11) | copy-start | bytes 983044
  39.6 11.0 %collective-permute-start.4 = (f32[10,64,128]{2,1,0:T(8,128)S(1)}, f32[10,64,128]{2,1,0:T(8,128)S(1)}, u32[]{:S(2)}, u32[]{:S(2)}) collective-permute-start(f32[10,64,128]{2,1,0:T(8,128)S(1)} %multiply_add_fusion.1), channel_id=1, source_target_pairs={{4,0},{8,4},{12,8},{5,1},{9,5},{13,9},{6,2},{10,6},{14,10},{7,3},{... | collective-permute-start | bytes 983048 | tf_op jit(solution)/shard_map/ppermute | solution.py:19
  40.9 9.7 %copy-start.5 = (f32[10,64,128]{2,1,0:T(8,128)S(1)}, f32[10,64,128]{2,1,0:T(8,128)}, u32[]{:S(2)}) copy-start(f32[10,64,128]{2,1,0:T(8,128)} %get-tuple-element.7) | copy-start | bytes 983044
  42.0 11.5 %copy-start.32 = (f32[1,10]{1,0:T(1,128)S(1)}, f32[1,10]{1,0:T(1,128)}, u32[]{:S(2)}) copy-start(f32[1,10]{1,0:T(1,128)} %get-tuple-element.30) | copy-start | bytes 124
  45.5 14.0 %collective-permute-start.2 = (f32[10,64,128]{2,1,0:T(8,128)}, f32[10,64,128]{2,1,0:T(8,128)}, u32[]{:S(2)}, u32[]{:S(2)}) collective-permute-start(f32[10,64,128]{2,1,0:T(8,128)} %multiply_add_fusion.2), channel_id=1, source_target_pairs={{0,4},{4,8},{8,12},{1,5},{5,9},{9,13},{2,6},{6,10},{10,14},{3,7},{... | collective-permute-start | bytes 983048 | tf_op jit(solution)/shard_map/ppermute | solution.py:19
  51.4 10.6 %collective-permute-start.5 = (f32[10,64,128]{2,1,0:T(8,128)}, f32[10,64,128]{2,1,0:T(8,128)}, u32[]{:S(2)}, u32[]{:S(2)}) collective-permute-start(f32[10,64,128]{2,1,0:T(8,128)} %multiply_add_fusion), channel_id=1, source_target_pairs={{4,0},{8,4},{12,8},{5,1},{9,5},{13,9},{6,2},{10,6},{14,10},{7,3},{... | collective-permute-start | bytes 983048 | tf_op jit(solution)/shard_map/ppermute | solution.py:19
  73.2 3.1 %collective-permute-start.7 = (f32[128,2560]{1,0:T(8,128)S(1)}, f32[128,2560]{1,0:T(8,128)S(1)}, u32[]{:S(2)}, u32[]{:S(2)}) collective-permute-start(f32[128,2560]{1,0:T(8,128)S(1)} %convolution_add_fusion), channel_id=1, source_target_pairs={{0,1},{1,0},{2,3},{3,2},{4,5},{5,4},{6,7},{7,6},{8,9},{9,8},{10,11... | collective-permute-start | bytes 3932168 | tf_op jit(solution)/shard_map/ppermute | solution.py:101
  75.7 3.2 %collective-permute-start.6 = (f32[128,2560]{1,0:T(8,128)S(1)}, f32[128,2560]{1,0:T(8,128)S(1)}, u32[]{:S(2)}, u32[]{:S(2)}) collective-permute-start(f32[128,2560]{1,0:T(8,128)S(1)} %convolution_add_fusion.2), channel_id=1, source_target_pairs={{0,1},{1,0},{2,3},{3,2},{4,5},{5,4},{6,7},{7,6},{8,9},{9,8},{10,11... | collective-permute-start | bytes 3932168 | tf_op jit(solution)/shard_map/ppermute | solution.py:101
  77.1 30.9 %collective-permute-start.8 = (f32[128,2560]{1,0:T(8,128)S(1)}, f32[128,2560]{1,0:T(8,128)S(1)}, u32[]{:S(2)}, u32[]{:S(2)}) collective-permute-start(f32[128,2560]{1,0:T(8,128)S(1)} %fusion), channel_id=1, source_target_pairs={{0,2},{2,0},{1,3},{3,1},{4,6},{6,4},{5,7},{7,5},{8,10},{10,8},{9,1... | collective-permute-start | bytes 3932168 | tf_op jit(solution)/shard_map/ppermute | solution.py:101
  109.9 5.7 %collective-permute-start.11 = (bf16[128,2560]{1,0:T(8,128)(2,1)}, bf16[128,2560]{1,0:T(8,128)(2,1)}, u32[]{:S(2)}, u32[]{:S(2)}) collective-permute-start(bf16[128,2560]{1,0:T(8,128)(2,1)} %multiply_convert_fusion.8), channel_id=1, source_target_pairs={{0,1},{1,0},{2,3},{3,2},{4,5},{5,4},{6,7},{7,6},{8,9},{9,8},{10,11... | collective-permute-start | bytes 1966088 | tf_op jit(solution)/shard_map/ppermute | solution.py:101
  109.9 4.0 %copy-start.2 = (bf16[2560,512]{1,0:T(8,128)(2,1)S(1)}, bf16[2560,512]{1,0:T(8,128)(2,1)}, u32[]{:S(2)}) copy-start(bf16[2560,512]{1,0:T(8,128)(2,1)} %param.26) | copy-start | bytes 7864324
  109.9 17.4 %collective-permute-start.9 = (bf16[128,2560]{1,0:T(8,128)(2,1)}, bf16[128,2560]{1,0:T(8,128)(2,1)S(1)}, u32[]{:S(2)}, u32[]{:S(2)}) collective-permute-start(bf16[128,2560]{1,0:T(8,128)(2,1)} %multiply_convert_fusion.8), channel_id=1, source_target_pairs={{0,2},{2,0},{1,3},{3,1},{4,6},{6,4},{5,7},{7,5},{8,10},{10,8},{9,1... | collective-permute-start | bytes 1966088 | tf_op jit(solution)/shard_map/ppermute | solution.py:101
  127.2 2.1 %collective-permute-start.10 = (bf16[128,2560]{1,0:T(8,128)(2,1)S(1)}, bf16[128,2560]{1,0:T(8,128)(2,1)S(1)}, u32[]{:S(2)}, u32[]{:S(2)}) collective-permute-start(bf16[128,2560]{1,0:T(8,128)(2,1)S(1)} %collective-permute-done.9), channel_id=1, source_target_pairs={{0,1},{1,0},{2,3},{3,2},{4,5},{5,4},{6,7},{7,6},{8,9},{9,8},{10,11... | collective-permute-start | bytes 1966088 | tf_op jit(solution)/shard_map/ppermute | solution.py:101
  (21 other events, 37.1 us)

commit v14 on v13

--- a/solution.py
+++ b/solution.py
@@ -1,6 +1,7 @@
 import jax
 import jax.numpy as jnp
 from jax import lax
+from jax.experimental.layout import Layout, with_layout_constraint
 from jax.sharding import Mesh, PartitionSpec as P
 
 STRETCH = 256
@@ -198,7 +199,8 @@
         acts, write_map[1], read_map[1], steps_bwd, steps_bwd * decay_rate[None, :], True, "seq"
     )
     summed = fwd_all + bwd_all + skip_gain[None, :, None] * acts.astype(jnp.float32)
-    gated = summed.reshape(tokens, heads * width) * jax.nn.silu(gate_acts.astype(jnp.float32))
+    summed = with_layout_constraint(summed.reshape(tokens, heads * width), Layout((0, 1)))
+    gated = summed * jax.nn.silu(gate_acts.astype(jnp.float32))
     grouped = gated.reshape(tokens, NORM_GROUPS // (lax.axis_size("head_chip") * lax.axis_size("head_core")), -1)
     scaled = grouped * lax.rsqrt(jnp.mean(grouped * grouped, axis=2, keepdims=True) + epsilon)
     mixed = (scaled.reshape(tokens, -1) * norm_gain[None, :]).astype(jnp.bfloat16)

time: 133 us -> 132 us (level)
  waiting for transfers between devices: 41.1 us -> 43.6 us
  local copies, waits for them, and re-layouts: 22.8 us -> 20.9 us
    reshape x1 -> x0, local copies, waits for them, and re-layouts: 2.8 us -> none  [per_device(): scaled.reshape(tokens, -1) * norm_gain[None, :]]
    add x1 -> x2, local copies, waits for them, and re-layouts: 1.01 us -> 3.81 us  [per_device(): fwd_all + bwd_all + skip_gain[None, :, None] * acts.astype(jnp.float32)]
    ppermute x6, waiting for transfers between devices: 2.59 us -> 4.96 us  [passed_along(): lax.ppermute(value, axis, [(source, source + steps) for source in range(f...]
    reduce_sum x1, other arithmetic: 0.57 us -> 2.27 us  [per_device(): jnp.mean(grouped * grouped, axis=2, keepdims=True) + epsilon]
    convert_element_type x1, other arithmetic: 1.51 us -> 0.09 us  [per_device(): (scaled.reshape(tokens, -1) * norm_gain[None, :]).astype(jnp.bfloat16)]
    unnamed x73 -> x70, local copies, waits for them, and re-layouts: 9.24 us -> 8 us
  transfers between devices with their start and end apart: 12 -> 12, of which waited for: 5 -> 6; matrix products, arithmetic and copies ran while one was open for 25% -> 23% of each run, Pallas kernels for 0% -> 0%
where the time goes in v14:
time: 132 us; the launch traced here: 131 us
  waiting for transfers between devices  43.6 us (33%)
  matrix products  25.1 us (19%)
  starting transfers between devices  22.3 us (17%)
  local copies, waits for them, and re-layouts  20.9 us (16%)
  other arithmetic  18.2 us (14%)
    ppermute x6, waiting for transfers between devices, swapped(): lax.ppermute(value, axis, [(source, count - 1 - source) for source in ran...  38.6 us
    ppermute x6, starting transfers between devices, passed_along(): lax.ppermute(value, axis, [(source, source + steps) for source in range(f...  18.9 us
    unnamed x70, local copies, waits for them, and re-layouts  8 us
    add x6, other arithmetic, relay(): entering = passed_along(gain[:, None, None] * entering + state, axis, steps)  6.05 us
    dot_general x2, matrix products, block_parts(): jnp.einsum('bhts,bshp->bthp', weights, acts_b, preferred_element_type=jnp...  5.22 us
    dot_general x4, matrix products, project(): jnp.dot(rows, value_weight, preferred_element_type=jnp.float32)  5.05 us
    ppermute x6, waiting for transfers between devices, passed_along(): lax.ppermute(value, axis, [(source, source + steps) for source in range(f...  4.96 us
    dot_general x4, matrix products, project(): jnp.dot(rows, key_weight, preferred_element_type=jnp.float32)  4.34 us
  transfers between devices with their start and end apart: 12, of which 6 were waited for; matrix products, arithmetic and copies ran while one was open for 23% of the time, Pallas kernels for 0%

profile of v14, /device:TPU:0, one launch (start us, length us, event | category | flops | bytes accessed | tf_op | source)
XLA Modules:
  0.0 131.3 jit_solution(15125271600071711027)
XLA Ops:
  5.2 1.4 %bitcast_exponential_fusion = (f32[2,256,10]{1,2,0:T(8,128)}, f32[2,256,10]{1,2,0:T(8,128)S(1)}, f32[2,10,256]{2,1,0:T(8,128)}, f32[2,10,256]{2,1,0:T(8,128)}, f...) fusion(f32[2,10,256]{2,1,0:T(8,128)S(1)} %fusion.56, f32[10]{0:T(128)} %param.19, f32[2,256,10]{1,0,2:T(2,128)S(1)} %squeeze.53, ...), kind=kLoop, calls=%fused_computation.166 | loop fusion | flops 92160 | bytes 205000 | tf_op jit(solution)/shard_map/exp | solution.py:96
  7.8 2.2 %copy.21 = bf16[512,640]{0,1:T(8,128)(2,1)} copy(bf16[512,640]{1,0:T(8,128)(2,1)} %param.14) | data formatting | bytes 1310720 | tf_op args[0]
  10.1 2.7 %reshape_reshape.4 = bf16[2,256,10,64]{1,0,3,2:T(2,128)(2,1)} reshape(bf16[512,640]{0,1:T(8,128)(2,1)} %copy.21) | data formatting | bytes 1310720 | tf_op jit(solution)/shard_map/reshape;reshape | solution.py:26
  12.8 1.8 %convert_multiply_fusion.1 = (f32[2,256,10,64]{1,0,3,2:T(2,128)S(1)}, f32[2,256,10,64]{1,0,3,2:T(2,128)S(1)}) fusion(bf16[2,256,10,64]{1,0,3,2:T(2,128)(2,1)} %reshape_reshape.4, f32[2,256,10]{1,0,2:T(2,128)} %copy.27, f32[2,256,10]{1,0,2:T(2,128)} %copy.23), kind=kLoop, calls=%fused_computation.25 | loop fusion | flops 983040 | bytes 3317760 | tf_op jit(solution)/shard_map/mul | solution.py:49
  19.4 6.4 %collective-permute-start = (f32[10,64,128]{2,1,0:T(8,128)}, f32[10,64,128]{2,1,0:T(8,128)}, u32[]{:S(2)}, u32[]{:S(2)}) collective-permute-start(f32[10,64,128]{2,1,0:T(8,128)} %get-tuple-element.10), channel_id=1, source_target_pairs={{0,4},{4,8},{8,12},{1,5},{5,9},{9,13},{2,6},{6,10},{10,14},{3,7},{... | collective-permute-start | bytes 983048 | tf_op jit(solution)/shard_map/ppermute | solution.py:20
  26.4 2.6 %fusion.18 = f32[2,256,10,64]{1,3,2,0:T(8,128)} fusion(f32[2,10,256]{2,1,0:T(8,128)S(1)} %copy-done.24, f32[2,10,256]{2,1,0:T(8,128)S(1)} %copy-done.22, f32[2,256,256]{2,1,0:T(8,128)S(1)} %fusion.105, pred[256,256]{1,0:T(8,128)(4,1)S(1)} %iota_compare_fusion.1, bf16[2,256,10,64]{1,0,3,2:T(2,128)(2,1)S(1)} %copy-done.6), kind=kOutput, calls=%fused_computation.28 | convolution fusion | flops 174325760 | bytes 2596864 | tf_op jit(solution)/shard_map/bhts,bshp->bthp/dot_general | solution.py:47
  29.1 2.6 %fusion.17 = f32[2,256,10,64]{1,3,2,0:T(8,128)} fusion(f32[2,10,256]{2,1,0:T(8,128)S(1)} %copy-done.23, f32[2,10,256]{2,1,0:T(8,128)S(1)} %copy-done.20, f32[2,256,256]{2,1,0:T(8,128)S(1)} %fusion.106, pred[256,256]{1,0:T(8,128)(4,1)S(1)} %iota_compare_fusion, bf16[2,256,10,64]{1,0,3,2:T(2,128)(2,1)S(1)} %copy-done.6), kind=kOutput, calls=%fused_computation.27 | convolution fusion | flops 174325760 | bytes 2596864 | tf_op jit(solution)/shard_map/bhts,bshp->bthp/dot_general | solution.py:47
  34.6 3.4 %collective-permute-start.1 = (f32[10,64,128]{2,1,0:T(8,128)S(1)}, f32[10,64,128]{2,1,0:T(8,128)S(1)}, u32[]{:S(2)}, u32[]{:S(2)}) collective-permute-start(f32[10,64,128]{2,1,0:T(8,128)S(1)} %multiply_add_fusion.3), channel_id=1, source_target_pairs={{0,4},{4,8},{8,12},{1,5},{5,9},{9,13},{2,6},{6,10},{10,14},{3,7},{... | collective-permute-start | bytes 983048 | tf_op jit(solution)/shard_map/ppermute | solution.py:20
  41.6 2.5 %collective-permute-done.1 = f32[10,64,128]{2,1,0:T(8,128)S(1)} collective-permute-done((f32[10,64,128]{2,1,0:T(8,128)S(1)}, f32[10,64,128]{2,1,0:T(8,128)S(1)}, u32[]{:S(2)}, u32[]{:S(2)}) %collective-permute-start.1) | collective-permute-done | bytes 327712 | tf_op jit(solution)/shard_map/ppermute | solution.py:20
  45.0 5.1 %collective-permute-start.2 = (f32[10,64,128]{2,1,0:T(8,128)}, f32[10,64,128]{2,1,0:T(8,128)}, u32[]{:S(2)}, u32[]{:S(2)}) collective-permute-start(f32[10,64,128]{2,1,0:T(8,128)} %multiply_add_fusion.2), channel_id=1, source_target_pairs={{0,4},{4,8},{8,12},{1,5},{5,9},{9,13},{2,6},{6,10},{10,14},{3,7},{... | collective-permute-start | bytes 983048 | tf_op jit(solution)/shard_map/ppermute | solution.py:20
  51.0 1.5 %collective-permute-start.5 = (f32[10,64,128]{2,1,0:T(8,128)}, f32[10,64,128]{2,1,0:T(8,128)}, u32[]{:S(2)}, u32[]{:S(2)}) collective-permute-start(f32[10,64,128]{2,1,0:T(8,128)} %multiply_add_fusion), channel_id=1, source_target_pairs={{4,0},{8,4},{12,8},{5,1},{9,5},{13,9},{6,2},{10,6},{14,10},{7,3},{... | collective-permute-start | bytes 983048 | tf_op jit(solution)/shard_map/ppermute | solution.py:20
  56.8 1.9 %fusion.23 = f32[2,256,10,64]{1,3,2,0:T(8,128)S(1)} fusion(f32[2,256,10,64]{1,3,2,0:T(8,128)S(1)} %copy-done.7, bf16[2,256,128,1]{2,1,3,0:T(8,128)(2,1)S(1)} %bitcast.201, f32[1,10,64,128]{3,2,1,0:T(8,128)S(1)} %copy-done.8, f32[2,256,10]{1,2,0:T(8,128)S(1)} %copy-done.17, f32[10,64,128]{2,1,0:T(8,128)} %collective-permute-done.2, f32[2,10]{1,0:T(2,128)S(1)} %copy-done.26), kind=kOutput, calls=%fused_computation.35 | convolution fusion | flops 504299520 | bytes 3428432 | tf_op jit(solution)/shard_map/btn,bhpn->bthp/dot_general | solution.py:95
  58.7 2.4 %collective-permute-done.5 = f32[10,64,128]{2,1,0:T(8,128)} collective-permute-done((f32[10,64,128]{2,1,0:T(8,128)}, f32[10,64,128]{2,1,0:T(8,128)}, u32[]{:S(2)}, u32[]{:S(2)}) %collective-permute-start.5) | collective-permute-done | bytes 327712 | tf_op jit(solution)/shard_map/ppermute | solution.py:20
  61.1 1.8 %fusion.21 = f32[2,256,10,64]{1,3,2,0:T(8,128)S(1)} fusion(f32[2,256,10,64]{1,3,2,0:T(8,128)S(1)} %fusion.23, f32[2,256,10,64]{1,3,2,0:T(8,128)S(1)} %copy-done.9, bf16[2,256,128,1]{2,1,3,0:T(8,128)(2,1)S(1)} %bitcast.207, f32[1,10,64,128]{3,2,1,0:T(8,128)S(1)} %copy-done.13, f32[2,256,10]{1,2,0:T(8,128)S(1)} %copy-done.18, ...), kind=kOutput, calls=%fused_computation.32 | convolution fusion | flops 504627200 | bytes 4739152 | tf_op jit(solution)/shard_map/btn,bhpn->bthp/dot_general | solution.py:95
  65.1 2.8 %copy.30 = f32[512,640]{1,0:T(8,128)} copy(f32[512,640]{0,1:T(8,128)} %bitcast.192) | data formatting | bytes 2621440 | tf_op jit(solution)/shard_map/add | solution.py:201
  67.9 2.3 %multiply_reduce_fusion.1 = (f32[512]{0:T(512)S(1)}, f32[512,640]{1,0:T(8,128)S(1)}) fusion(bf16[512,640]{1,0:T(8,128)(2,1)} %param.15, f32[512,640]{1,0:T(8,128)} %copy.30, bf16[512,640]{1,0:T(8,128)(2,1)} %param.14, f32[640]{0:T(1024)S(1)} %mul.330), kind=kLoop, calls=%fused_computation.47 | loop fusion | flops 3603968 | bytes 3936768 | tf_op jit(solution)/shard_map/reduce_sum | solution.py:205
  76.3 1.5 %collective-permute-start.8 = (f32[128,2560]{1,0:T(8,128)S(1)}, f32[128,2560]{1,0:T(8,128)S(1)}, u32[]{:S(2)}, u32[]{:S(2)}) collective-permute-start(f32[128,2560]{1,0:T(8,128)S(1)} %fusion), channel_id=1, source_target_pairs={{0,2},{2,0},{1,3},{3,1},{4,6},{6,4},{5,7},{7,5},{8,10},{10,8},{9,1... | collective-permute-start | bytes 3932168 | tf_op jit(solution)/shard_map/ppermute | solution.py:102
  78.1 29.1 %collective-permute-done.8 = f32[128,2560]{1,0:T(8,128)S(1)} collective-permute-done((f32[128,2560]{1,0:T(8,128)S(1)}, f32[128,2560]{1,0:T(8,128)S(1)}, u32[]{:S(2)}, u32[]{:S(2)}) %collective-permute-start.8) | collective-permute-done | bytes 1310752 | tf_op jit(solution)/shard_map/ppermute | solution.py:102
  109.1 1.4 %collective-permute-start.9 = (bf16[128,2560]{1,0:T(8,128)(2,1)}, bf16[128,2560]{1,0:T(8,128)(2,1)S(1)}, u32[]{:S(2)}, u32[]{:S(2)}) collective-permute-start(bf16[128,2560]{1,0:T(8,128)(2,1)} %multiply_convert_fusion.8), channel_id=1, source_target_pairs={{0,2},{2,0},{1,3},{3,1},{4,6},{6,4},{5,7},{7,5},{8,10},{10,8},{9,1... | collective-permute-start | bytes 1966088 | tf_op jit(solution)/shard_map/ppermute | solution.py:102
  110.5 2.4 %fusion.39 = bf16[1,1,128,512]{3,2,1,0:T(8,128)(2,1)S(1)} fusion(bf16[128,2560]{1,0:T(8,128)(2,1)} %multiply_convert_fusion.8, bf16[2560,512]{1,0:T(8,128)(2,1)} %param.27), kind=kOutput, calls=%fused_computation.63 | convolution fusion | flops 335609856 | bytes 3407872 | tf_op jit(solution)/shard_map/dot_general | solution.py:151
  113.0 1.7 %fusion.35 = bf16[1,1,128,512]{3,2,1,0:T(8,128)(2,1)S(1)} fusion(bf16[128,2560]{1,0:T(8,128)(2,1)} %multiply_convert_fusion.8, bf16[2560,512]{1,0:T(8,128)(2,1)S(1)} %copy-done.2), kind=kOutput, calls=%fused_computation.59 | convolution fusion | flops 335609856 | bytes 3407872 | tf_op jit(solution)/shard_map/dot_general | solution.py:150
  114.9 1.6 %fusion.38 = bf16[1,1,128,512]{3,2,1,0:T(8,128)(2,1)S(1)} fusion(bf16[128,2560]{1,0:T(8,128)(2,1)} %collective-permute-done.11, bf16[2560,512]{1,0:T(8,128)(2,1)S(1)} %copy-done.1), kind=kOutput, calls=%fused_computation.62 | convolution fusion | flops 335609856 | bytes 3407872 | tf_op jit(solution)/shard_map/dot_general | solution.py:151
  116.5 1.6 %fusion.34 = bf16[1,1,128,512]{3,2,1,0:T(8,128)(2,1)S(1)} fusion(bf16[128,2560]{1,0:T(8,128)(2,1)} %collective-permute-done.11, bf16[2560,512]{1,0:T(8,128)(2,1)S(1)} %copy-done.2), kind=kOutput, calls=%fused_computation.58 | convolution fusion | flops 335609856 | bytes 3407872 | tf_op jit(solution)/shard_map/dot_general | solution.py:150
  118.1 8.3 %collective-permute-done.9 = bf16[128,2560]{1,0:T(8,128)(2,1)S(1)} collective-permute-done((bf16[128,2560]{1,0:T(8,128)(2,1)}, bf16[128,2560]{1,0:T(8,128)(2,1)S(1)}, u32[]{:S(2)}, u32[]{:S(2)}) %collective-permute-start.9) | collective-permute-done | bytes 655392 | tf_op jit(solution)/shard_map/ppermute | solution.py:102
  (145 shorter events, 39.0 us)
Async XLA Ops:
  0.6 70.4 %copy-start = (bf16[640,2560]{1,0:T(8,128)(2,1)S(1)}, bf16[640,2560]{1,0:T(8,128)(2,1)}, u32[]{:S(2)}) copy-start(bf16[640,2560]{1,0:T(8,128)(2,1)} %param.23) | copy-start | bytes 9830404
  7.8 4.9 %copy-start.15 = (bf16[2,512,128]{2,1,0:T(8,128)(2,1)S(1)}, bf16[2,512,128]{2,1,0:T(8,128)(2,1)}, u32[]{:S(2)}) copy-start(bf16[2,512,128]{2,1,0:T(8,128)(2,1)} %param.16) | copy-start | bytes 786436
  16.4 21.6 %collective-permute-start.3 = (f32[10,64,128]{2,1,0:T(8,128)}, f32[10,64,128]{2,1,0:T(8,128)}, u32[]{:S(2)}, u32[]{:S(2)}) collective-permute-start(f32[10,64,128]{2,1,0:T(8,128)} %get-tuple-element.6), channel_id=1, source_target_pairs={{4,0},{8,4},{12,8},{5,1},{9,5},{13,9},{6,2},{10,6},{14,10},{7,3},{... | collective-permute-start | bytes 983048 | tf_op jit(solution)/shard_map/ppermute | solution.py:20
  17.7 8.2 %copy-start.16 = (bf16[2,512,128]{2,1,0:T(8,128)(2,1)S(1)}, bf16[2,512,128]{2,1,0:T(8,128)(2,1)}, u32[]{:S(2)}) copy-start(bf16[2,512,128]{2,1,0:T(8,128)(2,1)} %param.17) | copy-start | bytes 786436
  19.4 7.0 %copy-start.6 = (bf16[2,256,10,64]{1,0,3,2:T(2,128)(2,1)S(1)}, bf16[2,256,10,64]{1,0,3,2:T(2,128)(2,1)}, u32[]{:S(2)}) copy-start(bf16[2,256,10,64]{1,0,3,2:T(2,128)(2,1)} %reshape_reshape.4) | copy-start | bytes 1966084
  19.4 7.0 %copy-start.22 = (f32[2,10,256]{2,1,0:T(8,128)S(1)}, f32[2,10,256]{2,1,0:T(8,128)}, u32[]{:S(2)}) copy-start(f32[2,10,256]{2,1,0:T(8,128)} %copy-done.21) | copy-start | bytes 61444
  19.4 7.0 %copy-start.24 = (f32[2,10,256]{2,1,0:T(8,128)S(1)}, f32[2,10,256]{2,1,0:T(8,128)}, u32[]{:S(2)}) copy-start(f32[2,10,256]{2,1,0:T(8,128)} %get-tuple-element.38) | copy-start | bytes 61444
  19.4 13.9 %collective-permute-start = (f32[10,64,128]{2,1,0:T(8,128)}, f32[10,64,128]{2,1,0:T(8,128)}, u32[]{:S(2)}, u32[]{:S(2)}) collective-permute-start(f32[10,64,128]{2,1,0:T(8,128)} %get-tuple-element.10), channel_id=1, source_target_pairs={{0,4},{4,8},{8,12},{1,5},{5,9},{9,13},{2,6},{6,10},{10,14},{3,7},{... | collective-permute-start | bytes 983048 | tf_op jit(solution)/shard_map/ppermute | solution.py:20
  33.3 7.2 %copy-start.14 = (bf16[512,640]{1,0:T(8,128)(2,1)S(1)}, bf16[512,640]{1,0:T(8,128)(2,1)}, u32[]{:S(2)}) copy-start(bf16[512,640]{1,0:T(8,128)(2,1)} %param.24) | copy-start | bytes 1966084
  34.6 9.6 %collective-permute-start.1 = (f32[10,64,128]{2,1,0:T(8,128)S(1)}, f32[10,64,128]{2,1,0:T(8,128)S(1)}, u32[]{:S(2)}, u32[]{:S(2)}) collective-permute-start(f32[10,64,128]{2,1,0:T(8,128)S(1)} %multiply_add_fusion.3), channel_id=1, source_target_pairs={{0,4},{4,8},{8,12},{1,5},{5,9},{9,13},{2,6},{6,10},{10,14},{3,7},{... | collective-permute-start | bytes 983048 | tf_op jit(solution)/shard_map/ppermute | solution.py:20
  38.0 6.2 %copy-start.5 = (f32[10,64,128]{2,1,0:T(8,128)S(1)}, f32[10,64,128]{2,1,0:T(8,128)}, u32[]{:S(2)}) copy-start(f32[10,64,128]{2,1,0:T(8,128)} %get-tuple-element.11) | copy-start | bytes 983044
  39.2 10.9 %collective-permute-start.4 = (f32[10,64,128]{2,1,0:T(8,128)S(1)}, f32[10,64,128]{2,1,0:T(8,128)S(1)}, u32[]{:S(2)}, u32[]{:S(2)}) collective-permute-start(f32[10,64,128]{2,1,0:T(8,128)S(1)} %multiply_add_fusion.1), channel_id=1, source_target_pairs={{4,0},{8,4},{12,8},{5,1},{9,5},{13,9},{6,2},{10,6},{14,10},{7,3},{... | collective-permute-start | bytes 983048 | tf_op jit(solution)/shard_map/ppermute | solution.py:20
  40.5 9.6 %copy-start.4 = (f32[10,64,128]{2,1,0:T(8,128)S(1)}, f32[10,64,128]{2,1,0:T(8,128)}, u32[]{:S(2)}) copy-start(f32[10,64,128]{2,1,0:T(8,128)} %get-tuple-element.7) | copy-start | bytes 983044
  41.6 11.4 %copy-start.30 = (f32[1,10]{1,0:T(1,128)S(1)}, f32[1,10]{1,0:T(1,128)}, u32[]{:S(2)}) copy-start(f32[1,10]{1,0:T(1,128)} %get-tuple-element.30) | copy-start | bytes 124
  41.6 12.0 %copy-start.31 = (f32[10]{0:T(128)S(1)}, f32[10]{0:T(128)}, u32[]{:S(2)}) copy-start(f32[10]{0:T(128)} %param.21) | copy-start | bytes 124
  45.0 11.1 %collective-permute-start.2 = (f32[10,64,128]{2,1,0:T(8,128)}, f32[10,64,128]{2,1,0:T(8,128)}, u32[]{:S(2)}, u32[]{:S(2)}) collective-permute-start(f32[10,64,128]{2,1,0:T(8,128)} %multiply_add_fusion.2), channel_id=1, source_target_pairs={{0,4},{4,8},{8,12},{1,5},{5,9},{9,13},{2,6},{6,10},{10,14},{3,7},{... | collective-permute-start | bytes 983048 | tf_op jit(solution)/shard_map/ppermute | solution.py:20
  51.0 10.1 %collective-permute-start.5 = (f32[10,64,128]{2,1,0:T(8,128)}, f32[10,64,128]{2,1,0:T(8,128)}, u32[]{:S(2)}, u32[]{:S(2)}) collective-permute-start(f32[10,64,128]{2,1,0:T(8,128)} %multiply_add_fusion), channel_id=1, source_target_pairs={{4,0},{8,4},{12,8},{5,1},{9,5},{13,9},{6,2},{10,6},{14,10},{7,3},{... | collective-permute-start | bytes 983048 | tf_op jit(solution)/shard_map/ppermute | solution.py:20
  56.8 4.3 %copy-start.13 = (f32[1,10,64,128]{3,2,1,0:T(8,128)S(1)}, f32[1,10,64,128]{3,2,1,0:T(8,128)}, u32[]{:S(2)}) copy-start(f32[1,10,64,128]{3,2,1,0:T(8,128)} %slice_add_fusion) | copy-start | bytes 983044
  72.4 3.1 %collective-permute-start.7 = (f32[128,2560]{1,0:T(8,128)S(1)}, f32[128,2560]{1,0:T(8,128)S(1)}, u32[]{:S(2)}, u32[]{:S(2)}) collective-permute-start(f32[128,2560]{1,0:T(8,128)S(1)} %convolution_add_fusion), channel_id=1, source_target_pairs={{0,1},{1,0},{2,3},{3,2},{4,5},{5,4},{6,7},{7,6},{8,9},{9,8},{10,11... | collective-permute-start | bytes 3932168 | tf_op jit(solution)/shard_map/ppermute | solution.py:102
  74.9 3.2 %collective-permute-start.6 = (f32[128,2560]{1,0:T(8,128)S(1)}, f32[128,2560]{1,0:T(8,128)S(1)}, u32[]{:S(2)}, u32[]{:S(2)}) collective-permute-start(f32[128,2560]{1,0:T(8,128)S(1)} %convolution_add_fusion.2), channel_id=1, source_target_pairs={{0,1},{1,0},{2,3},{3,2},{4,5},{5,4},{6,7},{7,6},{8,9},{9,8},{10,11... | collective-permute-start | bytes 3932168 | tf_op jit(solution)/shard_map/ppermute | solution.py:102
  76.3 30.9 %collective-permute-start.8 = (f32[128,2560]{1,0:T(8,128)S(1)}, f32[128,2560]{1,0:T(8,128)S(1)}, u32[]{:S(2)}, u32[]{:S(2)}) collective-permute-start(f32[128,2560]{1,0:T(8,128)S(1)} %fusion), channel_id=1, source_target_pairs={{0,2},{2,0},{1,3},{3,1},{4,6},{6,4},{5,7},{7,5},{8,10},{10,8},{9,1... | collective-permute-start | bytes 3932168 | tf_op jit(solution)/shard_map/ppermute | solution.py:102
  109.0 5.7 %collective-permute-start.11 = (bf16[128,2560]{1,0:T(8,128)(2,1)}, bf16[128,2560]{1,0:T(8,128)(2,1)}, u32[]{:S(2)}, u32[]{:S(2)}) collective-permute-start(bf16[128,2560]{1,0:T(8,128)(2,1)} %multiply_convert_fusion.8), channel_id=1, source_target_pairs={{0,1},{1,0},{2,3},{3,2},{4,5},{5,4},{6,7},{7,6},{8,9},{9,8},{10,11... | collective-permute-start | bytes 1966088 | tf_op jit(solution)/shard_map/ppermute | solution.py:102
  109.1 17.4 %collective-permute-start.9 = (bf16[128,2560]{1,0:T(8,128)(2,1)}, bf16[128,2560]{1,0:T(8,128)(2,1)S(1)}, u32[]{:S(2)}, u32[]{:S(2)}) collective-permute-start(bf16[128,2560]{1,0:T(8,128)(2,1)} %multiply_convert_fusion.8), channel_id=1, source_target_pairs={{0,2},{2,0},{1,3},{3,1},{4,6},{6,4},{5,7},{7,5},{8,10},{10,8},{9,1... | collective-permute-start | bytes 1966088 | tf_op jit(solution)/shard_map/ppermute | solution.py:102
  126.4 2.1 %collective-permute-start.10 = (bf16[128,2560]{1,0:T(8,128)(2,1)S(1)}, bf16[128,2560]{1,0:T(8,128)(2,1)S(1)}, u32[]{:S(2)}, u32[]{:S(2)}) collective-permute-start(bf16[128,2560]{1,0:T(8,128)(2,1)S(1)} %collective-permute-done.9), channel_id=1, source_target_pairs={{0,1},{1,0},{2,3},{3,2},{4,5},{5,4},{6,7},{7,6},{8,9},{9,8},{10,11... | collective-permute-start | bytes 1966088 | tf_op jit(solution)/shard_map/ppermute | solution.py:102
  (20 other events, 45.1 us)

commit v15 on v14

--- a/solution.py
+++ b/solution.py
@@ -45,6 +45,7 @@
         intersection[:, None] * decays * jnp.transpose(steps_b, (0, 2, 1))[:, :, None, :]
     ).astype(jnp.bfloat16)
     within = jnp.einsum("bhts,bshp->bthp", weights, acts_b, preferred_element_type=jnp.float32)
+    within = with_layout_constraint(within, Layout((0, 1, 2, 3)))
     tail = jnp.exp(block_total[:, None, :] - cum_rate) * steps_b
     weighted = acts_b.astype(jnp.float32) * tail[:, :, :, None]
     ends = jnp.einsum(

time: 132 us -> 158 us (1.20)
  other arithmetic: 18.2 us -> 31.2 us
  local copies, waits for them, and re-layouts: 20.9 us -> 32.9 us
    dot_general x0 -> x2, local copies, waits for them, and re-layouts: none -> 9.52 us  [direction_out(): jnp.einsum('btn,bhpn->bthp', reads_b, block_states, precision=highest)]
    add x0 -> x1, other arithmetic: none -> 9.44 us  [per_device(): fwd_all + bwd_all + skip_gain[None, :, None] * acts.astype(jnp.float32)]
    exp x0 -> x2, local copies, waits for them, and re-layouts: none -> 3.2 us  [direction_out(): outputs = within + jnp.exp(cum_rate)[:, :, :, None] * carried]
    add x6, other arithmetic: 6.05 us -> 8.85 us  [relay(): entering = passed_along(gain[:, None, None] * entering + state, axis, steps)]
    unnamed x70 -> x57, local copies, waits for them, and re-layouts: 8 us -> 6.18 us
    add x2 -> x1, local copies, waits for them, and re-layouts: 3.81 us -> 4.13 us  [per_device(): fwd_all + bwd_all + skip_gain[None, :, None] * acts.astype(jnp.float32)]
  transfers between devices with their start and end apart: 12 -> 12, of which waited for: 6 -> 8; matrix products, arithmetic and copies ran while one was open for 23% -> 27% of each run, Pallas kernels for 0% -> 0%
where the time goes in v15:
time: 158 us; the launch traced here: 157 us
  waiting for transfers between devices  42.1 us (27%)
  local copies, waits for them, and re-layouts  32.9 us (21%)
  other arithmetic  31.2 us (20%)
  matrix products  26.5 us (17%)
  starting transfers between devices  22.8 us (14%)
    ppermute x6, waiting for transfers between devices, swapped(): lax.ppermute(value, axis, [(source, count - 1 - source) for source in ran...  38.5 us
    ppermute x6, starting transfers between devices, passed_along(): lax.ppermute(value, axis, [(source, source + steps) for source in range(f...  19.3 us
    dot_general x2, local copies, waits for them, and re-layouts, direction_out(): jnp.einsum('btn,bhpn->bthp', reads_b, block_states, precision=highest)  9.52 us
    add x1, other arithmetic, per_device(): fwd_all + bwd_all + skip_gain[None, :, None] * acts.astype(jnp.float32)  9.44 us
    add x6, other arithmetic, relay(): entering = passed_along(gain[:, None, None] * entering + state, axis, steps)  8.85 us
    unnamed x57, local copies, waits for them, and re-layouts  6.18 us
    dot_general x2, matrix products, block_parts(): jnp.einsum('bhts,bshp->bthp', weights, acts_b, preferred_element_type=jnp...  5.54 us
    dot_general x4, matrix products, project(): jnp.dot(rows, value_weight, preferred_element_type=jnp.float32)  5.05 us
  transfers between devices with their start and end apart: 12, of which 8 were waited for; matrix products, arithmetic and copies ran while one was open for 27% of the time, Pallas kernels for 0%

profile of v15, /device:TPU:0, one launch (start us, length us, event | category | flops | bytes accessed | tf_op | source)
XLA Modules:
  0.0 156.6 jit_solution(13241803595316281925)
XLA Ops:
  7.8 2.2 %copy.26 = bf16[512,640]{0,1:T(8,128)(2,1)} copy(bf16[512,640]{1,0:T(8,128)(2,1)} %param.14) | data formatting | bytes 1310720 | tf_op args[0]
  10.1 2.7 %reshape_reshape.4 = bf16[2,256,10,64]{1,0,3,2:T(2,128)(2,1)} reshape(bf16[512,640]{0,1:T(8,128)(2,1)} %copy.26) | data formatting | bytes 1310720 | tf_op jit(solution)/shard_map/reshape;reshape | solution.py:26
  12.8 2.3 %convert_multiply_fusion.2 = (f32[2,256,10,64]{1,0,3,2:T(2,128)S(1)}, f32[2,256,10,64]{1,0,3,2:T(2,128)S(1)}) fusion(bf16[2,256,10,64]{1,0,3,2:T(2,128)(2,1)} %reshape_reshape.4, f32[2,256,10]{1,0,2:T(2,128)} %copy.30, f32[2,256,10]{1,0,2:T(2,128)} %copy.37), kind=kLoop, calls=%fused_computation.31 | loop fusion | flops 983040 | bytes 3317760 | tf_op jit(solution)/shard_map/mul | solution.py:50
  16.8 5.6 %collective-permute-start = (f32[10,64,128]{2,1,0:T(8,128)}, f32[10,64,128]{2,1,0:T(8,128)}, u32[]{:S(2)}, u32[]{:S(2)}) collective-permute-start(f32[10,64,128]{2,1,0:T(8,128)} %get-tuple-element.6), channel_id=1, source_target_pairs={{0,4},{4,8},{8,12},{1,5},{5,9},{9,13},{2,6},{6,10},{10,14},{3,7},{... | collective-permute-start | bytes 983048 | tf_op jit(solution)/shard_map/ppermute | solution.py:20
  27.2 2.7 %fusion.6 = f32[2,10,256,64]{3,2,1,0:T(8,128)} fusion(f32[2,10,256]{2,1,0:T(8,128)S(1)} %copy-done.18, f32[2,10,256]{2,1,0:T(8,128)S(1)} %copy-done.14, f32[2,256,256]{2,1,0:T(8,128)S(1)} %fusion.103, pred[256,256]{1,0:T(8,128)(4,1)S(1)} %iota_compare_fusion.1, bf16[2,256,10,64]{1,0,3,2:T(2,128)(2,1)S(1)} %copy-done.4), kind=kOutput, calls=%fused_computation.14 | convolution fusion | flops 174325760 | bytes 2596864 | tf_op jit(solution)/shard_map/bhts,bshp->bthp/dot_general | solution.py:47
  30.0 2.8 %fusion.7 = f32[2,10,256,64]{3,2,1,0:T(8,128)} fusion(f32[2,10,256]{2,1,0:T(8,128)S(1)} %copy-done.17, f32[2,10,256]{2,1,0:T(8,128)S(1)} %copy-done.16, f32[2,256,256]{2,1,0:T(8,128)S(1)} %fusion.104, pred[256,256]{1,0:T(8,128)(4,1)S(1)} %iota_compare_fusion, bf16[2,256,10,64]{1,0,3,2:T(2,128)(2,1)S(1)} %copy-done.4), kind=kOutput, calls=%fused_computation.15 | convolution fusion | flops 174325760 | bytes 2596864 | tf_op jit(solution)/shard_map/bhts,bshp->bthp/dot_general | solution.py:47
  36.2 1.6 %copy.29 = f32[2,256,10]{2,1,0:T(8,128)} copy(f32[2,256,10]{1,2,0:T(8,128)} %get-tuple-element.40) | data formatting | bytes 40960 | tf_op jit(solution)/shard_map/exp | solution.py:97
  37.8 1.6 %copy.36 = f32[2,256,10]{2,1,0:T(8,128)} copy(f32[2,256,10]{1,2,0:T(8,128)} %get-tuple-element.26) | data formatting | bytes 40960 | tf_op jit(solution)/shard_map/exp | solution.py:97
  40.2 2.0 %multiply_add_fusion.3 = f32[10,64,128]{2,1,0:T(8,128)} fusion(f32[10,64,128]{2,1,0:T(8,128)} %get-tuple-element.7, f32[10,64,128]{2,1,0:T(8,128)} %collective-permute-done, f32[10]{0:T(128)S(1)} %get-tuple-element.9), kind=kLoop, calls=%fused_computation.87 | loop fusion | flops 163840 | bytes 983080 | tf_op jit(solution)/shard_map/add | solution.py:77
  42.2 5.3 %collective-permute-start.1 = (f32[10,64,128]{2,1,0:T(8,128)}, f32[10,64,128]{2,1,0:T(8,128)}, u32[]{:S(2)}, u32[]{:S(2)}) collective-permute-start(f32[10,64,128]{2,1,0:T(8,128)} %multiply_add_fusion.3), channel_id=1, source_target_pairs={{0,4},{4,8},{8,12},{1,5},{5,9},{9,13},{2,6},{6,10},{10,14},{3,7},{... | collective-permute-start | bytes 983048 | tf_op jit(solution)/shard_map/ppermute | solution.py:20
  47.5 1.9 %multiply_add_fusion.1 = f32[10,64,128]{2,1,0:T(8,128)} fusion(f32[10,64,128]{2,1,0:T(8,128)} %get-tuple-element.11, f32[10,64,128]{2,1,0:T(8,128)} %collective-permute-done.3, f32[10]{0:T(128)} %get-tuple-element.13), kind=kLoop, calls=%fused_computation.83 | loop fusion | flops 163840 | bytes 983080 | tf_op jit(solution)/shard_map/add | solution.py:77
  54.6 4.4 %collective-permute-start.2 = (f32[10,64,128]{2,1,0:T(8,128)S(1)}, f32[10,64,128]{2,1,0:T(8,128)S(1)}, u32[]{:S(2)}, u32[]{:S(2)}) collective-permute-start(f32[10,64,128]{2,1,0:T(8,128)S(1)} %multiply_add_fusion.2), channel_id=1, source_target_pairs={{0,4},{4,8},{8,12},{1,5},{5,9},{9,13},{2,6},{6,10},{10,14},{3,7},{... | collective-permute-start | bytes 983048 | tf_op jit(solution)/shard_map/ppermute | solution.py:20
  60.2 1.9 %multiply_add_fusion = f32[10,64,128]{2,1,0:T(8,128)} fusion(f32[10,64,128]{2,1,0:T(8,128)} %get-tuple-element.11, f32[10,64,128]{2,1,0:T(8,128)} %collective-permute-done.4, f32[10]{0:T(128)S(1)} %copy-done.20), kind=kLoop, calls=%fused_computation.82 | loop fusion | flops 163840 | bytes 983080 | tf_op jit(solution)/shard_map/add | solution.py:77
  64.6 1.8 %fusion.40 = f32[2,10,64,256]{3,2,1,0:T(8,128)} fusion(bf16[2,256,128,1]{2,1,3,0:T(8,128)(2,1)S(1)} %bitcast.198, f32[1,10,64,128]{3,2,1,0:T(8,128)S(1)} %copy-done.8, f32[10,64,128]{2,1,0:T(8,128)S(1)} %collective-permute-done.2, f32[2,10]{1,0:T(2,128)S(1)} %copy-done.23), kind=kOutput, calls=%fused_computation.65 | convolution fusion | flops 503644160 | bytes 2097232 | tf_op jit(solution)/shard_map/btn,bhpn->bthp/dot_general | solution.py:96
  66.5 4.7 %copy.32 = f32[2,10,64,256]{2,1,3,0:T(8,128)} copy(f32[2,10,64,256]{3,2,1,0:T(8,128)} %fusion.40) | data formatting | bytes 2621440 | tf_op jit(solution)/shard_map/btn,bhpn->bthp/dot_general | solution.py:96
  72.0 2.9 %fusion.36 = f32[2,10,64,256]{3,2,1,0:T(8,128)} fusion(bf16[2,256,128,1]{2,1,3,0:T(8,128)(2,1)S(1)} %bitcast.196, f32[1,10,64,128]{3,2,1,0:T(8,128)} %slice_add_fusion, f32[10,64,128]{2,1,0:T(8,128)} %collective-permute-done.5, f32[2,10]{1,0:T(2,128)S(1)} %copy-done.22), kind=kOutput, calls=%fused_computation.61 | convolution fusion | flops 503644160 | bytes 2097232 | tf_op jit(solution)/shard_map/btn,bhpn->bthp/dot_general | solution.py:96
  74.8 4.8 %copy.39 = f32[2,10,64,256]{2,1,3,0:T(8,128)} copy(f32[2,10,64,256]{3,2,1,0:T(8,128)} %fusion.36) | data formatting | bytes 2621440 | tf_op jit(solution)/shard_map/btn,bhpn->bthp/dot_general | solution.py:96
  79.7 9.4 %fusion.1 = f32[2,256,10,64]{3,2,1,0:T(8,128)} fusion(f32[2,10,64,256]{2,1,3,0:T(8,128)} %copy.39, f32[2,10,64,256]{2,1,3,0:T(8,128)} %copy.32, f32[2,10,256,64]{3,2,1,0:T(8,128)} %fusion.7, f32[2,10,256,64]{3,2,1,0:T(8,128)} %fusion.6, f32[2,256,10]{2,1,0:T(8,128)} %copy.36, f32[2,256,10]{2,1,0:T(8,128)S(1)} %copy-done.9), kind=kLoop, calls=%fused_computation.4 | loop fusion | flops 1638400 | bytes 6594560 | tf_op jit(solution)/shard_map/add | solution.py:202
  89.1 4.1 %reshape.463 = f32[512,640]{1,0:T(8,128)} reshape(f32[2,256,10,64]{3,2,1,0:T(8,128)} %fusion.1) | data formatting | bytes 2621440 | tf_op jit(solution)/shard_map/add | solution.py:202
  93.2 2.3 %multiply_reduce_fusion.1 = (f32[512]{0:T(512)S(1)}, f32[512,640]{1,0:T(8,128)S(1)}) fusion(bf16[512,640]{1,0:T(8,128)(2,1)} %param.15, f32[512,640]{1,0:T(8,128)} %reshape.463, bf16[512,640]{1,0:T(8,128)(2,1)} %param.14, f32[640]{0:T(1024)S(1)} %mul.330), kind=kLoop, calls=%fused_computation.43 | loop fusion | flops 3603968 | bytes 3936768 | tf_op jit(solution)/shard_map/reduce_sum | solution.py:206
  103.5 29.0 %collective-permute-done.8 = f32[128,2560]{1,0:T(8,128)S(1)} collective-permute-done((f32[128,2560]{1,0:T(8,128)S(1)}, f32[128,2560]{1,0:T(8,128)S(1)}, u32[]{:S(2)}, u32[]{:S(2)}) %collective-permute-start.8) | collective-permute-done | bytes 1310752 | tf_op jit(solution)/shard_map/ppermute | solution.py:103
  135.8 2.4 %fusion.35 = bf16[1,1,128,512]{3,2,1,0:T(8,128)(2,1)S(1)} fusion(bf16[128,2560]{1,0:T(8,128)(2,1)} %multiply_convert_fusion.4, bf16[2560,512]{1,0:T(8,128)(2,1)} %param.27), kind=kOutput, calls=%fused_computation.59 | convolution fusion | flops 335609856 | bytes 3407872 | tf_op jit(solution)/shard_map/dot_general | solution.py:152
  138.3 1.7 %fusion.31 = bf16[1,1,128,512]{3,2,1,0:T(8,128)(2,1)S(1)} fusion(bf16[128,2560]{1,0:T(8,128)(2,1)} %multiply_convert_fusion.4, bf16[2560,512]{1,0:T(8,128)(2,1)S(1)} %copy-done.2), kind=kOutput, calls=%fused_computation.55 | convolution fusion | flops 335609856 | bytes 3407872 | tf_op jit(solution)/shard_map/dot_general | solution.py:151
  143.5 8.2 %collective-permute-done.9 = bf16[128,2560]{1,0:T(8,128)(2,1)S(1)} collective-permute-done((bf16[128,2560]{1,0:T(8,128)(2,1)}, bf16[128,2560]{1,0:T(8,128)(2,1)S(1)}, u32[]{:S(2)}, u32[]{:S(2)}) %collective-permute-start.9) | collective-permute-done | bytes 655392 | tf_op jit(solution)/shard_map/ppermute | solution.py:103
  (136 shorter events, 47.0 us)
Async XLA Ops:
  0.6 95.7 %copy-start = (bf16[640,2560]{1,0:T(8,128)(2,1)S(1)}, bf16[640,2560]{1,0:T(8,128)(2,1)}, u32[]{:S(2)}) copy-start(bf16[640,2560]{1,0:T(8,128)(2,1)} %param.23) | copy-start | bytes 9830404
  3.3 3.9 %copy-start.13 = (f32[2,10,256]{2,1,0:T(8,128)}, f32[2,10,256]{2,1,0:T(8,128)S(1)}, u32[]{:S(2)}) copy-start(f32[2,10,256]{2,1,0:T(8,128)S(1)} %fusion.56) | copy-start | bytes 61444
  7.8 4.9 %copy-start.11 = (bf16[2,512,128]{2,1,0:T(8,128)(2,1)S(1)}, bf16[2,512,128]{2,1,0:T(8,128)(2,1)}, u32[]{:S(2)}) copy-start(bf16[2,512,128]{2,1,0:T(8,128)(2,1)} %param.16) | copy-start | bytes 786436
  16.8 23.4 %collective-permute-start = (f32[10,64,128]{2,1,0:T(8,128)}, f32[10,64,128]{2,1,0:T(8,128)}, u32[]{:S(2)}, u32[]{:S(2)}) collective-permute-start(f32[10,64,128]{2,1,0:T(8,128)} %get-tuple-element.6), channel_id=1, source_target_pairs={{0,4},{4,8},{8,12},{1,5},{5,9},{9,13},{2,6},{6,10},{10,14},{3,7},{... | collective-permute-start | bytes 983048 | tf_op jit(solution)/shard_map/ppermute | solution.py:20
  23.5 3.2 %copy-start.12 = (bf16[2,512,128]{2,1,0:T(8,128)(2,1)S(1)}, bf16[2,512,128]{2,1,0:T(8,128)(2,1)}, u32[]{:S(2)}) copy-start(bf16[2,512,128]{2,1,0:T(8,128)(2,1)} %param.17) | copy-start | bytes 786436
  25.2 22.3 %collective-permute-start.3 = (f32[10,64,128]{2,1,0:T(8,128)}, f32[10,64,128]{2,1,0:T(8,128)}, u32[]{:S(2)}, u32[]{:S(2)}) collective-permute-start(f32[10,64,128]{2,1,0:T(8,128)} %get-tuple-element.10), channel_id=1, source_target_pairs={{4,0},{8,4},{12,8},{5,1},{9,5},{13,9},{6,2},{10,6},{14,10},{7,3},{... | collective-permute-start | bytes 983048 | tf_op jit(solution)/shard_map/ppermute | solution.py:20
  27.2 2.8 %copy-start.16 = (f32[2,10,256]{2,1,0:T(8,128)S(1)}, f32[2,10,256]{2,1,0:T(8,128)}, u32[]{:S(2)}) copy-start(f32[2,10,256]{2,1,0:T(8,128)} %copy-done.15) | copy-start | bytes 61444
  40.2 10.4 %copy-start.10 = (bf16[512,640]{1,0:T(8,128)(2,1)S(1)}, bf16[512,640]{1,0:T(8,128)(2,1)}, u32[]{:S(2)}) copy-start(bf16[512,640]{1,0:T(8,128)(2,1)} %param.24) | copy-start | bytes 1966084
  42.2 11.3 %collective-permute-start.1 = (f32[10,64,128]{2,1,0:T(8,128)}, f32[10,64,128]{2,1,0:T(8,128)}, u32[]{:S(2)}, u32[]{:S(2)}) collective-permute-start(f32[10,64,128]{2,1,0:T(8,128)} %multiply_add_fusion.3), channel_id=1, source_target_pairs={{0,4},{4,8},{8,12},{1,5},{5,9},{9,13},{2,6},{6,10},{10,14},{3,7},{... | collective-permute-start | bytes 983048 | tf_op jit(solution)/shard_map/ppermute | solution.py:20
  49.3 10.8 %collective-permute-start.4 = (f32[10,64,128]{2,1,0:T(8,128)}, f32[10,64,128]{2,1,0:T(8,128)}, u32[]{:S(2)}, u32[]{:S(2)}) collective-permute-start(f32[10,64,128]{2,1,0:T(8,128)} %multiply_add_fusion.1), channel_id=1, source_target_pairs={{4,0},{8,4},{12,8},{5,1},{9,5},{13,9},{6,2},{10,6},{14,10},{7,3},{... | collective-permute-start | bytes 983048 | tf_op jit(solution)/shard_map/ppermute | solution.py:20
  51.8 8.3 %copy-start.20 = (f32[10]{0:T(128)S(1)}, f32[10]{0:T(128)}, u32[]{:S(2)}) copy-start(f32[10]{0:T(128)} %get-tuple-element.13) | copy-start | bytes 124
  53.0 11.6 %copy-start.23 = (f32[2,10]{1,0:T(2,128)S(1)}, f32[2,10]{1,0:T(2,128)}, u32[]{:S(2)}) copy-start(f32[2,10]{1,0:T(2,128)} %stack.91) | copy-start | bytes 244
  53.0 11.6 %copy-start.8 = (f32[1,10,64,128]{3,2,1,0:T(8,128)S(1)}, f32[1,10,64,128]{3,2,1,0:T(8,128)}, u32[]{:S(2)}) copy-start(f32[1,10,64,128]{3,2,1,0:T(8,128)} %slice_add_fusion.1) | copy-start | bytes 983044
  54.6 10.0 %collective-permute-start.2 = (f32[10,64,128]{2,1,0:T(8,128)S(1)}, f32[10,64,128]{2,1,0:T(8,128)S(1)}, u32[]{:S(2)}, u32[]{:S(2)}) collective-permute-start(f32[10,64,128]{2,1,0:T(8,128)S(1)} %multiply_add_fusion.2), channel_id=1, source_target_pairs={{0,4},{4,8},{8,12},{1,5},{5,9},{9,13},{2,6},{6,10},{10,14},{3,7},{... | collective-permute-start | bytes 983048 | tf_op jit(solution)/shard_map/ppermute | solution.py:20
  62.1 9.9 %collective-permute-start.5 = (f32[10,64,128]{2,1,0:T(8,128)}, f32[10,64,128]{2,1,0:T(8,128)}, u32[]{:S(2)}, u32[]{:S(2)}) collective-permute-start(f32[10,64,128]{2,1,0:T(8,128)} %multiply_add_fusion), channel_id=1, source_target_pairs={{4,0},{8,4},{12,8},{5,1},{9,5},{13,9},{6,2},{10,6},{14,10},{7,3},{... | collective-permute-start | bytes 983048 | tf_op jit(solution)/shard_map/ppermute | solution.py:20
  66.5 5.5 %copy-start.22 = (f32[2,10]{1,0:T(2,128)S(1)}, f32[2,10]{1,0:T(2,128)}, u32[]{:S(2)}) copy-start(f32[2,10]{1,0:T(2,128)} %stack.93) | copy-start | bytes 244
  74.8 4.8 %copy-start.9 = (f32[2,256,10]{2,1,0:T(8,128)S(1)}, f32[2,256,10]{2,1,0:T(8,128)}, u32[]{:S(2)}) copy-start(f32[2,256,10]{2,1,0:T(8,128)} %copy.29) | copy-start | bytes 61444
  97.7 3.1 %collective-permute-start.7 = (f32[128,2560]{1,0:T(8,128)S(1)}, f32[128,2560]{1,0:T(8,128)S(1)}, u32[]{:S(2)}, u32[]{:S(2)}) collective-permute-start(f32[128,2560]{1,0:T(8,128)S(1)} %convolution_add_fusion), channel_id=1, source_target_pairs={{0,1},{1,0},{2,3},{3,2},{4,5},{5,4},{6,7},{7,6},{8,9},{9,8},{10,11... | collective-permute-start | bytes 3932168 | tf_op jit(solution)/shard_map/ppermute | solution.py:103
  100.2 3.2 %collective-permute-start.6 = (f32[128,2560]{1,0:T(8,128)S(1)}, f32[128,2560]{1,0:T(8,128)S(1)}, u32[]{:S(2)}, u32[]{:S(2)}) collective-permute-start(f32[128,2560]{1,0:T(8,128)S(1)} %convolution_add_fusion.2), channel_id=1, source_target_pairs={{0,1},{1,0},{2,3},{3,2},{4,5},{5,4},{6,7},{7,6},{8,9},{9,8},{10,11... | collective-permute-start | bytes 3932168 | tf_op jit(solution)/shard_map/ppermute | solution.py:103
  101.6 30.9 %collective-permute-start.8 = (f32[128,2560]{1,0:T(8,128)S(1)}, f32[128,2560]{1,0:T(8,128)S(1)}, u32[]{:S(2)}, u32[]{:S(2)}) collective-permute-start(f32[128,2560]{1,0:T(8,128)S(1)} %fusion.3), channel_id=1, source_target_pairs={{0,2},{2,0},{1,3},{3,1},{4,6},{6,4},{5,7},{7,5},{8,10},{10,8},{9,1... | collective-permute-start | bytes 3932168 | tf_op jit(solution)/shard_map/ppermute | solution.py:103
  134.3 5.7 %collective-permute-start.11 = (bf16[128,2560]{1,0:T(8,128)(2,1)}, bf16[128,2560]{1,0:T(8,128)(2,1)}, u32[]{:S(2)}, u32[]{:S(2)}) collective-permute-start(bf16[128,2560]{1,0:T(8,128)(2,1)} %multiply_convert_fusion.4), channel_id=1, source_target_pairs={{0,1},{1,0},{2,3},{3,2},{4,5},{5,4},{6,7},{7,6},{8,9},{9,8},{10,11... | collective-permute-start | bytes 1966088 | tf_op jit(solution)/shard_map/ppermute | solution.py:103
  134.3 3.9 %copy-start.2 = (bf16[2560,512]{1,0:T(8,128)(2,1)S(1)}, bf16[2560,512]{1,0:T(8,128)(2,1)}, u32[]{:S(2)}) copy-start(bf16[2560,512]{1,0:T(8,128)(2,1)} %param.26) | copy-start | bytes 7864324
  134.3 17.4 %collective-permute-start.9 = (bf16[128,2560]{1,0:T(8,128)(2,1)}, bf16[128,2560]{1,0:T(8,128)(2,1)S(1)}, u32[]{:S(2)}, u32[]{:S(2)}) collective-permute-start(bf16[128,2560]{1,0:T(8,128)(2,1)} %multiply_convert_fusion.4), channel_id=1, source_target_pairs={{0,2},{2,0},{1,3},{3,1},{4,6},{6,4},{5,7},{7,5},{8,10},{10,8},{9,1... | collective-permute-start | bytes 1966088 | tf_op jit(solution)/shard_map/ppermute | solution.py:103
  151.7 2.1 %collective-permute-start.10 = (bf16[128,2560]{1,0:T(8,128)(2,1)S(1)}, bf16[128,2560]{1,0:T(8,128)(2,1)S(1)}, u32[]{:S(2)}, u32[]{:S(2)}) collective-permute-start(bf16[128,2560]{1,0:T(8,128)(2,1)S(1)} %collective-permute-done.9), channel_id=1, source_target_pairs={{0,1},{1,0},{2,3},{3,2},{4,5},{5,4},{6,7},{7,6},{8,9},{9,8},{10,11... | collective-permute-start | bytes 1966088 | tf_op jit(solution)/shard_map/ppermute | solution.py:103
  (14 other events, 22.4 us)

commit v16 on v14

--- a/solution.py
+++ b/solution.py
@@ -139,6 +139,7 @@
         return partial_of(block_at(mixed4, at_chip, at_core), block_at(residual4, at_chip, at_core))
 
     far = part(1 - chip, core) + swapped(part(1 - chip, 1 - core), "head_core")
+    far, (mixed4, residual4) = lax.optimization_barrier((far, (mixed4, residual4)))
     arrived = swapped(far, "head_chip")
     near = part(chip, core) + swapped(part(chip, 1 - core), "head_core")
     return near + arrived

time: 132 us -> 138 us (1.045)
  matrix products: 25.1 us -> 28 us
  local copies, waits for them, and re-layouts: 20.9 us -> 22.9 us
    dot_general x4, matrix products: 3.02 us -> 5.91 us  [partial_of(): value = jnp.dot(rows, out_weight, preferred_element_type=jnp.float32)]
  transfers between devices with their start and end apart: 12 -> 12, of which waited for: 6 -> 7; matrix products, arithmetic and copies ran while one was open for 23% -> 22% of each run, Pallas kernels for 0% -> 0%
where the time goes in v16:
time: 138 us; the launch traced here: 137 us
  waiting for transfers between devices  44.8 us (32%)
  matrix products  28 us (20%)
  local copies, waits for them, and re-layouts  22.9 us (17%)
  starting transfers between devices  22 us (16%)
  other arithmetic  18.4 us (13%)
    ppermute x6, waiting for transfers between devices, swapped(): lax.ppermute(value, axis, [(source, count - 1 - source) for source in ran...  39.7 us
    ppermute x6, starting transfers between devices, passed_along(): lax.ppermute(value, axis, [(source, source + steps) for source in range(f...  19 us
    unnamed x70, local copies, waits for them, and re-layouts  9.04 us
    add x6, other arithmetic, relay(): entering = passed_along(gain[:, None, None] * entering + state, axis, steps)  6.06 us
    dot_general x4, matrix products, partial_of(): value = jnp.dot(rows, out_weight, preferred_element_type=jnp.float32)  5.91 us
    dot_general x2, matrix products, block_parts(): jnp.einsum('bhts,bshp->bthp', weights, acts_b, preferred_element_type=jnp...  5.25 us
    ppermute x6, waiting for transfers between devices, passed_along(): lax.ppermute(value, axis, [(source, source + steps) for source in range(f...  5.08 us
    dot_general x4, matrix products, project(): jnp.dot(rows, value_weight, preferred_element_type=jnp.float32)  5.04 us
  transfers between devices with their start and end apart: 12, of which 7 were waited for; matrix products, arithmetic and copies ran while one was open for 22% of the time, Pallas kernels for 0%

profile of v16, /device:TPU:0, one launch (start us, length us, event | category | flops | bytes accessed | tf_op | source)
XLA Modules:
  0.0 137.4 jit_solution(540562577200676031)
XLA Ops:
  7.8 2.2 %copy.21 = bf16[512,640]{0,1:T(8,128)(2,1)} copy(bf16[512,640]{1,0:T(8,128)(2,1)} %param.14) | data formatting | bytes 1310720 | tf_op args[0]
  10.1 2.7 %reshape_reshape.4 = bf16[2,256,10,64]{1,0,3,2:T(2,128)(2,1)} reshape(bf16[512,640]{0,1:T(8,128)(2,1)} %copy.21) | data formatting | bytes 1310720 | tf_op jit(solution)/shard_map/reshape;reshape | solution.py:26
  12.8 2.3 %convert_multiply_fusion.1 = (f32[2,256,10,64]{1,0,3,2:T(2,128)S(1)}, f32[2,256,10,64]{1,0,3,2:T(2,128)S(1)}) fusion(bf16[2,256,10,64]{1,0,3,2:T(2,128)(2,1)} %reshape_reshape.4, f32[2,256,10]{1,0,2:T(2,128)} %copy.27, f32[2,256,10]{1,0,2:T(2,128)} %copy.23), kind=kLoop, calls=%fused_computation.25 | loop fusion | flops 983040 | bytes 3317760 | tf_op jit(solution)/shard_map/mul | solution.py:49
  19.8 6.4 %collective-permute-start = (f32[10,64,128]{2,1,0:T(8,128)}, f32[10,64,128]{2,1,0:T(8,128)}, u32[]{:S(2)}, u32[]{:S(2)}) collective-permute-start(f32[10,64,128]{2,1,0:T(8,128)} %get-tuple-element.16), channel_id=1, source_target_pairs={{0,4},{4,8},{8,12},{1,5},{5,9},{9,13},{2,6},{6,10},{10,14},{3,7},{... | collective-permute-start | bytes 983048 | tf_op jit(solution)/shard_map/ppermute | solution.py:20
  26.8 2.6 %fusion.18 = f32[2,256,10,64]{1,3,2,0:T(8,128)} fusion(f32[2,10,256]{2,1,0:T(8,128)S(1)} %copy-done.24, f32[2,10,256]{2,1,0:T(8,128)S(1)} %copy-done.22, f32[2,256,256]{2,1,0:T(8,128)S(1)} %fusion.105, pred[256,256]{1,0:T(8,128)(4,1)S(1)} %iota_compare_fusion.1, bf16[2,256,10,64]{1,0,3,2:T(2,128)(2,1)S(1)} %copy-done.6), kind=kOutput, calls=%fused_computation.28 | convolution fusion | flops 174325760 | bytes 2596864 | tf_op jit(solution)/shard_map/bhts,bshp->bthp/dot_general | solution.py:47
  29.5 2.6 %fusion.17 = f32[2,256,10,64]{1,3,2,0:T(8,128)} fusion(f32[2,10,256]{2,1,0:T(8,128)S(1)} %copy-done.23, f32[2,10,256]{2,1,0:T(8,128)S(1)} %copy-done.20, f32[2,256,256]{2,1,0:T(8,128)S(1)} %fusion.106, pred[256,256]{1,0:T(8,128)(4,1)S(1)} %iota_compare_fusion, bf16[2,256,10,64]{1,0,3,2:T(2,128)(2,1)S(1)} %copy-done.6), kind=kOutput, calls=%fused_computation.27 | convolution fusion | flops 174325760 | bytes 2596864 | tf_op jit(solution)/shard_map/bhts,bshp->bthp/dot_general | solution.py:47
  35.0 3.4 %collective-permute-start.1 = (f32[10,64,128]{2,1,0:T(8,128)S(1)}, f32[10,64,128]{2,1,0:T(8,128)S(1)}, u32[]{:S(2)}, u32[]{:S(2)}) collective-permute-start(f32[10,64,128]{2,1,0:T(8,128)S(1)} %multiply_add_fusion.3), channel_id=1, source_target_pairs={{0,4},{4,8},{8,12},{1,5},{5,9},{9,13},{2,6},{6,10},{10,14},{3,7},{... | collective-permute-start | bytes 983048 | tf_op jit(solution)/shard_map/ppermute | solution.py:20
  41.9 2.7 %collective-permute-done.1 = f32[10,64,128]{2,1,0:T(8,128)S(1)} collective-permute-done((f32[10,64,128]{2,1,0:T(8,128)S(1)}, f32[10,64,128]{2,1,0:T(8,128)S(1)}, u32[]{:S(2)}, u32[]{:S(2)}) %collective-permute-start.1) | collective-permute-done | bytes 327712 | tf_op jit(solution)/shard_map/ppermute | solution.py:20
  45.4 5.1 %collective-permute-start.2 = (f32[10,64,128]{2,1,0:T(8,128)}, f32[10,64,128]{2,1,0:T(8,128)}, u32[]{:S(2)}, u32[]{:S(2)}) collective-permute-start(f32[10,64,128]{2,1,0:T(8,128)} %multiply_add_fusion.2), channel_id=1, source_target_pairs={{0,4},{4,8},{8,12},{1,5},{5,9},{9,13},{2,6},{6,10},{10,14},{3,7},{... | collective-permute-start | bytes 983048 | tf_op jit(solution)/shard_map/ppermute | solution.py:20
  51.4 1.5 %collective-permute-start.5 = (f32[10,64,128]{2,1,0:T(8,128)}, f32[10,64,128]{2,1,0:T(8,128)}, u32[]{:S(2)}, u32[]{:S(2)}) collective-permute-start(f32[10,64,128]{2,1,0:T(8,128)} %multiply_add_fusion), channel_id=1, source_target_pairs={{4,0},{8,4},{12,8},{5,1},{9,5},{13,9},{6,2},{10,6},{14,10},{7,3},{... | collective-permute-start | bytes 983048 | tf_op jit(solution)/shard_map/ppermute | solution.py:20
  57.3 1.9 %fusion.23 = f32[2,256,10,64]{1,3,2,0:T(8,128)S(1)} fusion(f32[2,256,10,64]{1,3,2,0:T(8,128)S(1)} %copy-done.9, bf16[2,256,128,1]{2,1,3,0:T(8,128)(2,1)S(1)} %bitcast.201, f32[1,10,64,128]{3,2,1,0:T(8,128)S(1)} %copy-done.10, f32[2,256,10]{1,2,0:T(8,128)S(1)} %copy-done.17, f32[10,64,128]{2,1,0:T(8,128)} %collective-permute-done.2, f32[2,10]{1,0:T(2,128)S(1)} %copy-done.26), kind=kOutput, calls=%fused_computation.35 | convolution fusion | flops 504299520 | bytes 3428432 | tf_op jit(solution)/shard_map/btn,bhpn->bthp/dot_general | solution.py:95
  59.2 2.3 %collective-permute-done.5 = f32[10,64,128]{2,1,0:T(8,128)} collective-permute-done((f32[10,64,128]{2,1,0:T(8,128)}, f32[10,64,128]{2,1,0:T(8,128)}, u32[]{:S(2)}, u32[]{:S(2)}) %collective-permute-start.5) | collective-permute-done | bytes 327712 | tf_op jit(solution)/shard_map/ppermute | solution.py:20
  61.5 1.8 %fusion.21 = f32[2,256,10,64]{1,3,2,0:T(8,128)S(1)} fusion(f32[2,256,10,64]{1,3,2,0:T(8,128)S(1)} %fusion.23, f32[2,256,10,64]{1,3,2,0:T(8,128)S(1)} %copy-done.11, bf16[2,256,128,1]{2,1,3,0:T(8,128)(2,1)S(1)} %bitcast.207, f32[1,10,64,128]{3,2,1,0:T(8,128)S(1)} %copy-done.12, f32[2,256,10]{1,2,0:T(8,128)S(1)} %copy-done.18, ...), kind=kOutput, calls=%fused_computation.32 | convolution fusion | flops 504627200 | bytes 4739152 | tf_op jit(solution)/shard_map/btn,bhpn->bthp/dot_general | solution.py:95
  65.6 2.8 %copy.30 = f32[512,640]{1,0:T(8,128)} copy(f32[512,640]{0,1:T(8,128)} %bitcast.192) | data formatting | bytes 2621440 | tf_op jit(solution)/shard_map/add | solution.py:202
  68.4 2.3 %multiply_reduce_fusion.1 = (f32[512]{0:T(512)S(1)}, f32[512,640]{1,0:T(8,128)S(1)}) fusion(bf16[512,640]{1,0:T(8,128)(2,1)} %param.15, f32[512,640]{1,0:T(8,128)} %copy.30, bf16[512,640]{1,0:T(8,128)(2,1)} %param.14, f32[640]{0:T(1024)S(1)} %mul.330), kind=kLoop, calls=%fused_computation.47 | loop fusion | flops 3603968 | bytes 3936768 | tf_op jit(solution)/shard_map/reduce_sum | solution.py:206
  72.1 1.8 %convolution_add_fusion.2 = f32[128,2560]{1,0:T(8,128)} fusion(bf16[640,2560]{1,0:T(8,128)(2,1)S(1)} %copy-done, f32[128,2560]{1,0:T(8,128)S(1)} %bitcast.196, pred[2560]{0:T(1024)(128)(4,1)S(1)} %fusion.84, bf16[2,2,128,640]{3,2,1,0:T(8,128)(2,1)S(1)} %multiply_convert_fusion.9, s32[]{:T(128)S(6)} %select_n.138, s32[]{:T(128)S(6)} %select_n.142), kind=kOutput, calls=%fused_computation.6 | convolution fusion | flops 420085760 | bytes 6065160 | tf_op jit(solution)/shard_map/dot_general | solution.py:125
  77.3 2.5 %fusion.2 = f32[128,2560]{1,0:T(8,128)S(1)} fusion(f32[128,2560]{1,0:T(8,128)} %collective-permute-done.6, bf16[640,2560]{1,0:T(8,128)(2,1)S(1)} %copy-done, f32[128,2560]{1,0:T(8,128)} %bitcast.189, pred[2560]{0:T(1024)(128)(4,1)S(1)} %fusion.84, bf16[2,2,128,640]{3,2,1,0:T(8,128)(2,1)} %copy-done.7, s32[]{:T(128)S(6)} %select_n.138, s32[]{:T(128)S(6)} %select_n.139), kind=kOutput, calls=%fused_computation.8 | convolution fusion | flops 420413440 | bytes 7375368 | tf_op jit(solution)/shard_map/dot_general | solution.py:125
  82.2 1.4 %collective-permute-start.8 = (f32[128,2560]{1,0:T(8,128)S(1)}, f32[128,2560]{1,0:T(8,128)S(1)}, u32[]{:S(2)}, u32[]{:S(2)}) collective-permute-start(f32[128,2560]{1,0:T(8,128)S(1)} %fusion.2), channel_id=1, source_target_pairs={{0,2},{2,0},{1,3},{3,1},{4,6},{6,4},{5,7},{7,5},{8,10},{10,8},{9,1... | collective-permute-start | bytes 3932168 | tf_op jit(solution)/shard_map/ppermute | solution.py:102
  85.1 28.2 %collective-permute-done.8 = f32[128,2560]{1,0:T(8,128)S(1)} collective-permute-done((f32[128,2560]{1,0:T(8,128)S(1)}, f32[128,2560]{1,0:T(8,128)S(1)}, u32[]{:S(2)}, u32[]{:S(2)}) %collective-permute-start.8) | collective-permute-done | bytes 1310752 | tf_op jit(solution)/shard_map/ppermute | solution.py:102
  116.6 2.4 %fusion.39 = bf16[1,1,128,512]{3,2,1,0:T(8,128)(2,1)S(1)} fusion(bf16[128,2560]{1,0:T(8,128)(2,1)} %multiply_convert_fusion.8, bf16[2560,512]{1,0:T(8,128)(2,1)} %param.27), kind=kOutput, calls=%fused_computation.63 | convolution fusion | flops 335609856 | bytes 3407872 | tf_op jit(solution)/shard_map/dot_general | solution.py:152
  119.0 1.7 %fusion.35 = bf16[1,1,128,512]{3,2,1,0:T(8,128)(2,1)S(1)} fusion(bf16[128,2560]{1,0:T(8,128)(2,1)} %multiply_convert_fusion.8, bf16[2560,512]{1,0:T(8,128)(2,1)S(1)} %copy-done.2), kind=kOutput, calls=%fused_computation.59 | convolution fusion | flops 335609856 | bytes 3407872 | tf_op jit(solution)/shard_map/dot_general | solution.py:151
  121.0 1.6 %fusion.38 = bf16[1,1,128,512]{3,2,1,0:T(8,128)(2,1)S(1)} fusion(bf16[128,2560]{1,0:T(8,128)(2,1)} %collective-permute-done.11, bf16[2560,512]{1,0:T(8,128)(2,1)S(1)} %copy-done.1), kind=kOutput, calls=%fused_computation.62 | convolution fusion | flops 335609856 | bytes 3407872 | tf_op jit(solution)/shard_map/dot_general | solution.py:152
  122.6 1.6 %fusion.34 = bf16[1,1,128,512]{3,2,1,0:T(8,128)(2,1)S(1)} fusion(bf16[128,2560]{1,0:T(8,128)(2,1)} %collective-permute-done.11, bf16[2560,512]{1,0:T(8,128)(2,1)S(1)} %copy-done.2), kind=kOutput, calls=%fused_computation.58 | convolution fusion | flops 335609856 | bytes 3407872 | tf_op jit(solution)/shard_map/dot_general | solution.py:151
  124.2 8.3 %collective-permute-done.9 = bf16[128,2560]{1,0:T(8,128)(2,1)S(1)} collective-permute-done((bf16[128,2560]{1,0:T(8,128)(2,1)}, bf16[128,2560]{1,0:T(8,128)(2,1)S(1)}, u32[]{:S(2)}, u32[]{:S(2)}) %collective-permute-start.9) | collective-permute-done | bytes 655392 | tf_op jit(solution)/shard_map/ppermute | solution.py:102
  (146 shorter events, 43.9 us)
Async XLA Ops:
  0.6 70.8 %copy-start = (bf16[640,2560]{1,0:T(8,128)(2,1)S(1)}, bf16[640,2560]{1,0:T(8,128)(2,1)}, u32[]{:S(2)}) copy-start(bf16[640,2560]{1,0:T(8,128)(2,1)} %param.23) | copy-start | bytes 9830404
  7.8 4.9 %copy-start.15 = (bf16[2,512,128]{2,1,0:T(8,128)(2,1)S(1)}, bf16[2,512,128]{2,1,0:T(8,128)(2,1)}, u32[]{:S(2)}) copy-start(bf16[2,512,128]{2,1,0:T(8,128)(2,1)} %param.16) | copy-start | bytes 786436
  16.8 21.6 %collective-permute-start.3 = (f32[10,64,128]{2,1,0:T(8,128)}, f32[10,64,128]{2,1,0:T(8,128)}, u32[]{:S(2)}, u32[]{:S(2)}) collective-permute-start(f32[10,64,128]{2,1,0:T(8,128)} %get-tuple-element.12), channel_id=1, source_target_pairs={{4,0},{8,4},{12,8},{5,1},{9,5},{13,9},{6,2},{10,6},{14,10},{7,3},{... | collective-permute-start | bytes 983048 | tf_op jit(solution)/shard_map/ppermute | solution.py:20
  18.1 8.2 %copy-start.16 = (bf16[2,512,128]{2,1,0:T(8,128)(2,1)S(1)}, bf16[2,512,128]{2,1,0:T(8,128)(2,1)}, u32[]{:S(2)}) copy-start(bf16[2,512,128]{2,1,0:T(8,128)(2,1)} %param.17) | copy-start | bytes 786436
  19.8 7.0 %copy-start.6 = (bf16[2,256,10,64]{1,0,3,2:T(2,128)(2,1)S(1)}, bf16[2,256,10,64]{1,0,3,2:T(2,128)(2,1)}, u32[]{:S(2)}) copy-start(bf16[2,256,10,64]{1,0,3,2:T(2,128)(2,1)} %reshape_reshape.4) | copy-start | bytes 1966084
  19.8 7.0 %copy-start.22 = (f32[2,10,256]{2,1,0:T(8,128)S(1)}, f32[2,10,256]{2,1,0:T(8,128)}, u32[]{:S(2)}) copy-start(f32[2,10,256]{2,1,0:T(8,128)} %copy-done.21) | copy-start | bytes 61444
  19.8 7.0 %copy-start.24 = (f32[2,10,256]{2,1,0:T(8,128)S(1)}, f32[2,10,256]{2,1,0:T(8,128)}, u32[]{:S(2)}) copy-start(f32[2,10,256]{2,1,0:T(8,128)} %get-tuple-element.44) | copy-start | bytes 61444
  19.8 13.9 %collective-permute-start = (f32[10,64,128]{2,1,0:T(8,128)}, f32[10,64,128]{2,1,0:T(8,128)}, u32[]{:S(2)}, u32[]{:S(2)}) collective-permute-start(f32[10,64,128]{2,1,0:T(8,128)} %get-tuple-element.16), channel_id=1, source_target_pairs={{0,4},{4,8},{8,12},{1,5},{5,9},{9,13},{2,6},{6,10},{10,14},{3,7},{... | collective-permute-start | bytes 983048 | tf_op jit(solution)/shard_map/ppermute | solution.py:20
  33.7 7.2 %copy-start.13 = (bf16[512,640]{1,0:T(8,128)(2,1)S(1)}, bf16[512,640]{1,0:T(8,128)(2,1)}, u32[]{:S(2)}) copy-start(bf16[512,640]{1,0:T(8,128)(2,1)} %param.24) | copy-start | bytes 1966084
  33.7 10.9 %copy-start.5 = (f32[10,64,128]{2,1,0:T(8,128)S(1)}, f32[10,64,128]{2,1,0:T(8,128)}, u32[]{:S(2)}) copy-start(f32[10,64,128]{2,1,0:T(8,128)} %get-tuple-element.17) | copy-start | bytes 983044
  35.0 9.6 %collective-permute-start.1 = (f32[10,64,128]{2,1,0:T(8,128)S(1)}, f32[10,64,128]{2,1,0:T(8,128)S(1)}, u32[]{:S(2)}, u32[]{:S(2)}) collective-permute-start(f32[10,64,128]{2,1,0:T(8,128)S(1)} %multiply_add_fusion.3), channel_id=1, source_target_pairs={{0,4},{4,8},{8,12},{1,5},{5,9},{9,13},{2,6},{6,10},{10,14},{3,7},{... | collective-permute-start | bytes 983048 | tf_op jit(solution)/shard_map/ppermute | solution.py:20
  38.4 12.1 %copy-start.4 = (f32[10,64,128]{2,1,0:T(8,128)S(1)}, f32[10,64,128]{2,1,0:T(8,128)}, u32[]{:S(2)}) copy-start(f32[10,64,128]{2,1,0:T(8,128)} %get-tuple-element.13) | copy-start | bytes 983044
  39.7 10.9 %collective-permute-start.4 = (f32[10,64,128]{2,1,0:T(8,128)S(1)}, f32[10,64,128]{2,1,0:T(8,128)S(1)}, u32[]{:S(2)}, u32[]{:S(2)}) collective-permute-start(f32[10,64,128]{2,1,0:T(8,128)S(1)} %multiply_add_fusion.1), channel_id=1, source_target_pairs={{4,0},{8,4},{12,8},{5,1},{9,5},{13,9},{6,2},{10,6},{14,10},{7,3},{... | collective-permute-start | bytes 983048 | tf_op jit(solution)/shard_map/ppermute | solution.py:20
  41.0 12.5 %copy-start.30 = (f32[1,10]{1,0:T(1,128)S(1)}, f32[1,10]{1,0:T(1,128)}, u32[]{:S(2)}) copy-start(f32[1,10]{1,0:T(1,128)} %get-tuple-element.36) | copy-start | bytes 124
  41.0 13.1 %copy-start.31 = (f32[10]{0:T(128)S(1)}, f32[10]{0:T(128)}, u32[]{:S(2)}) copy-start(f32[10]{0:T(128)} %param.21) | copy-start | bytes 124
  45.4 11.2 %collective-permute-start.2 = (f32[10,64,128]{2,1,0:T(8,128)}, f32[10,64,128]{2,1,0:T(8,128)}, u32[]{:S(2)}, u32[]{:S(2)}) collective-permute-start(f32[10,64,128]{2,1,0:T(8,128)} %multiply_add_fusion.2), channel_id=1, source_target_pairs={{0,4},{4,8},{8,12},{1,5},{5,9},{9,13},{2,6},{6,10},{10,14},{3,7},{... | collective-permute-start | bytes 983048 | tf_op jit(solution)/shard_map/ppermute | solution.py:20
  51.4 10.1 %collective-permute-start.5 = (f32[10,64,128]{2,1,0:T(8,128)}, f32[10,64,128]{2,1,0:T(8,128)}, u32[]{:S(2)}, u32[]{:S(2)}) collective-permute-start(f32[10,64,128]{2,1,0:T(8,128)} %multiply_add_fusion), channel_id=1, source_target_pairs={{4,0},{8,4},{12,8},{5,1},{9,5},{13,9},{6,2},{10,6},{14,10},{7,3},{... | collective-permute-start | bytes 983048 | tf_op jit(solution)/shard_map/ppermute | solution.py:20
  57.3 4.2 %copy-start.12 = (f32[1,10,64,128]{3,2,1,0:T(8,128)S(1)}, f32[1,10,64,128]{3,2,1,0:T(8,128)}, u32[]{:S(2)}) copy-start(f32[1,10,64,128]{3,2,1,0:T(8,128)} %slice_add_fusion) | copy-start | bytes 983044
  74.0 3.4 %collective-permute-start.6 = (f32[128,2560]{1,0:T(8,128)}, f32[128,2560]{1,0:T(8,128)}, u32[]{:S(2)}, u32[]{:S(2)}) collective-permute-start(f32[128,2560]{1,0:T(8,128)} %convolution_add_fusion.2), channel_id=1, source_target_pairs={{0,1},{1,0},{2,3},{3,2},{4,5},{5,4},{6,7},{7,6},{8,9},{9,8},{10,11... | collective-permute-start | bytes 3932168 | tf_op jit(solution)/shard_map/ppermute | solution.py:102
  82.0 3.1 %collective-permute-start.7 = (f32[128,2560]{1,0:T(8,128)S(1)}, f32[128,2560]{1,0:T(8,128)S(1)}, u32[]{:S(2)}, u32[]{:S(2)}) collective-permute-start(f32[128,2560]{1,0:T(8,128)S(1)} %convolution_add_fusion), channel_id=1, source_target_pairs={{0,1},{1,0},{2,3},{3,2},{4,5},{5,4},{6,7},{7,6},{8,9},{9,8},{10,11... | collective-permute-start | bytes 3932168 | tf_op jit(solution)/shard_map/ppermute | solution.py:102
  82.2 31.1 %collective-permute-start.8 = (f32[128,2560]{1,0:T(8,128)S(1)}, f32[128,2560]{1,0:T(8,128)S(1)}, u32[]{:S(2)}, u32[]{:S(2)}) collective-permute-start(f32[128,2560]{1,0:T(8,128)S(1)} %fusion.2), channel_id=1, source_target_pairs={{0,2},{2,0},{1,3},{3,1},{4,6},{6,4},{5,7},{7,5},{8,10},{10,8},{9,1... | collective-permute-start | bytes 3932168 | tf_op jit(solution)/shard_map/ppermute | solution.py:102
  115.1 5.6 %collective-permute-start.11 = (bf16[128,2560]{1,0:T(8,128)(2,1)}, bf16[128,2560]{1,0:T(8,128)(2,1)}, u32[]{:S(2)}, u32[]{:S(2)}) collective-permute-start(bf16[128,2560]{1,0:T(8,128)(2,1)} %multiply_convert_fusion.8), channel_id=1, source_target_pairs={{0,1},{1,0},{2,3},{3,2},{4,5},{5,4},{6,7},{7,6},{8,9},{9,8},{10,11... | collective-permute-start | bytes 1966088 | tf_op jit(solution)/shard_map/ppermute | solution.py:102
  115.2 17.4 %collective-permute-start.9 = (bf16[128,2560]{1,0:T(8,128)(2,1)}, bf16[128,2560]{1,0:T(8,128)(2,1)S(1)}, u32[]{:S(2)}, u32[]{:S(2)}) collective-permute-start(bf16[128,2560]{1,0:T(8,128)(2,1)} %multiply_convert_fusion.8), channel_id=1, source_target_pairs={{0,2},{2,0},{1,3},{3,1},{4,6},{6,4},{5,7},{7,5},{8,10},{10,8},{9,1... | collective-permute-start | bytes 1966088 | tf_op jit(solution)/shard_map/ppermute | solution.py:102
  132.5 2.1 %collective-permute-start.10 = (bf16[128,2560]{1,0:T(8,128)(2,1)S(1)}, bf16[128,2560]{1,0:T(8,128)(2,1)S(1)}, u32[]{:S(2)}, u32[]{:S(2)}) collective-permute-start(bf16[128,2560]{1,0:T(8,128)(2,1)S(1)} %collective-permute-done.9), channel_id=1, source_target_pairs={{0,1},{1,0},{2,3},{3,2},{4,5},{5,4},{6,7},{7,6},{8,9},{9,8},{10,11... | collective-permute-start | bytes 1966088 | tf_op jit(solution)/shard_map/ppermute | solution.py:102
  (20 other events, 46.9 us)

commit v17 on v14

--- a/solution.py
+++ b/solution.py
@@ -10,6 +10,7 @@
 
 epsilon = 1e-05
 highest = lax.Precision.HIGHEST
+high = lax.Precision.HIGH
 
 
 def passed_along(value, axis, steps):
@@ -48,7 +49,7 @@
     tail = jnp.exp(block_total[:, None, :] - cum_rate) * steps_b
     weighted = acts_b.astype(jnp.float32) * tail[:, :, :, None]
     ends = jnp.einsum(
-        "bshp,bsn->bhpn", weighted, writes_b.astype(jnp.float32), precision=highest
+        "bshp,bsn->bhpn", weighted, writes_b.astype(jnp.float32), precision=high
     )
     return within, cum_rate, ends, jnp.exp(block_total)
 
@@ -92,7 +93,7 @@
     block_states = starts + gains[:, :, None, None] * entering[None]
     count = within.shape[0]
     reads_b = reads.reshape(count, STRETCH, -1).astype(jnp.float32)
-    carried = jnp.einsum("btn,bhpn->bthp", reads_b, block_states, precision=highest)
+    carried = jnp.einsum("btn,bhpn->bthp", reads_b, block_states, precision=high)
     outputs = within + jnp.exp(cum_rate)[:, :, :, None] * carried
     return outputs.reshape(acts.shape)
 

time: 132 us -> 132 us (level)
  no operation moved by 1% of the time
where the time goes in v17:
time: 132 us; the launch traced here: 131 us
  waiting for transfers between devices  43.7 us (33%)
  matrix products  24.4 us (18%)
  starting transfers between devices  22.3 us (17%)
  local copies, waits for them, and re-layouts  20.9 us (16%)
  other arithmetic  18.2 us (14%)
    ppermute x6, waiting for transfers between devices, swapped(): lax.ppermute(value, axis, [(source, count - 1 - source) for source in ran...  38.6 us
    ppermute x6, starting transfers between devices, passed_along(): lax.ppermute(value, axis, [(source, source + steps) for source in range(f...  19 us
    unnamed x70, local copies, waits for them, and re-layouts  8.02 us
    add x6, other arithmetic, relay(): entering = passed_along(gain[:, None, None] * entering + state, axis, steps)  6.05 us
    dot_general x2, matrix products, block_parts(): jnp.einsum('bhts,bshp->bthp', weights, acts_b, preferred_element_type=jnp...  5.22 us
    ppermute x6, waiting for transfers between devices, passed_along(): lax.ppermute(value, axis, [(source, source + steps) for source in range(f...  5.14 us
    dot_general x4, matrix products, project(): jnp.dot(rows, value_weight, preferred_element_type=jnp.float32)  5.04 us
    dot_general x4, matrix products, project(): jnp.dot(rows, key_weight, preferred_element_type=jnp.float32)  4.35 us
  transfers between devices with their start and end apart: 12, of which 6 were waited for; matrix products, arithmetic and copies ran while one was open for 23% of the time, Pallas kernels for 0%

profile of v17, /device:TPU:0, one launch (start us, length us, event | category | flops | bytes accessed | tf_op | source)
XLA Modules:
  0.0 130.8 jit_solution(7012676691151181738)
XLA Ops:
  5.2 1.4 %bitcast_exponential_fusion = (f32[2,256,10]{1,2,0:T(8,128)}, f32[2,256,10]{1,2,0:T(8,128)S(1)}, f32[2,10,256]{2,1,0:T(8,128)}, f32[2,10,256]{2,1,0:T(8,128)}, f...) fusion(f32[2,10,256]{2,1,0:T(8,128)S(1)} %fusion.56, f32[10]{0:T(128)} %param.19, f32[2,256,10]{1,0,2:T(2,128)S(1)} %squeeze.53, ...), kind=kLoop, calls=%fused_computation.166 | loop fusion | flops 92160 | bytes 205000 | tf_op jit(solution)/shard_map/exp | solution.py:97
  7.8 2.2 %copy.21 = bf16[512,640]{0,1:T(8,128)(2,1)} copy(bf16[512,640]{1,0:T(8,128)(2,1)} %param.14) | data formatting | bytes 1310720 | tf_op args[0]
  10.1 2.7 %reshape_reshape.4 = bf16[2,256,10,64]{1,0,3,2:T(2,128)(2,1)} reshape(bf16[512,640]{0,1:T(8,128)(2,1)} %copy.21) | data formatting | bytes 1310720 | tf_op jit(solution)/shard_map/reshape;reshape | solution.py:27
  12.8 1.8 %convert_multiply_fusion.1 = (f32[2,256,10,64]{1,0,3,2:T(2,128)S(1)}, f32[2,256,10,64]{1,0,3,2:T(2,128)S(1)}) fusion(bf16[2,256,10,64]{1,0,3,2:T(2,128)(2,1)} %reshape_reshape.4, f32[2,256,10]{1,0,2:T(2,128)} %copy.27, f32[2,256,10]{1,0,2:T(2,128)} %copy.23), kind=kLoop, calls=%fused_computation.25 | loop fusion | flops 983040 | bytes 3317760 | tf_op jit(solution)/shard_map/mul | solution.py:50
  19.0 6.4 %collective-permute-start = (f32[10,64,128]{2,1,0:T(8,128)}, f32[10,64,128]{2,1,0:T(8,128)}, u32[]{:S(2)}, u32[]{:S(2)}) collective-permute-start(f32[10,64,128]{2,1,0:T(8,128)} %get-tuple-element.10), channel_id=1, source_target_pairs={{0,4},{4,8},{8,12},{1,5},{5,9},{9,13},{2,6},{6,10},{10,14},{3,7},{... | collective-permute-start | bytes 983048 | tf_op jit(solution)/shard_map/ppermute | solution.py:21
  26.1 2.6 %fusion.18 = f32[2,256,10,64]{1,3,2,0:T(8,128)} fusion(f32[2,10,256]{2,1,0:T(8,128)S(1)} %copy-done.24, f32[2,10,256]{2,1,0:T(8,128)S(1)} %copy-done.22, f32[2,256,256]{2,1,0:T(8,128)S(1)} %fusion.105, pred[256,256]{1,0:T(8,128)(4,1)S(1)} %iota_compare_fusion.1, bf16[2,256,10,64]{1,0,3,2:T(2,128)(2,1)S(1)} %copy-done.6), kind=kOutput, calls=%fused_computation.28 | convolution fusion | flops 174325760 | bytes 2596864 | tf_op jit(solution)/shard_map/bhts,bshp->bthp/dot_general | solution.py:48
  28.7 2.6 %fusion.17 = f32[2,256,10,64]{1,3,2,0:T(8,128)} fusion(f32[2,10,256]{2,1,0:T(8,128)S(1)} %copy-done.23, f32[2,10,256]{2,1,0:T(8,128)S(1)} %copy-done.20, f32[2,256,256]{2,1,0:T(8,128)S(1)} %fusion.106, pred[256,256]{1,0:T(8,128)(4,1)S(1)} %iota_compare_fusion, bf16[2,256,10,64]{1,0,3,2:T(2,128)(2,1)S(1)} %copy-done.6), kind=kOutput, calls=%fused_computation.27 | convolution fusion | flops 174325760 | bytes 2596864 | tf_op jit(solution)/shard_map/bhts,bshp->bthp/dot_general | solution.py:48
  34.2 3.4 %collective-permute-start.1 = (f32[10,64,128]{2,1,0:T(8,128)S(1)}, f32[10,64,128]{2,1,0:T(8,128)S(1)}, u32[]{:S(2)}, u32[]{:S(2)}) collective-permute-start(f32[10,64,128]{2,1,0:T(8,128)S(1)} %multiply_add_fusion.3), channel_id=1, source_target_pairs={{0,4},{4,8},{8,12},{1,5},{5,9},{9,13},{2,6},{6,10},{10,14},{3,7},{... | collective-permute-start | bytes 983048 | tf_op jit(solution)/shard_map/ppermute | solution.py:21
  41.2 2.5 %collective-permute-done.1 = f32[10,64,128]{2,1,0:T(8,128)S(1)} collective-permute-done((f32[10,64,128]{2,1,0:T(8,128)S(1)}, f32[10,64,128]{2,1,0:T(8,128)S(1)}, u32[]{:S(2)}, u32[]{:S(2)}) %collective-permute-start.1) | collective-permute-done | bytes 327712 | tf_op jit(solution)/shard_map/ppermute | solution.py:21
  44.6 5.1 %collective-permute-start.2 = (f32[10,64,128]{2,1,0:T(8,128)}, f32[10,64,128]{2,1,0:T(8,128)}, u32[]{:S(2)}, u32[]{:S(2)}) collective-permute-start(f32[10,64,128]{2,1,0:T(8,128)} %multiply_add_fusion.2), channel_id=1, source_target_pairs={{0,4},{4,8},{8,12},{1,5},{5,9},{9,13},{2,6},{6,10},{10,14},{3,7},{... | collective-permute-start | bytes 983048 | tf_op jit(solution)/shard_map/ppermute | solution.py:21
  50.6 1.5 %collective-permute-start.5 = (f32[10,64,128]{2,1,0:T(8,128)}, f32[10,64,128]{2,1,0:T(8,128)}, u32[]{:S(2)}, u32[]{:S(2)}) collective-permute-start(f32[10,64,128]{2,1,0:T(8,128)} %multiply_add_fusion), channel_id=1, source_target_pairs={{4,0},{8,4},{12,8},{5,1},{9,5},{13,9},{6,2},{10,6},{14,10},{7,3},{... | collective-permute-start | bytes 983048 | tf_op jit(solution)/shard_map/ppermute | solution.py:21
  56.4 1.7 %fusion.23 = f32[2,256,10,64]{1,3,2,0:T(8,128)S(1)} fusion(f32[2,256,10,64]{1,3,2,0:T(8,128)S(1)} %copy-done.7, bf16[2,256,128,1]{2,1,3,0:T(8,128)(2,1)S(1)} %bitcast.201, f32[1,10,64,128]{3,2,1,0:T(8,128)S(1)} %copy-done.8, f32[2,256,10]{1,2,0:T(8,128)S(1)} %copy-done.17, f32[10,64,128]{2,1,0:T(8,128)} %collective-permute-done.2, f32[2,10]{1,0:T(2,128)S(1)} %copy-done.26), kind=kOutput, calls=%fused_computation.35 | convolution fusion | flops 252641280 | bytes 3428432 | tf_op jit(solution)/shard_map/btn,bhpn->bthp/dot_general | solution.py:96
  58.1 2.6 %collective-permute-done.5 = f32[10,64,128]{2,1,0:T(8,128)} collective-permute-done((f32[10,64,128]{2,1,0:T(8,128)}, f32[10,64,128]{2,1,0:T(8,128)}, u32[]{:S(2)}, u32[]{:S(2)}) %collective-permute-start.5) | collective-permute-done | bytes 327712 | tf_op jit(solution)/shard_map/ppermute | solution.py:21
  60.7 1.7 %fusion.21 = f32[2,256,10,64]{1,3,2,0:T(8,128)S(1)} fusion(f32[2,256,10,64]{1,3,2,0:T(8,128)S(1)} %fusion.23, f32[2,256,10,64]{1,3,2,0:T(8,128)S(1)} %copy-done.9, bf16[2,256,128,1]{2,1,3,0:T(8,128)(2,1)S(1)} %bitcast.207, f32[1,10,64,128]{3,2,1,0:T(8,128)S(1)} %copy-done.13, f32[2,256,10]{1,2,0:T(8,128)S(1)} %copy-done.18, ...), kind=kOutput, calls=%fused_computation.32 | convolution fusion | flops 252968960 | bytes 4739152 | tf_op jit(solution)/shard_map/btn,bhpn->bthp/dot_general | solution.py:96
  64.6 2.8 %copy.30 = f32[512,640]{1,0:T(8,128)} copy(f32[512,640]{0,1:T(8,128)} %bitcast.192) | data formatting | bytes 2621440 | tf_op jit(solution)/shard_map/add | solution.py:202
  67.4 2.3 %multiply_reduce_fusion.1 = (f32[512]{0:T(512)S(1)}, f32[512,640]{1,0:T(8,128)S(1)}) fusion(bf16[512,640]{1,0:T(8,128)(2,1)} %param.15, f32[512,640]{1,0:T(8,128)} %copy.30, bf16[512,640]{1,0:T(8,128)(2,1)} %param.14, f32[640]{0:T(1024)S(1)} %mul.330), kind=kLoop, calls=%fused_computation.47 | loop fusion | flops 3603968 | bytes 3936768 | tf_op jit(solution)/shard_map/reduce_sum | solution.py:206
  75.7 1.5 %collective-permute-start.8 = (f32[128,2560]{1,0:T(8,128)S(1)}, f32[128,2560]{1,0:T(8,128)S(1)}, u32[]{:S(2)}, u32[]{:S(2)}) collective-permute-start(f32[128,2560]{1,0:T(8,128)S(1)} %fusion), channel_id=1, source_target_pairs={{0,2},{2,0},{1,3},{3,1},{4,6},{6,4},{5,7},{7,5},{8,10},{10,8},{9,1... | collective-permute-start | bytes 3932168 | tf_op jit(solution)/shard_map/ppermute | solution.py:103
  77.5 29.1 %collective-permute-done.8 = f32[128,2560]{1,0:T(8,128)S(1)} collective-permute-done((f32[128,2560]{1,0:T(8,128)S(1)}, f32[128,2560]{1,0:T(8,128)S(1)}, u32[]{:S(2)}, u32[]{:S(2)}) %collective-permute-start.8) | collective-permute-done | bytes 1310752 | tf_op jit(solution)/shard_map/ppermute | solution.py:103
  108.5 1.4 %collective-permute-start.9 = (bf16[128,2560]{1,0:T(8,128)(2,1)}, bf16[128,2560]{1,0:T(8,128)(2,1)S(1)}, u32[]{:S(2)}, u32[]{:S(2)}) collective-permute-start(bf16[128,2560]{1,0:T(8,128)(2,1)} %multiply_convert_fusion.8), channel_id=1, source_target_pairs={{0,2},{2,0},{1,3},{3,1},{4,6},{6,4},{5,7},{7,5},{8,10},{10,8},{9,1... | collective-permute-start | bytes 1966088 | tf_op jit(solution)/shard_map/ppermute | solution.py:103
  109.9 2.4 %fusion.39 = bf16[1,1,128,512]{3,2,1,0:T(8,128)(2,1)S(1)} fusion(bf16[128,2560]{1,0:T(8,128)(2,1)} %multiply_convert_fusion.8, bf16[2560,512]{1,0:T(8,128)(2,1)} %param.27), kind=kOutput, calls=%fused_computation.63 | convolution fusion | flops 335609856 | bytes 3407872 | tf_op jit(solution)/shard_map/dot_general | solution.py:152
  112.4 1.7 %fusion.35 = bf16[1,1,128,512]{3,2,1,0:T(8,128)(2,1)S(1)} fusion(bf16[128,2560]{1,0:T(8,128)(2,1)} %multiply_convert_fusion.8, bf16[2560,512]{1,0:T(8,128)(2,1)S(1)} %copy-done.2), kind=kOutput, calls=%fused_computation.59 | convolution fusion | flops 335609856 | bytes 3407872 | tf_op jit(solution)/shard_map/dot_general | solution.py:151
  114.3 1.6 %fusion.38 = bf16[1,1,128,512]{3,2,1,0:T(8,128)(2,1)S(1)} fusion(bf16[128,2560]{1,0:T(8,128)(2,1)} %collective-permute-done.11, bf16[2560,512]{1,0:T(8,128)(2,1)S(1)} %copy-done.1), kind=kOutput, calls=%fused_computation.62 | convolution fusion | flops 335609856 | bytes 3407872 | tf_op jit(solution)/shard_map/dot_general | solution.py:152
  116.0 1.6 %fusion.34 = bf16[1,1,128,512]{3,2,1,0:T(8,128)(2,1)S(1)} fusion(bf16[128,2560]{1,0:T(8,128)(2,1)} %collective-permute-done.11, bf16[2560,512]{1,0:T(8,128)(2,1)S(1)} %copy-done.2), kind=kOutput, calls=%fused_computation.58 | convolution fusion | flops 335609856 | bytes 3407872 | tf_op jit(solution)/shard_map/dot_general | solution.py:151
  117.6 8.3 %collective-permute-done.9 = bf16[128,2560]{1,0:T(8,128)(2,1)S(1)} collective-permute-done((bf16[128,2560]{1,0:T(8,128)(2,1)}, bf16[128,2560]{1,0:T(8,128)(2,1)S(1)}, u32[]{:S(2)}, u32[]{:S(2)}) %collective-permute-start.9) | collective-permute-done | bytes 655392 | tf_op jit(solution)/shard_map/ppermute | solution.py:103
  (145 shorter events, 38.6 us)
Async XLA Ops:
  0.6 69.8 %copy-start = (bf16[640,2560]{1,0:T(8,128)(2,1)S(1)}, bf16[640,2560]{1,0:T(8,128)(2,1)}, u32[]{:S(2)}) copy-start(bf16[640,2560]{1,0:T(8,128)(2,1)} %param.23) | copy-start | bytes 9830404
  7.8 4.9 %copy-start.15 = (bf16[2,512,128]{2,1,0:T(8,128)(2,1)S(1)}, bf16[2,512,128]{2,1,0:T(8,128)(2,1)}, u32[]{:S(2)}) copy-start(bf16[2,512,128]{2,1,0:T(8,128)(2,1)} %param.16) | copy-start | bytes 786436
  16.2 21.4 %collective-permute-start.3 = (f32[10,64,128]{2,1,0:T(8,128)}, f32[10,64,128]{2,1,0:T(8,128)}, u32[]{:S(2)}, u32[]{:S(2)}) collective-permute-start(f32[10,64,128]{2,1,0:T(8,128)} %get-tuple-element.6), channel_id=1, source_target_pairs={{4,0},{8,4},{12,8},{5,1},{9,5},{13,9},{6,2},{10,6},{14,10},{7,3},{... | collective-permute-start | bytes 983048 | tf_op jit(solution)/shard_map/ppermute | solution.py:21
  17.5 8.0 %copy-start.16 = (bf16[2,512,128]{2,1,0:T(8,128)(2,1)S(1)}, bf16[2,512,128]{2,1,0:T(8,128)(2,1)}, u32[]{:S(2)}) copy-start(bf16[2,512,128]{2,1,0:T(8,128)(2,1)} %param.17) | copy-start | bytes 786436
  19.0 7.0 %copy-start.6 = (bf16[2,256,10,64]{1,0,3,2:T(2,128)(2,1)S(1)}, bf16[2,256,10,64]{1,0,3,2:T(2,128)(2,1)}, u32[]{:S(2)}) copy-start(bf16[2,256,10,64]{1,0,3,2:T(2,128)(2,1)} %reshape_reshape.4) | copy-start | bytes 1966084
  19.0 7.0 %copy-start.22 = (f32[2,10,256]{2,1,0:T(8,128)S(1)}, f32[2,10,256]{2,1,0:T(8,128)}, u32[]{:S(2)}) copy-start(f32[2,10,256]{2,1,0:T(8,128)} %copy-done.21) | copy-start | bytes 61444
  19.0 7.0 %copy-start.24 = (f32[2,10,256]{2,1,0:T(8,128)S(1)}, f32[2,10,256]{2,1,0:T(8,128)}, u32[]{:S(2)}) copy-start(f32[2,10,256]{2,1,0:T(8,128)} %get-tuple-element.38) | copy-start | bytes 61444
  19.0 13.9 %collective-permute-start = (f32[10,64,128]{2,1,0:T(8,128)}, f32[10,64,128]{2,1,0:T(8,128)}, u32[]{:S(2)}, u32[]{:S(2)}) collective-permute-start(f32[10,64,128]{2,1,0:T(8,128)} %get-tuple-element.10), channel_id=1, source_target_pairs={{0,4},{4,8},{8,12},{1,5},{5,9},{9,13},{2,6},{6,10},{10,14},{3,7},{... | collective-permute-start | bytes 983048 | tf_op jit(solution)/shard_map/ppermute | solution.py:21
  32.9 7.2 %copy-start.14 = (bf16[512,640]{1,0:T(8,128)(2,1)S(1)}, bf16[512,640]{1,0:T(8,128)(2,1)}, u32[]{:S(2)}) copy-start(bf16[512,640]{1,0:T(8,128)(2,1)} %param.24) | copy-start | bytes 1966084
  34.2 9.6 %collective-permute-start.1 = (f32[10,64,128]{2,1,0:T(8,128)S(1)}, f32[10,64,128]{2,1,0:T(8,128)S(1)}, u32[]{:S(2)}, u32[]{:S(2)}) collective-permute-start(f32[10,64,128]{2,1,0:T(8,128)S(1)} %multiply_add_fusion.3), channel_id=1, source_target_pairs={{0,4},{4,8},{8,12},{1,5},{5,9},{9,13},{2,6},{6,10},{10,14},{3,7},{... | collective-permute-start | bytes 983048 | tf_op jit(solution)/shard_map/ppermute | solution.py:21
  37.6 6.2 %copy-start.5 = (f32[10,64,128]{2,1,0:T(8,128)S(1)}, f32[10,64,128]{2,1,0:T(8,128)}, u32[]{:S(2)}) copy-start(f32[10,64,128]{2,1,0:T(8,128)} %get-tuple-element.11) | copy-start | bytes 983044
  38.8 10.9 %collective-permute-start.4 = (f32[10,64,128]{2,1,0:T(8,128)S(1)}, f32[10,64,128]{2,1,0:T(8,128)S(1)}, u32[]{:S(2)}, u32[]{:S(2)}) collective-permute-start(f32[10,64,128]{2,1,0:T(8,128)S(1)} %multiply_add_fusion.1), channel_id=1, source_target_pairs={{4,0},{8,4},{12,8},{5,1},{9,5},{13,9},{6,2},{10,6},{14,10},{7,3},{... | collective-permute-start | bytes 983048 | tf_op jit(solution)/shard_map/ppermute | solution.py:21
  40.1 9.6 %copy-start.4 = (f32[10,64,128]{2,1,0:T(8,128)S(1)}, f32[10,64,128]{2,1,0:T(8,128)}, u32[]{:S(2)}) copy-start(f32[10,64,128]{2,1,0:T(8,128)} %get-tuple-element.7) | copy-start | bytes 983044
  41.2 11.4 %copy-start.30 = (f32[1,10]{1,0:T(1,128)S(1)}, f32[1,10]{1,0:T(1,128)}, u32[]{:S(2)}) copy-start(f32[1,10]{1,0:T(1,128)} %get-tuple-element.30) | copy-start | bytes 124
  41.2 12.0 %copy-start.31 = (f32[10]{0:T(128)S(1)}, f32[10]{0:T(128)}, u32[]{:S(2)}) copy-start(f32[10]{0:T(128)} %param.21) | copy-start | bytes 124
  44.6 11.1 %collective-permute-start.2 = (f32[10,64,128]{2,1,0:T(8,128)}, f32[10,64,128]{2,1,0:T(8,128)}, u32[]{:S(2)}, u32[]{:S(2)}) collective-permute-start(f32[10,64,128]{2,1,0:T(8,128)} %multiply_add_fusion.2), channel_id=1, source_target_pairs={{0,4},{4,8},{8,12},{1,5},{5,9},{9,13},{2,6},{6,10},{10,14},{3,7},{... | collective-permute-start | bytes 983048 | tf_op jit(solution)/shard_map/ppermute | solution.py:21
  50.6 10.1 %collective-permute-start.5 = (f32[10,64,128]{2,1,0:T(8,128)}, f32[10,64,128]{2,1,0:T(8,128)}, u32[]{:S(2)}, u32[]{:S(2)}) collective-permute-start(f32[10,64,128]{2,1,0:T(8,128)} %multiply_add_fusion), channel_id=1, source_target_pairs={{4,0},{8,4},{12,8},{5,1},{9,5},{13,9},{6,2},{10,6},{14,10},{7,3},{... | collective-permute-start | bytes 983048 | tf_op jit(solution)/shard_map/ppermute | solution.py:21
  56.4 4.3 %copy-start.13 = (f32[1,10,64,128]{3,2,1,0:T(8,128)S(1)}, f32[1,10,64,128]{3,2,1,0:T(8,128)}, u32[]{:S(2)}) copy-start(f32[1,10,64,128]{3,2,1,0:T(8,128)} %slice_add_fusion) | copy-start | bytes 983044
  71.9 3.1 %collective-permute-start.7 = (f32[128,2560]{1,0:T(8,128)S(1)}, f32[128,2560]{1,0:T(8,128)S(1)}, u32[]{:S(2)}, u32[]{:S(2)}) collective-permute-start(f32[128,2560]{1,0:T(8,128)S(1)} %convolution_add_fusion), channel_id=1, source_target_pairs={{0,1},{1,0},{2,3},{3,2},{4,5},{5,4},{6,7},{7,6},{8,9},{9,8},{10,11... | collective-permute-start | bytes 3932168 | tf_op jit(solution)/shard_map/ppermute | solution.py:103
  74.4 3.2 %collective-permute-start.6 = (f32[128,2560]{1,0:T(8,128)S(1)}, f32[128,2560]{1,0:T(8,128)S(1)}, u32[]{:S(2)}, u32[]{:S(2)}) collective-permute-start(f32[128,2560]{1,0:T(8,128)S(1)} %convolution_add_fusion.2), channel_id=1, source_target_pairs={{0,1},{1,0},{2,3},{3,2},{4,5},{5,4},{6,7},{7,6},{8,9},{9,8},{10,11... | collective-permute-start | bytes 3932168 | tf_op jit(solution)/shard_map/ppermute | solution.py:103
  75.7 30.9 %collective-permute-start.8 = (f32[128,2560]{1,0:T(8,128)S(1)}, f32[128,2560]{1,0:T(8,128)S(1)}, u32[]{:S(2)}, u32[]{:S(2)}) collective-permute-start(f32[128,2560]{1,0:T(8,128)S(1)} %fusion), channel_id=1, source_target_pairs={{0,2},{2,0},{1,3},{3,1},{4,6},{6,4},{5,7},{7,5},{8,10},{10,8},{9,1... | collective-permute-start | bytes 3932168 | tf_op jit(solution)/shard_map/ppermute | solution.py:103
  108.5 5.7 %collective-permute-start.11 = (bf16[128,2560]{1,0:T(8,128)(2,1)}, bf16[128,2560]{1,0:T(8,128)(2,1)}, u32[]{:S(2)}, u32[]{:S(2)}) collective-permute-start(bf16[128,2560]{1,0:T(8,128)(2,1)} %multiply_convert_fusion.8), channel_id=1, source_target_pairs={{0,1},{1,0},{2,3},{3,2},{4,5},{5,4},{6,7},{7,6},{8,9},{9,8},{10,11... | collective-permute-start | bytes 1966088 | tf_op jit(solution)/shard_map/ppermute | solution.py:103
  108.5 17.4 %collective-permute-start.9 = (bf16[128,2560]{1,0:T(8,128)(2,1)}, bf16[128,2560]{1,0:T(8,128)(2,1)S(1)}, u32[]{:S(2)}, u32[]{:S(2)}) collective-permute-start(bf16[128,2560]{1,0:T(8,128)(2,1)} %multiply_convert_fusion.8), channel_id=1, source_target_pairs={{0,2},{2,0},{1,3},{3,1},{4,6},{6,4},{5,7},{7,5},{8,10},{10,8},{9,1... | collective-permute-start | bytes 1966088 | tf_op jit(solution)/shard_map/ppermute | solution.py:103
  125.9 2.1 %collective-permute-start.10 = (bf16[128,2560]{1,0:T(8,128)(2,1)S(1)}, bf16[128,2560]{1,0:T(8,128)(2,1)S(1)}, u32[]{:S(2)}, u32[]{:S(2)}) collective-permute-start(bf16[128,2560]{1,0:T(8,128)(2,1)S(1)} %collective-permute-done.9), channel_id=1, source_target_pairs={{0,1},{1,0},{2,3},{3,2},{4,5},{5,4},{6,7},{7,6},{8,9},{9,8},{10,11... | collective-permute-start | bytes 1966088 | tf_op jit(solution)/shard_map/ppermute | solution.py:103
  (20 other events, 45.0 us)

commit v18 on v14

--- a/solution.py
+++ b/solution.py
@@ -202,7 +202,10 @@
     summed = with_layout_constraint(summed.reshape(tokens, heads * width), Layout((0, 1)))
     gated = summed * jax.nn.silu(gate_acts.astype(jnp.float32))
     grouped = gated.reshape(tokens, NORM_GROUPS // (lax.axis_size("head_chip") * lax.axis_size("head_core")), -1)
-    scaled = grouped * lax.rsqrt(jnp.mean(grouped * grouped, axis=2, keepdims=True) + epsilon)
+    squares = jnp.einsum(
+        "tgc,c->tg", grouped * grouped, jnp.ones((grouped.shape[2],), jnp.float32), precision=highest
+    )
+    scaled = grouped * lax.rsqrt(squares[:, :, None] / grouped.shape[2] + epsilon)
     mixed = (scaled.reshape(tokens, -1) * norm_gain[None, :]).astype(jnp.bfloat16)
     encoded = owned_rows(mixed, out_weight, residual)
     normed = (

time: 132 us -> 133 us (level)
    reduce_sum x1 -> x0, other arithmetic: 2.27 us -> none  [per_device(): jnp.mean(grouped * grouped, axis=2, keepdims=True) + epsilon]
    mul x1 -> x2, other arithmetic: 0.15 us -> 2.27 us  [the longest x1 2.11 us: per_device(): gated = summed * jax.nn.silu(gate_acts.astype(jnp.float32))]
where the time goes in v18:
time: 133 us; the launch traced here: 132 us
  waiting for transfers between devices  43.5 us (33%)
  matrix products  26.4 us (20%)
  starting transfers between devices  22.4 us (17%)
  local copies, waits for them, and re-layouts  20.8 us (16%)
  other arithmetic  18 us (14%)
    ppermute x6, waiting for transfers between devices, swapped(): lax.ppermute(value, axis, [(source, count - 1 - source) for source in ran...  38.5 us
    ppermute x6, starting transfers between devices, passed_along(): lax.ppermute(value, axis, [(source, source + steps) for source in range(f...  18.9 us
    unnamed x70, local copies, waits for them, and re-layouts  8.06 us
    add x6, other arithmetic, relay(): entering = passed_along(gain[:, None, None] * entering + state, axis, steps)  6.05 us
    dot_general x2, matrix products, block_parts(): jnp.einsum('bhts,bshp->bthp', weights, acts_b, preferred_element_type=jnp...  5.27 us
    dot_general x4, matrix products, project(): jnp.dot(rows, value_weight, preferred_element_type=jnp.float32)  5.05 us
    ppermute x6, waiting for transfers between devices, passed_along(): lax.ppermute(value, axis, [(source, source + steps) for source in range(f...  4.97 us
    dot_general x4, matrix products, project(): jnp.dot(rows, key_weight, preferred_element_type=jnp.float32)  4.35 us
  transfers between devices with their start and end apart: 12, of which 6 were waited for; matrix products, arithmetic and copies ran while one was open for 23% of the time, Pallas kernels for 0%

profile of v18, /device:TPU:0, one launch (start us, length us, event | category | flops | bytes accessed | tf_op | source)
XLA Modules:
  0.0 132.5 jit_solution(17655421364294542178)
XLA Ops:
  5.1 1.4 %bitcast_exponential_fusion = (f32[2,256,10]{1,2,0:T(8,128)}, f32[2,256,10]{1,2,0:T(8,128)S(1)}, f32[2,10,256]{2,1,0:T(8,128)}, f32[2,10,256]{2,1,0:T(8,128)}, f...) fusion(f32[2,10,256]{2,1,0:T(8,128)S(1)} %fusion.58, f32[10]{0:T(128)} %param.19, f32[2,256,10]{1,0,2:T(2,128)S(1)} %squeeze.53, ...), kind=kLoop, calls=%fused_computation.168 | loop fusion | flops 92160 | bytes 205000 | tf_op jit(solution)/shard_map/exp | solution.py:96
  7.8 2.3 %copy.21 = bf16[512,640]{0,1:T(8,128)(2,1)} copy(bf16[512,640]{1,0:T(8,128)(2,1)} %param.14) | data formatting | bytes 1310720 | tf_op args[0]
  10.0 2.7 %reshape_reshape.4 = bf16[2,256,10,64]{1,0,3,2:T(2,128)(2,1)} reshape(bf16[512,640]{0,1:T(8,128)(2,1)} %copy.21) | data formatting | bytes 1310720 | tf_op jit(solution)/shard_map/reshape;reshape | solution.py:26
  12.7 1.8 %convert_multiply_fusion.1 = (f32[2,256,10,64]{1,0,3,2:T(2,128)S(1)}, f32[2,256,10,64]{1,0,3,2:T(2,128)S(1)}) fusion(bf16[2,256,10,64]{1,0,3,2:T(2,128)(2,1)} %reshape_reshape.4, f32[2,256,10]{1,0,2:T(2,128)} %copy.27, f32[2,256,10]{1,0,2:T(2,128)} %copy.23), kind=kLoop, calls=%fused_computation.25 | loop fusion | flops 983040 | bytes 3317760 | tf_op jit(solution)/shard_map/mul | solution.py:49
  19.4 6.4 %collective-permute-start = (f32[10,64,128]{2,1,0:T(8,128)}, f32[10,64,128]{2,1,0:T(8,128)}, u32[]{:S(2)}, u32[]{:S(2)}) collective-permute-start(f32[10,64,128]{2,1,0:T(8,128)} %get-tuple-element.8), channel_id=1, source_target_pairs={{0,4},{4,8},{8,12},{1,5},{5,9},{9,13},{2,6},{6,10},{10,14},{3,7},{... | collective-permute-start | bytes 983048 | tf_op jit(solution)/shard_map/ppermute | solution.py:20
  26.4 2.6 %fusion.18 = f32[2,256,10,64]{1,3,2,0:T(8,128)} fusion(f32[2,10,256]{2,1,0:T(8,128)S(1)} %copy-done.24, f32[2,10,256]{2,1,0:T(8,128)S(1)} %copy-done.22, f32[2,256,256]{2,1,0:T(8,128)S(1)} %fusion.108, pred[256,256]{1,0:T(8,128)(4,1)S(1)} %iota_compare_fusion.1, bf16[2,256,10,64]{1,0,3,2:T(2,128)(2,1)S(1)} %copy-done.6), kind=kOutput, calls=%fused_computation.28 | convolution fusion | flops 174325760 | bytes 2596864 | tf_op jit(solution)/shard_map/bhts,bshp->bthp/dot_general | solution.py:47
  29.0 2.6 %fusion.17 = f32[2,256,10,64]{1,3,2,0:T(8,128)} fusion(f32[2,10,256]{2,1,0:T(8,128)S(1)} %copy-done.23, f32[2,10,256]{2,1,0:T(8,128)S(1)} %copy-done.20, f32[2,256,256]{2,1,0:T(8,128)S(1)} %fusion.109, pred[256,256]{1,0:T(8,128)(4,1)S(1)} %iota_compare_fusion, bf16[2,256,10,64]{1,0,3,2:T(2,128)(2,1)S(1)} %copy-done.6), kind=kOutput, calls=%fused_computation.27 | convolution fusion | flops 174325760 | bytes 2596864 | tf_op jit(solution)/shard_map/bhts,bshp->bthp/dot_general | solution.py:47
  34.5 3.4 %collective-permute-start.1 = (f32[10,64,128]{2,1,0:T(8,128)S(1)}, f32[10,64,128]{2,1,0:T(8,128)S(1)}, u32[]{:S(2)}, u32[]{:S(2)}) collective-permute-start(f32[10,64,128]{2,1,0:T(8,128)S(1)} %multiply_add_fusion.3), channel_id=1, source_target_pairs={{0,4},{4,8},{8,12},{1,5},{5,9},{9,13},{2,6},{6,10},{10,14},{3,7},{... | collective-permute-start | bytes 983048 | tf_op jit(solution)/shard_map/ppermute | solution.py:20
  41.6 2.6 %collective-permute-done.1 = f32[10,64,128]{2,1,0:T(8,128)S(1)} collective-permute-done((f32[10,64,128]{2,1,0:T(8,128)S(1)}, f32[10,64,128]{2,1,0:T(8,128)S(1)}, u32[]{:S(2)}, u32[]{:S(2)}) %collective-permute-start.1) | collective-permute-done | bytes 327712 | tf_op jit(solution)/shard_map/ppermute | solution.py:20
  45.0 5.1 %collective-permute-start.2 = (f32[10,64,128]{2,1,0:T(8,128)}, f32[10,64,128]{2,1,0:T(8,128)}, u32[]{:S(2)}, u32[]{:S(2)}) collective-permute-start(f32[10,64,128]{2,1,0:T(8,128)} %multiply_add_fusion.2), channel_id=1, source_target_pairs={{0,4},{4,8},{8,12},{1,5},{5,9},{9,13},{2,6},{6,10},{10,14},{3,7},{... | collective-permute-start | bytes 983048 | tf_op jit(solution)/shard_map/ppermute | solution.py:20
  50.9 1.5 %collective-permute-start.5 = (f32[10,64,128]{2,1,0:T(8,128)}, f32[10,64,128]{2,1,0:T(8,128)}, u32[]{:S(2)}, u32[]{:S(2)}) collective-permute-start(f32[10,64,128]{2,1,0:T(8,128)} %multiply_add_fusion), channel_id=1, source_target_pairs={{4,0},{8,4},{12,8},{5,1},{9,5},{13,9},{6,2},{10,6},{14,10},{7,3},{... | collective-permute-start | bytes 983048 | tf_op jit(solution)/shard_map/ppermute | solution.py:20
  56.8 1.9 %fusion.23 = f32[2,256,10,64]{1,3,2,0:T(8,128)S(1)} fusion(f32[2,256,10,64]{1,3,2,0:T(8,128)S(1)} %copy-done.7, bf16[2,256,128,1]{2,1,3,0:T(8,128)(2,1)S(1)} %bitcast.202, f32[1,10,64,128]{3,2,1,0:T(8,128)S(1)} %copy-done.8, f32[2,256,10]{1,2,0:T(8,128)S(1)} %copy-done.17, f32[10,64,128]{2,1,0:T(8,128)} %collective-permute-done.2, f32[2,10]{1,0:T(2,128)S(1)} %copy-done.26), kind=kOutput, calls=%fused_computation.35 | convolution fusion | flops 504299520 | bytes 3428432 | tf_op jit(solution)/shard_map/btn,bhpn->bthp/dot_general | solution.py:95
  58.7 2.4 %collective-permute-done.5 = f32[10,64,128]{2,1,0:T(8,128)} collective-permute-done((f32[10,64,128]{2,1,0:T(8,128)}, f32[10,64,128]{2,1,0:T(8,128)}, u32[]{:S(2)}, u32[]{:S(2)}) %collective-permute-start.5) | collective-permute-done | bytes 327712 | tf_op jit(solution)/shard_map/ppermute | solution.py:20
  61.1 1.8 %fusion.21 = f32[2,256,10,64]{1,3,2,0:T(8,128)S(1)} fusion(f32[2,256,10,64]{1,3,2,0:T(8,128)S(1)} %fusion.23, f32[2,256,10,64]{1,3,2,0:T(8,128)S(1)} %copy-done.9, bf16[2,256,128,1]{2,1,3,0:T(8,128)(2,1)S(1)} %bitcast.208, f32[1,10,64,128]{3,2,1,0:T(8,128)S(1)} %copy-done.13, f32[2,256,10]{1,2,0:T(8,128)S(1)} %copy-done.18, ...), kind=kOutput, calls=%fused_computation.32 | convolution fusion | flops 504627200 | bytes 4739152 | tf_op jit(solution)/shard_map/btn,bhpn->bthp/dot_general | solution.py:95
  65.2 2.8 %copy.30 = f32[512,640]{1,0:T(8,128)} copy(f32[512,640]{0,1:T(8,128)} %bitcast.193) | data formatting | bytes 2621440 | tf_op jit(solution)/shard_map/add | solution.py:201
  68.0 2.1 %fusion.27 = f32[512,640]{1,0:T(8,128)S(1)} fusion(bf16[512,640]{1,0:T(8,128)(2,1)} %param.15, f32[512,640]{1,0:T(8,128)} %copy.30, bf16[512,640]{1,0:T(8,128)(2,1)} %param.14, f32[640]{0:T(1024)S(1)} %mul.330), kind=kLoop, calls=%fused_computation.39 | loop fusion | flops 2949120 | bytes 3934720 | tf_op jit(solution)/shard_map/mul | solution.py:203
  77.4 1.5 %collective-permute-start.8 = (f32[128,2560]{1,0:T(8,128)S(1)}, f32[128,2560]{1,0:T(8,128)S(1)}, u32[]{:S(2)}, u32[]{:S(2)}) collective-permute-start(f32[128,2560]{1,0:T(8,128)S(1)} %fusion), channel_id=1, source_target_pairs={{0,2},{2,0},{1,3},{3,1},{4,6},{6,4},{5,7},{7,5},{8,10},{10,8},{9,1... | collective-permute-start | bytes 3932168 | tf_op jit(solution)/shard_map/ppermute | solution.py:102
  79.3 29.0 %collective-permute-done.8 = f32[128,2560]{1,0:T(8,128)S(1)} collective-permute-done((f32[128,2560]{1,0:T(8,128)S(1)}, f32[128,2560]{1,0:T(8,128)S(1)}, u32[]{:S(2)}, u32[]{:S(2)}) %collective-permute-start.8) | collective-permute-done | bytes 1310752 | tf_op jit(solution)/shard_map/ppermute | solution.py:102
  110.2 1.5 %collective-permute-start.9 = (bf16[128,2560]{1,0:T(8,128)(2,1)}, bf16[128,2560]{1,0:T(8,128)(2,1)S(1)}, u32[]{:S(2)}, u32[]{:S(2)}) collective-permute-start(bf16[128,2560]{1,0:T(8,128)(2,1)} %multiply_convert_fusion.8), channel_id=1, source_target_pairs={{0,2},{2,0},{1,3},{3,1},{4,6},{6,4},{5,7},{7,5},{8,10},{10,8},{9,1... | collective-permute-start | bytes 1966088 | tf_op jit(solution)/shard_map/ppermute | solution.py:102
  111.6 2.4 %fusion.41 = bf16[1,1,128,512]{3,2,1,0:T(8,128)(2,1)S(1)} fusion(bf16[128,2560]{1,0:T(8,128)(2,1)} %multiply_convert_fusion.8, bf16[2560,512]{1,0:T(8,128)(2,1)} %param.27), kind=kOutput, calls=%fused_computation.64 | convolution fusion | flops 335609856 | bytes 3407872 | tf_op jit(solution)/shard_map/dot_general | solution.py:151
  114.1 1.7 %fusion.37 = bf16[1,1,128,512]{3,2,1,0:T(8,128)(2,1)S(1)} fusion(bf16[128,2560]{1,0:T(8,128)(2,1)} %multiply_convert_fusion.8, bf16[2560,512]{1,0:T(8,128)(2,1)S(1)} %copy-done.2), kind=kOutput, calls=%fused_computation.60 | convolution fusion | flops 335609856 | bytes 3407872 | tf_op jit(solution)/shard_map/dot_general | solution.py:150
  116.0 1.6 %fusion.40 = bf16[1,1,128,512]{3,2,1,0:T(8,128)(2,1)S(1)} fusion(bf16[128,2560]{1,0:T(8,128)(2,1)} %collective-permute-done.11, bf16[2560,512]{1,0:T(8,128)(2,1)S(1)} %copy-done.1), kind=kOutput, calls=%fused_computation.63 | convolution fusion | flops 335609856 | bytes 3407872 | tf_op jit(solution)/shard_map/dot_general | solution.py:151
  117.7 1.6 %fusion.36 = bf16[1,1,128,512]{3,2,1,0:T(8,128)(2,1)S(1)} fusion(bf16[128,2560]{1,0:T(8,128)(2,1)} %collective-permute-done.11, bf16[2560,512]{1,0:T(8,128)(2,1)S(1)} %copy-done.2), kind=kOutput, calls=%fused_computation.59 | convolution fusion | flops 335609856 | bytes 3407872 | tf_op jit(solution)/shard_map/dot_general | solution.py:150
  119.3 8.2 %collective-permute-done.9 = bf16[128,2560]{1,0:T(8,128)(2,1)S(1)} collective-permute-done((bf16[128,2560]{1,0:T(8,128)(2,1)}, bf16[128,2560]{1,0:T(8,128)(2,1)S(1)}, u32[]{:S(2)}, u32[]{:S(2)}) %collective-permute-start.9) | collective-permute-done | bytes 655392 | tf_op jit(solution)/shard_map/ppermute | solution.py:102
  (146 shorter events, 40.2 us)
Async XLA Ops:
  0.6 71.5 %copy-start = (bf16[640,2560]{1,0:T(8,128)(2,1)S(1)}, bf16[640,2560]{1,0:T(8,128)(2,1)}, u32[]{:S(2)}) copy-start(bf16[640,2560]{1,0:T(8,128)(2,1)} %param.23) | copy-start | bytes 9830404
  7.8 4.9 %copy-start.15 = (bf16[2,512,128]{2,1,0:T(8,128)(2,1)S(1)}, bf16[2,512,128]{2,1,0:T(8,128)(2,1)}, u32[]{:S(2)}) copy-start(bf16[2,512,128]{2,1,0:T(8,128)(2,1)} %param.16) | copy-start | bytes 786436
  16.3 21.6 %collective-permute-start.3 = (f32[10,64,128]{2,1,0:T(8,128)}, f32[10,64,128]{2,1,0:T(8,128)}, u32[]{:S(2)}, u32[]{:S(2)}) collective-permute-start(f32[10,64,128]{2,1,0:T(8,128)} %get-tuple-element.4), channel_id=1, source_target_pairs={{4,0},{8,4},{12,8},{5,1},{9,5},{13,9},{6,2},{10,6},{14,10},{7,3},{... | collective-permute-start | bytes 983048 | tf_op jit(solution)/shard_map/ppermute | solution.py:20
  17.6 8.2 %copy-start.16 = (bf16[2,512,128]{2,1,0:T(8,128)(2,1)S(1)}, bf16[2,512,128]{2,1,0:T(8,128)(2,1)}, u32[]{:S(2)}) copy-start(bf16[2,512,128]{2,1,0:T(8,128)(2,1)} %param.17) | copy-start | bytes 786436
  19.4 7.0 %copy-start.6 = (bf16[2,256,10,64]{1,0,3,2:T(2,128)(2,1)S(1)}, bf16[2,256,10,64]{1,0,3,2:T(2,128)(2,1)}, u32[]{:S(2)}) copy-start(bf16[2,256,10,64]{1,0,3,2:T(2,128)(2,1)} %reshape_reshape.4) | copy-start | bytes 1966084
  19.4 7.0 %copy-start.22 = (f32[2,10,256]{2,1,0:T(8,128)S(1)}, f32[2,10,256]{2,1,0:T(8,128)}, u32[]{:S(2)}) copy-start(f32[2,10,256]{2,1,0:T(8,128)} %copy-done.21) | copy-start | bytes 61444
  19.4 7.0 %copy-start.24 = (f32[2,10,256]{2,1,0:T(8,128)S(1)}, f32[2,10,256]{2,1,0:T(8,128)}, u32[]{:S(2)}) copy-start(f32[2,10,256]{2,1,0:T(8,128)} %get-tuple-element.36) | copy-start | bytes 61444
  19.4 13.9 %collective-permute-start = (f32[10,64,128]{2,1,0:T(8,128)}, f32[10,64,128]{2,1,0:T(8,128)}, u32[]{:S(2)}, u32[]{:S(2)}) collective-permute-start(f32[10,64,128]{2,1,0:T(8,128)} %get-tuple-element.8), channel_id=1, source_target_pairs={{0,4},{4,8},{8,12},{1,5},{5,9},{9,13},{2,6},{6,10},{10,14},{3,7},{... | collective-permute-start | bytes 983048 | tf_op jit(solution)/shard_map/ppermute | solution.py:20
  33.3 7.2 %copy-start.14 = (bf16[512,640]{1,0:T(8,128)(2,1)S(1)}, bf16[512,640]{1,0:T(8,128)(2,1)}, u32[]{:S(2)}) copy-start(bf16[512,640]{1,0:T(8,128)(2,1)} %param.24) | copy-start | bytes 1966084
  34.5 9.6 %collective-permute-start.1 = (f32[10,64,128]{2,1,0:T(8,128)S(1)}, f32[10,64,128]{2,1,0:T(8,128)S(1)}, u32[]{:S(2)}, u32[]{:S(2)}) collective-permute-start(f32[10,64,128]{2,1,0:T(8,128)S(1)} %multiply_add_fusion.3), channel_id=1, source_target_pairs={{0,4},{4,8},{8,12},{1,5},{5,9},{9,13},{2,6},{6,10},{10,14},{3,7},{... | collective-permute-start | bytes 983048 | tf_op jit(solution)/shard_map/ppermute | solution.py:20
  37.9 6.2 %copy-start.5 = (f32[10,64,128]{2,1,0:T(8,128)S(1)}, f32[10,64,128]{2,1,0:T(8,128)}, u32[]{:S(2)}) copy-start(f32[10,64,128]{2,1,0:T(8,128)} %get-tuple-element.9) | copy-start | bytes 983044
  39.2 10.9 %collective-permute-start.4 = (f32[10,64,128]{2,1,0:T(8,128)S(1)}, f32[10,64,128]{2,1,0:T(8,128)S(1)}, u32[]{:S(2)}, u32[]{:S(2)}) collective-permute-start(f32[10,64,128]{2,1,0:T(8,128)S(1)} %multiply_add_fusion.1), channel_id=1, source_target_pairs={{4,0},{8,4},{12,8},{5,1},{9,5},{13,9},{6,2},{10,6},{14,10},{7,3},{... | collective-permute-start | bytes 983048 | tf_op jit(solution)/shard_map/ppermute | solution.py:20
  40.5 9.6 %copy-start.4 = (f32[10,64,128]{2,1,0:T(8,128)S(1)}, f32[10,64,128]{2,1,0:T(8,128)}, u32[]{:S(2)}) copy-start(f32[10,64,128]{2,1,0:T(8,128)} %get-tuple-element.5) | copy-start | bytes 983044
  41.6 11.4 %copy-start.30 = (f32[1,10]{1,0:T(1,128)S(1)}, f32[1,10]{1,0:T(1,128)}, u32[]{:S(2)}) copy-start(f32[1,10]{1,0:T(1,128)} %get-tuple-element.28) | copy-start | bytes 124
  41.6 12.0 %copy-start.31 = (f32[10]{0:T(128)S(1)}, f32[10]{0:T(128)}, u32[]{:S(2)}) copy-start(f32[10]{0:T(128)} %param.21) | copy-start | bytes 124
  45.0 11.1 %collective-permute-start.2 = (f32[10,64,128]{2,1,0:T(8,128)}, f32[10,64,128]{2,1,0:T(8,128)}, u32[]{:S(2)}, u32[]{:S(2)}) collective-permute-start(f32[10,64,128]{2,1,0:T(8,128)} %multiply_add_fusion.2), channel_id=1, source_target_pairs={{0,4},{4,8},{8,12},{1,5},{5,9},{9,13},{2,6},{6,10},{10,14},{3,7},{... | collective-permute-start | bytes 983048 | tf_op jit(solution)/shard_map/ppermute | solution.py:20
  50.9 10.1 %collective-permute-start.5 = (f32[10,64,128]{2,1,0:T(8,128)}, f32[10,64,128]{2,1,0:T(8,128)}, u32[]{:S(2)}, u32[]{:S(2)}) collective-permute-start(f32[10,64,128]{2,1,0:T(8,128)} %multiply_add_fusion), channel_id=1, source_target_pairs={{4,0},{8,4},{12,8},{5,1},{9,5},{13,9},{6,2},{10,6},{14,10},{7,3},{... | collective-permute-start | bytes 983048 | tf_op jit(solution)/shard_map/ppermute | solution.py:20
  56.8 4.3 %copy-start.13 = (f32[1,10,64,128]{3,2,1,0:T(8,128)S(1)}, f32[1,10,64,128]{3,2,1,0:T(8,128)}, u32[]{:S(2)}) copy-start(f32[1,10,64,128]{3,2,1,0:T(8,128)} %slice_add_fusion) | copy-start | bytes 983044
  73.5 3.1 %collective-permute-start.7 = (f32[128,2560]{1,0:T(8,128)S(1)}, f32[128,2560]{1,0:T(8,128)S(1)}, u32[]{:S(2)}, u32[]{:S(2)}) collective-permute-start(f32[128,2560]{1,0:T(8,128)S(1)} %convolution_add_fusion), channel_id=1, source_target_pairs={{0,1},{1,0},{2,3},{3,2},{4,5},{5,4},{6,7},{7,6},{8,9},{9,8},{10,11... | collective-permute-start | bytes 3932168 | tf_op jit(solution)/shard_map/ppermute | solution.py:102
  76.0 3.2 %collective-permute-start.6 = (f32[128,2560]{1,0:T(8,128)S(1)}, f32[128,2560]{1,0:T(8,128)S(1)}, u32[]{:S(2)}, u32[]{:S(2)}) collective-permute-start(f32[128,2560]{1,0:T(8,128)S(1)} %convolution_add_fusion.2), channel_id=1, source_target_pairs={{0,1},{1,0},{2,3},{3,2},{4,5},{5,4},{6,7},{7,6},{8,9},{9,8},{10,11... | collective-permute-start | bytes 3932168 | tf_op jit(solution)/shard_map/ppermute | solution.py:102
  77.4 30.9 %collective-permute-start.8 = (f32[128,2560]{1,0:T(8,128)S(1)}, f32[128,2560]{1,0:T(8,128)S(1)}, u32[]{:S(2)}, u32[]{:S(2)}) collective-permute-start(f32[128,2560]{1,0:T(8,128)S(1)} %fusion), channel_id=1, source_target_pairs={{0,2},{2,0},{1,3},{3,1},{4,6},{6,4},{5,7},{7,5},{8,10},{10,8},{9,1... | collective-permute-start | bytes 3932168 | tf_op jit(solution)/shard_map/ppermute | solution.py:102
  110.2 5.7 %collective-permute-start.11 = (bf16[128,2560]{1,0:T(8,128)(2,1)}, bf16[128,2560]{1,0:T(8,128)(2,1)}, u32[]{:S(2)}, u32[]{:S(2)}) collective-permute-start(bf16[128,2560]{1,0:T(8,128)(2,1)} %multiply_convert_fusion.8), channel_id=1, source_target_pairs={{0,1},{1,0},{2,3},{3,2},{4,5},{5,4},{6,7},{7,6},{8,9},{9,8},{10,11... | collective-permute-start | bytes 1966088 | tf_op jit(solution)/shard_map/ppermute | solution.py:102
  110.2 17.4 %collective-permute-start.9 = (bf16[128,2560]{1,0:T(8,128)(2,1)}, bf16[128,2560]{1,0:T(8,128)(2,1)S(1)}, u32[]{:S(2)}, u32[]{:S(2)}) collective-permute-start(bf16[128,2560]{1,0:T(8,128)(2,1)} %multiply_convert_fusion.8), channel_id=1, source_target_pairs={{0,2},{2,0},{1,3},{3,1},{4,6},{6,4},{5,7},{7,5},{8,10},{10,8},{9,1... | collective-permute-start | bytes 1966088 | tf_op jit(solution)/shard_map/ppermute | solution.py:102
  127.5 2.1 %collective-permute-start.10 = (bf16[128,2560]{1,0:T(8,128)(2,1)S(1)}, bf16[128,2560]{1,0:T(8,128)(2,1)S(1)}, u32[]{:S(2)}, u32[]{:S(2)}) collective-permute-start(bf16[128,2560]{1,0:T(8,128)(2,1)S(1)} %collective-permute-done.9), channel_id=1, source_target_pairs={{0,1},{1,0},{2,3},{3,2},{4,5},{5,4},{6,7},{7,6},{8,9},{9,8},{10,11... | collective-permute-start | bytes 1966088 | tf_op jit(solution)/shard_map/ppermute | solution.py:102
  (20 other events, 45.2 us)

commit v19 on v14

--- a/solution.py
+++ b/solution.py
@@ -72,8 +72,9 @@
     count = lax.axis_size(axis)
     if count <= 4:
         entering = jnp.zeros_like(state)
-        for _ in range(count - 1):
-            entering = passed_along(gain[:, None, None] * entering + state, axis, steps)
+        for turn in range(count - 1):
+            leaving = state if turn == 0 else gain[:, None, None] * entering + state
+            entering = passed_along(leaving, axis, steps)
         return entering
     distance = 1
     while distance < count:

time: 132 us -> 134 us (1.015)
    add x2 -> x4, other arithmetic: 1.64 us -> 3.5 us  [chain_blocks(): state = decays[index][:, None, None] * state + ends[index]]
    add x6 -> x4, other arithmetic: 6.05 us -> 4.27 us  [relay(): leaving = state if turn == 0 else gain[:, None, None] * entering + state]
    unnamed x70 -> x78, local copies, waits for them, and re-layouts: 8 us -> 8.07 us
  transfers between devices with their start and end apart: 12 -> 12, of which waited for: 6 -> 6; matrix products, arithmetic and copies ran while one was open for 23% -> 24% of each run, Pallas kernels for 0% -> 0%
where the time goes in v19:
time: 134 us; the launch traced here: 133 us
  waiting for transfers between devices  43.5 us (32%)
  matrix products  25.2 us (19%)
  starting transfers between devices  22.5 us (17%)
  local copies, waits for them, and re-layouts  21.4 us (16%)
  other arithmetic  19.4 us (14%)
    ppermute x6, waiting for transfers between devices, swapped(): lax.ppermute(value, axis, [(source, count - 1 - source) for source in ran...  38.5 us
    ppermute x6, starting transfers between devices, passed_along(): lax.ppermute(value, axis, [(source, source + steps) for source in range(f...  19.1 us
    unnamed x78, local copies, waits for them, and re-layouts  8.07 us
    dot_general x2, matrix products, block_parts(): jnp.einsum('bhts,bshp->bthp', weights, acts_b, preferred_element_type=jnp...  5.27 us
    dot_general x4, matrix products, project(): jnp.dot(rows, value_weight, preferred_element_type=jnp.float32)  5.04 us
    ppermute x6, waiting for transfers between devices, passed_along(): lax.ppermute(value, axis, [(source, source + steps) for source in range(f...  4.95 us
    dot_general x4, matrix products, project(): jnp.dot(rows, key_weight, preferred_element_type=jnp.float32)  4.34 us
    add x4, other arithmetic, relay(): leaving = state if turn == 0 else gain[:, None, None] * entering + state  4.27 us
  transfers between devices with their start and end apart: 12, of which 6 were waited for; matrix products, arithmetic and copies ran while one was open for 24% of the time, Pallas kernels for 0%

profile of v19, /device:TPU:0, one launch (start us, length us, event | category | flops | bytes accessed | tf_op | source)
XLA Modules:
  0.0 133.2 jit_solution(14293897240795200246)
XLA Ops:
  8.3 2.3 %copy.21 = bf16[512,640]{0,1:T(8,128)(2,1)} copy(bf16[512,640]{1,0:T(8,128)(2,1)} %param.14) | data formatting | bytes 1310720 | tf_op args[0]
  10.5 2.7 %reshape_reshape.4 = bf16[2,256,10,64]{1,0,3,2:T(2,128)(2,1)} reshape(bf16[512,640]{0,1:T(8,128)(2,1)} %copy.21) | data formatting | bytes 1310720 | tf_op jit(solution)/shard_map/reshape;reshape | solution.py:26
  13.2 1.8 %convert_multiply_fusion.1 = (f32[2,256,10,64]{1,0,3,2:T(2,128)S(1)}, f32[2,256,10,64]{1,0,3,2:T(2,128)S(1)}) fusion(bf16[2,256,10,64]{1,0,3,2:T(2,128)(2,1)} %reshape_reshape.4, f32[2,256,10]{1,0,2:T(2,128)} %copy.27, f32[2,256,10]{1,0,2:T(2,128)} %copy.23), kind=kLoop, calls=%fused_computation.25 | loop fusion | flops 983040 | bytes 3317760 | tf_op jit(solution)/shard_map/mul | solution.py:49
  20.9 6.4 %collective-permute-start = (f32[10,64,128]{2,1,0:T(8,128)}, f32[10,64,128]{2,1,0:T(8,128)}, u32[]{:S(2)}, u32[]{:S(2)}) collective-permute-start(f32[10,64,128]{2,1,0:T(8,128)} %fusion.49), channel_id=1, source_target_pairs={{0,4},{4,8},{8,12},{1,5},{5,9},{9,13},{2,6},{6,10},{10,14},{3,7},{... | collective-permute-start | bytes 983048 | tf_op jit(solution)/shard_map/ppermute | solution.py:20
  28.0 2.6 %fusion.18 = f32[2,256,10,64]{1,3,2,0:T(8,128)} fusion(f32[2,10,256]{2,1,0:T(8,128)S(1)} %copy-done.26, f32[2,10,256]{2,1,0:T(8,128)S(1)} %copy-done.24, f32[2,256,256]{2,1,0:T(8,128)S(1)} %fusion.103, pred[256,256]{1,0:T(8,128)(4,1)S(1)} %iota_compare_fusion.1, bf16[2,256,10,64]{1,0,3,2:T(2,128)(2,1)S(1)} %copy-done.8), kind=kOutput, calls=%fused_computation.28 | convolution fusion | flops 174325760 | bytes 2596864 | tf_op jit(solution)/shard_map/bhts,bshp->bthp/dot_general | solution.py:47
  30.6 2.6 %fusion.17 = f32[2,256,10,64]{1,3,2,0:T(8,128)} fusion(f32[2,10,256]{2,1,0:T(8,128)S(1)} %copy-done.25, f32[2,10,256]{2,1,0:T(8,128)S(1)} %copy-done.22, f32[2,256,256]{2,1,0:T(8,128)S(1)} %fusion.104, pred[256,256]{1,0:T(8,128)(4,1)S(1)} %iota_compare_fusion, bf16[2,256,10,64]{1,0,3,2:T(2,128)(2,1)S(1)} %copy-done.8), kind=kOutput, calls=%fused_computation.27 | convolution fusion | flops 174325760 | bytes 2596864 | tf_op jit(solution)/shard_map/bhts,bshp->bthp/dot_general | solution.py:47
  36.3 3.4 %collective-permute-start.1 = (f32[10,64,128]{2,1,0:T(8,128)S(1)}, f32[10,64,128]{2,1,0:T(8,128)S(1)}, u32[]{:S(2)}, u32[]{:S(2)}) collective-permute-start(f32[10,64,128]{2,1,0:T(8,128)S(1)} %multiply_add_fusion.3), channel_id=1, source_target_pairs={{0,4},{4,8},{8,12},{1,5},{5,9},{9,13},{2,6},{6,10},{10,14},{3,7},{... | collective-permute-start | bytes 983048 | tf_op jit(solution)/shard_map/ppermute | solution.py:20
  40.9 1.4 %collective-permute-start.4 = (f32[10,64,128]{2,1,0:T(8,128)S(1)}, f32[10,64,128]{2,1,0:T(8,128)S(1)}, u32[]{:S(2)}, u32[]{:S(2)}) collective-permute-start(f32[10,64,128]{2,1,0:T(8,128)S(1)} %multiply_add_fusion.1), channel_id=1, source_target_pairs={{4,0},{8,4},{12,8},{5,1},{9,5},{13,9},{6,2},{10,6},{14,10},{7,3},{... | collective-permute-start | bytes 983048 | tf_op jit(solution)/shard_map/ppermute | solution.py:20
  43.4 2.5 %collective-permute-done.1 = f32[10,64,128]{2,1,0:T(8,128)S(1)} collective-permute-done((f32[10,64,128]{2,1,0:T(8,128)S(1)}, f32[10,64,128]{2,1,0:T(8,128)S(1)}, u32[]{:S(2)}, u32[]{:S(2)}) %collective-permute-start.1) | collective-permute-done | bytes 327712 | tf_op jit(solution)/shard_map/ppermute | solution.py:20
  46.8 5.1 %collective-permute-start.2 = (f32[10,64,128]{2,1,0:T(8,128)}, f32[10,64,128]{2,1,0:T(8,128)}, u32[]{:S(2)}, u32[]{:S(2)}) collective-permute-start(f32[10,64,128]{2,1,0:T(8,128)} %multiply_add_fusion.2), channel_id=1, source_target_pairs={{0,4},{4,8},{8,12},{1,5},{5,9},{9,13},{2,6},{6,10},{10,14},{3,7},{... | collective-permute-start | bytes 983048 | tf_op jit(solution)/shard_map/ppermute | solution.py:20
  52.8 1.5 %collective-permute-start.5 = (f32[10,64,128]{2,1,0:T(8,128)}, f32[10,64,128]{2,1,0:T(8,128)}, u32[]{:S(2)}, u32[]{:S(2)}) collective-permute-start(f32[10,64,128]{2,1,0:T(8,128)} %multiply_add_fusion), channel_id=1, source_target_pairs={{4,0},{8,4},{12,8},{5,1},{9,5},{13,9},{6,2},{10,6},{14,10},{7,3},{... | collective-permute-start | bytes 983048 | tf_op jit(solution)/shard_map/ppermute | solution.py:20
  58.7 1.9 %fusion.23 = f32[2,256,10,64]{1,3,2,0:T(8,128)S(1)} fusion(f32[2,256,10,64]{1,3,2,0:T(8,128)S(1)} %copy-done.9, bf16[2,256,128,1]{2,1,3,0:T(8,128)(2,1)S(1)} %bitcast.209, f32[1,10,64,128]{3,2,1,0:T(8,128)S(1)} %copy-done.10, f32[2,256,10]{1,2,0:T(8,128)S(1)} %copy-done.19, f32[10,64,128]{2,1,0:T(8,128)} %collective-permute-done.2, f32[2,10]{1,0:T(2,128)S(1)} %copy-done.30), kind=kOutput, calls=%fused_computation.35 | convolution fusion | flops 504299520 | bytes 3428432 | tf_op jit(solution)/shard_map/btn,bhpn->bthp/dot_general | solution.py:96
  60.5 2.4 %collective-permute-done.5 = f32[10,64,128]{2,1,0:T(8,128)} collective-permute-done((f32[10,64,128]{2,1,0:T(8,128)}, f32[10,64,128]{2,1,0:T(8,128)}, u32[]{:S(2)}, u32[]{:S(2)}) %collective-permute-start.5) | collective-permute-done | bytes 327712 | tf_op jit(solution)/shard_map/ppermute | solution.py:20
  63.0 1.8 %fusion.21 = f32[2,256,10,64]{1,3,2,0:T(8,128)S(1)} fusion(f32[2,256,10,64]{1,3,2,0:T(8,128)S(1)} %fusion.23, f32[2,256,10,64]{1,3,2,0:T(8,128)S(1)} %copy-done.11, bf16[2,256,128,1]{2,1,3,0:T(8,128)(2,1)S(1)} %bitcast.215, f32[1,10,64,128]{3,2,1,0:T(8,128)S(1)} %copy-done.15, f32[2,256,10]{1,2,0:T(8,128)S(1)} %copy-done.20, ...), kind=kOutput, calls=%fused_computation.32 | convolution fusion | flops 504627200 | bytes 4739152 | tf_op jit(solution)/shard_map/btn,bhpn->bthp/dot_general | solution.py:96
  67.0 2.8 %copy.30 = f32[512,640]{1,0:T(8,128)} copy(f32[512,640]{0,1:T(8,128)} %bitcast.200) | data formatting | bytes 2621440 | tf_op jit(solution)/shard_map/add | solution.py:202
  69.8 2.3 %multiply_reduce_fusion.1 = (f32[512]{0:T(512)S(1)}, f32[512,640]{1,0:T(8,128)S(1)}) fusion(bf16[512,640]{1,0:T(8,128)(2,1)} %param.15, f32[512,640]{1,0:T(8,128)} %copy.30, bf16[512,640]{1,0:T(8,128)(2,1)} %param.14, f32[640]{0:T(1024)S(1)} %mul.308), kind=kLoop, calls=%fused_computation.47 | loop fusion | flops 3603968 | bytes 3936768 | tf_op jit(solution)/shard_map/reduce_sum | solution.py:206
  78.2 1.5 %collective-permute-start.8 = (f32[128,2560]{1,0:T(8,128)S(1)}, f32[128,2560]{1,0:T(8,128)S(1)}, u32[]{:S(2)}, u32[]{:S(2)}) collective-permute-start(f32[128,2560]{1,0:T(8,128)S(1)} %fusion), channel_id=1, source_target_pairs={{0,2},{2,0},{1,3},{3,1},{4,6},{6,4},{5,7},{7,5},{8,10},{10,8},{9,1... | collective-permute-start | bytes 3932168 | tf_op jit(solution)/shard_map/ppermute | solution.py:103
  80.1 29.0 %collective-permute-done.8 = f32[128,2560]{1,0:T(8,128)S(1)} collective-permute-done((f32[128,2560]{1,0:T(8,128)S(1)}, f32[128,2560]{1,0:T(8,128)S(1)}, u32[]{:S(2)}, u32[]{:S(2)}) %collective-permute-start.8) | collective-permute-done | bytes 1310752 | tf_op jit(solution)/shard_map/ppermute | solution.py:103
  111.0 1.5 %collective-permute-start.9 = (bf16[128,2560]{1,0:T(8,128)(2,1)}, bf16[128,2560]{1,0:T(8,128)(2,1)S(1)}, u32[]{:S(2)}, u32[]{:S(2)}) collective-permute-start(bf16[128,2560]{1,0:T(8,128)(2,1)} %multiply_convert_fusion.8), channel_id=1, source_target_pairs={{0,2},{2,0},{1,3},{3,1},{4,6},{6,4},{5,7},{7,5},{8,10},{10,8},{9,1... | collective-permute-start | bytes 1966088 | tf_op jit(solution)/shard_map/ppermute | solution.py:103
  112.4 2.4 %fusion.39 = bf16[1,1,128,512]{3,2,1,0:T(8,128)(2,1)S(1)} fusion(bf16[128,2560]{1,0:T(8,128)(2,1)} %multiply_convert_fusion.8, bf16[2560,512]{1,0:T(8,128)(2,1)} %param.27), kind=kOutput, calls=%fused_computation.63 | convolution fusion | flops 335609856 | bytes 3407872 | tf_op jit(solution)/shard_map/dot_general | solution.py:152
  114.9 1.7 %fusion.35 = bf16[1,1,128,512]{3,2,1,0:T(8,128)(2,1)S(1)} fusion(bf16[128,2560]{1,0:T(8,128)(2,1)} %multiply_convert_fusion.8, bf16[2560,512]{1,0:T(8,128)(2,1)S(1)} %copy-done.2), kind=kOutput, calls=%fused_computation.59 | convolution fusion | flops 335609856 | bytes 3407872 | tf_op jit(solution)/shard_map/dot_general | solution.py:151
  116.8 1.6 %fusion.38 = bf16[1,1,128,512]{3,2,1,0:T(8,128)(2,1)S(1)} fusion(bf16[128,2560]{1,0:T(8,128)(2,1)} %collective-permute-done.11, bf16[2560,512]{1,0:T(8,128)(2,1)S(1)} %copy-done.1), kind=kOutput, calls=%fused_computation.62 | convolution fusion | flops 335609856 | bytes 3407872 | tf_op jit(solution)/shard_map/dot_general | solution.py:152
  118.5 1.6 %fusion.34 = bf16[1,1,128,512]{3,2,1,0:T(8,128)(2,1)S(1)} fusion(bf16[128,2560]{1,0:T(8,128)(2,1)} %collective-permute-done.11, bf16[2560,512]{1,0:T(8,128)(2,1)S(1)} %copy-done.2), kind=kOutput, calls=%fused_computation.58 | convolution fusion | flops 335609856 | bytes 3407872 | tf_op jit(solution)/shard_map/dot_general | solution.py:151
  120.1 8.2 %collective-permute-done.9 = bf16[128,2560]{1,0:T(8,128)(2,1)S(1)} collective-permute-done((bf16[128,2560]{1,0:T(8,128)(2,1)}, bf16[128,2560]{1,0:T(8,128)(2,1)S(1)}, u32[]{:S(2)}, u32[]{:S(2)}) %collective-permute-start.9) | collective-permute-done | bytes 655392 | tf_op jit(solution)/shard_map/ppermute | solution.py:103
  (153 shorter events, 40.8 us)
Async XLA Ops:
  0.6 72.3 %copy-start = (bf16[640,2560]{1,0:T(8,128)(2,1)S(1)}, bf16[640,2560]{1,0:T(8,128)(2,1)}, u32[]{:S(2)}) copy-start(bf16[640,2560]{1,0:T(8,128)(2,1)} %param.23) | copy-start | bytes 9830404
  15.8 18.3 %copy-start.3 = (f32[2,10,64,128]{3,2,1,0:T(8,128)}, f32[2,10,64,128]{3,2,1,0:T(8,128)S(1)}, u32[]{:S(2)}) copy-start(f32[2,10,64,128]{3,2,1,0:T(8,128)S(1)} %fusion.28) | copy-start | bytes 1966084
  16.8 22.9 %collective-permute-start.3 = (f32[10,64,128]{2,1,0:T(8,128)}, f32[10,64,128]{2,1,0:T(8,128)}, u32[]{:S(2)}, u32[]{:S(2)}) collective-permute-start(f32[10,64,128]{2,1,0:T(8,128)} %fusion.48), channel_id=1, source_target_pairs={{4,0},{8,4},{12,8},{5,1},{9,5},{13,9},{6,2},{10,6},{14,10},{7,3},{... | collective-permute-start | bytes 983048 | tf_op jit(solution)/shard_map/ppermute | solution.py:20
  19.3 8.2 %copy-start.18 = (bf16[2,512,128]{2,1,0:T(8,128)(2,1)S(1)}, bf16[2,512,128]{2,1,0:T(8,128)(2,1)}, u32[]{:S(2)}) copy-start(bf16[2,512,128]{2,1,0:T(8,128)(2,1)} %param.17) | copy-start | bytes 786436
  20.0 13.3 %copy-start.5 = (f32[2,10,64,128]{3,2,1,0:T(8,128)}, f32[2,10,64,128]{3,2,1,0:T(8,128)S(1)}, u32[]{:S(2)}) copy-start(f32[2,10,64,128]{3,2,1,0:T(8,128)S(1)} %fusion.30) | copy-start | bytes 1966084
  20.9 7.0 %copy-start.8 = (bf16[2,256,10,64]{1,0,3,2:T(2,128)(2,1)S(1)}, bf16[2,256,10,64]{1,0,3,2:T(2,128)(2,1)}, u32[]{:S(2)}) copy-start(bf16[2,256,10,64]{1,0,3,2:T(2,128)(2,1)} %reshape_reshape.4) | copy-start | bytes 1966084
  20.9 7.0 %copy-start.24 = (f32[2,10,256]{2,1,0:T(8,128)S(1)}, f32[2,10,256]{2,1,0:T(8,128)}, u32[]{:S(2)}) copy-start(f32[2,10,256]{2,1,0:T(8,128)} %copy-done.23) | copy-start | bytes 61444
  20.9 7.0 %copy-start.26 = (f32[2,10,256]{2,1,0:T(8,128)S(1)}, f32[2,10,256]{2,1,0:T(8,128)}, u32[]{:S(2)}) copy-start(f32[2,10,256]{2,1,0:T(8,128)} %get-tuple-element.32) | copy-start | bytes 61444
  20.9 14.0 %collective-permute-start = (f32[10,64,128]{2,1,0:T(8,128)}, f32[10,64,128]{2,1,0:T(8,128)}, u32[]{:S(2)}, u32[]{:S(2)}) collective-permute-start(f32[10,64,128]{2,1,0:T(8,128)} %fusion.49), channel_id=1, source_target_pairs={{0,4},{4,8},{8,12},{1,5},{5,9},{9,13},{2,6},{6,10},{10,14},{3,7},{... | collective-permute-start | bytes 983048 | tf_op jit(solution)/shard_map/ppermute | solution.py:20
  34.9 7.4 %copy-start.16 = (bf16[512,640]{1,0:T(8,128)(2,1)S(1)}, bf16[512,640]{1,0:T(8,128)(2,1)}, u32[]{:S(2)}) copy-start(bf16[512,640]{1,0:T(8,128)(2,1)} %param.24) | copy-start | bytes 1966084
  36.3 9.6 %collective-permute-start.1 = (f32[10,64,128]{2,1,0:T(8,128)S(1)}, f32[10,64,128]{2,1,0:T(8,128)S(1)}, u32[]{:S(2)}, u32[]{:S(2)}) collective-permute-start(f32[10,64,128]{2,1,0:T(8,128)S(1)} %multiply_add_fusion.3), channel_id=1, source_target_pairs={{0,4},{4,8},{8,12},{1,5},{5,9},{9,13},{2,6},{6,10},{10,14},{3,7},{... | collective-permute-start | bytes 983048 | tf_op jit(solution)/shard_map/ppermute | solution.py:20
  40.9 11.1 %collective-permute-start.4 = (f32[10,64,128]{2,1,0:T(8,128)S(1)}, f32[10,64,128]{2,1,0:T(8,128)S(1)}, u32[]{:S(2)}, u32[]{:S(2)}) collective-permute-start(f32[10,64,128]{2,1,0:T(8,128)S(1)} %multiply_add_fusion.1), channel_id=1, source_target_pairs={{4,0},{8,4},{12,8},{5,1},{9,5},{13,9},{6,2},{10,6},{14,10},{7,3},{... | collective-permute-start | bytes 983048 | tf_op jit(solution)/shard_map/ppermute | solution.py:20
  42.3 9.6 %copy-start.28 = (f32[10]{0:T(128)S(1)}, f32[10]{0:T(128)}, u32[]{:S(2)}) copy-start(f32[10]{0:T(128)} %get-tuple-element.24) | copy-start | bytes 124
  43.4 10.9 %copy-start.34 = (f32[1,10]{1,0:T(1,128)S(1)}, f32[1,10]{1,0:T(1,128)}, u32[]{:S(2)}) copy-start(f32[1,10]{1,0:T(1,128)} %get-tuple-element.26) | copy-start | bytes 124
  43.4 11.5 %copy-start.33 = (f32[1,10]{1,0:T(1,128)S(1)}, f32[1,10]{1,0:T(1,128)}, u32[]{:S(2)}) copy-start(f32[1,10]{1,0:T(1,128)} %get-tuple-element.22) | copy-start | bytes 124
  43.4 12.0 %copy-start.35 = (f32[10]{0:T(128)S(1)}, f32[10]{0:T(128)}, u32[]{:S(2)}) copy-start(f32[10]{0:T(128)} %param.21) | copy-start | bytes 124
  46.8 11.2 %collective-permute-start.2 = (f32[10,64,128]{2,1,0:T(8,128)}, f32[10,64,128]{2,1,0:T(8,128)}, u32[]{:S(2)}, u32[]{:S(2)}) collective-permute-start(f32[10,64,128]{2,1,0:T(8,128)} %multiply_add_fusion.2), channel_id=1, source_target_pairs={{0,4},{4,8},{8,12},{1,5},{5,9},{9,13},{2,6},{6,10},{10,14},{3,7},{... | collective-permute-start | bytes 983048 | tf_op jit(solution)/shard_map/ppermute | solution.py:20
  52.8 10.1 %collective-permute-start.5 = (f32[10,64,128]{2,1,0:T(8,128)}, f32[10,64,128]{2,1,0:T(8,128)}, u32[]{:S(2)}, u32[]{:S(2)}) collective-permute-start(f32[10,64,128]{2,1,0:T(8,128)} %multiply_add_fusion), channel_id=1, source_target_pairs={{4,0},{8,4},{12,8},{5,1},{9,5},{13,9},{6,2},{10,6},{14,10},{7,3},{... | collective-permute-start | bytes 983048 | tf_op jit(solution)/shard_map/ppermute | solution.py:20
  74.3 3.1 %collective-permute-start.7 = (f32[128,2560]{1,0:T(8,128)S(1)}, f32[128,2560]{1,0:T(8,128)S(1)}, u32[]{:S(2)}, u32[]{:S(2)}) collective-permute-start(f32[128,2560]{1,0:T(8,128)S(1)} %convolution_add_fusion), channel_id=1, source_target_pairs={{0,1},{1,0},{2,3},{3,2},{4,5},{5,4},{6,7},{7,6},{8,9},{9,8},{10,11... | collective-permute-start | bytes 3932168 | tf_op jit(solution)/shard_map/ppermute | solution.py:103
  76.8 3.2 %collective-permute-start.6 = (f32[128,2560]{1,0:T(8,128)S(1)}, f32[128,2560]{1,0:T(8,128)S(1)}, u32[]{:S(2)}, u32[]{:S(2)}) collective-permute-start(f32[128,2560]{1,0:T(8,128)S(1)} %convolution_add_fusion.2), channel_id=1, source_target_pairs={{0,1},{1,0},{2,3},{3,2},{4,5},{5,4},{6,7},{7,6},{8,9},{9,8},{10,11... | collective-permute-start | bytes 3932168 | tf_op jit(solution)/shard_map/ppermute | solution.py:103
  78.2 30.9 %collective-permute-start.8 = (f32[128,2560]{1,0:T(8,128)S(1)}, f32[128,2560]{1,0:T(8,128)S(1)}, u32[]{:S(2)}, u32[]{:S(2)}) collective-permute-start(f32[128,2560]{1,0:T(8,128)S(1)} %fusion), channel_id=1, source_target_pairs={{0,2},{2,0},{1,3},{3,1},{4,6},{6,4},{5,7},{7,5},{8,10},{10,8},{9,1... | collective-permute-start | bytes 3932168 | tf_op jit(solution)/shard_map/ppermute | solution.py:103
  111.0 5.7 %collective-permute-start.11 = (bf16[128,2560]{1,0:T(8,128)(2,1)}, bf16[128,2560]{1,0:T(8,128)(2,1)}, u32[]{:S(2)}, u32[]{:S(2)}) collective-permute-start(bf16[128,2560]{1,0:T(8,128)(2,1)} %multiply_convert_fusion.8), channel_id=1, source_target_pairs={{0,1},{1,0},{2,3},{3,2},{4,5},{5,4},{6,7},{7,6},{8,9},{9,8},{10,11... | collective-permute-start | bytes 1966088 | tf_op jit(solution)/shard_map/ppermute | solution.py:103
  111.0 17.4 %collective-permute-start.9 = (bf16[128,2560]{1,0:T(8,128)(2,1)}, bf16[128,2560]{1,0:T(8,128)(2,1)S(1)}, u32[]{:S(2)}, u32[]{:S(2)}) collective-permute-start(bf16[128,2560]{1,0:T(8,128)(2,1)} %multiply_convert_fusion.8), channel_id=1, source_target_pairs={{0,2},{2,0},{1,3},{3,1},{4,6},{6,4},{5,7},{7,5},{8,10},{10,8},{9,1... | collective-permute-start | bytes 1966088 | tf_op jit(solution)/shard_map/ppermute | solution.py:103
  128.3 2.1 %collective-permute-start.10 = (bf16[128,2560]{1,0:T(8,128)(2,1)S(1)}, bf16[128,2560]{1,0:T(8,128)(2,1)S(1)}, u32[]{:S(2)}, u32[]{:S(2)}) collective-permute-start(bf16[128,2560]{1,0:T(8,128)(2,1)S(1)} %collective-permute-done.9), channel_id=1, source_target_pairs={{0,1},{1,0},{2,3},{3,2},{4,5},{5,4},{6,7},{7,6},{8,9},{9,8},{10,11... | collective-permute-start | bytes 1966088 | tf_op jit(solution)/shard_map/ppermute | solution.py:103
  (24 other events, 69.3 us)

commit v20 on v14

--- a/solution.py
+++ b/solution.py
@@ -162,9 +162,9 @@
     assembled = []
     for which in range(2):
         own_p, partner_p, other_p, partner_other_p = (result[which] for result in results)
-        near = pick([jnp.stack([own_p, partner_p]), jnp.stack([partner_p, own_p])], core)
-        far = pick([jnp.stack([other_p, partner_other_p]), jnp.stack([partner_other_p, other_p])], core)
-        whole = pick([jnp.stack([near, far]), jnp.stack([far, near])], chip)
+        stacked = jnp.stack([own_p, partner_p, other_p, partner_other_p])
+        order = jnp.bitwise_xor(jnp.arange(4), chip * 2 + core)
+        whole = jnp.take(stacked, order, axis=0)
         assembled.append(whole.reshape(-1, whole.shape[-1]))
     return tuple(assembled)
 

time: 132 us -> 140 us (1.061)
  local copies, waits for them, and re-layouts: 20.9 us -> 27 us
  waiting for transfers between devices: 43.6 us -> 46.4 us
  matrix products: 25.1 us -> 22.5 us
    gather x0 -> x2, local copies, waits for them, and re-layouts: none -> 4.85 us  [project_all_rows(): whole = jnp.take(stacked, order, axis=0)]
    ppermute x6, waiting for transfers between devices: 38.6 us -> 41.5 us  [swapped(): lax.ppermute(value, axis, [(source, count - 1 - source) for source in ran...]
    dot_general x4, matrix products: 4.34 us -> 2.02 us  [project(): jnp.dot(rows, key_weight, preferred_element_type=jnp.float32)]
    another operation x0 -> x2, other arithmetic: none -> 1.72 us  [project_all_rows(): stacked = jnp.stack([own_p, partner_p, other_p, partner_other_p])]
    unnamed x70 -> x74, local copies, waits for them, and re-layouts: 8 us -> 9.33 us
  transfers between devices with their start and end apart: 12 -> 12, of which waited for: 6 -> 5; matrix products, arithmetic and copies ran while one was open for 23% -> 19% of each run, Pallas kernels for 0% -> 0%
where the time goes in v20:
time: 140 us; the launch traced here: 139 us
  waiting for transfers between devices  46.4 us (33%)
  local copies, waits for them, and re-layouts  27 us (19%)
  matrix products  22.5 us (16%)
  starting transfers between devices  22.5 us (16%)
  other arithmetic  19.5 us (14%)
    ppermute x6, waiting for transfers between devices, swapped(): lax.ppermute(value, axis, [(source, count - 1 - source) for source in ran...  41.5 us
    ppermute x6, starting transfers between devices, passed_along(): lax.ppermute(value, axis, [(source, source + steps) for source in range(f...  18.9 us
    unnamed x74, local copies, waits for them, and re-layouts  9.33 us
    add x6, other arithmetic, relay(): entering = passed_along(gain[:, None, None] * entering + state, axis, steps)  6.06 us
    dot_general x2, matrix products, block_parts(): jnp.einsum('bhts,bshp->bthp', weights, acts_b, preferred_element_type=jnp...  5.24 us
    ppermute x6, waiting for transfers between devices, passed_along(): lax.ppermute(value, axis, [(source, source + steps) for source in range(f...  4.95 us
    gather x2, local copies, waits for them, and re-layouts, project_all_rows(): whole = jnp.take(stacked, order, axis=0)  4.85 us
    dot_general x4, matrix products, project(): jnp.dot(rows, value_weight, preferred_element_type=jnp.float32)  4.67 us
  transfers between devices with their start and end apart: 12, of which 5 were waited for; matrix products, arithmetic and copies ran while one was open for 19% of the time, Pallas kernels for 0%

profile of v20, /device:TPU:0, one launch (start us, length us, event | category | flops | bytes accessed | tf_op | source)
XLA Modules:
  0.0 139.2 jit_solution(2990533637155866333)
XLA Ops:
  5.2 1.4 bitcast_exponential_fusion
  7.9 2.2 %copy.21 = bf16[512,640]{0,1:T(8,128)(2,1)} copy(bf16[512,640]{1,0:T(8,128)(2,1)} %param.16) | data formatting | bytes 1310720 | tf_op args[0]
  10.1 2.7 %reshape_reshape.4 = bf16[2,256,10,64]{1,0,3,2:T(2,128)(2,1)} reshape(bf16[512,640]{0,1:T(8,128)(2,1)} %copy.21) | data formatting | bytes 1310720 | tf_op jit(solution)/shard_map/reshape;reshape | solution.py:26
  12.8 1.8 %convert_multiply_fusion.1 = (f32[2,256,10,64]{1,0,3,2:T(2,128)S(1)}, f32[2,256,10,64]{1,0,3,2:T(2,128)S(1)}) fusion(bf16[2,256,10,64]{1,0,3,2:T(2,128)(2,1)} %reshape_reshape.4, f32[2,256,10]{1,0,2:T(2,128)} %copy.27, f32[2,256,10]{1,0,2:T(2,128)} %copy.23), kind=kLoop, calls=%fused_computation.27 | loop fusion | flops 983040 | bytes 3317760 | tf_op jit(solution)/shard_map/mul | solution.py:49
  19.4 6.4 %collective-permute-start = (f32[10,64,128]{2,1,0:T(8,128)}, f32[10,64,128]{2,1,0:T(8,128)}, u32[]{:S(2)}, u32[]{:S(2)}) collective-permute-start(f32[10,64,128]{2,1,0:T(8,128)} %get-tuple-element.11), channel_id=1, source_target_pairs={{0,4},{4,8},{8,12},{1,5},{5,9},{9,13},{2,6},{6,10},{10,14},{3,7},{... | collective-permute-start | bytes 983048 | tf_op jit(solution)/shard_map/ppermute | solution.py:20
  26.4 2.6 %fusion.18 = f32[2,256,10,64]{1,3,2,0:T(8,128)} fusion(f32[2,10,256]{2,1,0:T(8,128)S(1)} %copy-done.26, f32[2,10,256]{2,1,0:T(8,128)S(1)} %copy-done.24, f32[2,256,256]{2,1,0:T(8,128)S(1)} %fusion.105, pred[256,256]{1,0:T(8,128)(4,1)S(1)} %iota_compare_fusion.1, bf16[2,256,10,64]{1,0,3,2:T(2,128)(2,1)S(1)} %copy-done.6), kind=kOutput, calls=%fused_computation.30 | convolution fusion | flops 174325760 | bytes 2596864 | tf_op jit(solution)/shard_map/bhts,bshp->bthp/dot_general | solution.py:47
  29.1 2.6 %fusion.17 = f32[2,256,10,64]{1,3,2,0:T(8,128)} fusion(f32[2,10,256]{2,1,0:T(8,128)S(1)} %copy-done.25, f32[2,10,256]{2,1,0:T(8,128)S(1)} %copy-done.22, f32[2,256,256]{2,1,0:T(8,128)S(1)} %fusion.106, pred[256,256]{1,0:T(8,128)(4,1)S(1)} %iota_compare_fusion, bf16[2,256,10,64]{1,0,3,2:T(2,128)(2,1)S(1)} %copy-done.6), kind=kOutput, calls=%fused_computation.29 | convolution fusion | flops 174325760 | bytes 2596864 | tf_op jit(solution)/shard_map/bhts,bshp->bthp/dot_general | solution.py:47
  34.6 3.4 %collective-permute-start.1 = (f32[10,64,128]{2,1,0:T(8,128)S(1)}, f32[10,64,128]{2,1,0:T(8,128)S(1)}, u32[]{:S(2)}, u32[]{:S(2)}) collective-permute-start(f32[10,64,128]{2,1,0:T(8,128)S(1)} %multiply_add_fusion.3), channel_id=1, source_target_pairs={{0,4},{4,8},{8,12},{1,5},{5,9},{9,13},{2,6},{6,10},{10,14},{3,7},{... | collective-permute-start | bytes 983048 | tf_op jit(solution)/shard_map/ppermute | solution.py:20
  41.6 2.6 %collective-permute-done.1 = f32[10,64,128]{2,1,0:T(8,128)S(1)} collective-permute-done((f32[10,64,128]{2,1,0:T(8,128)S(1)}, f32[10,64,128]{2,1,0:T(8,128)S(1)}, u32[]{:S(2)}, u32[]{:S(2)}) %collective-permute-start.1) | collective-permute-done | bytes 327712 | tf_op jit(solution)/shard_map/ppermute | solution.py:20
  45.0 5.1 %collective-permute-start.2 = (f32[10,64,128]{2,1,0:T(8,128)}, f32[10,64,128]{2,1,0:T(8,128)}, u32[]{:S(2)}, u32[]{:S(2)}) collective-permute-start(f32[10,64,128]{2,1,0:T(8,128)} %multiply_add_fusion.2), channel_id=1, source_target_pairs={{0,4},{4,8},{8,12},{1,5},{5,9},{9,13},{2,6},{6,10},{10,14},{3,7},{... | collective-permute-start | bytes 983048 | tf_op jit(solution)/shard_map/ppermute | solution.py:20
  51.0 1.5 %collective-permute-start.5 = (f32[10,64,128]{2,1,0:T(8,128)}, f32[10,64,128]{2,1,0:T(8,128)}, u32[]{:S(2)}, u32[]{:S(2)}) collective-permute-start(f32[10,64,128]{2,1,0:T(8,128)} %multiply_add_fusion), channel_id=1, source_target_pairs={{4,0},{8,4},{12,8},{5,1},{9,5},{13,9},{6,2},{10,6},{14,10},{7,3},{... | collective-permute-start | bytes 983048 | tf_op jit(solution)/shard_map/ppermute | solution.py:20
  56.8 1.9 %fusion.23 = f32[2,256,10,64]{1,3,2,0:T(8,128)S(1)} fusion(f32[2,256,10,64]{1,3,2,0:T(8,128)S(1)} %copy-done.8, bf16[2,256,128,1]{2,1,3,0:T(8,128)(2,1)S(1)} %bitcast.201, f32[1,10,64,128]{3,2,1,0:T(8,128)S(1)} %copy-done.9, f32[2,256,10]{1,2,0:T(8,128)S(1)} %copy-done.19, f32[10,64,128]{2,1,0:T(8,128)} %collective-permute-done.2, f32[2,10]{1,0:T(2,128)S(1)} %copy-done.28), kind=kOutput, calls=%fused_computation.37 | convolution fusion | flops 504299520 | bytes 3428432 | tf_op jit(solution)/shard_map/btn,bhpn->bthp/dot_general | solution.py:95
  58.7 2.4 %collective-permute-done.5 = f32[10,64,128]{2,1,0:T(8,128)} collective-permute-done((f32[10,64,128]{2,1,0:T(8,128)}, f32[10,64,128]{2,1,0:T(8,128)}, u32[]{:S(2)}, u32[]{:S(2)}) %collective-permute-start.5) | collective-permute-done | bytes 327712 | tf_op jit(solution)/shard_map/ppermute | solution.py:20
  61.1 1.8 %fusion.21 = f32[2,256,10,64]{1,3,2,0:T(8,128)S(1)} fusion(f32[2,256,10,64]{1,3,2,0:T(8,128)S(1)} %fusion.23, f32[2,256,10,64]{1,3,2,0:T(8,128)S(1)} %copy-done.10, bf16[2,256,128,1]{2,1,3,0:T(8,128)(2,1)S(1)} %bitcast.207, f32[1,10,64,128]{3,2,1,0:T(8,128)S(1)} %copy-done.14, f32[2,256,10]{1,2,0:T(8,128)S(1)} %copy-done.20, ...), kind=kOutput, calls=%fused_computation.34 | convolution fusion | flops 504627200 | bytes 4739152 | tf_op jit(solution)/shard_map/btn,bhpn->bthp/dot_general | solution.py:95
  65.2 2.8 %copy.30 = f32[512,640]{1,0:T(8,128)} copy(f32[512,640]{0,1:T(8,128)} %bitcast.192) | data formatting | bytes 2621440 | tf_op jit(solution)/shard_map/add | solution.py:201
  67.9 2.3 %multiply_reduce_fusion.1 = (f32[512]{0:T(512)S(1)}, f32[512,640]{1,0:T(8,128)S(1)}) fusion(bf16[512,640]{1,0:T(8,128)(2,1)} %param.17, f32[512,640]{1,0:T(8,128)} %copy.30, bf16[512,640]{1,0:T(8,128)(2,1)} %param.16, f32[640]{0:T(1024)S(1)} %mul.332), kind=kLoop, calls=%fused_computation.49 | loop fusion | flops 3603968 | bytes 3936768 | tf_op jit(solution)/shard_map/reduce_sum | solution.py:205
  76.3 1.5 %collective-permute-start.8 = (f32[128,2560]{1,0:T(8,128)S(1)}, f32[128,2560]{1,0:T(8,128)S(1)}, u32[]{:S(2)}, u32[]{:S(2)}) collective-permute-start(f32[128,2560]{1,0:T(8,128)S(1)} %fusion), channel_id=1, source_target_pairs={{0,2},{2,0},{1,3},{3,1},{4,6},{6,4},{5,7},{7,5},{8,10},{10,8},{9,1... | collective-permute-start | bytes 3932168 | tf_op jit(solution)/shard_map/ppermute | solution.py:102
  78.2 29.0 %collective-permute-done.8 = f32[128,2560]{1,0:T(8,128)S(1)} collective-permute-done((f32[128,2560]{1,0:T(8,128)S(1)}, f32[128,2560]{1,0:T(8,128)S(1)}, u32[]{:S(2)}, u32[]{:S(2)}) %collective-permute-start.8) | collective-permute-done | bytes 1310752 | tf_op jit(solution)/shard_map/ppermute | solution.py:102
  108.2 1.5 %collective-permute-start.10 = (bf16[128,2560]{1,0:T(8,128)(2,1)S(1)}, bf16[128,2560]{1,0:T(8,128)(2,1)S(1)}, u32[]{:S(2)}, u32[]{:S(2)}) collective-permute-start(bf16[128,2560]{1,0:T(8,128)(2,1)S(1)} %multiply_convert_fusion.8), channel_id=1, source_target_pairs={{0,2},{2,0},{1,3},{3,1},{4,6},{6,4},{5,7},{7,5},{8,10},{10,8},{9,1... | collective-permute-start | bytes 1966088 | tf_op jit(solution)/shard_map/ppermute | solution.py:102
  112.0 12.2 %collective-permute-done.10 = bf16[128,2560]{1,0:T(8,128)(2,1)S(1)} collective-permute-done((bf16[128,2560]{1,0:T(8,128)(2,1)S(1)}, bf16[128,2560]{1,0:T(8,128)(2,1)S(1)}, u32[]{:S(2)}, u32[]{:S(2)}) %collective-permute-start.10) | collective-permute-done | bytes 655392 | tf_op jit(solution)/shard_map/ppermute | solution.py:102
  128.7 2.4 %gather_fusion = bf16[4,128,512]{2,1,0:T(8,128)(2,1)} fusion(bf16[4,128,512]{2,1,0:T(8,128)(2,1)} %pad_maximum_fusion, s32[1024]{0:T(1024)S(1)} %pad_clamp_fusion), kind=kCustom, calls=%fused_computation.clone | custom fusion | bytes 1048592 | tf_op jit(solution)/shard_map/jit(_take)/gather | solution.py:167
  131.1 2.5 %fusion.39 = bf16[1,128,512]{2,1,0:T(8,128)(2,1)S(1)} fusion(bf16[128,2560]{1,0:T(8,128)(2,1)} %copy-done.7, bf16[2560,512]{1,0:T(8,128)(2,1)} %param.29), kind=kOutput, calls=%fused_computation.65 | convolution fusion | flops 335609856 | bytes 3407872 | tf_op jit(solution)/shard_map/dot_general | solution.py:151
  134.5 2.4 %gather_fusion.1 = bf16[4,128,512]{2,1,0:T(8,128)(2,1)} fusion(bf16[4,128,512]{2,1,0:T(8,128)(2,1)} %pad_maximum_fusion.1, s32[1024]{0:T(1024)S(1)} %pad_clamp_fusion), kind=kCustom, calls=%fused_computation.1.clone | custom fusion | bytes 1048592 | tf_op jit(solution)/shard_map/jit(_take)/gather | solution.py:167
  136.9 2.3 %broadcast_select_fusion = (bf16[4,128,512]{2,1,0:T(8,128)(2,1)}, bf16[4,128,512]{2,1,0:T(8,128)(2,1)}) fusion(bf16[4,128,512]{2,1,0:T(8,128)(2,1)} %gather_fusion.1, pred[4]{0:T(512)(128)(4,1)S(1)} %compare_and_fusion, bf16[4,128,512]{2,1,0:T(8,128)(2,1)} %gather_fusion), kind=kLoop, calls=%fused_computation.77 | loop fusion | flops 524288 | bytes 2097156 | tf_op jit(solution)/shard_map/jit(_take)/select_n | solution.py:167
  (151 shorter events, 40.6 us)
Async XLA Ops:
  0.6 70.4 %copy-start = (bf16[640,2560]{1,0:T(8,128)(2,1)S(1)}, bf16[640,2560]{1,0:T(8,128)(2,1)}, u32[]{:S(2)}) copy-start(bf16[640,2560]{1,0:T(8,128)(2,1)} %param.25) | copy-start | bytes 9830404
  7.8 4.9 %copy-start.17 = (bf16[2,512,128]{2,1,0:T(8,128)(2,1)S(1)}, bf16[2,512,128]{2,1,0:T(8,128)(2,1)}, u32[]{:S(2)}) copy-start(bf16[2,512,128]{2,1,0:T(8,128)(2,1)} %param.18) | copy-start | bytes 786436
  16.4 21.6 %collective-permute-start.3 = (f32[10,64,128]{2,1,0:T(8,128)}, f32[10,64,128]{2,1,0:T(8,128)}, u32[]{:S(2)}, u32[]{:S(2)}) collective-permute-start(f32[10,64,128]{2,1,0:T(8,128)} %get-tuple-element.7), channel_id=1, source_target_pairs={{4,0},{8,4},{12,8},{5,1},{9,5},{13,9},{6,2},{10,6},{14,10},{7,3},{... | collective-permute-start | bytes 983048 | tf_op jit(solution)/shard_map/ppermute | solution.py:20
  17.7 8.2 %copy-start.18 = (bf16[2,512,128]{2,1,0:T(8,128)(2,1)S(1)}, bf16[2,512,128]{2,1,0:T(8,128)(2,1)}, u32[]{:S(2)}) copy-start(bf16[2,512,128]{2,1,0:T(8,128)(2,1)} %param.19) | copy-start | bytes 786436
  19.4 7.0 %copy-start.6 = (bf16[2,256,10,64]{1,0,3,2:T(2,128)(2,1)S(1)}, bf16[2,256,10,64]{1,0,3,2:T(2,128)(2,1)}, u32[]{:S(2)}) copy-start(bf16[2,256,10,64]{1,0,3,2:T(2,128)(2,1)} %reshape_reshape.4) | copy-start | bytes 1966084
  19.4 7.0 %copy-start.24 = (f32[2,10,256]{2,1,0:T(8,128)S(1)}, f32[2,10,256]{2,1,0:T(8,128)}, u32[]{:S(2)}) copy-start(f32[2,10,256]{2,1,0:T(8,128)} %copy-done.23) | copy-start | bytes 61444
  19.4 7.0 %copy-start.26 = (f32[2,10,256]{2,1,0:T(8,128)S(1)}, f32[2,10,256]{2,1,0:T(8,128)}, u32[]{:S(2)}) copy-start(f32[2,10,256]{2,1,0:T(8,128)} %get-tuple-element.41) | copy-start | bytes 61444
  19.4 13.9 %collective-permute-start = (f32[10,64,128]{2,1,0:T(8,128)}, f32[10,64,128]{2,1,0:T(8,128)}, u32[]{:S(2)}, u32[]{:S(2)}) collective-permute-start(f32[10,64,128]{2,1,0:T(8,128)} %get-tuple-element.11), channel_id=1, source_target_pairs={{0,4},{4,8},{8,12},{1,5},{5,9},{9,13},{2,6},{6,10},{10,14},{3,7},{... | collective-permute-start | bytes 983048 | tf_op jit(solution)/shard_map/ppermute | solution.py:20
  33.3 7.2 %copy-start.15 = (bf16[512,640]{1,0:T(8,128)(2,1)S(1)}, bf16[512,640]{1,0:T(8,128)(2,1)}, u32[]{:S(2)}) copy-start(bf16[512,640]{1,0:T(8,128)(2,1)} %param.26) | copy-start | bytes 1966084
  34.6 9.6 %collective-permute-start.1 = (f32[10,64,128]{2,1,0:T(8,128)S(1)}, f32[10,64,128]{2,1,0:T(8,128)S(1)}, u32[]{:S(2)}, u32[]{:S(2)}) collective-permute-start(f32[10,64,128]{2,1,0:T(8,128)S(1)} %multiply_add_fusion.3), channel_id=1, source_target_pairs={{0,4},{4,8},{8,12},{1,5},{5,9},{9,13},{2,6},{6,10},{10,14},{3,7},{... | collective-permute-start | bytes 983048 | tf_op jit(solution)/shard_map/ppermute | solution.py:20
  38.0 6.2 %copy-start.5 = (f32[10,64,128]{2,1,0:T(8,128)S(1)}, f32[10,64,128]{2,1,0:T(8,128)}, u32[]{:S(2)}) copy-start(f32[10,64,128]{2,1,0:T(8,128)} %get-tuple-element.12) | copy-start | bytes 983044
  39.2 10.9 %collective-permute-start.4 = (f32[10,64,128]{2,1,0:T(8,128)S(1)}, f32[10,64,128]{2,1,0:T(8,128)S(1)}, u32[]{:S(2)}, u32[]{:S(2)}) collective-permute-start(f32[10,64,128]{2,1,0:T(8,128)S(1)} %multiply_add_fusion.1), channel_id=1, source_target_pairs={{4,0},{8,4},{12,8},{5,1},{9,5},{13,9},{6,2},{10,6},{14,10},{7,3},{... | collective-permute-start | bytes 983048 | tf_op jit(solution)/shard_map/ppermute | solution.py:20
  40.5 9.6 %copy-start.4 = (f32[10,64,128]{2,1,0:T(8,128)S(1)}, f32[10,64,128]{2,1,0:T(8,128)}, u32[]{:S(2)}) copy-start(f32[10,64,128]{2,1,0:T(8,128)} %get-tuple-element.8) | copy-start | bytes 983044
  41.6 11.4 %copy-start.32 = (f32[1,10]{1,0:T(1,128)S(1)}, f32[1,10]{1,0:T(1,128)}, u32[]{:S(2)}) copy-start(f32[1,10]{1,0:T(1,128)} %get-tuple-element.31) | copy-start | bytes 124
  41.6 12.0 %copy-start.33 = (f32[10]{0:T(128)S(1)}, f32[10]{0:T(128)}, u32[]{:S(2)}) copy-start(f32[10]{0:T(128)} %param.23) | copy-start | bytes 124
  45.0 11.1 %collective-permute-start.2 = (f32[10,64,128]{2,1,0:T(8,128)}, f32[10,64,128]{2,1,0:T(8,128)}, u32[]{:S(2)}, u32[]{:S(2)}) collective-permute-start(f32[10,64,128]{2,1,0:T(8,128)} %multiply_add_fusion.2), channel_id=1, source_target_pairs={{0,4},{4,8},{8,12},{1,5},{5,9},{9,13},{2,6},{6,10},{10,14},{3,7},{... | collective-permute-start | bytes 983048 | tf_op jit(solution)/shard_map/ppermute | solution.py:20
  51.0 10.1 %collective-permute-start.5 = (f32[10,64,128]{2,1,0:T(8,128)}, f32[10,64,128]{2,1,0:T(8,128)}, u32[]{:S(2)}, u32[]{:S(2)}) collective-permute-start(f32[10,64,128]{2,1,0:T(8,128)} %multiply_add_fusion), channel_id=1, source_target_pairs={{4,0},{8,4},{12,8},{5,1},{9,5},{13,9},{6,2},{10,6},{14,10},{7,3},{... | collective-permute-start | bytes 983048 | tf_op jit(solution)/shard_map/ppermute | solution.py:20
  56.8 4.3 %copy-start.14 = (f32[1,10,64,128]{3,2,1,0:T(8,128)S(1)}, f32[1,10,64,128]{3,2,1,0:T(8,128)}, u32[]{:S(2)}) copy-start(f32[1,10,64,128]{3,2,1,0:T(8,128)} %slice_add_fusion) | copy-start | bytes 983044
  72.4 3.1 %collective-permute-start.7 = (f32[128,2560]{1,0:T(8,128)S(1)}, f32[128,2560]{1,0:T(8,128)S(1)}, u32[]{:S(2)}, u32[]{:S(2)}) collective-permute-start(f32[128,2560]{1,0:T(8,128)S(1)} %convolution_add_fusion), channel_id=1, source_target_pairs={{0,1},{1,0},{2,3},{3,2},{4,5},{5,4},{6,7},{7,6},{8,9},{9,8},{10,11... | collective-permute-start | bytes 3932168 | tf_op jit(solution)/shard_map/ppermute | solution.py:102
  74.9 3.2 %collective-permute-start.6 = (f32[128,2560]{1,0:T(8,128)S(1)}, f32[128,2560]{1,0:T(8,128)S(1)}, u32[]{:S(2)}, u32[]{:S(2)}) collective-permute-start(f32[128,2560]{1,0:T(8,128)S(1)} %convolution_add_fusion.2), channel_id=1, source_target_pairs={{0,1},{1,0},{2,3},{3,2},{4,5},{5,4},{6,7},{7,6},{8,9},{9,8},{10,11... | collective-permute-start | bytes 3932168 | tf_op jit(solution)/shard_map/ppermute | solution.py:102
  76.3 30.9 %collective-permute-start.8 = (f32[128,2560]{1,0:T(8,128)S(1)}, f32[128,2560]{1,0:T(8,128)S(1)}, u32[]{:S(2)}, u32[]{:S(2)}) collective-permute-start(f32[128,2560]{1,0:T(8,128)S(1)} %fusion), channel_id=1, source_target_pairs={{0,2},{2,0},{1,3},{3,1},{4,6},{6,4},{5,7},{7,5},{8,10},{10,8},{9,1... | collective-permute-start | bytes 3932168 | tf_op jit(solution)/shard_map/ppermute | solution.py:102
  108.2 16.0 %collective-permute-start.10 = (bf16[128,2560]{1,0:T(8,128)(2,1)S(1)}, bf16[128,2560]{1,0:T(8,128)(2,1)S(1)}, u32[]{:S(2)}, u32[]{:S(2)}) collective-permute-start(bf16[128,2560]{1,0:T(8,128)(2,1)S(1)} %multiply_convert_fusion.8), channel_id=1, source_target_pairs={{0,2},{2,0},{1,3},{3,1},{4,6},{6,4},{5,7},{7,5},{8,10},{10,8},{9,1... | collective-permute-start | bytes 1966088 | tf_op jit(solution)/shard_map/ppermute | solution.py:102
  109.7 15.0 %collective-permute-start.9 = (bf16[128,2560]{1,0:T(8,128)(2,1)S(1)}, bf16[128,2560]{1,0:T(8,128)(2,1)S(1)}, u32[]{:S(2)}, u32[]{:S(2)}) collective-permute-start(bf16[128,2560]{1,0:T(8,128)(2,1)S(1)} %multiply_convert_fusion.8), channel_id=1, source_target_pairs={{0,1},{1,0},{2,3},{3,2},{4,5},{5,4},{6,7},{7,6},{8,9},{9,8},{10,11... | collective-permute-start | bytes 1966088 | tf_op jit(solution)/shard_map/ppermute | solution.py:102
  124.2 2.7 %collective-permute-start.11 = (bf16[128,2560]{1,0:T(8,128)(2,1)S(1)}, bf16[128,2560]{1,0:T(8,128)(2,1)S(1)}, u32[]{:S(2)}, u32[]{:S(2)}) collective-permute-start(bf16[128,2560]{1,0:T(8,128)(2,1)S(1)} %collective-permute-done.10), channel_id=1, source_target_pairs={{0,1},{1,0},{2,3},{3,2},{4,5},{5,4},{6,7},{7,6},{8,9},{9,8},{10,11... | collective-permute-start | bytes 1966088 | tf_op jit(solution)/shard_map/ppermute | solution.py:102
  (22 other events, 47.0 us)

commit v21 on v14

--- a/solution.py
+++ b/solution.py
@@ -123,8 +123,10 @@
 
     def partial_of(rows, extra):
         value = jnp.dot(rows, out_weight, preferred_element_type=jnp.float32)
-        spread = jnp.tile(extra.astype(jnp.float32), (1, repeats))
-        return value + jnp.where(own_block[None, :], spread, 0.0)
+        window = lax.dynamic_slice_in_dim(value, index * own_width, own_width, 1)
+        return lax.dynamic_update_slice_in_dim(
+            value, window + extra.astype(jnp.float32), index * own_width, 1
+        )
 
     if chips != 2 or cores != 2:
         return lax.psum_scatter(

time: 132 us -> 131 us (level)
  waiting for transfers between devices: 43.6 us -> 51.5 us
  local copies, waits for them, and re-layouts: 20.9 us -> 16 us
  other arithmetic: 18.2 us -> 14.1 us
    ppermute x6, waiting for transfers between devices: 4.96 us -> 9.37 us  [passed_along(): lax.ppermute(value, axis, [(source, source + steps) for source in range(f...]
    add x6, other arithmetic: 6.05 us -> 2.09 us  [relay(): entering = passed_along(gain[:, None, None] * entering + state, axis, steps)]
    ppermute x6, waiting for transfers between devices: 38.6 us -> 42.1 us  [swapped(): lax.ppermute(value, axis, [(source, count - 1 - source) for source in ran...]
    unnamed x70 -> x52, local copies, waits for them, and re-layouts: 8 us -> 5.1 us
    another operation x4 -> x0, local copies, waits for them, and re-layouts: 1.88 us -> none  [partial_of(): spread = jnp.tile(extra.astype(jnp.float32), (1, repeats))]
  transfers between devices with their start and end apart: 12 -> 12, of which waited for: 6 -> 9; matrix products, arithmetic and copies ran while one was open for 23% -> 16% of each run, Pallas kernels for 0% -> 0%
where the time goes in v21:
time: 131 us; the launch traced here: 130 us
  waiting for transfers between devices  51.5 us (39%)
  matrix products  25.5 us (19%)
  starting transfers between devices  22 us (17%)
  local copies, waits for them, and re-layouts  16 us (12%)
  other arithmetic  14.1 us (11%)
    ppermute x6, waiting for transfers between devices, swapped(): lax.ppermute(value, axis, [(source, count - 1 - source) for source in ran...  42.1 us
    ppermute x6, starting transfers between devices, passed_along(): lax.ppermute(value, axis, [(source, source + steps) for source in range(f...  19.3 us
    ppermute x6, waiting for transfers between devices, passed_along(): lax.ppermute(value, axis, [(source, source + steps) for source in range(f...  9.37 us
    dot_general x2, matrix products, block_parts(): jnp.einsum('bhts,bshp->bthp', weights, acts_b, preferred_element_type=jnp...  5.26 us
    unnamed x52, local copies, waits for them, and re-layouts  5.1 us
    dot_general x4, matrix products, project(): jnp.dot(rows, value_weight, preferred_element_type=jnp.float32)  5.04 us
    dot_general x4, matrix products, project(): jnp.dot(rows, key_weight, preferred_element_type=jnp.float32)  4.35 us
    dot_general x2, matrix products, direction_out(): jnp.einsum('btn,bhpn->bthp', reads_b, block_states, precision=highest)  4.26 us
  transfers between devices with their start and end apart: 12, of which 9 were waited for; matrix products, arithmetic and copies ran while one was open for 16% of the time, Pallas kernels for 0%

profile of v21, /device:TPU:0, one launch (start us, length us, event | category | flops | bytes accessed | tf_op | source)
XLA Modules:
  0.0 130.2 jit_solution(5199133222540384580)
XLA Ops:
  5.4 1.4 %bitcast_exponential_fusion = (f32[2,256,10]{1,2,0:T(8,128)}, f32[2,256,10]{1,2,0:T(8,128)S(1)}, f32[2,10,256]{2,1,0:T(8,128)}, f32[2,10,256]{2,1,0:T(8,128)}, f...) fusion(f32[2,10,256]{2,1,0:T(8,128)S(1)} %fusion.57, f32[10]{0:T(128)} %param.19, f32[2,256,10]{1,0,2:T(2,128)S(1)} %squeeze.53, ...), kind=kLoop, calls=%fused_computation.160 | loop fusion | flops 92160 | bytes 205000 | tf_op jit(solution)/shard_map/exp | solution.py:96
  9.0 2.3 %copy.21 = bf16[512,640]{0,1:T(8,128)(2,1)} copy(bf16[512,640]{1,0:T(8,128)(2,1)} %param.14) | data formatting | bytes 1310720 | tf_op args[0]
  11.3 2.7 %reshape_reshape.4 = bf16[2,256,10,64]{1,0,3,2:T(2,128)(2,1)} reshape(bf16[512,640]{0,1:T(8,128)(2,1)} %copy.21) | data formatting | bytes 1310720 | tf_op jit(solution)/shard_map/reshape;reshape | solution.py:26
  13.9 1.8 %convert_multiply_fusion.1 = (f32[2,256,10,64]{1,0,3,2:T(2,128)S(1)}, f32[2,256,10,64]{1,0,3,2:T(2,128)S(1)}) fusion(bf16[2,256,10,64]{1,0,3,2:T(2,128)(2,1)} %reshape_reshape.4, f32[2,256,10]{1,0,2:T(2,128)} %copy.27, f32[2,256,10]{1,0,2:T(2,128)} %copy.23), kind=kLoop, calls=%fused_computation.18 | loop fusion | flops 983040 | bytes 3317760 | tf_op jit(solution)/shard_map/mul | solution.py:49
  19.0 5.7 %collective-permute-start = (f32[10,64,128]{2,1,0:T(8,128)S(1)}, f32[10,64,128]{2,1,0:T(8,128)S(1)}, u32[]{:S(2)}, u32[]{:S(2)}) collective-permute-start(f32[10,64,128]{2,1,0:T(8,128)S(1)} %get-tuple-element.10), channel_id=1, source_target_pairs={{0,4},{4,8},{8,12},{1,5},{5,9},{9,13},{2,6},{6,10},{10,14},{3,7},{... | collective-permute-start | bytes 983048 | tf_op jit(solution)/shard_map/ppermute | solution.py:20
  25.5 2.7 %fusion.14 = f32[2,256,10,64]{1,3,2,0:T(8,128)} fusion(f32[2,10,256]{2,1,0:T(8,128)S(1)} %copy-done.19, f32[2,10,256]{2,1,0:T(8,128)S(1)} %copy-done.15, f32[2,256,256]{2,1,0:T(8,128)S(1)} %fusion.107, pred[256,256]{1,0:T(8,128)(4,1)S(1)} %iota_compare_fusion, bf16[2,256,10,64]{1,0,3,2:T(2,128)(2,1)S(1)} %copy-done.3), kind=kOutput, calls=%fused_computation.20 | convolution fusion | flops 174325760 | bytes 2596864 | tf_op jit(solution)/shard_map/bhts,bshp->bthp/dot_general | solution.py:47
  28.1 2.6 %fusion.15 = f32[2,256,10,64]{1,3,2,0:T(8,128)} fusion(f32[2,10,256]{2,1,0:T(8,128)S(1)} %copy-done.18, f32[2,10,256]{2,1,0:T(8,128)S(1)} %copy-done.17, f32[2,256,256]{2,1,0:T(8,128)S(1)} %fusion.106, pred[256,256]{1,0:T(8,128)(4,1)S(1)} %iota_compare_fusion.1, bf16[2,256,10,64]{1,0,3,2:T(2,128)(2,1)S(1)} %copy-done.3), kind=kOutput, calls=%fused_computation.21 | convolution fusion | flops 174325760 | bytes 2596864 | tf_op jit(solution)/shard_map/bhts,bshp->bthp/dot_general | solution.py:47
  31.7 4.4 %collective-permute-start.1 = (f32[10,64,128]{2,1,0:T(8,128)S(1)}, f32[10,64,128]{2,1,0:T(8,128)S(1)}, u32[]{:S(2)}, u32[]{:S(2)}) collective-permute-start(f32[10,64,128]{2,1,0:T(8,128)S(1)} %multiply_add_fusion.3), channel_id=1, source_target_pairs={{0,4},{4,8},{8,12},{1,5},{5,9},{9,13},{2,6},{6,10},{10,14},{3,7},{... | collective-permute-start | bytes 983048 | tf_op jit(solution)/shard_map/ppermute | solution.py:20
  38.3 3.8 %collective-permute-done.1 = f32[10,64,128]{2,1,0:T(8,128)S(1)} collective-permute-done((f32[10,64,128]{2,1,0:T(8,128)S(1)}, f32[10,64,128]{2,1,0:T(8,128)S(1)}, u32[]{:S(2)}, u32[]{:S(2)}) %collective-permute-start.1) | collective-permute-done | bytes 327712 | tf_op jit(solution)/shard_map/ppermute | solution.py:20
  43.0 5.1 %collective-permute-start.2 = (f32[10,64,128]{2,1,0:T(8,128)}, f32[10,64,128]{2,1,0:T(8,128)}, u32[]{:S(2)}, u32[]{:S(2)}) collective-permute-start(f32[10,64,128]{2,1,0:T(8,128)} %multiply_add_fusion.2), channel_id=1, source_target_pairs={{0,4},{4,8},{8,12},{1,5},{5,9},{9,13},{2,6},{6,10},{10,14},{3,7},{... | collective-permute-start | bytes 983048 | tf_op jit(solution)/shard_map/ppermute | solution.py:20
  48.9 1.5 %collective-permute-start.5 = (f32[10,64,128]{2,1,0:T(8,128)}, f32[10,64,128]{2,1,0:T(8,128)}, u32[]{:S(2)}, u32[]{:S(2)}) collective-permute-start(f32[10,64,128]{2,1,0:T(8,128)} %multiply_add_fusion), channel_id=1, source_target_pairs={{4,0},{8,4},{12,8},{5,1},{9,5},{13,9},{6,2},{10,6},{14,10},{7,3},{... | collective-permute-start | bytes 983048 | tf_op jit(solution)/shard_map/ppermute | solution.py:20
  51.4 1.4 %collective-permute-done.2 = f32[10,64,128]{2,1,0:T(8,128)} collective-permute-done((f32[10,64,128]{2,1,0:T(8,128)}, f32[10,64,128]{2,1,0:T(8,128)}, u32[]{:S(2)}, u32[]{:S(2)}) %collective-permute-start.2) | collective-permute-done | bytes 327712 | tf_op jit(solution)/shard_map/ppermute | solution.py:20
  52.9 2.4 %fusion.20 = f32[2,256,10,64]{1,3,2,0:T(8,128)S(1)} fusion(f32[2,256,10,64]{1,3,2,0:T(8,128)} %fusion.15, bf16[2,256,128,1]{2,1,3,0:T(8,128)(2,1)S(1)} %bitcast.183, f32[1,10,64,128]{3,2,1,0:T(8,128)} %slice_add_fusion.1, f32[2,256,10]{1,2,0:T(8,128)S(1)} %copy-done.12, f32[10,64,128]{2,1,0:T(8,128)} %collective-permute-done.2, f32[2,10]{1,0:T(2,128)S(1)} %stack.91), kind=kOutput, calls=%fused_computation.28 | convolution fusion | flops 504299520 | bytes 3428432 | tf_op jit(solution)/shard_map/btn,bhpn->bthp/dot_general | solution.py:95
  55.3 3.2 %collective-permute-done.5 = f32[10,64,128]{2,1,0:T(8,128)} collective-permute-done((f32[10,64,128]{2,1,0:T(8,128)}, f32[10,64,128]{2,1,0:T(8,128)}, u32[]{:S(2)}, u32[]{:S(2)}) %collective-permute-start.5) | collective-permute-done | bytes 327712 | tf_op jit(solution)/shard_map/ppermute | solution.py:20
  58.5 1.8 %fusion.18 = f32[2,256,10,64]{1,3,2,0:T(8,128)S(1)} fusion(f32[2,256,10,64]{1,3,2,0:T(8,128)S(1)} %fusion.20, f32[2,256,10,64]{1,3,2,0:T(8,128)S(1)} %copy-done.4, bf16[2,256,128,1]{2,1,3,0:T(8,128)(2,1)S(1)} %bitcast.189, f32[1,10,64,128]{3,2,1,0:T(8,128)S(1)} %copy-done.5, f32[2,256,10]{1,2,0:T(8,128)S(1)} %copy-done.13, ...), kind=kOutput, calls=%fused_computation.25 | convolution fusion | flops 504627200 | bytes 4739152 | tf_op jit(solution)/shard_map/btn,bhpn->bthp/dot_general | solution.py:95
  62.6 2.8 %copy.30 = f32[512,640]{1,0:T(8,128)} copy(f32[512,640]{0,1:T(8,128)} %bitcast.180) | data formatting | bytes 2621440 | tf_op jit(solution)/shard_map/add | solution.py:203
  65.4 2.3 %multiply_reduce_fusion.1 = (f32[512]{0:T(512)S(1)}, f32[512,640]{1,0:T(8,128)S(1)}) fusion(bf16[512,640]{1,0:T(8,128)(2,1)} %param.15, f32[512,640]{1,0:T(8,128)} %copy.30, bf16[512,640]{1,0:T(8,128)(2,1)} %param.14, f32[640]{0:T(1024)S(1)} %mul.340), kind=kLoop, calls=%fused_computation.41 | loop fusion | flops 3603968 | bytes 3936768 | tf_op jit(solution)/shard_map/reduce_sum | solution.py:207
  72.5 2.5 %collective-permute-done.7 = f32[128,2560]{1,0:T(8,128)S(1)} collective-permute-done((f32[128,2560]{1,0:T(8,128)S(1)}, f32[128,2560]{1,0:T(8,128)S(1)}, u32[]{:S(2)}, u32[]{:S(2)}) %collective-permute-start.7) | collective-permute-done | bytes 1310752 | tf_op jit(solution)/shard_map/ppermute | solution.py:102
  76.9 29.2 %collective-permute-done.8 = f32[128,2560]{1,0:T(8,128)S(1)} collective-permute-done((f32[128,2560]{1,0:T(8,128)S(1)}, f32[128,2560]{1,0:T(8,128)S(1)}, u32[]{:S(2)}, u32[]{:S(2)}) %collective-permute-start.8) | collective-permute-done | bytes 1310752 | tf_op jit(solution)/shard_map/ppermute | solution.py:102
  109.0 2.4 %fusion.36 = bf16[1,1,128,512]{3,2,1,0:T(8,128)(2,1)S(1)} fusion(bf16[128,2560]{1,0:T(8,128)(2,1)} %multiply_convert_fusion.8, bf16[2560,512]{1,0:T(8,128)(2,1)} %param.27), kind=kOutput, calls=%fused_computation.57 | convolution fusion | flops 335609856 | bytes 3407872 | tf_op jit(solution)/shard_map/dot_general | solution.py:153
  111.4 1.6 %fusion.32 = bf16[1,1,128,512]{3,2,1,0:T(8,128)(2,1)S(1)} fusion(bf16[128,2560]{1,0:T(8,128)(2,1)} %multiply_convert_fusion.8, bf16[2560,512]{1,0:T(8,128)(2,1)S(1)} %copy-done.1), kind=kOutput, calls=%fused_computation.53 | convolution fusion | flops 335609856 | bytes 3407872 | tf_op jit(solution)/shard_map/dot_general | solution.py:152
  113.0 1.7 %fusion.31 = bf16[1,1,128,512]{3,2,1,0:T(8,128)(2,1)S(1)} fusion(bf16[128,2560]{1,0:T(8,128)(2,1)} %collective-permute-done.11, bf16[2560,512]{1,0:T(8,128)(2,1)S(1)} %copy-done.1), kind=kOutput, calls=%fused_computation.52 | convolution fusion | flops 335609856 | bytes 3407872 | tf_op jit(solution)/shard_map/dot_general | solution.py:152
  115.0 1.6 %fusion.35 = bf16[1,1,128,512]{3,2,1,0:T(8,128)(2,1)S(1)} fusion(bf16[128,2560]{1,0:T(8,128)(2,1)} %collective-permute-done.11, bf16[2560,512]{1,0:T(8,128)(2,1)S(1)} %copy-done.2), kind=kOutput, calls=%fused_computation.56 | convolution fusion | flops 335609856 | bytes 3407872 | tf_op jit(solution)/shard_map/dot_general | solution.py:153
  116.6 8.7 %collective-permute-done.9 = bf16[128,2560]{1,0:T(8,128)(2,1)S(1)} collective-permute-done((bf16[128,2560]{1,0:T(8,128)(2,1)}, bf16[128,2560]{1,0:T(8,128)(2,1)S(1)}, u32[]{:S(2)}, u32[]{:S(2)}) %collective-permute-start.9) | collective-permute-done | bytes 655392 | tf_op jit(solution)/shard_map/ppermute | solution.py:102
  (124 shorter events, 33.3 us)
Async XLA Ops:
  0.6 67.8 %copy-start = (bf16[640,2560]{1,0:T(8,128)(2,1)S(1)}, bf16[640,2560]{1,0:T(8,128)(2,1)}, u32[]{:S(2)}) copy-start(bf16[640,2560]{1,0:T(8,128)(2,1)} %param.23) | copy-start | bytes 9830404
  9.0 9.0 %copy-start.6 = (bf16[1,512,128]{2,1,0:T(8,128)(2,1)}, bf16[1,512,128]{2,1,0:T(8,128)(2,1)S(1)}, u32[]{:S(2)}) copy-start(bf16[1,512,128]{2,1,0:T(8,128)(2,1)S(1)} %get-tuple-element.21) | copy-start | bytes 393220
  16.7 19.4 %collective-permute-start.3 = (f32[10,64,128]{2,1,0:T(8,128)S(1)}, f32[10,64,128]{2,1,0:T(8,128)S(1)}, u32[]{:S(2)}, u32[]{:S(2)}) collective-permute-start(f32[10,64,128]{2,1,0:T(8,128)S(1)} %get-tuple-element.6), channel_id=1, source_target_pairs={{4,0},{8,4},{12,8},{5,1},{9,5},{13,9},{6,2},{10,6},{14,10},{7,3},{... | collective-permute-start | bytes 983048 | tf_op jit(solution)/shard_map/ppermute | solution.py:20
  18.0 6.7 %copy-start.11 = (bf16[2,512,128]{2,1,0:T(8,128)(2,1)S(1)}, bf16[2,512,128]{2,1,0:T(8,128)(2,1)}, u32[]{:S(2)}) copy-start(bf16[2,512,128]{2,1,0:T(8,128)(2,1)} %param.17) | copy-start | bytes 786436
  18.8 6.0 %copy-start.7 = (bf16[1,512,128]{2,1,0:T(8,128)(2,1)S(1)}, bf16[1,512,128]{2,1,0:T(8,128)(2,1)}, u32[]{:S(2)}) copy-start(bf16[1,512,128]{2,1,0:T(8,128)(2,1)} %copy-done.6) | copy-start | bytes 393220
  18.9 6.5 %copy-start.3 = (bf16[2,256,10,64]{1,0,3,2:T(2,128)(2,1)S(1)}, bf16[2,256,10,64]{1,0,3,2:T(2,128)(2,1)}, u32[]{:S(2)}) copy-start(bf16[2,256,10,64]{1,0,3,2:T(2,128)(2,1)} %reshape_reshape.4) | copy-start | bytes 1966084
  18.9 6.5 %copy-start.15 = (f32[2,10,256]{2,1,0:T(8,128)S(1)}, f32[2,10,256]{2,1,0:T(8,128)}, u32[]{:S(2)}) copy-start(f32[2,10,256]{2,1,0:T(8,128)} %copy-done.14) | copy-start | bytes 61444
  18.9 6.5 %copy-start.19 = (f32[2,10,256]{2,1,0:T(8,128)S(1)}, f32[2,10,256]{2,1,0:T(8,128)}, u32[]{:S(2)}) copy-start(f32[2,10,256]{2,1,0:T(8,128)} %get-tuple-element.29) | copy-start | bytes 61444
  19.0 12.6 %collective-permute-start = (f32[10,64,128]{2,1,0:T(8,128)S(1)}, f32[10,64,128]{2,1,0:T(8,128)S(1)}, u32[]{:S(2)}, u32[]{:S(2)}) collective-permute-start(f32[10,64,128]{2,1,0:T(8,128)S(1)} %get-tuple-element.10), channel_id=1, source_target_pairs={{0,4},{4,8},{8,12},{1,5},{5,9},{9,13},{2,6},{6,10},{10,14},{3,7},{... | collective-permute-start | bytes 983048 | tf_op jit(solution)/shard_map/ppermute | solution.py:20
  31.7 10.5 %collective-permute-start.1 = (f32[10,64,128]{2,1,0:T(8,128)S(1)}, f32[10,64,128]{2,1,0:T(8,128)S(1)}, u32[]{:S(2)}, u32[]{:S(2)}) collective-permute-start(f32[10,64,128]{2,1,0:T(8,128)S(1)} %multiply_add_fusion.3), channel_id=1, source_target_pairs={{0,4},{4,8},{8,12},{1,5},{5,9},{9,13},{2,6},{6,10},{10,14},{3,7},{... | collective-permute-start | bytes 983048 | tf_op jit(solution)/shard_map/ppermute | solution.py:20
  36.2 11.9 %collective-permute-start.4 = (f32[10,64,128]{2,1,0:T(8,128)S(1)}, f32[10,64,128]{2,1,0:T(8,128)S(1)}, u32[]{:S(2)}, u32[]{:S(2)}) collective-permute-start(f32[10,64,128]{2,1,0:T(8,128)S(1)} %multiply_add_fusion.1), channel_id=1, source_target_pairs={{4,0},{8,4},{12,8},{5,1},{9,5},{13,9},{6,2},{10,6},{14,10},{7,3},{... | collective-permute-start | bytes 983048 | tf_op jit(solution)/shard_map/ppermute | solution.py:20
  38.3 12.9 %copy-start.24 = (f32[10]{0:T(128)S(1)}, f32[10]{0:T(128)}, u32[]{:S(2)}) copy-start(f32[10]{0:T(128)} %param.21) | copy-start | bytes 124
  38.3 13.0 %copy-start.23 = (f32[1,10]{1,0:T(1,128)S(1)}, f32[1,10]{1,0:T(1,128)}, u32[]{:S(2)}) copy-start(f32[1,10]{1,0:T(1,128)} %get-tuple-element.30) | copy-start | bytes 124
  38.3 14.5 %copy-start.12 = (f32[2,256,10]{1,2,0:T(8,128)S(1)}, f32[2,256,10]{1,2,0:T(8,128)}, u32[]{:S(2)}) copy-start(f32[2,256,10]{1,2,0:T(8,128)} %get-tuple-element.38) | copy-start | bytes 61444
  43.0 9.9 %collective-permute-start.2 = (f32[10,64,128]{2,1,0:T(8,128)}, f32[10,64,128]{2,1,0:T(8,128)}, u32[]{:S(2)}, u32[]{:S(2)}) collective-permute-start(f32[10,64,128]{2,1,0:T(8,128)} %multiply_add_fusion.2), channel_id=1, source_target_pairs={{0,4},{4,8},{8,12},{1,5},{5,9},{9,13},{2,6},{6,10},{10,14},{3,7},{... | collective-permute-start | bytes 983048 | tf_op jit(solution)/shard_map/ppermute | solution.py:20
  48.9 9.6 %collective-permute-start.5 = (f32[10,64,128]{2,1,0:T(8,128)}, f32[10,64,128]{2,1,0:T(8,128)}, u32[]{:S(2)}, u32[]{:S(2)}) collective-permute-start(f32[10,64,128]{2,1,0:T(8,128)} %multiply_add_fusion), channel_id=1, source_target_pairs={{4,0},{8,4},{12,8},{5,1},{9,5},{13,9},{6,2},{10,6},{14,10},{7,3},{... | collective-permute-start | bytes 983048 | tf_op jit(solution)/shard_map/ppermute | solution.py:20
  52.9 5.7 %copy-start.9 = (bf16[1,512,128]{2,1,0:T(8,128)(2,1)S(1)}, bf16[1,512,128]{2,1,0:T(8,128)(2,1)}, u32[]{:S(2)}) copy-start(bf16[1,512,128]{2,1,0:T(8,128)(2,1)} %copy-done.8) | copy-start | bytes 393220
  52.9 5.7 %copy-start.13 = (f32[2,256,10]{1,2,0:T(8,128)S(1)}, f32[2,256,10]{1,2,0:T(8,128)}, u32[]{:S(2)}) copy-start(f32[2,256,10]{1,2,0:T(8,128)} %get-tuple-element.24) | copy-start | bytes 61444
  71.9 3.1 %collective-permute-start.7 = (f32[128,2560]{1,0:T(8,128)S(1)}, f32[128,2560]{1,0:T(8,128)S(1)}, u32[]{:S(2)}, u32[]{:S(2)}) collective-permute-start(f32[128,2560]{1,0:T(8,128)S(1)} %get-tuple-element.17), channel_id=1, source_target_pairs={{0,1},{1,0},{2,3},{3,2},{4,5},{5,4},{6,7},{7,6},{8,9},{9,8},{10,11... | collective-permute-start | bytes 3932168 | tf_op jit(solution)/shard_map/ppermute | solution.py:102
  72.0 4.9 %collective-permute-start.6 = (f32[128,2560]{1,0:T(8,128)S(1)}, f32[128,2560]{1,0:T(8,128)S(1)}, u32[]{:S(2)}, u32[]{:S(2)}) collective-permute-start(f32[128,2560]{1,0:T(8,128)S(1)} %get-tuple-element.14), channel_id=1, source_target_pairs={{0,1},{1,0},{2,3},{3,2},{4,5},{5,4},{6,7},{7,6},{8,9},{9,8},{10,11... | collective-permute-start | bytes 3932168 | tf_op jit(solution)/shard_map/ppermute | solution.py:102
  75.2 30.9 %collective-permute-start.8 = (f32[128,2560]{1,0:T(8,128)S(1)}, f32[128,2560]{1,0:T(8,128)S(1)}, u32[]{:S(2)}, u32[]{:S(2)}) collective-permute-start(f32[128,2560]{1,0:T(8,128)S(1)} %add.220), channel_id=1, source_target_pairs={{0,2},{2,0},{1,3},{3,1},{4,6},{6,4},{5,7},{7,5},{8,10},{10,8},{9,1... | collective-permute-start | bytes 3932168 | tf_op jit(solution)/shard_map/ppermute | solution.py:102
  107.9 5.1 %collective-permute-start.11 = (bf16[128,2560]{1,0:T(8,128)(2,1)}, bf16[128,2560]{1,0:T(8,128)(2,1)}, u32[]{:S(2)}, u32[]{:S(2)}) collective-permute-start(bf16[128,2560]{1,0:T(8,128)(2,1)} %multiply_convert_fusion.8), channel_id=1, source_target_pairs={{0,1},{1,0},{2,3},{3,2},{4,5},{5,4},{6,7},{7,6},{8,9},{9,8},{10,11... | collective-permute-start | bytes 1966088 | tf_op jit(solution)/shard_map/ppermute | solution.py:102
  107.9 17.4 %collective-permute-start.9 = (bf16[128,2560]{1,0:T(8,128)(2,1)}, bf16[128,2560]{1,0:T(8,128)(2,1)S(1)}, u32[]{:S(2)}, u32[]{:S(2)}) collective-permute-start(bf16[128,2560]{1,0:T(8,128)(2,1)} %multiply_convert_fusion.8), channel_id=1, source_target_pairs={{0,2},{2,0},{1,3},{3,1},{4,6},{6,4},{5,7},{7,5},{8,10},{10,8},{9,1... | collective-permute-start | bytes 1966088 | tf_op jit(solution)/shard_map/ppermute | solution.py:102
  125.3 2.1 %collective-permute-start.10 = (bf16[128,2560]{1,0:T(8,128)(2,1)S(1)}, bf16[128,2560]{1,0:T(8,128)(2,1)S(1)}, u32[]{:S(2)}, u32[]{:S(2)}) collective-permute-start(bf16[128,2560]{1,0:T(8,128)(2,1)S(1)} %collective-permute-done.9), channel_id=1, source_target_pairs={{0,1},{1,0},{2,3},{3,2},{4,5},{5,4},{6,7},{7,6},{8,9},{9,8},{10,11... | collective-permute-start | bytes 1966088 | tf_op jit(solution)/shard_map/ppermute | solution.py:102
  (13 other events, 32.7 us)
